TPU v7x, 32 devices: a whole 2x2x4 slice. The times are simulated.
32 devices in a mesh: gz: 2 (over x), gy: 4 (over z), gx: 4 (over y, core).
Axes of the slice: x: 2, y: 2, z: 4, core: 2. Of those that a mesh axis runs over, the one named last changes fastest.
Arguments:
- earlier_window_curl_state: float32 [2, 16, 512, 512], P(None, 'gz', 'gy', 'gx'), may hold values from -6 to 6
- material_resistivity_inverse: float32 [16, 512, 512], P('gz', 'gy', 'gx'), may hold values from 0.5 to 5
- winding_current_pattern: float32 [2, 512, 512], P(None, 'gy', 'gx'), may hold values from -8 to 8
- winding_axial_centre: int32 [1], replicated, may hold values from 0 to 15
- specimen_presence_flags: int32 [2, 64, 64], replicated, may hold values 0 or 1
- specimen_kelvin_values: float32 [16, 512, 384], P('gz', 'gy'), may hold values from -4 to 4
Outputs:
- potential_out: float32 [2, 16, 512, 512], P(None, 'gz', 'gy', 'gx')
- temperature_out: float32 [16, 512, 384], P('gz', 'gy')
All inputs are finite; a program needn't handle non-finite values.
Results may differ from a plain program's by a relative error of at most 0.00002.
Values sent between devices are 32-bit elements; how exact they have to be, the bound alone decides.
No kernel may reach another device: no remote copies, remote signals or barrier semaphores. Data moves between devices by JAX's collectives and lax.ppermute only.
A program may use at most 128 MiB of HBM per device.

v0:
```python
import jax
import jax.numpy as jnp
from jax import lax
from jax.sharding import PartitionSpec as P

MB = 8
STEPS = 4


WEIGHTS = (0.8, 1.0, 1.25)
SHIFT = 0.2
HEATING = 0.02
CONDUCT = 0.16
SOFTEN = 0.25


def padded(value, sides, width):
    for axis, dim in sides:
        peers, length = (lax.axis_size(axis), value.shape[dim])
        up = [(i, (i + 1) % peers) for i in range(peers - 1)]
        down = [(j, i) for i, j in up]
        last = lax.slice_in_dim(value, length - width, length, axis=dim)
        first = lax.slice_in_dim(value, 0, width, axis=dim)
        before = lax.ppermute(last, axis, up)
        after = lax.ppermute(first, axis, down)
        value = jnp.concatenate([before, value, after], axis=dim)
    return value


def expand_blocks(blocks):
    cells = jnp.repeat(blocks, MB, axis=0)
    cells = jnp.repeat(cells, MB, axis=1)
    return jnp.repeat(cells, MB, axis=2).astype(jnp.float32)


def neighbours(bordered_segment):
    total = bordered_segment[:, 2:, 1:-1, 1:-1] + bordered_segment[:, :-2, 1:-1, 1:-1]
    total = total + bordered_segment[:, 1:-1, 2:, 1:-1] + bordered_segment[:, 1:-1, :-2, 1:-1]
    return total + bordered_segment[:, 1:-1, 1:-1, 2:] + bordered_segment[:, 1:-1, 1:-1, :-2]


def relax(magnetic_curl_state, beside, source, coupling, factor):
    diagonal = 6.0 + SHIFT
    real_res = source[0] - (
        diagonal * magnetic_curl_state[0] - coupling * magnetic_curl_state[1] - beside[0]
    )
    imag_res = source[1] - (
        diagonal * magnetic_curl_state[1] + coupling * magnetic_curl_state[0] - beside[1]
    )
    scaled = factor / (diagonal * diagonal + coupling * coupling)
    return jnp.stack(
        [
            magnetic_curl_state[0] + scaled * (diagonal * real_res + coupling * imag_res),
            magnetic_curl_state[1] + scaled * (diagonal * imag_res - coupling * real_res),
        ]
    )


def six_faces(array):
    return [
        array[2:, 1:-1, 1:-1],
        array[:-2, 1:-1, 1:-1],
        array[1:-1, 2:, 1:-1],
        array[1:-1, :-2, 1:-1],
        array[1:-1, 1:-1, 2:],
        array[1:-1, 1:-1, :-2],
    ]


def diffusivity_coefficient(bordered_segment, bordered_segment_flags, ohmic_dissipation):
    centre = bordered_segment[1:-1, 1:-1, 1:-1]
    centre_mask = bordered_segment_flags[1:-1, 1:-1, 1:-1]
    centre_kappa = 1.0 / (1.0 + SOFTEN * centre * centre)
    flux = jnp.zeros_like(centre)
    for other, other_mask in zip(six_faces(bordered_segment), six_faces(bordered_segment_flags)):
        kappa = 1.0 / (1.0 + SOFTEN * other * other)
        flux = flux + other_mask * (centre_kappa + kappa) * (other - centre)
    return centre + 0.5 * CONDUCT * centre_mask * flux + ohmic_dissipation


def thermal_mask(
    specimen_presence_flags, z_start, row_start, depth, rows, specimen_column_sum, column_offset
):
    window = jnp.pad(specimen_presence_flags[:, :, column_offset // MB :], 1)
    blocks = lax.dynamic_slice(
        window,
        (z_start // MB, row_start // MB, 0),
        (depth // MB + 2, rows // MB + 2, window.shape[2]),
    )
    cells = expand_blocks(blocks)
    return cells[
        MB - 1 : MB + 1 + depth, MB - 1 : MB + 1 + rows, MB - 1 : MB + 1 + specimen_column_sum
    ]


def coil_profile(first, count, winding_axial_centre, coil_width):
    axial = (
        (first + jnp.arange(count)).astype(jnp.float32)
        - winding_axial_centre[0].astype(jnp.float32)
    ) / coil_width
    return 1.0 / (1.0 + axial * axial)


def on_device(
    earlier_window_curl_state,
    material_resistivity_inverse,
    winding_current_pattern,
    winding_axial_centre,
    specimen_presence_flags,
    specimen_kelvin_values,
):
    depth, height, breadth = material_resistivity_inverse.shape
    z_total = depth * lax.axis_size("gz")
    x_total = breadth * lax.axis_size("gx")
    z_start = lax.axis_index("gz") * depth
    y_start = lax.axis_index("gy") * height
    x_start = lax.axis_index("gx") * breadth
    own_blocks = lax.dynamic_slice(
        specimen_presence_flags,
        (z_start // MB, y_start // MB, x_start // MB),
        (depth // MB, height // MB, breadth // MB),
    )
    coupling = expand_blocks(own_blocks) * material_resistivity_inverse
    coil_width = z_total // 4
    magnetic_curl_state = earlier_window_curl_state
    profile = coil_profile(z_start, depth, winding_axial_centre, coil_width)
    source = profile[None, :, None, None] * winding_current_pattern[:, None, :, :]
    for factor in WEIGHTS:
        bordered_segment = padded(magnetic_curl_state, (("gz", 1), ("gy", 2), ("gx", 3)), 1)
        magnetic_curl_state = relax(
            magnetic_curl_state, neighbours(bordered_segment), source, coupling, factor
        )
    ohmic_dissipation = (
        HEATING
        * coupling
        * (
            magnetic_curl_state[0] * magnetic_curl_state[0]
            + magnetic_curl_state[1] * magnetic_curl_state[1]
        )
    )
    specimen_column_sum = specimen_kelvin_values.shape[2]
    column_offset = x_total - specimen_column_sum
    rows = height // lax.axis_size("gx")
    moved = lax.all_to_all(ohmic_dissipation, "gx", split_axis=1, concat_axis=2, tiled=True)
    block_heat_source = moved[:, :, column_offset:]
    row_start = y_start + lax.axis_index("gx") * rows
    segment_kelvin = lax.dynamic_slice_in_dim(
        specimen_kelvin_values, lax.axis_index("gx") * rows, rows, 1
    )
    bordered_segment_flags = thermal_mask(
        specimen_presence_flags, z_start, row_start, depth, rows, specimen_column_sum, column_offset
    )
    for number in range(STEPS):
        bordered_segment = padded(segment_kelvin, (("gz", 0), (("gy", "gx"), 1)), 1)
        segment_kelvin = diffusivity_coefficient(
            jnp.pad(bordered_segment, ((0, 0), (0, 0), (1, 1))),
            bordered_segment_flags,
            block_heat_source,
        )
    segment_kelvin = lax.all_gather(segment_kelvin, "gx", axis=1, tiled=True)
    return (magnetic_curl_state, segment_kelvin)


def solution(mesh):
    placed = (
        P(None, "gz", "gy", "gx"),
        P("gz", "gy", "gx"),
        P(None, "gy", "gx"),
        P(),
        P(),
        P("gz", "gy", None),
    )
    return jax.shard_map(
        on_device,
        mesh=mesh,
        in_specs=placed,
        out_specs=(P(None, "gz", "gy", "gx"), P("gz", "gy", None)),
        check_vma=False,
    )
```

profile of v0, /device:TPU:0, one launch (start us, length us, event | category | flops | bytes accessed | tf_op | source)
XLA Modules:
  0.0 264.0 jit_solution(12692609611169328279)
XLA Ops:
  9.9 5.0 %collective-permute-start.1 = (f32[2,1,128,128]{3,0,2,1:T(2,128)S(1)}, f32[2,1,128,128]{3,0,2,1:T(2,128)S(1)}, u32[]{:S(2)}, u32[]{:S(2)}) collective-permute-start(f32[2,1,128,128]{3,0,2,1:T(2,128)S(1)} %get-tuple-element.49), channel_id=1, source_target_pairs={{0,16},{1,17},{2,18},{3,19},{4,20},{5,21},{6,22},{7,23},{8,24},{9,... | collective-permute-start | bytes 393224 | tf_op jit(solution)/shard_map/ppermute | solution.py:24
  18.8 3.3 %collective-permute-done = f32[2,1,128,128]{3,0,2,1:T(2,128)} collective-permute-done((f32[2,1,128,128]{3,0,2,1:T(2,128)}, f32[2,1,128,128]{3,0,2,1:T(2,128)}, u32[]{:S(2)}, u32[]{:S(2)}) %collective-permute-start) | collective-permute-done | bytes 131104 | tf_op jit(solution)/shard_map/ppermute | solution.py:25
  24.9 5.1 %collective-permute-start.3 = (f32[2,10,1,128]{3,0,2,1:T(2,128)}, f32[2,10,1,128]{3,0,2,1:T(2,128)}, u32[]{:S(2)}, u32[]{:S(2)}) collective-permute-start(f32[2,10,1,128]{3,0,2,1:T(2,128)} %get-tuple-element.40), channel_id=1, source_target_pairs={{0,4},{4,8},{8,12},{1,5},{5,9},{9,13},{2,6},{6,10},{10,14},{3,7},{... | collective-permute-start | bytes 30728 | tf_op jit(solution)/shard_map/ppermute | solution.py:24
  33.6 3.0 %fusion.213 = (f32[2,10,130,1]{3,0,2,1:T(2,128)}, f32[2,10,130,1]{3,0,2,1:T(2,128)}) fusion(f32[2,10,130,128]{3,0,2,1:T(2,128)S(1)} %pad_maximum_fusion.2), kind=kLoop, calls=%fused_computation.410 | loop fusion | bytes 41600 | tf_op jit(solution)/shard_map/slice | solution.py:23
  36.5 2.5 copy.250
  40.3 2.5 copy.252
  42.9 3.6 %collective-permute-start.5 = (f32[2,10,130,1]{2,0,3,1:T(2,128)}, f32[2,10,130,1]{2,0,3,1:T(2,128)}, u32[]{:S(2)}, u32[]{:S(2)}) collective-permute-start(f32[2,10,130,1]{2,0,3,1:T(2,128)} %copy.252), channel_id=1, source_target_pairs={{0,1},{1,2},{2,3},{4,5},{5,6},{6,7},{8,9},{9,10},{10,11},{12,13},{... | collective-permute-start | bytes 31208 | tf_op jit(solution)/shard_map/ppermute | solution.py:24
  46.6 2.4 copy.251
  49.1 2.4 copy.253
  51.5 7.2 %fusion.10 = f32[2,8,128,128]{3,0,2,1:T(2,128)S(1)} fusion(f32[2,10,130,1]{3,0,2,1:T(2,128)} %copy.253, f32[2,10,1,128]{3,0,2,1:T(2,128)S(1)} %collective-permute-done.2, f32[2,10,128,128]{3,0,2,1:T(2,128)S(1)} %constant_dynamic-update-slice_fusion, f32[2,10,1,128]{3,0,2,1:T(2,128)} %collective-permute-done.3, f32[2,10,130,1]{3,0,2,1:T(2,128)} %copy.251, ...), kind=kLoop, calls=%fused_computation.65 | loop fusion | flops 3932160 | bytes 3711296 | tf_op jit(solution)/shard_map/add | solution.py:39
  61.5 4.6 %collective-permute-start.7 = (f32[2,1,128,128]{3,2,1,0:T(8,128)S(1)}, f32[2,1,128,128]{3,2,1,0:T(8,128)S(1)}, u32[]{:S(2)}, u32[]{:S(2)}) collective-permute-start(f32[2,1,128,128]{3,2,1,0:T(8,128)S(1)} %get-tuple-element.44), channel_id=1, source_target_pairs={{0,16},{1,17},{2,18},{3,19},{4,20},{5,21},{6,22},{7,23},{8,24},{9,... | collective-permute-start | bytes 393224 | tf_op jit(solution)/shard_map/ppermute | solution.py:24
  68.8 5.2 %collective-permute-start.19 = (f32[1,32,384]{2,1,0:T(8,128)}, f32[1,32,384]{2,1,0:T(8,128)}, u32[]{:S(2)}, u32[]{:S(2)}) collective-permute-start(f32[1,32,384]{2,1,0:T(8,128)} %get-tuple-element.28), channel_id=1, source_target_pairs={{0,16},{1,17},{2,18},{3,19},{4,20},{5,21},{6,22},{7,23},{8,24},{9,... | collective-permute-start | bytes 147464 | tf_op jit(solution)/shard_map/ppermute | solution.py:24
  75.4 4.5 %collective-permute-start.9 = (f32[2,10,1,128]{3,0,2,1:T(2,128)S(1)}, f32[2,10,1,128]{3,0,2,1:T(2,128)S(1)}, u32[]{:S(2)}, u32[]{:S(2)}) collective-permute-start(f32[2,10,1,128]{3,0,2,1:T(2,128)S(1)} %copy.257), channel_id=1, source_target_pairs={{0,4},{4,8},{8,12},{1,5},{5,9},{9,13},{2,6},{6,10},{10,14},{3,7},{... | collective-permute-start | bytes 30728 | tf_op jit(solution)/shard_map/ppermute | solution.py:24
  89.0 3.2 %collective-permute-start.11 = (f32[2,10,130,1]{2,0,3,1:T(2,128)S(1)}, f32[2,10,130,1]{2,0,3,1:T(2,128)S(1)}, u32[]{:S(2)}, u32[]{:S(2)}) collective-permute-start(f32[2,10,130,1]{2,0,3,1:T(2,128)S(1)} %copy.263), channel_id=1, source_target_pairs={{0,1},{1,2},{2,3},{4,5},{5,6},{6,7},{8,9},{9,10},{10,11},{12,13},{... | collective-permute-start | bytes 31208 | tf_op jit(solution)/shard_map/ppermute | solution.py:24
  96.7 3.4 %fusion.5 = f32[2,8,128,128]{3,2,1,0:T(8,128)S(1)} fusion(f32[2,10,130,1]{3,2,1,0:T(8,128)} %copy.264, f32[2,10,1,128]{3,2,1,0:T(1,128)S(1)} %copy.256, f32[2,10,1,128]{3,2,1,0:T(1,128)S(1)} %copy.258, f32[2,1,128,128]{3,2,1,0:T(8,128)S(1)} %collective-permute-done.6, f32[2,1,128,128]{3,2,1,0:T(8,128)S(1)} %collective-permute-done.7, ...), kind=kLoop, calls=%fused_computation.36 | loop fusion | flops 7602176 | bytes 2400576 | tf_op jit(solution)/shard_map/add | solution.py:39
  102.0 4.6 %collective-permute-start.13 = (f32[2,1,128,128]{3,2,1,0:T(8,128)S(1)}, f32[2,1,128,128]{3,2,1,0:T(8,128)S(1)}, u32[]{:S(2)}, u32[]{:S(2)}) collective-permute-start(f32[2,1,128,128]{3,2,1,0:T(8,128)S(1)} %get-tuple-element.42), channel_id=1, source_target_pairs={{0,16},{1,17},{2,18},{3,19},{4,20},{5,21},{6,22},{7,23},{8,24},{9,... | collective-permute-start | bytes 393224 | tf_op jit(solution)/shard_map/ppermute | solution.py:24
  106.5 2.5 broadcast_bitcast_fusion
  111.6 4.8 %collective-permute-start.15 = (f32[2,10,1,128]{3,0,2,1:T(2,128)S(1)}, f32[2,10,1,128]{3,0,2,1:T(2,128)S(1)}, u32[]{:S(2)}, u32[]{:S(2)}) collective-permute-start(f32[2,10,1,128]{3,0,2,1:T(2,128)S(1)} %copy.267), channel_id=1, source_target_pairs={{0,4},{4,8},{8,12},{1,5},{5,9},{9,13},{2,6},{6,10},{10,14},{3,7},{... | collective-permute-start | bytes 30728 | tf_op jit(solution)/shard_map/ppermute | solution.py:24
  125.5 3.0 %collective-permute-start.17 = (f32[2,10,130,1]{2,0,3,1:T(2,128)S(1)}, f32[2,10,130,1]{2,0,3,1:T(2,128)S(1)}, u32[]{:S(2)}, u32[]{:S(2)}) collective-permute-start(f32[2,10,130,1]{2,0,3,1:T(2,128)S(1)} %copy.273), channel_id=1, source_target_pairs={{0,1},{1,2},{2,3},{4,5},{5,6},{6,7},{8,9},{9,10},{10,11},{12,13},{... | collective-permute-start | bytes 31208 | tf_op jit(solution)/shard_map/ppermute | solution.py:24
  131.2 3.2 %collective-permute-start.21 = (f32[10,1,384]{2,1,0:T(1,128)}, f32[10,1,384]{2,1,0:T(1,128)S(1)}, u32[]{:S(2)}, u32[]{:S(2)}) collective-permute-start(f32[10,1,384]{2,1,0:T(1,128)} %get-tuple-element.57), channel_id=1, source_target_pairs={{0,1},{1,2},{2,3},{3,4},{4,5},{5,6},{6,7},{7,8},{8,9},{9,10},{10,1... | collective-permute-start | bytes 46088 | tf_op jit(solution)/shard_map/ppermute | solution.py:24
  137.7 3.4 %fusion = f32[2,8,128,128]{3,2,1,0:T(8,128)S(1)} fusion(f32[2,10,130,1]{3,2,1,0:T(8,128)} %copy.274, f32[2,10,1,128]{3,2,1,0:T(1,128)S(1)} %copy.266, f32[2,10,1,128]{3,2,1,0:T(1,128)S(1)} %copy.268, f32[2,1,128,128]{3,2,1,0:T(8,128)S(1)} %collective-permute-done.12, f32[2,1,128,128]{3,2,1,0:T(8,128)S(1)} %collective-permute-done.13, ...), kind=kLoop, calls=%fused_computation.7 | loop fusion | flops 7602176 | bytes 2400576 | tf_op jit(solution)/shard_map/add | solution.py:39
  143.7 4.1 %all-to-all-start = ((f32[8,128,128]{2,0,1:T(8,128)}), f32[8,128,128]{2,0,1:T(8,128)}, u32[]{:S(2)}, u32[]{:S(2)}) async-start(f32[8,128,128]{2,0,1:T(8,128)} %copy.283), calls=%async_computation | async-start | bytes 1048576 | tf_op jit(solution)/shard_map/all_to_all | solution.py:144
  148.1 12.0 %fusion.210 = (f32[8,32,384]{1,2,0:T(8,128)}, f32[8,32,384]{1,2,0:T(8,128)}, f32[8,32,384]{1,2,0:T(8,128)}, f32[8,32,384]{1,2,0:T(8,128)}, f32[8,32,384]{1,2,0:T...) fusion(f32[24,48,400]{1,2,0:T(8,128)} %broadcast_bitcast_fusion), kind=kLoop, calls=%fused_computation.407 | loop fusion | bytes 5505024 | tf_op jit(solution)/shard_map/slice | solution.py:72
  177.3 3.0 %fusion.47 = f32[8,32,384]{2,1,0:T(8,128)S(1)} fusion(f32[8,32,384]{2,1,0:T(8,128)} %copy-done.1, f32[8,32,384]{2,1,0:T(8,128)S(1)} %copy.289, f32[8,32,384]{2,1,0:T(8,128)S(1)} %copy.290, f32[8,32,384]{2,1,0:T(8,128)S(1)} %copy.291, f32[8,32,384]{2,1,0:T(8,128)S(1)} %copy.292, f32[8,32,384]{2,1,0:T(8,128)S(1)} %copy.293, f32[8,32,384]{2,1,0:T(8,128)S(1)} %copy.294, ...), kind=kLoop, calls=%fused_computation.176 | loop fusion | flops 6782976 | bytes 4847616 | tf_op jit(solution)/shard_map/add | solution.py:78
  181.6 4.5 %collective-permute-start.23 = (f32[1,32,384]{2,1,0:T(8,128)S(1)}, f32[1,32,384]{2,1,0:T(8,128)S(1)}, u32[]{:S(2)}, u32[]{:S(2)}) collective-permute-start(f32[1,32,384]{2,1,0:T(8,128)S(1)} %get-tuple-element.62), channel_id=1, source_target_pairs={{0,16},{1,17},{2,18},{3,19},{4,20},{5,21},{6,22},{7,23},{8,24},{9,... | collective-permute-start | bytes 147464 | tf_op jit(solution)/shard_map/ppermute | solution.py:24
  189.2 3.2 %collective-permute-start.25 = (f32[10,1,384]{2,1,0:T(1,128)S(1)}, f32[10,1,384]{2,1,0:T(1,128)S(1)}, u32[]{:S(2)}, u32[]{:S(2)}) collective-permute-start(f32[10,1,384]{2,1,0:T(1,128)S(1)} %get-tuple-element.55), channel_id=1, source_target_pairs={{0,1},{1,2},{2,3},{3,4},{4,5},{5,6},{6,7},{7,8},{8,9},{9,10},{10,1... | collective-permute-start | bytes 46088 | tf_op jit(solution)/shard_map/ppermute | solution.py:24
  195.9 4.5 %collective-permute-start.27 = (f32[1,32,384]{2,1,0:T(8,128)S(1)}, f32[1,32,384]{2,1,0:T(8,128)S(1)}, u32[]{:S(2)}, u32[]{:S(2)}) collective-permute-start(f32[1,32,384]{2,1,0:T(8,128)S(1)} %get-tuple-element.60), channel_id=1, source_target_pairs={{0,16},{1,17},{2,18},{3,19},{4,20},{5,21},{6,22},{7,23},{8,24},{9,... | collective-permute-start | bytes 147464 | tf_op jit(solution)/shard_map/ppermute | solution.py:24
  203.5 3.2 %collective-permute-start.29 = (f32[10,1,384]{2,1,0:T(1,128)S(1)}, f32[10,1,384]{2,1,0:T(1,128)S(1)}, u32[]{:S(2)}, u32[]{:S(2)}) collective-permute-start(f32[10,1,384]{2,1,0:T(1,128)S(1)} %get-tuple-element.53), channel_id=1, source_target_pairs={{0,1},{1,2},{2,3},{3,4},{4,5},{5,6},{6,7},{7,8},{8,9},{9,10},{10,1... | collective-permute-start | bytes 46088 | tf_op jit(solution)/shard_map/ppermute | solution.py:24
  210.1 4.5 %collective-permute-start.31 = (f32[1,32,384]{2,1,0:T(8,128)S(1)}, f32[1,32,384]{2,1,0:T(8,128)S(1)}, u32[]{:S(2)}, u32[]{:S(2)}) collective-permute-start(f32[1,32,384]{2,1,0:T(8,128)S(1)} %get-tuple-element.58), channel_id=1, source_target_pairs={{0,16},{1,17},{2,18},{3,19},{4,20},{5,21},{6,22},{7,23},{8,24},{9,... | collective-permute-start | bytes 147464 | tf_op jit(solution)/shard_map/ppermute | solution.py:24
  217.7 4.8 %collective-permute-start.33 = (f32[10,1,384]{2,1,0:T(1,128)S(1)}, f32[10,1,384]{2,1,0:T(1,128)S(1)}, u32[]{:S(2)}, u32[]{:S(2)}) collective-permute-start(f32[10,1,384]{2,1,0:T(1,128)S(1)} %get-tuple-element.51), channel_id=1, source_target_pairs={{0,1},{1,2},{2,3},{3,4},{4,5},{5,6},{6,7},{7,8},{8,9},{9,10},{10,1... | collective-permute-start | bytes 46088 | tf_op jit(solution)/shard_map/ppermute | solution.py:24
  227.0 27.3 %all-gather.2.cloned.1.call-done = f32[8,128,384]{2,0,1:T(8,128)} async-done(((f32[8,32,384]{2,0,1:T(8,128)}), f32[8,128,384]{2,0,1:T(8,128)}) %all-gather.2.cloned.1.call-update) | async-done | bytes 1572880 | tf_op jit(solution)/shard_map/all_gather | solution.py:160
  254.3 2.9 %copy.286 = f32[8,128,384]{2,1,0:T(8,128)} copy(f32[8,128,384]{2,0,1:T(8,128)} %all-gather.2.cloned.1.call-done) | data formatting | bytes 3145728
  (160 shorter events, 94.8 us)
Async XLA Ops:
  9.9 8.0 %collective-permute-start.1 = (f32[2,1,128,128]{3,0,2,1:T(2,128)S(1)}, f32[2,1,128,128]{3,0,2,1:T(2,128)S(1)}, u32[]{:S(2)}, u32[]{:S(2)}) collective-permute-start(f32[2,1,128,128]{3,0,2,1:T(2,128)S(1)} %get-tuple-element.49), channel_id=1, source_target_pairs={{0,16},{1,17},{2,18},{3,19},{4,20},{5,21},{6,22},{7,23},{8,24},{9,... | collective-permute-start | bytes 393224 | tf_op jit(solution)/shard_map/ppermute | solution.py:24
  14.9 7.2 %collective-permute-start = (f32[2,1,128,128]{3,0,2,1:T(2,128)}, f32[2,1,128,128]{3,0,2,1:T(2,128)}, u32[]{:S(2)}, u32[]{:S(2)}) collective-permute-start(f32[2,1,128,128]{3,0,2,1:T(2,128)} %get-tuple-element.48), channel_id=1, source_target_pairs={{16,0},{17,1},{18,2},{19,3},{20,4},{21,5},{22,6},{23,7},{24,8},{25... | collective-permute-start | bytes 393224 | tf_op jit(solution)/shard_map/ppermute | solution.py:25
  23.7 8.6 %collective-permute-start.2 = (f32[2,10,1,128]{3,0,2,1:T(2,128)}, f32[2,10,1,128]{3,0,2,1:T(2,128)S(1)}, u32[]{:S(2)}, u32[]{:S(2)}) collective-permute-start(f32[2,10,1,128]{3,0,2,1:T(2,128)} %get-tuple-element.41), channel_id=1, source_target_pairs={{4,0},{8,4},{12,8},{5,1},{9,5},{13,9},{6,2},{10,6},{14,10},{7,3},{... | collective-permute-start | bytes 30728 | tf_op jit(solution)/shard_map/ppermute | solution.py:25
  24.9 7.3 %collective-permute-start.3 = (f32[2,10,1,128]{3,0,2,1:T(2,128)}, f32[2,10,1,128]{3,0,2,1:T(2,128)}, u32[]{:S(2)}, u32[]{:S(2)}) collective-permute-start(f32[2,10,1,128]{3,0,2,1:T(2,128)} %get-tuple-element.40), channel_id=1, source_target_pairs={{0,4},{4,8},{8,12},{1,5},{5,9},{9,13},{2,6},{6,10},{10,14},{3,7},{... | collective-permute-start | bytes 30728 | tf_op jit(solution)/shard_map/ppermute | solution.py:24
  39.1 7.6 %collective-permute-start.4 = (f32[2,10,130,1]{2,0,3,1:T(2,128)}, f32[2,10,130,1]{2,0,3,1:T(2,128)}, u32[]{:S(2)}, u32[]{:S(2)}) collective-permute-start(f32[2,10,130,1]{2,0,3,1:T(2,128)} %copy.250), channel_id=1, source_target_pairs={{1,0},{2,1},{3,2},{5,4},{6,5},{7,6},{9,8},{10,9},{11,10},{13,12},{... | collective-permute-start | bytes 31208 | tf_op jit(solution)/shard_map/ppermute | solution.py:25
  42.9 6.2 %collective-permute-start.5 = (f32[2,10,130,1]{2,0,3,1:T(2,128)}, f32[2,10,130,1]{2,0,3,1:T(2,128)}, u32[]{:S(2)}, u32[]{:S(2)}) collective-permute-start(f32[2,10,130,1]{2,0,3,1:T(2,128)} %copy.252), channel_id=1, source_target_pairs={{0,1},{1,2},{2,3},{4,5},{5,6},{6,7},{8,9},{9,10},{10,11},{12,13},{... | collective-permute-start | bytes 31208 | tf_op jit(solution)/shard_map/ppermute | solution.py:24
  60.2 13.9 %collective-permute-start.6 = (f32[2,1,128,128]{3,2,1,0:T(8,128)S(1)}, f32[2,1,128,128]{3,2,1,0:T(8,128)S(1)}, u32[]{:S(2)}, u32[]{:S(2)}) collective-permute-start(f32[2,1,128,128]{3,2,1,0:T(8,128)S(1)} %get-tuple-element.45), channel_id=1, source_target_pairs={{16,0},{17,1},{18,2},{19,3},{20,4},{21,5},{22,6},{23,7},{24,8},{25... | collective-permute-start | bytes 393224 | tf_op jit(solution)/shard_map/ppermute | solution.py:25
  61.5 12.6 %collective-permute-start.7 = (f32[2,1,128,128]{3,2,1,0:T(8,128)S(1)}, f32[2,1,128,128]{3,2,1,0:T(8,128)S(1)}, u32[]{:S(2)}, u32[]{:S(2)}) collective-permute-start(f32[2,1,128,128]{3,2,1,0:T(8,128)S(1)} %get-tuple-element.44), channel_id=1, source_target_pairs={{0,16},{1,17},{2,18},{3,19},{4,20},{5,21},{6,22},{7,23},{8,24},{9,... | collective-permute-start | bytes 393224 | tf_op jit(solution)/shard_map/ppermute | solution.py:24
  67.5 61.0 %collective-permute-start.18 = (f32[1,32,384]{2,1,0:T(8,128)}, f32[1,32,384]{2,1,0:T(8,128)S(1)}, u32[]{:S(2)}, u32[]{:S(2)}) collective-permute-start(f32[1,32,384]{2,1,0:T(8,128)} %get-tuple-element.29), channel_id=1, source_target_pairs={{16,0},{17,1},{18,2},{19,3},{20,4},{21,5},{22,6},{23,7},{24,8},{25... | collective-permute-start | bytes 147464 | tf_op jit(solution)/shard_map/ppermute | solution.py:25
  68.8 59.7 %collective-permute-start.19 = (f32[1,32,384]{2,1,0:T(8,128)}, f32[1,32,384]{2,1,0:T(8,128)}, u32[]{:S(2)}, u32[]{:S(2)}) collective-permute-start(f32[1,32,384]{2,1,0:T(8,128)} %get-tuple-element.28), channel_id=1, source_target_pairs={{0,16},{1,17},{2,18},{3,19},{4,20},{5,21},{6,22},{7,23},{8,24},{9,... | collective-permute-start | bytes 147464 | tf_op jit(solution)/shard_map/ppermute | solution.py:24
  74.1 6.0 %collective-permute-start.8 = (f32[2,10,1,128]{3,0,2,1:T(2,128)S(1)}, f32[2,10,1,128]{3,0,2,1:T(2,128)S(1)}, u32[]{:S(2)}, u32[]{:S(2)}) collective-permute-start(f32[2,10,1,128]{3,0,2,1:T(2,128)S(1)} %copy.255), channel_id=1, source_target_pairs={{4,0},{8,4},{12,8},{5,1},{9,5},{13,9},{6,2},{10,6},{14,10},{7,3},{... | collective-permute-start | bytes 30728 | tf_op jit(solution)/shard_map/ppermute | solution.py:25
  75.4 5.9 %collective-permute-start.9 = (f32[2,10,1,128]{3,0,2,1:T(2,128)S(1)}, f32[2,10,1,128]{3,0,2,1:T(2,128)S(1)}, u32[]{:S(2)}, u32[]{:S(2)}) collective-permute-start(f32[2,10,1,128]{3,0,2,1:T(2,128)S(1)} %copy.257), channel_id=1, source_target_pairs={{0,4},{4,8},{8,12},{1,5},{5,9},{9,13},{2,6},{6,10},{10,14},{3,7},{... | collective-permute-start | bytes 30728 | tf_op jit(solution)/shard_map/ppermute | solution.py:24
  85.6 7.8 %collective-permute-start.10 = (f32[2,10,130,1]{2,0,3,1:T(2,128)S(1)}, f32[2,10,130,1]{2,0,3,1:T(2,128)S(1)}, u32[]{:S(2)}, u32[]{:S(2)}) collective-permute-start(f32[2,10,130,1]{2,0,3,1:T(2,128)S(1)} %copy.261), channel_id=1, source_target_pairs={{1,0},{2,1},{3,2},{5,4},{6,5},{7,6},{9,8},{10,9},{11,10},{13,12},{... | collective-permute-start | bytes 31208 | tf_op jit(solution)/shard_map/ppermute | solution.py:25
  89.0 6.1 %collective-permute-start.11 = (f32[2,10,130,1]{2,0,3,1:T(2,128)S(1)}, f32[2,10,130,1]{2,0,3,1:T(2,128)S(1)}, u32[]{:S(2)}, u32[]{:S(2)}) collective-permute-start(f32[2,10,130,1]{2,0,3,1:T(2,128)S(1)} %copy.263), channel_id=1, source_target_pairs={{0,1},{1,2},{2,3},{4,5},{5,6},{6,7},{8,9},{9,10},{10,11},{12,13},{... | collective-permute-start | bytes 31208 | tf_op jit(solution)/shard_map/ppermute | solution.py:24
  100.5 8.6 %collective-permute-start.12 = (f32[2,1,128,128]{3,2,1,0:T(8,128)S(1)}, f32[2,1,128,128]{3,2,1,0:T(8,128)S(1)}, u32[]{:S(2)}, u32[]{:S(2)}) collective-permute-start(f32[2,1,128,128]{3,2,1,0:T(8,128)S(1)} %get-tuple-element.43), channel_id=1, source_target_pairs={{16,0},{17,1},{18,2},{19,3},{20,4},{21,5},{22,6},{23,7},{24,8},{25... | collective-permute-start | bytes 393224 | tf_op jit(solution)/shard_map/ppermute | solution.py:25
  102.0 8.3 %collective-permute-start.13 = (f32[2,1,128,128]{3,2,1,0:T(8,128)S(1)}, f32[2,1,128,128]{3,2,1,0:T(8,128)S(1)}, u32[]{:S(2)}, u32[]{:S(2)}) collective-permute-start(f32[2,1,128,128]{3,2,1,0:T(8,128)S(1)} %get-tuple-element.42), channel_id=1, source_target_pairs={{0,16},{1,17},{2,18},{3,19},{4,20},{5,21},{6,22},{7,23},{8,24},{9,... | collective-permute-start | bytes 393224 | tf_op jit(solution)/shard_map/ppermute | solution.py:24
  110.3 7.2 %collective-permute-start.14 = (f32[2,10,1,128]{3,0,2,1:T(2,128)S(1)}, f32[2,10,1,128]{3,0,2,1:T(2,128)S(1)}, u32[]{:S(2)}, u32[]{:S(2)}) collective-permute-start(f32[2,10,1,128]{3,0,2,1:T(2,128)S(1)} %copy.265), channel_id=1, source_target_pairs={{4,0},{8,4},{12,8},{5,1},{9,5},{13,9},{6,2},{10,6},{14,10},{7,3},{... | collective-permute-start | bytes 30728 | tf_op jit(solution)/shard_map/ppermute | solution.py:25
  111.6 6.2 %collective-permute-start.15 = (f32[2,10,1,128]{3,0,2,1:T(2,128)S(1)}, f32[2,10,1,128]{3,0,2,1:T(2,128)S(1)}, u32[]{:S(2)}, u32[]{:S(2)}) collective-permute-start(f32[2,10,1,128]{3,0,2,1:T(2,128)S(1)} %copy.267), channel_id=1, source_target_pairs={{0,4},{4,8},{8,12},{1,5},{5,9},{9,13},{2,6},{6,10},{10,14},{3,7},{... | collective-permute-start | bytes 30728 | tf_op jit(solution)/shard_map/ppermute | solution.py:24
  122.1 12.4 %collective-permute-start.16 = (f32[2,10,130,1]{2,0,3,1:T(2,128)S(1)}, f32[2,10,130,1]{2,0,3,1:T(2,128)S(1)}, u32[]{:S(2)}, u32[]{:S(2)}) collective-permute-start(f32[2,10,130,1]{2,0,3,1:T(2,128)S(1)} %copy.271), channel_id=1, source_target_pairs={{1,0},{2,1},{3,2},{5,4},{6,5},{7,6},{9,8},{10,9},{11,10},{13,12},{... | collective-permute-start | bytes 31208 | tf_op jit(solution)/shard_map/ppermute | solution.py:25
  125.5 10.6 %collective-permute-start.17 = (f32[2,10,130,1]{2,0,3,1:T(2,128)S(1)}, f32[2,10,130,1]{2,0,3,1:T(2,128)S(1)}, u32[]{:S(2)}, u32[]{:S(2)}) collective-permute-start(f32[2,10,130,1]{2,0,3,1:T(2,128)S(1)} %copy.273), channel_id=1, source_target_pairs={{0,1},{1,2},{2,3},{4,5},{5,6},{6,7},{8,9},{9,10},{10,11},{12,13},{... | collective-permute-start | bytes 31208 | tf_op jit(solution)/shard_map/ppermute | solution.py:24
  129.9 41.8 %collective-permute-start.20 = (f32[10,1,384]{2,1,0:T(1,128)}, f32[10,1,384]{2,1,0:T(1,128)S(1)}, u32[]{:S(2)}, u32[]{:S(2)}) collective-permute-start(f32[10,1,384]{2,1,0:T(1,128)} %get-tuple-element.56), channel_id=1, source_target_pairs={{1,0},{2,1},{3,2},{4,3},{5,4},{6,5},{7,6},{8,7},{9,8},{10,9},{11,1... | collective-permute-start | bytes 46088 | tf_op jit(solution)/shard_map/ppermute | solution.py:25
  131.2 40.5 %collective-permute-start.21 = (f32[10,1,384]{2,1,0:T(1,128)}, f32[10,1,384]{2,1,0:T(1,128)S(1)}, u32[]{:S(2)}, u32[]{:S(2)}) collective-permute-start(f32[10,1,384]{2,1,0:T(1,128)} %get-tuple-element.57), channel_id=1, source_target_pairs={{0,1},{1,2},{2,3},{3,4},{4,5},{5,6},{6,7},{7,8},{8,9},{9,10},{10,1... | collective-permute-start | bytes 46088 | tf_op jit(solution)/shard_map/ppermute | solution.py:24
  143.7 30.1 %all-to-all-start = ((f32[8,128,128]{2,0,1:T(8,128)}), f32[8,128,128]{2,0,1:T(8,128)}, u32[]{:S(2)}, u32[]{:S(2)}) async-start(f32[8,128,128]{2,0,1:T(8,128)} %copy.283), calls=%async_computation | async-start | bytes 1048576 | tf_op jit(solution)/shard_map/all_to_all | solution.py:144
  147.9 106.5 %all-gather.2.cloned.1.call-start = ((), (), s32[]{:S(2)}) async-start(), calls=%async_computation.1 | async-start | bytes 1966080 | tf_op jit(solution)/shard_map/all_gather | solution.py:160
  180.3 6.0 %collective-permute-start.22 = (f32[1,32,384]{2,1,0:T(8,128)S(1)}, f32[1,32,384]{2,1,0:T(8,128)S(1)}, u32[]{:S(2)}, u32[]{:S(2)}) collective-permute-start(f32[1,32,384]{2,1,0:T(8,128)S(1)} %get-tuple-element.63), channel_id=1, source_target_pairs={{16,0},{17,1},{18,2},{19,3},{20,4},{21,5},{22,6},{23,7},{24,8},{25... | collective-permute-start | bytes 147464 | tf_op jit(solution)/shard_map/ppermute | solution.py:25
  181.6 6.3 %collective-permute-start.23 = (f32[1,32,384]{2,1,0:T(8,128)S(1)}, f32[1,32,384]{2,1,0:T(8,128)S(1)}, u32[]{:S(2)}, u32[]{:S(2)}) collective-permute-start(f32[1,32,384]{2,1,0:T(8,128)S(1)} %get-tuple-element.62), channel_id=1, source_target_pairs={{0,16},{1,17},{2,18},{3,19},{4,20},{5,21},{6,22},{7,23},{8,24},{9,... | collective-permute-start | bytes 147464 | tf_op jit(solution)/shard_map/ppermute | solution.py:24
  194.6 6.0 %collective-permute-start.26 = (f32[1,32,384]{2,1,0:T(8,128)S(1)}, f32[1,32,384]{2,1,0:T(8,128)S(1)}, u32[]{:S(2)}, u32[]{:S(2)}) collective-permute-start(f32[1,32,384]{2,1,0:T(8,128)S(1)} %get-tuple-element.61), channel_id=1, source_target_pairs={{16,0},{17,1},{18,2},{19,3},{20,4},{21,5},{22,6},{23,7},{24,8},{25... | collective-permute-start | bytes 147464 | tf_op jit(solution)/shard_map/ppermute | solution.py:25
  195.9 6.3 %collective-permute-start.27 = (f32[1,32,384]{2,1,0:T(8,128)S(1)}, f32[1,32,384]{2,1,0:T(8,128)S(1)}, u32[]{:S(2)}, u32[]{:S(2)}) collective-permute-start(f32[1,32,384]{2,1,0:T(8,128)S(1)} %get-tuple-element.60), channel_id=1, source_target_pairs={{0,16},{1,17},{2,18},{3,19},{4,20},{5,21},{6,22},{7,23},{8,24},{9,... | collective-permute-start | bytes 147464 | tf_op jit(solution)/shard_map/ppermute | solution.py:24
  208.8 6.0 %collective-permute-start.30 = (f32[1,32,384]{2,1,0:T(8,128)S(1)}, f32[1,32,384]{2,1,0:T(8,128)S(1)}, u32[]{:S(2)}, u32[]{:S(2)}) collective-permute-start(f32[1,32,384]{2,1,0:T(8,128)S(1)} %get-tuple-element.59), channel_id=1, source_target_pairs={{16,0},{17,1},{18,2},{19,3},{20,4},{21,5},{22,6},{23,7},{24,8},{25... | collective-permute-start | bytes 147464 | tf_op jit(solution)/shard_map/ppermute | solution.py:25
  210.1 6.3 %collective-permute-start.31 = (f32[1,32,384]{2,1,0:T(8,128)S(1)}, f32[1,32,384]{2,1,0:T(8,128)S(1)}, u32[]{:S(2)}, u32[]{:S(2)}) collective-permute-start(f32[1,32,384]{2,1,0:T(8,128)S(1)} %get-tuple-element.58), channel_id=1, source_target_pairs={{0,16},{1,17},{2,18},{3,19},{4,20},{5,21},{6,22},{7,23},{8,24},{9,... | collective-permute-start | bytes 147464 | tf_op jit(solution)/shard_map/ppermute | solution.py:24
  216.4 6.2 %collective-permute-start.32 = (f32[10,1,384]{2,1,0:T(1,128)S(1)}, f32[10,1,384]{2,1,0:T(1,128)S(1)}, u32[]{:S(2)}, u32[]{:S(2)}) collective-permute-start(f32[10,1,384]{2,1,0:T(1,128)S(1)} %get-tuple-element.50), channel_id=1, source_target_pairs={{1,0},{2,1},{3,2},{4,3},{5,4},{6,5},{7,6},{8,7},{9,8},{10,9},{11,1... | collective-permute-start | bytes 46088 | tf_op jit(solution)/shard_map/ppermute | solution.py:25
  217.7 5.7 %collective-permute-start.33 = (f32[10,1,384]{2,1,0:T(1,128)S(1)}, f32[10,1,384]{2,1,0:T(1,128)S(1)}, u32[]{:S(2)}, u32[]{:S(2)}) collective-permute-start(f32[10,1,384]{2,1,0:T(1,128)S(1)} %get-tuple-element.51), channel_id=1, source_target_pairs={{0,1},{1,2},{2,3},{3,4},{4,5},{5,6},{6,7},{7,8},{8,9},{9,10},{10,1... | collective-permute-start | bytes 46088 | tf_op jit(solution)/shard_map/ppermute | solution.py:24
  (20 other events, 202.6 us)
Sparse Core Ops, SparseCore 0:
  225.8 28.5 all-gather.1
where the time goes:
time: 266 us; the launch traced here: 264 us
  starting transfers between devices  98.2 us (37%)
  local copies, waits for them, and re-layouts  78.9 us (30%)
  waiting for transfers between devices  41 us (15%)
  other arithmetic  30.4 us (11%)
  between operations  15.5 us (6%)
    ppermute x17, starting transfers between devices, padded(): before = lax.ppermute(last, axis, up)  71.7 us
    all_gather x1, waiting for transfers between devices, on_device(): segment_kelvin = lax.all_gather(segment_kelvin, 'gx', axis=1, tiled=True)  27.3 us
    ppermute x17, starting transfers between devices, padded(): after = lax.ppermute(first, axis, down)  22.1 us
    unnamed x43, local copies, waits for them, and re-layouts  17.8 us
    slice x9, local copies, waits for them, and re-layouts, padded(): first = lax.slice_in_dim(value, 0, width, axis=dim)  14.4 us
    add x3, other arithmetic, neighbours(): total + bordered_segment[:, 1:-1, 1:-1, 2:]  14 us
    slice x1, local copies, waits for them, and re-layouts, diffusivity_coefficient(): centre_mask = bordered_segment_flags[1:-1, 1:-1, 1:-1]  12 us
    ppermute x17, waiting for transfers between devices, padded(): before = lax.ppermute(last, axis, up)  9.99 us
  transfers between devices with their start and end apart: 36, of which 14 were waited for; matrix products, arithmetic and copies ran while one was open for 27% of the time, Pallas kernels for 0%

commit v1 on v0

v1 whole, which is shorter than its diff:
```python
import jax
import jax.numpy as jnp
from jax import lax
from jax.experimental import pallas as pl
from jax.experimental.pallas import tpu as pltpu
from jax.sharding import PartitionSpec as P

MB = 8
STEPS = 4


WEIGHTS = (0.8, 1.0, 1.25)
SHIFT = 0.2
HEATING = 0.02
CONDUCT = 0.16
SOFTEN = 0.25


def expand_blocks(blocks):
    cells = jnp.repeat(blocks, MB, axis=0)
    cells = jnp.repeat(cells, MB, axis=1)
    return jnp.repeat(cells, MB, axis=2).astype(jnp.float32)


def _shifts(a, lo_row, hi_row, xlo_t, xhi_t):
    ny, nx = a.shape
    row = lax.broadcasted_iota(jnp.int32, (ny, nx), 0)
    col = lax.broadcasted_iota(jnp.int32, (ny, nx), 1)
    y_up = jnp.where(row == ny - 1, jnp.broadcast_to(hi_row, (ny, nx)), pltpu.roll(a, ny - 1, 0))
    y_dn = jnp.where(row == 0, jnp.broadcast_to(lo_row, (ny, nx)), pltpu.roll(a, 1, 0))
    srow = lax.broadcasted_iota(jnp.int32, (nx, ny), 0)
    edge = jnp.where(srow == 0, xlo_t, jnp.where(srow == nx - 1, xhi_t, 0.0)).T
    x_up = jnp.where(col == nx - 1, edge, pltpu.roll(a, nx - 1, 1))
    x_dn = jnp.where(col == 0, edge, pltpu.roll(a, 1, 1))
    return y_up, y_dn, x_up, x_dn


def _write_faces(new, z, depth, oz0, oz1, oy0, oy1, ox0, ox1, lead=()):
    ny = new.shape[0]
    if z == 0:
        oz0[lead] = new
    if z == depth - 1:
        oz1[lead] = new
    oy0[lead + (pl.ds(z, 1),)] = new[0:1, :]
    oy1[lead + (pl.ds(z, 1),)] = new[ny - 1 : ny, :]
    t = new.T
    ox0[lead + (pl.ds(z, 1),)] = t[0:1, :]
    ox1[lead + (pl.ds(z, 1),)] = t[-1:, :]


def _em_kernel(factor, last, prof, f, cpl, w, zlo, zhi, ylo, yhi, xlo, xhi, *outs):
    depth = f.shape[1]
    diagonal = 6.0 + SHIFT
    if last:
        (o, heat) = outs
    else:
        (o, oz0, oz1, oy0, oy1, ox0, ox1) = outs
    for z in range(depth):
        beside = []
        cur = [f[c, z] for c in range(2)]
        for c in range(2):
            a = cur[c]
            z_up = f[c, z + 1] if z + 1 < depth else zhi[c]
            z_dn = f[c, z - 1] if z > 0 else zlo[c]
            y_up, y_dn, x_up, x_dn = _shifts(
                a, ylo[c, pl.ds(z, 1), :], yhi[c, pl.ds(z, 1), :],
                jnp.broadcast_to(xlo[c, pl.ds(z, 1), :], a.shape[::-1]),
                jnp.broadcast_to(xhi[c, pl.ds(z, 1), :], a.shape[::-1]),
            )
            total = z_up + z_dn
            total = total + y_up + y_dn
            beside.append(total + x_up + x_dn)
        k = cpl[z]
        s0 = prof[z] * w[0]
        s1 = prof[z] * w[1]
        real_res = s0 - (diagonal * cur[0] - k * cur[1] - beside[0])
        imag_res = s1 - (diagonal * cur[1] + k * cur[0] - beside[1])
        scaled = factor / (diagonal * diagonal + k * k)
        n0 = cur[0] + scaled * (diagonal * real_res + k * imag_res)
        n1 = cur[1] + scaled * (diagonal * imag_res - k * real_res)
        o[0, z] = n0
        o[1, z] = n1
        if last:
            heat[z] = HEATING * k * (n0 * n0 + n1 * n1)
        else:
            for c, n in ((0, n0), (1, n1)):
                _write_faces(n, z, depth, oz0, oz1, oy0, oy1, ox0, ox1, lead=(c,))


def _heat_kernel(t, q, m, mzlo, mzhi, mylo, myhi, mxlo, mxhi,
                 tzlo, tzhi, tylo, tyhi, txlo, txhi, o, oz0, oz1, oy0, oy1, ox0, ox1):
    depth = t.shape[0]
    for z in range(depth):
        c = t[z]
        shape = c.shape
        z_up = t[z + 1] if z + 1 < depth else tzhi[...]
        z_dn = t[z - 1] if z > 0 else tzlo[...]
        mz_up = m[z + 1] if z + 1 < depth else mzhi[...]
        mz_dn = m[z - 1] if z > 0 else mzlo[...]
        y_up, y_dn, x_up, x_dn = _shifts(
            c, tylo[pl.ds(z, 1), :], tyhi[pl.ds(z, 1), :],
            jnp.broadcast_to(txlo[pl.ds(z, 1), :], shape[::-1]),
            jnp.broadcast_to(txhi[pl.ds(z, 1), :], shape[::-1]),
        )
        my_up, my_dn, mx_up, mx_dn = _shifts(
            m[z], mylo[pl.ds(z, 1), :], myhi[pl.ds(z, 1), :],
            jnp.broadcast_to(mxlo[pl.ds(z, 1), :], shape[::-1]),
            jnp.broadcast_to(mxhi[pl.ds(z, 1), :], shape[::-1]),
        )
        centre_kappa = 1.0 / (1.0 + SOFTEN * c * c)
        flux = jnp.zeros_like(c)
        for other, other_mask in (
            (z_up, mz_up), (z_dn, mz_dn), (y_up, my_up), (y_dn, my_dn), (x_up, mx_up), (x_dn, mx_dn)
        ):
            kappa = 1.0 / (1.0 + SOFTEN * other * other)
            flux = flux + other_mask * (centre_kappa + kappa) * (other - c)
        new = c + 0.5 * CONDUCT * m[z] * flux + q[z]
        o[z] = new
        _write_faces(new, z, depth, oz0, oz1, oy0, oy1, ox0, ox1)


def _vmem_call(kernel, out_shape, n_in, smem_first=False):
    specs = [pl.BlockSpec(memory_space=pltpu.VMEM)] * n_in
    if smem_first:
        specs[0] = pl.BlockSpec(memory_space=pltpu.SMEM)
    return pl.pallas_call(
        kernel,
        out_shape=out_shape,
        in_specs=specs,
        out_specs=[pl.BlockSpec(memory_space=pltpu.VMEM)] * len(out_shape),
    )


def _faces(a, lead):
    return (
        a[lead + (0,)], a[lead + (-1,)],
        a[lead + (slice(None), 0, slice(None))], a[lead + (slice(None), -1, slice(None))],
        a[lead + (slice(None), slice(None), 0)], a[lead + (slice(None), slice(None), -1)],
    )


def _exchange(faces, axes, pairs):
    received = []
    for (lo_face, hi_face), axis, (up, down) in zip(
        ((faces[0], faces[1]), (faces[2], faces[3]), (faces[4], faces[5])), axes, pairs
    ):
        received.append(lax.ppermute(hi_face, axis, up))
        received.append(lax.ppermute(lo_face, axis, down))
    return received


def _line_pairs(n, first=0):
    up = [(i, i + 1) for i in range(first, n - 1)]
    down = [(j, i) for i, j in up]
    return up, down


def on_device(
    earlier_window_curl_state,
    material_resistivity_inverse,
    winding_current_pattern,
    winding_axial_centre,
    specimen_presence_flags,
    specimen_kelvin_values,
):
    depth, height, breadth = material_resistivity_inverse.shape
    n_gz, n_gy, n_gx = lax.axis_size("gz"), lax.axis_size("gy"), lax.axis_size("gx")
    z_total = depth * n_gz
    x_total = breadth * n_gx
    gz_i, gy_i, gx_i = lax.axis_index("gz"), lax.axis_index("gy"), lax.axis_index("gx")
    z_start = gz_i * depth
    y_start = gy_i * height
    x_start = gx_i * breadth
    own_blocks = lax.dynamic_slice(
        specimen_presence_flags,
        (z_start // MB, y_start // MB, x_start // MB),
        (depth // MB, height // MB, breadth // MB),
    )
    coupling = expand_blocks(own_blocks) * material_resistivity_inverse
    coil_width = z_total // 4
    axial = (
        (z_start + jnp.arange(depth)).astype(jnp.float32)
        - winding_axial_centre[0].astype(jnp.float32)
    ) / coil_width
    profile = 1.0 / (1.0 + axial * axial)

    axes = ("gz", "gy", "gx")
    pairs = (_line_pairs(n_gz), _line_pairs(n_gy), _line_pairs(n_gx))
    field = earlier_window_curl_state
    faces = _faces(field, (slice(None),))
    fshape = jax.ShapeDtypeStruct(field.shape, jnp.float32)
    zf = jax.ShapeDtypeStruct((2, height, breadth), jnp.float32)
    yf = jax.ShapeDtypeStruct((2, depth, breadth), jnp.float32)
    xf = jax.ShapeDtypeStruct((2, depth, height), jnp.float32)
    qshape = jax.ShapeDtypeStruct((depth, height, breadth), jnp.float32)
    for i, factor in enumerate(WEIGHTS):
        last = i == len(WEIGHTS) - 1
        received = _exchange(faces, axes, pairs)
        outs = (fshape, qshape) if last else (fshape, zf, zf, yf, yf, xf, xf)
        res = _vmem_call(
            lambda *r, factor=factor, last=last: _em_kernel(factor, last, *r), outs, 10, True
        )(profile, field, coupling, winding_current_pattern, *received)
        if last:
            field, heat = res
        else:
            field, faces = res[0], tuple(res[1:])

    specimen_columns = specimen_kelvin_values.shape[2]
    offset = x_total - specimen_columns
    assert offset % breadth == 0 and specimen_columns % breadth == 0
    first_owner = offset // breadth
    j_start = x_start - offset
    j_clamped = jnp.maximum(j_start, 0)
    kelvin = lax.dynamic_slice_in_dim(specimen_kelvin_values, j_clamped, breadth, 2)

    window = jnp.pad(specimen_presence_flags[:, :, offset // MB :], 1)
    blocks = lax.dynamic_slice(
        window,
        (z_start // MB, y_start // MB, j_clamped // MB),
        (depth // MB + 2, height // MB + 2, breadth // MB + 2),
    )
    m_ext = expand_blocks(blocks)[MB - 1 : MB + 1 + depth, MB - 1 : MB + 1 + height, MB - 1 : MB + 1 + breadth]
    m_own = m_ext[1:-1, 1:-1, 1:-1]
    m_faces = (
        m_ext[0, 1:-1, 1:-1], m_ext[-1, 1:-1, 1:-1],
        m_ext[1:-1, 0, 1:-1], m_ext[1:-1, -1, 1:-1],
        m_ext[1:-1, 1:-1, 0], m_ext[1:-1, 1:-1, -1],
    )
    t_pairs = (_line_pairs(n_gz), _line_pairs(n_gy), _line_pairs(n_gx, first_owner))
    t_faces = _faces(kelvin, ())
    tshape = jax.ShapeDtypeStruct(kelvin.shape, jnp.float32)
    tz = jax.ShapeDtypeStruct((height, breadth), jnp.float32)
    ty = jax.ShapeDtypeStruct((depth, breadth), jnp.float32)
    tx = jax.ShapeDtypeStruct((depth, height), jnp.float32)
    heat_call = _vmem_call(_heat_kernel, (tshape, tz, tz, ty, ty, tx, tx), 15)
    for number in range(STEPS):
        received = _exchange(t_faces, axes, t_pairs)
        res = heat_call(kelvin, heat, m_own, *m_faces, *received)
        kelvin, t_faces = res[0], tuple(res[1:])
    gathered = lax.all_gather(kelvin, "gx", axis=2, tiled=True)
    segment_kelvin = gathered[:, :, first_owner * breadth :]
    return (field, segment_kelvin)


def solution(mesh):
    placed = (
        P(None, "gz", "gy", "gx"),
        P("gz", "gy", "gx"),
        P(None, "gy", "gx"),
        P(),
        P(),
        P("gz", "gy", None),
    )
    return jax.shard_map(
        on_device,
        mesh=mesh,
        in_specs=placed,
        out_specs=(P(None, "gz", "gy", "gx"), P("gz", "gy", None)),
        check_vma=False,
    )
```

time: 266 us -> 251 us (0.944)
  local copies, waits for them, and re-layouts: 78.9 us -> 44.6 us
  other arithmetic: 30.4 us -> 1.61 us
  Pallas kernels: 0 us -> 28 us
  waiting for transfers between devices: 41 us -> 57.5 us
  starting transfers between devices: 98.2 us -> 102 us
    pallas_call x0 -> x7, Pallas kernels: none -> 28 us  [the longest x4 15.9 us: on_device(): res = heat_call(kelvin, heat, m_own, *m_faces, *received)]
    add x9 -> x0, other arithmetic: 20.5 us -> none  [the longest x3 14 us: neighbours(): total + bordered_segment[:, 1:-1, 1:-1, 2:]]
    all_gather x1, waiting for transfers between devices: 27.3 us -> 44.5 us  [on_device(): gathered = lax.all_gather(kelvin, 'gx', axis=2, tiled=True)]
    slice x22 -> x13, local copies, waits for them, and re-layouts: 36.3 us -> 21 us  [the longest x2 4.46 us: _faces(): a[lead + (slice(None), slice(None), 0)]]
    ppermute x10 -> x2, local copies, waits for them, and re-layouts: 11.3 us -> 3.13 us  [the longest x1 1.57 us: _exchange(): received.append(lax.ppermute(lo_face, axis, down))]
    ppermute x34 -> x42, starting transfers between devices: 93.8 us -> 102 us  [the longest x21 76.5 us: _exchange(): received.append(lax.ppermute(hi_face, axis, up))]
    unnamed x43 -> x66, local copies, waits for them, and re-layouts: 17.8 us -> 10.5 us
    concatenate x9 -> x0, other arithmetic: 4.79 us -> none  [padded(): value = jnp.concatenate([before, value, after], axis=dim)]
  transfers between devices with their start and end apart: 36 -> 43, of which waited for: 14 -> 5; matrix products, arithmetic and copies ran while one was open for 27% -> 16% of each run, Pallas kernels for 0% -> 3%
where the time goes in v1:
time: 251 us; the launch traced here: 249 us
  starting transfers between devices  102 us (41%)
  waiting for transfers between devices  57.5 us (23%)
  local copies, waits for them, and re-layouts  44.6 us (18%)
  Pallas kernels  28 us (11%)
  between operations  15.4 us (6%)
    ppermute x21, starting transfers between devices, _exchange(): received.append(lax.ppermute(hi_face, axis, up))  76.5 us
    all_gather x1, waiting for transfers between devices, on_device(): gathered = lax.all_gather(kelvin, 'gx', axis=2, tiled=True)  44.5 us
    ppermute x21, starting transfers between devices, _exchange(): received.append(lax.ppermute(lo_face, axis, down))  25.3 us
    pallas_call x4, Pallas kernels, on_device(): res = heat_call(kelvin, heat, m_own, *m_faces, *received)  15.9 us
    ppermute x21, waiting for transfers between devices, _exchange(): received.append(lax.ppermute(lo_face, axis, down))  13 us
    pallas_call x3, Pallas kernels, on_device(): _vmem_call(lambda *r, factor=factor, last=last: _em_kernel(factor, last,...  12.1 us
    unnamed x66, local copies, waits for them, and re-layouts  10.5 us
  transfers between devices with their start and end apart: 43, of which 5 were waited for; matrix products, arithmetic and copies ran while one was open for 16% of the time, Pallas kernels for 3%

profile of v1, /device:TPU:0, one launch (start us, length us, event | category | flops | bytes accessed | tf_op | source)
XLA Modules:
  0.0 248.8 jit_solution(2204162839611126882)
XLA Ops:
  10.1 2.3 collective-permute-start.4
  16.3 4.9 %collective-permute-start = (f32[2,128,128]{2,1,0:T(8,128)}, f32[2,128,128]{2,1,0:T(8,128)}, u32[]{:S(2)}, u32[]{:S(2)}) collective-permute-start(f32[2,128,128]{2,1,0:T(8,128)} %get-tuple-element.95), channel_id=1, source_target_pairs={{0,16},{1,17},{2,18},{3,19},{4,20},{5,21},{6,22},{7,23},{8,24},{9,... | collective-permute-start | bytes 393224 | tf_op jit(solution)/shard_map/ppermute | solution.py:147
  24.0 4.1 %collective-permute-start.2 = (f32[2,8,128]{2,1,0:T(8,128)}, f32[2,8,128]{2,1,0:T(8,128)}, u32[]{:S(2)}, u32[]{:S(2)}) collective-permute-start(f32[2,8,128]{2,1,0:T(8,128)} %bitcast.6), channel_id=1, source_target_pairs={{0,4},{4,8},{8,12},{1,5},{5,9},{9,13},{2,6},{6,10},{10,14},{3,7},{... | collective-permute-start | bytes 24584 | tf_op jit(solution)/shard_map/ppermute | solution.py:147
  37.9 3.8 %collective-permute-done.3.r_7_ = f32[2,8,128]{2,1,0:T(8,128)} collective-permute-done((f32[2,8,128]{2,1,0:T(8,128)S(1)}, f32[2,8,128]{2,1,0:T(8,128)}, u32[]{:S(2)}, u32[]{:S(2)}) %collective-permute-start.3) | collective-permute-done | bytes 8224 | tf_op jit(solution)/shard_map/ppermute | solution.py:148
  41.7 4.1 %shard_map.77 = (f32[2,8,128,128]{3,2,1,0:T(8,128)}, f32[2,128,128]{2,1,0:T(8,128)}, f32[2,128,128]{2,1,0:T(8,128)}, f32[2,8,128]{2,1,0:T(8,128)}, f32[2,8,128]{...) custom-call(f32[8]{0:T(128)} %add_divide_fusion.r_0_, f32[2,8,128,128]{3,2,1,0:T(8,128)} %r_1_.1, ...), custom_call_target="tpu_custom_call" | custom-call | tf_op jit(solution)/shard_map/pallas_call | solution.py:200
  45.8 5.8 %collective-permute-start.6 = (f32[2,128,128]{2,1,0:T(8,128)}, f32[2,128,128]{2,1,0:T(8,128)}, u32[]{:S(2)}, u32[]{:S(2)}) collective-permute-start(f32[2,128,128]{2,1,0:T(8,128)} %get-tuple-element.41), channel_id=1, source_target_pairs={{0,16},{1,17},{2,18},{3,19},{4,20},{5,21},{6,22},{7,23},{8,24},{9,... | collective-permute-start | bytes 393224 | tf_op jit(solution)/shard_map/ppermute | solution.py:147
  52.9 2.1 collective-permute-start.10
  57.0 3.5 %collective-permute-start.8 = (f32[2,8,128]{2,1,0:T(8,128)}, f32[2,8,128]{2,1,0:T(8,128)}, u32[]{:S(2)}, u32[]{:S(2)}) collective-permute-start(f32[2,8,128]{2,1,0:T(8,128)} %get-tuple-element.43), channel_id=1, source_target_pairs={{0,4},{4,8},{8,12},{1,5},{5,9},{9,13},{2,6},{6,10},{10,14},{3,7},{... | collective-permute-start | bytes 24584 | tf_op jit(solution)/shard_map/ppermute | solution.py:147
  66.7 5.5 %collective-permute-start.18 = (f32[128,128]{0,1:T(8,128)}, f32[128,128]{0,1:T(8,128)}, u32[]{:S(2)}, u32[]{:S(2)}) collective-permute-start(f32[128,128]{0,1:T(8,128)} %bitcast.61), channel_id=1, source_target_pairs={{0,16},{1,17},{2,18},{3,19},{4,20},{5,21},{6,22},{7,23},{8,24},{9,... | collective-permute-start | bytes 196616 | tf_op jit(solution)/shard_map/ppermute | solution.py:147
  73.5 4.1 %shard_map.78 = (f32[2,8,128,128]{3,2,1,0:T(8,128)}, f32[2,128,128]{2,1,0:T(8,128)}, f32[2,128,128]{2,1,0:T(8,128)}, f32[2,8,128]{2,1,0:T(8,128)}, f32[2,8,128]{...) custom-call(f32[8]{0:T(128)} %add_divide_fusion.r_0_, f32[2,8,128,128]{3,2,1,0:T(8,128)} %get-tuple-element.40.r_1_, ...), custom_call_target="tpu_custom_call" | custom-call | tf_op jit(solution)/shard_map/pallas_call | solution.py:200
  77.6 5.8 %collective-permute-start.12 = (f32[2,128,128]{2,1,0:T(8,128)}, f32[2,128,128]{2,1,0:T(8,128)}, u32[]{:S(2)}, u32[]{:S(2)}) collective-permute-start(f32[2,128,128]{2,1,0:T(8,128)} %get-tuple-element.48), channel_id=1, source_target_pairs={{0,16},{1,17},{2,18},{3,19},{4,20},{5,21},{6,22},{7,23},{8,24},{9,... | collective-permute-start | bytes 393224 | tf_op jit(solution)/shard_map/ppermute | solution.py:147
  83.4 4.5 %collective-permute-start.14 = (f32[2,8,128]{2,1,0:T(8,128)}, f32[2,8,128]{2,1,0:T(8,128)S(1)}, u32[]{:S(2)}, u32[]{:S(2)}) collective-permute-start(f32[2,8,128]{2,1,0:T(8,128)} %get-tuple-element.50), channel_id=1, source_target_pairs={{0,4},{4,8},{8,12},{1,5},{5,9},{9,13},{2,6},{6,10},{10,14},{3,7},{... | collective-permute-start | bytes 24584 | tf_op jit(solution)/shard_map/ppermute | solution.py:147
  88.0 2.5 %constant_dynamic-slice_fusion = (f32[8,128,1]{2,1,0:T(8,128)}, f32[8,128,1]{2,1,0:T(8,128)}) fusion(f32[8,128,384]{2,1,0:T(8,128)} %param.11, s32[]{:T(128)S(6)} %max.3, s32[]{:T(128)S(6)} %add.46), kind=kLoop, calls=%fused_computation.12 | loop fusion | bytes 16392 | tf_op jit(solution)/shard_map/slice | solution.py:138
  93.1 5.7 %collective-permute-start.16 = (f32[2,8,128]{2,1,0:T(8,128)}, f32[2,8,128]{2,1,0:T(8,128)}, u32[]{:S(2)}, u32[]{:S(2)}) collective-permute-start(f32[2,8,128]{2,1,0:T(8,128)} %get-tuple-element.52), channel_id=1, source_target_pairs={{0,1},{1,2},{2,3},{4,5},{5,6},{6,7},{8,9},{9,10},{10,11},{12,13},{... | collective-permute-start | bytes 24584 | tf_op jit(solution)/shard_map/ppermute | solution.py:147
  107.8 4.8 %collective-permute-start.20 = (f32[8,128]{1,0:T(8,128)}, f32[8,128]{1,0:T(8,128)}, u32[]{:S(2)}, u32[]{:S(2)}) collective-permute-start(f32[8,128]{1,0:T(8,128)} %bitcast.66), channel_id=1, source_target_pairs={{0,4},{4,8},{8,12},{1,5},{5,9},{9,13},{2,6},{6,10},{10,14},{3,7},{... | collective-permute-start | bytes 12296 | tf_op jit(solution)/shard_map/ppermute | solution.py:147
  114.1 2.2 constant_dynamic-slice_fusion.6.t
  127.7 3.9 %shard_map.79 = (f32[2,8,128,128]{3,2,1,0:T(8,128)}, f32[8,128,128]{2,1,0:T(8,128)}) custom-call(f32[8]{0:T(128)} %add_divide_fusion.r_0_, f32[2,8,128,128]{3,2,1,0:T(8,128)} %get-tuple-element.47.r_1_, f32[8,128,128]{2,1,0:T(8,128)} %broadcast_multiply_fusion.r_2_, f32[2,128,128]{2,1,0:T(8,128)} %r_3_.5, f32[2,128,128]{2,1,0:T(8,128)} %collective-permute-done.12.r_4_, ...), custom_call_target="tpu_custom_call" | custom-call | tf_op jit(solution)/shard_map/pallas_call | solution.py:200
  131.6 4.0 %shard_map.80 = (f32[8,128,128]{2,1,0:T(8,128)}, f32[128,128]{1,0:T(8,128)}, f32[128,128]{1,0:T(8,128)}, f32[8,128]{1,0:T(8,128)}, f32[8,128]{1,0:T(8,128)}, /*index=5*/f32[8,128]{1,0:T(8,128)}, f32[8,128]{1,0:T(8,128)}) custom-call(f32[8,128,128]{2,1,0:T(8,128)} %constant_dynamic-slice_fusion.6.t, f32[8,128,128]{2,1,0:T(8,128)} %get-tuple-element.55.q, ...), custom_call_target="tpu_custom_call" | custom-call | tf_op jit(solution)/shard_map/pallas_call | solution.py:238
  135.6 4.9 %collective-permute-start.24 = (f32[128,128]{1,0:T(8,128)}, f32[128,128]{1,0:T(8,128)S(1)}, u32[]{:S(2)}, u32[]{:S(2)}) collective-permute-start(f32[128,128]{1,0:T(8,128)} %get-tuple-element.57), channel_id=1, source_target_pairs={{0,16},{1,17},{2,18},{3,19},{4,20},{5,21},{6,22},{7,23},{8,24},{9,... | collective-permute-start | bytes 196616 | tf_op jit(solution)/shard_map/ppermute | solution.py:147
  141.8 4.5 %collective-permute-start.26 = (f32[8,128]{1,0:T(8,128)}, f32[8,128]{1,0:T(8,128)S(1)}, u32[]{:S(2)}, u32[]{:S(2)}) collective-permute-start(f32[8,128]{1,0:T(8,128)} %get-tuple-element.59), channel_id=1, source_target_pairs={{0,4},{4,8},{8,12},{1,5},{5,9},{9,13},{2,6},{6,10},{10,14},{3,7},{... | collective-permute-start | bytes 12296 | tf_op jit(solution)/shard_map/ppermute | solution.py:147
  149.0 3.1 %collective-permute-done.27.tyhi = f32[8,128]{1,0:T(8,128)S(1)} collective-permute-done((f32[8,128]{1,0:T(8,128)}, f32[8,128]{1,0:T(8,128)S(1)}, u32[]{:S(2)}, u32[]{:S(2)}) %collective-permute-start.27) | collective-permute-done | bytes 4128 | tf_op jit(solution)/shard_map/ppermute | solution.py:148
  152.8 4.0 %shard_map.81 = (f32[8,128,128]{2,1,0:T(8,128)}, f32[128,128]{1,0:T(8,128)}, f32[128,128]{1,0:T(8,128)}, f32[8,128]{1,0:T(8,128)}, f32[8,128]{1,0:T(8,128)}, /*index=5*/f32[8,128]{1,0:T(8,128)}, f32[8,128]{1,0:T(8,128)}) custom-call(f32[8,128,128]{2,1,0:T(8,128)} %get-tuple-element.56.t, f32[8,128,128]{2,1,0:T(8,128)} %get-tuple-element.55.q, ...), custom_call_target="tpu_custom_call" | custom-call | tf_op jit(solution)/shard_map/pallas_call | solution.py:238
  156.8 4.5 %collective-permute-start.30 = (f32[128,128]{1,0:T(8,128)}, f32[128,128]{1,0:T(8,128)S(1)}, u32[]{:S(2)}, u32[]{:S(2)}) collective-permute-start(f32[128,128]{1,0:T(8,128)} %get-tuple-element.64), channel_id=1, source_target_pairs={{0,16},{1,17},{2,18},{3,19},{4,20},{5,21},{6,22},{7,23},{8,24},{9,... | collective-permute-start | bytes 196616 | tf_op jit(solution)/shard_map/ppermute | solution.py:147
  162.6 2.4 collective-permute-start.32
  167.6 3.1 %collective-permute-done.33.tyhi = f32[8,128]{1,0:T(8,128)S(1)} collective-permute-done((f32[8,128]{1,0:T(8,128)}, f32[8,128]{1,0:T(8,128)S(1)}, u32[]{:S(2)}, u32[]{:S(2)}) %collective-permute-start.33) | collective-permute-done | bytes 4128 | tf_op jit(solution)/shard_map/ppermute | solution.py:148
  171.4 4.0 %shard_map.82 = (f32[8,128,128]{2,1,0:T(8,128)}, f32[128,128]{1,0:T(8,128)}, f32[128,128]{1,0:T(8,128)}, f32[8,128]{1,0:T(8,128)}, f32[8,128]{1,0:T(8,128)}, /*index=5*/f32[8,128]{1,0:T(8,128)}, f32[8,128]{1,0:T(8,128)}) custom-call(f32[8,128,128]{2,1,0:T(8,128)} %get-tuple-element.63.t, f32[8,128,128]{2,1,0:T(8,128)} %get-tuple-element.55.q, ...), custom_call_target="tpu_custom_call" | custom-call | tf_op jit(solution)/shard_map/pallas_call | solution.py:238
  175.3 4.5 %collective-permute-start.36 = (f32[128,128]{1,0:T(8,128)}, f32[128,128]{1,0:T(8,128)S(1)}, u32[]{:S(2)}, u32[]{:S(2)}) collective-permute-start(f32[128,128]{1,0:T(8,128)} %get-tuple-element.71), channel_id=1, source_target_pairs={{0,16},{1,17},{2,18},{3,19},{4,20},{5,21},{6,22},{7,23},{8,24},{9,... | collective-permute-start | bytes 196616 | tf_op jit(solution)/shard_map/ppermute | solution.py:147
  181.2 3.2 %collective-permute-start.38 = (f32[8,128]{1,0:T(8,128)}, f32[8,128]{1,0:T(8,128)S(1)}, u32[]{:S(2)}, u32[]{:S(2)}) collective-permute-start(f32[8,128]{1,0:T(8,128)} %get-tuple-element.73), channel_id=1, source_target_pairs={{0,4},{4,8},{8,12},{1,5},{5,9},{9,13},{2,6},{6,10},{10,14},{3,7},{... | collective-permute-start | bytes 12296 | tf_op jit(solution)/shard_map/ppermute | solution.py:147
  187.0 3.1 %collective-permute-done.39.tyhi = f32[8,128]{1,0:T(8,128)S(1)} collective-permute-done((f32[8,128]{1,0:T(8,128)}, f32[8,128]{1,0:T(8,128)S(1)}, u32[]{:S(2)}, u32[]{:S(2)}) %collective-permute-start.39) | collective-permute-done | bytes 4128 | tf_op jit(solution)/shard_map/ppermute | solution.py:148
  190.8 4.0 %shard_map.83 = (f32[8,128,128]{2,1,0:T(8,128)}, f32[128,128]{1,0:T(8,128)}, f32[128,128]{1,0:T(8,128)}, f32[8,128]{1,0:T(8,128)}, f32[8,128]{1,0:T(8,128)}, /*index=5*/f32[8,128]{1,0:T(8,128)}, f32[8,128]{1,0:T(8,128)}) custom-call(f32[8,128,128]{2,1,0:T(8,128)} %get-tuple-element.70.t, f32[8,128,128]{2,1,0:T(8,128)} %get-tuple-element.55.q, ...), custom_call_target="tpu_custom_call" | custom-call | tf_op jit(solution)/shard_map/pallas_call | solution.py:238
  194.8 44.5 %all-gather.2.cloned.1.call-done = f32[8,128,512]{2,1,0:T(8,128)} async-done(((f32[8,128,128]{2,1,0:T(8,128)}), f32[8,128,512]{2,1,0:T(8,128)}) %all-gather.2.cloned.1.call-update) | async-done | bytes 2097168 | tf_op jit(solution)/shard_map/all_gather | solution.py:240
  239.2 2.7 %slice.99 = f32[8,128,384]{2,1,0:T(8,128)} slice(f32[8,128,512]{2,1,0:T(8,128)} %all-gather.2.cloned.1.call-done), slice={[0:8], [0:128], [128:512]} | slice | bytes 3145728 | tf_op jit(solution)/shard_map/slice | solution.py:241
  (162 shorter events, 67.4 us)
Async XLA Ops:
  7.2 232.1 %all-gather.2.cloned.1.call-start = ((), (), s32[]{:S(2)}) async-start(), calls=%async_computation | async-start | bytes 2621440 | tf_op jit(solution)/shard_map/all_gather | solution.py:240
  10.1 25.9 %collective-permute-start.4 = (f32[2,8,128]{2,1,0:T(8,128)}, f32[2,8,128]{2,1,0:T(8,128)S(1)}, u32[]{:S(2)}, u32[]{:S(2)}) collective-permute-start(f32[2,8,128]{2,1,0:T(8,128)} %bitcast.8), channel_id=1, source_target_pairs={{0,1},{1,2},{2,3},{4,5},{5,6},{6,7},{8,9},{9,10},{10,11},{12,13},{... | collective-permute-start | bytes 24584 | tf_op jit(solution)/shard_map/ppermute | solution.py:147
  13.4 24.6 %collective-permute-start.5 = (f32[2,8,128]{2,1,0:T(8,128)}, f32[2,8,128]{2,1,0:T(8,128)S(1)}, u32[]{:S(2)}, u32[]{:S(2)}) collective-permute-start(f32[2,8,128]{2,1,0:T(8,128)} %bitcast.9), channel_id=1, source_target_pairs={{1,0},{2,1},{3,2},{5,4},{6,5},{7,6},{9,8},{10,9},{11,10},{13,12},{... | collective-permute-start | bytes 24584 | tf_op jit(solution)/shard_map/ppermute | solution.py:148
  16.3 25.4 %collective-permute-start = (f32[2,128,128]{2,1,0:T(8,128)}, f32[2,128,128]{2,1,0:T(8,128)}, u32[]{:S(2)}, u32[]{:S(2)}) collective-permute-start(f32[2,128,128]{2,1,0:T(8,128)} %get-tuple-element.95), channel_id=1, source_target_pairs={{0,16},{1,17},{2,18},{3,19},{4,20},{5,21},{6,22},{7,23},{8,24},{9,... | collective-permute-start | bytes 393224 | tf_op jit(solution)/shard_map/ppermute | solution.py:147
  21.2 20.5 %collective-permute-start.1 = (f32[2,128,128]{2,1,0:T(8,128)}, f32[2,128,128]{2,1,0:T(8,128)}, u32[]{:S(2)}, u32[]{:S(2)}) collective-permute-start(f32[2,128,128]{2,1,0:T(8,128)} %get-tuple-element.94), channel_id=1, source_target_pairs={{16,0},{17,1},{18,2},{19,3},{20,4},{21,5},{22,6},{23,7},{24,8},{25... | collective-permute-start | bytes 393224 | tf_op jit(solution)/shard_map/ppermute | solution.py:148
  24.0 14.0 %collective-permute-start.2 = (f32[2,8,128]{2,1,0:T(8,128)}, f32[2,8,128]{2,1,0:T(8,128)}, u32[]{:S(2)}, u32[]{:S(2)}) collective-permute-start(f32[2,8,128]{2,1,0:T(8,128)} %bitcast.6), channel_id=1, source_target_pairs={{0,4},{4,8},{8,12},{1,5},{5,9},{9,13},{2,6},{6,10},{10,14},{3,7},{... | collective-permute-start | bytes 24584 | tf_op jit(solution)/shard_map/ppermute | solution.py:147
  45.8 27.7 %collective-permute-start.6 = (f32[2,128,128]{2,1,0:T(8,128)}, f32[2,128,128]{2,1,0:T(8,128)}, u32[]{:S(2)}, u32[]{:S(2)}) collective-permute-start(f32[2,128,128]{2,1,0:T(8,128)} %get-tuple-element.41), channel_id=1, source_target_pairs={{0,16},{1,17},{2,18},{3,19},{4,20},{5,21},{6,22},{7,23},{8,24},{9,... | collective-permute-start | bytes 393224 | tf_op jit(solution)/shard_map/ppermute | solution.py:147
  51.7 21.9 %collective-permute-start.7 = (f32[2,128,128]{2,1,0:T(8,128)}, f32[2,128,128]{2,1,0:T(8,128)}, u32[]{:S(2)}, u32[]{:S(2)}) collective-permute-start(f32[2,128,128]{2,1,0:T(8,128)} %get-tuple-element.42), channel_id=1, source_target_pairs={{16,0},{17,1},{18,2},{19,3},{20,4},{21,5},{22,6},{23,7},{24,8},{25... | collective-permute-start | bytes 393224 | tf_op jit(solution)/shard_map/ppermute | solution.py:148
  52.9 7.6 %collective-permute-start.10 = (f32[2,8,128]{2,1,0:T(8,128)}, f32[2,8,128]{2,1,0:T(8,128)S(1)}, u32[]{:S(2)}, u32[]{:S(2)}) collective-permute-start(f32[2,8,128]{2,1,0:T(8,128)} %get-tuple-element.45), channel_id=1, source_target_pairs={{0,1},{1,2},{2,3},{4,5},{5,6},{6,7},{8,9},{9,10},{10,11},{12,13},{... | collective-permute-start | bytes 24584 | tf_op jit(solution)/shard_map/ppermute | solution.py:147
  55.7 11.0 %collective-permute-start.11 = (f32[2,8,128]{2,1,0:T(8,128)}, f32[2,8,128]{2,1,0:T(8,128)S(1)}, u32[]{:S(2)}, u32[]{:S(2)}) collective-permute-start(f32[2,8,128]{2,1,0:T(8,128)} %get-tuple-element.46), channel_id=1, source_target_pairs={{1,0},{2,1},{3,2},{5,4},{6,5},{7,6},{9,8},{10,9},{11,10},{13,12},{... | collective-permute-start | bytes 24584 | tf_op jit(solution)/shard_map/ppermute | solution.py:148
  57.0 15.2 %collective-permute-start.8 = (f32[2,8,128]{2,1,0:T(8,128)}, f32[2,8,128]{2,1,0:T(8,128)}, u32[]{:S(2)}, u32[]{:S(2)}) collective-permute-start(f32[2,8,128]{2,1,0:T(8,128)} %get-tuple-element.43), channel_id=1, source_target_pairs={{0,4},{4,8},{8,12},{1,5},{5,9},{9,13},{2,6},{6,10},{10,14},{3,7},{... | collective-permute-start | bytes 24584 | tf_op jit(solution)/shard_map/ppermute | solution.py:147
  60.5 13.0 %collective-permute-start.9 = (f32[2,8,128]{2,1,0:T(8,128)}, f32[2,8,128]{2,1,0:T(8,128)}, u32[]{:S(2)}, u32[]{:S(2)}) collective-permute-start(f32[2,8,128]{2,1,0:T(8,128)} %get-tuple-element.44), channel_id=1, source_target_pairs={{4,0},{8,4},{12,8},{5,1},{9,5},{13,9},{6,2},{10,6},{14,10},{7,3},{... | collective-permute-start | bytes 24584 | tf_op jit(solution)/shard_map/ppermute | solution.py:148
  66.7 25.1 %collective-permute-start.18 = (f32[128,128]{0,1:T(8,128)}, f32[128,128]{0,1:T(8,128)}, u32[]{:S(2)}, u32[]{:S(2)}) collective-permute-start(f32[128,128]{0,1:T(8,128)} %bitcast.61), channel_id=1, source_target_pairs={{0,16},{1,17},{2,18},{3,19},{4,20},{5,21},{6,22},{7,23},{8,24},{9,... | collective-permute-start | bytes 196616 | tf_op jit(solution)/shard_map/ppermute | solution.py:147
  72.2 20.9 %collective-permute-start.19 = (f32[128,128]{0,1:T(8,128)}, f32[128,128]{0,1:T(8,128)}, u32[]{:S(2)}, u32[]{:S(2)}) collective-permute-start(f32[128,128]{0,1:T(8,128)} %bitcast.60), channel_id=1, source_target_pairs={{16,0},{17,1},{18,2},{19,3},{20,4},{21,5},{22,6},{23,7},{24,8},{25... | collective-permute-start | bytes 196616 | tf_op jit(solution)/shard_map/ppermute | solution.py:148
  77.6 35.0 %collective-permute-start.12 = (f32[2,128,128]{2,1,0:T(8,128)}, f32[2,128,128]{2,1,0:T(8,128)}, u32[]{:S(2)}, u32[]{:S(2)}) collective-permute-start(f32[2,128,128]{2,1,0:T(8,128)} %get-tuple-element.48), channel_id=1, source_target_pairs={{0,16},{1,17},{2,18},{3,19},{4,20},{5,21},{6,22},{7,23},{8,24},{9,... | collective-permute-start | bytes 393224 | tf_op jit(solution)/shard_map/ppermute | solution.py:147
  83.4 15.4 %collective-permute-start.14 = (f32[2,8,128]{2,1,0:T(8,128)}, f32[2,8,128]{2,1,0:T(8,128)S(1)}, u32[]{:S(2)}, u32[]{:S(2)}) collective-permute-start(f32[2,8,128]{2,1,0:T(8,128)} %get-tuple-element.50), channel_id=1, source_target_pairs={{0,4},{4,8},{8,12},{1,5},{5,9},{9,13},{2,6},{6,10},{10,14},{3,7},{... | collective-permute-start | bytes 24584 | tf_op jit(solution)/shard_map/ppermute | solution.py:147
  90.5 37.2 %collective-permute-start.13 = (f32[2,128,128]{2,1,0:T(8,128)}, f32[2,128,128]{2,1,0:T(8,128)}, u32[]{:S(2)}, u32[]{:S(2)}) collective-permute-start(f32[2,128,128]{2,1,0:T(8,128)} %get-tuple-element.49), channel_id=1, source_target_pairs={{16,0},{17,1},{18,2},{19,3},{20,4},{21,5},{22,6},{23,7},{24,8},{25... | collective-permute-start | bytes 393224 | tf_op jit(solution)/shard_map/ppermute | solution.py:148
  91.8 13.5 %collective-permute-start.15 = (f32[2,8,128]{2,1,0:T(8,128)}, f32[2,8,128]{2,1,0:T(8,128)S(1)}, u32[]{:S(2)}, u32[]{:S(2)}) collective-permute-start(f32[2,8,128]{2,1,0:T(8,128)} %get-tuple-element.51), channel_id=1, source_target_pairs={{4,0},{8,4},{12,8},{5,1},{9,5},{13,9},{6,2},{10,6},{14,10},{7,3},{... | collective-permute-start | bytes 24584 | tf_op jit(solution)/shard_map/ppermute | solution.py:148
  93.1 13.5 %collective-permute-start.16 = (f32[2,8,128]{2,1,0:T(8,128)}, f32[2,8,128]{2,1,0:T(8,128)}, u32[]{:S(2)}, u32[]{:S(2)}) collective-permute-start(f32[2,8,128]{2,1,0:T(8,128)} %get-tuple-element.52), channel_id=1, source_target_pairs={{0,1},{1,2},{2,3},{4,5},{5,6},{6,7},{8,9},{9,10},{10,11},{12,13},{... | collective-permute-start | bytes 24584 | tf_op jit(solution)/shard_map/ppermute | solution.py:147
  98.8 9.0 %collective-permute-start.17 = (f32[2,8,128]{2,1,0:T(8,128)}, f32[2,8,128]{2,1,0:T(8,128)}, u32[]{:S(2)}, u32[]{:S(2)}) collective-permute-start(f32[2,8,128]{2,1,0:T(8,128)} %get-tuple-element.53), channel_id=1, source_target_pairs={{1,0},{2,1},{3,2},{5,4},{6,5},{7,6},{9,8},{10,9},{11,10},{13,12},{... | collective-permute-start | bytes 24584 | tf_op jit(solution)/shard_map/ppermute | solution.py:148
  105.3 26.3 %collective-permute-start.22 = (f32[8,128]{1,0:T(8,128)}, f32[8,128]{1,0:T(8,128)}, u32[]{:S(2)}, u32[]{:S(2)}) collective-permute-start(f32[8,128]{1,0:T(8,128)} %bitcast.64), channel_id=1, source_target_pairs={{1,2},{2,3},{5,6},{6,7},{9,10},{10,11},{13,14},{14,15},{17,18},{18... | collective-permute-start | bytes 12296 | tf_op jit(solution)/shard_map/ppermute | solution.py:147
  106.6 25.0 %collective-permute-start.23 = (f32[8,128]{1,0:T(8,128)}, f32[8,128]{1,0:T(8,128)}, u32[]{:S(2)}, u32[]{:S(2)}) collective-permute-start(f32[8,128]{1,0:T(8,128)} %bitcast.63), channel_id=1, source_target_pairs={{2,1},{3,2},{6,5},{7,6},{10,9},{11,10},{14,13},{15,14},{18,17},{19... | collective-permute-start | bytes 12296 | tf_op jit(solution)/shard_map/ppermute | solution.py:148
  107.8 23.8 %collective-permute-start.20 = (f32[8,128]{1,0:T(8,128)}, f32[8,128]{1,0:T(8,128)}, u32[]{:S(2)}, u32[]{:S(2)}) collective-permute-start(f32[8,128]{1,0:T(8,128)} %bitcast.66), channel_id=1, source_target_pairs={{0,4},{4,8},{8,12},{1,5},{5,9},{9,13},{2,6},{6,10},{10,14},{3,7},{... | collective-permute-start | bytes 12296 | tf_op jit(solution)/shard_map/ppermute | solution.py:147
  112.7 19.0 %collective-permute-start.21 = (f32[8,128]{1,0:T(8,128)}, f32[8,128]{1,0:T(8,128)}, u32[]{:S(2)}, u32[]{:S(2)}) collective-permute-start(f32[8,128]{1,0:T(8,128)} %bitcast.65), channel_id=1, source_target_pairs={{4,0},{8,4},{12,8},{5,1},{9,5},{13,9},{6,2},{10,6},{14,10},{7,3},{... | collective-permute-start | bytes 12296 | tf_op jit(solution)/shard_map/ppermute | solution.py:148
  135.6 16.5 %collective-permute-start.24 = (f32[128,128]{1,0:T(8,128)}, f32[128,128]{1,0:T(8,128)S(1)}, u32[]{:S(2)}, u32[]{:S(2)}) collective-permute-start(f32[128,128]{1,0:T(8,128)} %get-tuple-element.57), channel_id=1, source_target_pairs={{0,16},{1,17},{2,18},{3,19},{4,20},{5,21},{6,22},{7,23},{8,24},{9,... | collective-permute-start | bytes 196616 | tf_op jit(solution)/shard_map/ppermute | solution.py:147
  140.5 11.6 %collective-permute-start.25 = (f32[128,128]{1,0:T(8,128)}, f32[128,128]{1,0:T(8,128)S(1)}, u32[]{:S(2)}, u32[]{:S(2)}) collective-permute-start(f32[128,128]{1,0:T(8,128)} %get-tuple-element.58), channel_id=1, source_target_pairs={{16,0},{17,1},{18,2},{19,3},{20,4},{21,5},{22,6},{23,7},{24,8},{25... | collective-permute-start | bytes 196616 | tf_op jit(solution)/shard_map/ppermute | solution.py:148
  141.8 6.5 %collective-permute-start.26 = (f32[8,128]{1,0:T(8,128)}, f32[8,128]{1,0:T(8,128)S(1)}, u32[]{:S(2)}, u32[]{:S(2)}) collective-permute-start(f32[8,128]{1,0:T(8,128)} %get-tuple-element.59), channel_id=1, source_target_pairs={{0,4},{4,8},{8,12},{1,5},{5,9},{9,13},{2,6},{6,10},{10,14},{3,7},{... | collective-permute-start | bytes 12296 | tf_op jit(solution)/shard_map/ppermute | solution.py:147
  146.4 5.7 %collective-permute-start.27 = (f32[8,128]{1,0:T(8,128)}, f32[8,128]{1,0:T(8,128)S(1)}, u32[]{:S(2)}, u32[]{:S(2)}) collective-permute-start(f32[8,128]{1,0:T(8,128)} %get-tuple-element.60), channel_id=1, source_target_pairs={{4,0},{8,4},{12,8},{5,1},{9,5},{13,9},{6,2},{10,6},{14,10},{7,3},{... | collective-permute-start | bytes 12296 | tf_op jit(solution)/shard_map/ppermute | solution.py:148
  156.8 14.0 %collective-permute-start.30 = (f32[128,128]{1,0:T(8,128)}, f32[128,128]{1,0:T(8,128)S(1)}, u32[]{:S(2)}, u32[]{:S(2)}) collective-permute-start(f32[128,128]{1,0:T(8,128)} %get-tuple-element.64), channel_id=1, source_target_pairs={{0,16},{1,17},{2,18},{3,19},{4,20},{5,21},{6,22},{7,23},{8,24},{9,... | collective-permute-start | bytes 196616 | tf_op jit(solution)/shard_map/ppermute | solution.py:147
  161.3 9.4 %collective-permute-start.31 = (f32[128,128]{1,0:T(8,128)}, f32[128,128]{1,0:T(8,128)S(1)}, u32[]{:S(2)}, u32[]{:S(2)}) collective-permute-start(f32[128,128]{1,0:T(8,128)} %get-tuple-element.65), channel_id=1, source_target_pairs={{16,0},{17,1},{18,2},{19,3},{20,4},{21,5},{22,6},{23,7},{24,8},{25... | collective-permute-start | bytes 196616 | tf_op jit(solution)/shard_map/ppermute | solution.py:148
  175.3 14.8 %collective-permute-start.36 = (f32[128,128]{1,0:T(8,128)}, f32[128,128]{1,0:T(8,128)S(1)}, u32[]{:S(2)}, u32[]{:S(2)}) collective-permute-start(f32[128,128]{1,0:T(8,128)} %get-tuple-element.71), channel_id=1, source_target_pairs={{0,16},{1,17},{2,18},{3,19},{4,20},{5,21},{6,22},{7,23},{8,24},{9,... | collective-permute-start | bytes 196616 | tf_op jit(solution)/shard_map/ppermute | solution.py:147
  179.9 10.2 %collective-permute-start.37 = (f32[128,128]{1,0:T(8,128)}, f32[128,128]{1,0:T(8,128)S(1)}, u32[]{:S(2)}, u32[]{:S(2)}) collective-permute-start(f32[128,128]{1,0:T(8,128)} %get-tuple-element.72), channel_id=1, source_target_pairs={{16,0},{17,1},{18,2},{19,3},{20,4},{21,5},{22,6},{23,7},{24,8},{25... | collective-permute-start | bytes 196616 | tf_op jit(solution)/shard_map/ppermute | solution.py:148
  (41 other events, 172.6 us)
Sparse Core Ops, SparseCore 0:
  194.9 44.3 all-gather.1

commit v2 on v1

v2 whole, which is shorter than its diff:
```python
import jax
import jax.numpy as jnp
from jax import lax
from jax.experimental import pallas as pl
from jax.experimental.pallas import tpu as pltpu
from jax.sharding import PartitionSpec as P

MB = 8
STEPS = 4


WEIGHTS = (0.8, 1.0, 1.25)
SHIFT = 0.2
HEATING = 0.02
CONDUCT = 0.16
SOFTEN = 0.25

H = MB


def _rolls(a):
    rows, lanes = a.shape
    return (
        pltpu.roll(a, rows - 1, 0), pltpu.roll(a, 1, 0),
        pltpu.roll(a, lanes - 1, 1), pltpu.roll(a, 1, 1),
    )


def _em_kernel(factor, last, depth, prof, f, cpl, w, inside, zlo, zhi, *outs):
    diagonal = 6.0 + SHIFT
    if last:
        (heat, own) = outs
        ny, nx = own.shape[2], own.shape[3]
    else:
        (o, oz0, oz1) = outs
    keep = inside[...] > 0.0
    for z in range(depth):
        cur = [f[c * depth + z] for c in range(2)]
        beside = []
        for c in range(2):
            z_up = f[c * depth + z + 1] if z + 1 < depth else zhi[c]
            z_dn = f[c * depth + z - 1] if z > 0 else zlo[c]
            y_up, y_dn, x_up, x_dn = _rolls(cur[c])
            total = z_up + z_dn
            total = total + y_up + y_dn
            beside.append(total + x_up + x_dn)
        k = cpl[z]
        s0 = prof[z] * w[0]
        s1 = prof[z] * w[1]
        real_res = s0 - (diagonal * cur[0] - k * cur[1] - beside[0])
        imag_res = s1 - (diagonal * cur[1] + k * cur[0] - beside[1])
        scaled = factor / (diagonal * diagonal + k * k)
        n0 = jnp.where(keep, cur[0] + scaled * (diagonal * real_res + k * imag_res), 0.0)
        n1 = jnp.where(keep, cur[1] + scaled * (diagonal * imag_res - k * real_res), 0.0)
        if last:
            heat[z] = HEATING * k * (n0 * n0 + n1 * n1)
            own[0, z] = n0[0:ny, 0:nx]
            own[1, z] = n1[0:ny, 0:nx]
        else:
            o[z] = n0
            o[depth + z] = n1
            if z == 0:
                oz0[0] = n0
                oz0[1] = n1
            if z == depth - 1:
                oz1[0] = n0
                oz1[1] = n1


def _heat_kernel(last, depth, t, q, m, tzlo, tzhi, *outs):
    if last:
        (own,) = outs
        ny, nx = own.shape[1], own.shape[2]
    else:
        (o, oz0, oz1) = outs
    for z in range(depth):
        c = t[z]
        z_up = t[z + 1] if z + 1 < depth else tzhi[...]
        z_dn = t[z - 1] if z > 0 else tzlo[...]
        y_up, y_dn, x_up, x_dn = _rolls(c)
        mc = m[z + 1]
        my_up, my_dn, mx_up, mx_dn = _rolls(mc)
        centre_kappa = 1.0 / (1.0 + SOFTEN * c * c)
        flux = jnp.zeros_like(c)
        for other, other_mask in (
            (z_up, m[z + 2]), (z_dn, m[z]), (y_up, my_up), (y_dn, my_dn), (x_up, mx_up), (x_dn, mx_dn)
        ):
            kappa = 1.0 / (1.0 + SOFTEN * other * other)
            flux = flux + other_mask * (centre_kappa + kappa) * (other - c)
        new = c + 0.5 * CONDUCT * mc * flux + q[z]
        if last:
            own[z] = new[0:ny, 0:nx]
        else:
            o[z] = new
            if z == 0:
                oz0[...] = new
            if z == depth - 1:
                oz1[...] = new


def _vmem_call(kernel, out_shape, n_in, smem_first=False):
    specs = [pl.BlockSpec(memory_space=pltpu.VMEM)] * n_in
    if smem_first:
        specs[0] = pl.BlockSpec(memory_space=pltpu.SMEM)
    return pl.pallas_call(
        kernel,
        out_shape=out_shape,
        in_specs=specs,
        out_specs=[pl.BlockSpec(memory_space=pltpu.VMEM)] * len(out_shape),
    )


def _line_pairs(n, first=0):
    up = [(i, i + 1) for i in range(first, n - 1)]
    down = [(j, i) for i, j in up]
    return up, down


def _frame_index(start, own, total):
    nb, tb, hb = own // MB, total // MB, H // MB
    body = jnp.arange(nb + hb)
    tail = jnp.arange(-hb, 0)
    gap = jnp.full((tb - nb - 2 * hb,), -(10 ** 6), jnp.int32)
    return start // MB + jnp.concatenate([body, gap, tail]).astype(jnp.int32)


def _expand(blocks):
    cells = jnp.repeat(blocks, MB, axis=0)
    cells = jnp.repeat(cells, MB, axis=1)
    return jnp.repeat(cells, MB, axis=2).astype(jnp.float32)


def _pick(flags, zi, yi, xi):
    ok = [(i >= 0) & (i < n) for i, n in zip((zi, yi, xi), flags.shape)]
    sel = jnp.take(flags, jnp.clip(zi, 0, flags.shape[0] - 1), axis=0)
    sel = jnp.take(sel, jnp.clip(yi, 0, flags.shape[1] - 1), axis=1)
    sel = jnp.take(sel, jnp.clip(xi, 0, flags.shape[2] - 1), axis=2)
    valid = ok[0][:, None, None] & ok[1][None, :, None] & ok[2][None, None, :]
    return jnp.where(valid, sel, 0)


def on_device(
    earlier_window_curl_state,
    material_resistivity_inverse,
    winding_current_pattern,
    winding_axial_centre,
    specimen_presence_flags,
    specimen_kelvin_values,
):
    depth, height, breadth = material_resistivity_inverse.shape
    n_gz, n_gy, n_gx = lax.axis_size("gz"), lax.axis_size("gy"), lax.axis_size("gx")
    z_total, y_total, x_total = depth * n_gz, height * n_gy, breadth * n_gx
    gz_i, gy_i, gx_i = lax.axis_index("gz"), lax.axis_index("gy"), lax.axis_index("gx")
    z_start, y_start, x_start = gz_i * depth, gy_i * height, gx_i * breadth
    rows = height + 2 * H
    lanes = -(-(breadth + 2 * H) // 128) * 128
    gap = lanes - breadth - 2 * H
    specimen_columns = specimen_kelvin_values.shape[2]
    offset = x_total - specimen_columns
    assert offset % breadth == 0 and depth % MB == 0 and height % MB == 0 and breadth % MB == 0
    first_owner = offset // breadth

    coil_width = z_total // 4
    axial = (
        (z_start + jnp.arange(depth)).astype(jnp.float32)
        - winding_axial_centre[0].astype(jnp.float32)
    ) / coil_width
    profile = 1.0 / (1.0 + axial * axial)

    stack = jnp.concatenate(
        [earlier_window_curl_state.reshape(2 * depth, height, breadth), material_resistivity_inverse,
         winding_current_pattern], axis=0)
    up_x, down_x = _line_pairs(n_gx)
    from_left = lax.ppermute(jnp.swapaxes(stack[:, :, breadth - H:], 1, 2), "gx", up_x)
    from_right = lax.ppermute(jnp.swapaxes(stack[:, :, :H], 1, 2), "gx", down_x)
    nch = stack.shape[0]
    xext = jnp.concatenate(
        [stack, jnp.swapaxes(from_right, 1, 2), jnp.zeros((nch, height, gap), jnp.float32),
         jnp.swapaxes(from_left, 1, 2)], axis=2)

    j_start = x_start - offset
    kpad = jnp.pad(specimen_kelvin_values, ((0, 0), (0, 0), (H, H)))
    t_body = lax.dynamic_slice_in_dim(kpad, j_start + H, breadth + H, 2)
    t_tail = lax.dynamic_slice_in_dim(kpad, j_start, H, 2)
    t_x = jnp.concatenate([t_body, jnp.zeros((depth, height, gap), jnp.float32), t_tail], axis=2)

    ystack = jnp.concatenate([xext, t_x], axis=0)
    up_y, down_y = _line_pairs(n_gy)
    from_above = lax.ppermute(ystack[:, height - H:, :], "gy", up_y)
    from_below = lax.ppermute(ystack[:, :H, :], "gy", down_y)
    frame = jnp.concatenate([ystack, from_below, from_above], axis=1)
    field = frame[: 2 * depth]
    material = frame[2 * depth: 3 * depth]
    winding = frame[3 * depth: 3 * depth + 2]
    kelvin = frame[3 * depth + 2:]

    yi = _frame_index(y_start, height, rows)
    xi = _frame_index(x_start, breadth, lanes)
    ycell = jnp.repeat(yi, MB) * MB + jnp.tile(jnp.arange(MB), rows // MB)
    xcell = jnp.repeat(xi, MB) * MB + jnp.tile(jnp.arange(MB), lanes // MB)
    inside = (((ycell >= 0) & (ycell < y_total))[:, None]
              & ((xcell >= 0) & (xcell < x_total))[None, :]).astype(jnp.float32)
    zb = z_start // MB + jnp.arange(depth // MB)
    coupling = _expand(_pick(specimen_presence_flags, zb, yi, xi)) * material
    tz = z_start // MB + jnp.arange(-1, depth // MB + 1)
    tb = _pick(specimen_presence_flags, tz, yi, xi)
    tb = jnp.where((xi >= offset // MB)[None, None, :], tb, 0)
    t_mask = _expand(tb)[MB - 1: MB + 1 + depth]

    up_z, down_z = _line_pairs(n_gz)
    fshape = jax.ShapeDtypeStruct((2 * depth, rows, lanes), jnp.float32)
    plane2 = jax.ShapeDtypeStruct((2, rows, lanes), jnp.float32)
    qshape = jax.ShapeDtypeStruct((depth, rows, lanes), jnp.float32)
    oshape = jax.ShapeDtypeStruct((2, depth, height, breadth), jnp.float32)
    lo_plane = field[jnp.array([0, depth])]
    hi_plane = field[jnp.array([depth - 1, 2 * depth - 1])]
    for i, factor in enumerate(WEIGHTS):
        last = i == len(WEIGHTS) - 1
        zlo = lax.ppermute(hi_plane, "gz", up_z)
        zhi = lax.ppermute(lo_plane, "gz", down_z)
        outs = (qshape, oshape) if last else (fshape, plane2, plane2)
        res = _vmem_call(
            lambda *r, factor=factor, last=last: _em_kernel(factor, last, depth, *r), outs, 7, True
        )(profile, field, coupling, winding, inside, zlo, zhi)
        if last:
            heat, field_out = res
        else:
            field, lo_plane, hi_plane = res

    tshape = jax.ShapeDtypeStruct((depth, rows, lanes), jnp.float32)
    tplane = jax.ShapeDtypeStruct((rows, lanes), jnp.float32)
    town = jax.ShapeDtypeStruct((depth, height, breadth), jnp.float32)
    lo_t, hi_t = kelvin[0], kelvin[depth - 1]
    for number in range(STEPS):
        last = number == STEPS - 1
        tzlo = lax.ppermute(hi_t, "gz", up_z)
        tzhi = lax.ppermute(lo_t, "gz", down_z)
        outs = (town,) if last else (tshape, tplane, tplane)
        res = _vmem_call(
            lambda *r, last=last: _heat_kernel(last, depth, *r), outs, 5
        )(kelvin, heat, t_mask, tzlo, tzhi)
        if last:
            (own_t,) = res
        else:
            kelvin, lo_t, hi_t = res

    owners = list(range(first_owner, n_gx))
    held = [own_t]
    for s in range(1, n_gx):
        held.append(lax.ppermute(own_t, "gx", [(k, (k + s) % n_gx) for k in owners]))
    held = jnp.stack(held)
    pieces = [lax.dynamic_index_in_dim(held, (gx_i - k) % n_gx, 0, keepdims=False) for k in owners]
    segment_kelvin = jnp.concatenate(pieces, axis=2)
    return (field_out, segment_kelvin)


def solution(mesh):
    placed = (
        P(None, "gz", "gy", "gx"),
        P("gz", "gy", "gx"),
        P(None, "gy", "gx"),
        P(),
        P(),
        P("gz", "gy", None),
    )
    return jax.shard_map(
        on_device,
        mesh=mesh,
        in_specs=placed,
        out_specs=(P(None, "gz", "gy", "gx"), P("gz", "gy", None)),
        check_vma=False,
    )
```

time: 251 us -> 189 us (0.75)
  starting transfers between devices: 102 us -> 42.2 us
  other arithmetic: 1.61 us -> 18.9 us
  local copies, waits for them, and re-layouts: 44.6 us -> 30.6 us
  Pallas kernels: 28 us -> 41.6 us
  between operations: 15.4 us -> 2.02 us
  waiting for transfers between devices: 57.5 us -> 52.9 us
    ppermute x42 -> x21, starting transfers between devices: 102 us -> 42.2 us  [the longest x4 10.5 us: on_device(): tzlo = lax.ppermute(hi_t, 'gz', up_z)]
    all_gather x1 -> x0, waiting for transfers between devices: 44.5 us -> none  [on_device(): gathered = lax.all_gather(kelvin, 'gx', axis=2, tiled=True)]
    ppermute x42 -> x21, waiting for transfers between devices: 13 us -> 52.9 us  [the longest x3 21.6 us: on_device(): lax.ppermute(own_t, 'gx', [(k, (k + s) % n_gx) for k in owners])]
    slice x13 -> x7, local copies, waits for them, and re-layouts: 21 us -> 4.07 us  [the longest x5 3.13 us: on_device(): t_mask = _expand(tb)[MB - 1:MB + 1 + depth]]
    concatenate x0 -> x3, other arithmetic: none -> 9.21 us  [the longest x1 6.38 us: on_device(): frame = jnp.concatenate([ystack, from_below, from_above], axis=1)]
    pallas_call x4, Pallas kernels: 15.9 us -> 23.8 us  [on_device(): _vmem_call(lambda *r, last=last: _heat_kernel(last, depth, *r), outs, 5)]
    pallas_call x3, Pallas kernels: 12.1 us -> 17.8 us  [on_device(): _vmem_call(lambda *r, factor=factor, last=last: _em_kernel(factor, last,...]
    slice x0 -> x2, other arithmetic: none -> 5.23 us  [the longest x1 3.29 us: on_device(): kelvin = frame[3 * depth + 2:]]
  transfers between devices with their start and end apart: 43 -> 21, of which waited for: 5 -> 13; matrix products, arithmetic and copies ran while one was open for 16% -> 13% of each run, Pallas kernels for 3% -> 6%
where the time goes in v2:
time: 189 us; the launch traced here: 188 us
  waiting for transfers between devices  52.9 us (28%)
  starting transfers between devices  42.2 us (22%)
  Pallas kernels  41.6 us (22%)
  local copies, waits for them, and re-layouts  30.6 us (16%)
  other arithmetic  18.9 us (10%)
  between operations  2.02 us (1%)
    pallas_call x4, Pallas kernels, on_device(): _vmem_call(lambda *r, last=last: _heat_kernel(last, depth, *r), outs, 5)  23.8 us
    ppermute x3, waiting for transfers between devices, on_device(): lax.ppermute(own_t, 'gx', [(k, (k + s) % n_gx) for k in owners])  21.6 us
    pallas_call x3, Pallas kernels, on_device(): _vmem_call(lambda *r, factor=factor, last=last: _em_kernel(factor, last,...  17.8 us
    ppermute x4, waiting for transfers between devices, on_device(): tzhi = lax.ppermute(lo_t, 'gz', down_z)  12.8 us
    ppermute x4, starting transfers between devices, on_device(): tzlo = lax.ppermute(hi_t, 'gz', up_z)  10.5 us
    ppermute x3, waiting for transfers between devices, on_device(): zhi = lax.ppermute(lo_plane, 'gz', down_z)  9.48 us
    ppermute x3, starting transfers between devices, on_device(): zlo = lax.ppermute(hi_plane, 'gz', up_z)  7.23 us
    unnamed x56, local copies, waits for them, and re-layouts  7.23 us
  transfers between devices with their start and end apart: 21, of which 13 were waited for; matrix products, arithmetic and copies ran while one was open for 13% of the time, Pallas kernels for 6%

profile of v2, /device:TPU:0, one launch (start us, length us, event | category | flops | bytes accessed | tf_op | source)
XLA Modules:
  0.0 188.2 jit_solution(3140573249045965569)
XLA Ops:
  0.6 1.6 pad_maximum_fusion.2
  4.0 3.1 %collective-permute-start.1 = (f32[26,8,128]{2,1,0:T(8,128)}, f32[26,8,128]{2,1,0:T(8,128)}, u32[]{:S(2)}, u32[]{:S(2)}) collective-permute-start(f32[26,8,128]{2,1,0:T(8,128)} %copy.50), channel_id=1, source_target_pairs={{0,1},{1,2},{2,3},{4,5},{5,6},{6,7},{8,9},{9,10},{10,11},{12,13},{... | collective-permute-start | bytes 319496 | tf_op jit(solution)/shard_map/ppermute | solution.py:174
  22.9 1.9 %maximum_maximum_fusion = (f32[34,8,256]{2,1,0:T(8,128)}, f32[34,8,256]{2,1,0:T(8,128)}) fusion(f32[8,128,8]{2,1,0:T(8,128)} %pad_dynamic-slice_fusion, f32[26,128,8]{2,1,0:T(8,128)S(1)} %bitcast.59, f32[8,128,112]{2,1,0:T(8,128)S(1)} %broadcast_in_dim.126, f32[8,128,136]{2,1,0:T(8,128)S(1)} %copy-done.4, f32[26,128,112]{2,1,0:T(8,128)S(1)} %broadcast_in_dim.125, ...), kind=kLoop, calls=%fused_computation.29 | loop fusion | flops 1114112 | bytes 5013504 | tf_op jit(solution)/shard_map/slice | solution.py:190
  26.1 5.7 %collective-permute-start.3 = (f32[34,8,256]{2,1,0:T(8,128)}, f32[34,8,256]{2,1,0:T(8,128)}, u32[]{:S(2)}, u32[]{:S(2)}) collective-permute-start(f32[34,8,256]{2,1,0:T(8,128)} %get-tuple-element.48), channel_id=1, source_target_pairs={{0,4},{4,8},{8,12},{1,5},{5,9},{9,13},{2,6},{6,10},{10,14},{3,7},{... | collective-permute-start | bytes 835592 | tf_op jit(solution)/shard_map/ppermute | solution.py:189
  33.0 1.7 copy.55
  37.5 6.4 %pad_maximum_fusion = f32[34,144,256]{2,1,0:T(8,128)S(1)} fusion(f32[34,8,256]{2,1,0:T(8,128)} %collective-permute-done.3, f32[34,8,256]{2,1,0:T(8,128)} %collective-permute-done.2, f32[8,128,8]{2,1,0:T(8,128)} %pad_dynamic-slice_fusion, f32[8,128,112]{2,1,0:T(8,128)} %copy-done.6, f32[8,128,136]{2,1,0:T(8,128)} %pad_dynamic-slice_fusion.1, ...), kind=kLoop, calls=%fused_computation.7 | loop fusion | flops 12533760 | bytes 10027008 | tf_op jit(solution)/shard_map/concatenate | solution.py:191
  48.3 4.2 %collective-permute-start.4 = (f32[2,144,256]{2,1,0:T(8,128)}, f32[2,144,256]{2,1,0:T(8,128)S(1)}, u32[]{:S(2)}, u32[]{:S(2)}) collective-permute-start(f32[2,144,256]{2,1,0:T(8,128)} %gather_fusion.2), channel_id=1, source_target_pairs={{0,16},{1,17},{2,18},{3,19},{4,20},{5,21},{6,22},{7,23},{8,24},{9,... | collective-permute-start | bytes 884744 | tf_op jit(solution)/shard_map/ppermute | solution.py:219
  53.8 3.3 %fusion.15 = (f32[8,144,256]{2,1,0:T(8,128)}, f32[8,144,256]{2,1,0:T(8,128)}) fusion(f32[34,144,256]{2,1,0:T(8,128)} %copy-done, f32[144,256]{1,0:T(8,128)S(1)} %copy-done.8), kind=kLoop, calls=%fused_computation.84 | loop fusion | flops 294912 | bytes 4866048 | tf_op jit(solution)/shard_map/slice | solution.py:195
  57.1 3.0 %collective-permute-done.4.r_5_ = f32[2,144,256]{2,1,0:T(8,128)S(1)} collective-permute-done((f32[2,144,256]{2,1,0:T(8,128)}, f32[2,144,256]{2,1,0:T(8,128)S(1)}, u32[]{:S(2)}, u32[]{:S(2)}) %collective-permute-start.4) | collective-permute-done | bytes 294944 | tf_op jit(solution)/shard_map/ppermute | solution.py:219
  60.1 3.8 %collective-permute-done.5.r_6_ = f32[2,144,256]{2,1,0:T(8,128)S(1)} collective-permute-done((f32[2,144,256]{2,1,0:T(8,128)S(1)}, f32[2,144,256]{2,1,0:T(8,128)S(1)}, u32[]{:S(2)}, u32[]{:S(2)}) %collective-permute-start.5) | collective-permute-done | bytes 294944 | tf_op jit(solution)/shard_map/ppermute | solution.py:220
  64.6 6.0 %shard_map.95 = (f32[16,144,256]{2,1,0:T(8,128)}, f32[2,144,256]{2,1,0:T(8,128)}, f32[2,144,256]{2,1,0:T(8,128)}) custom-call(f32[8]{0:T(128)} %add_divide_fusion.r_0_, f32[16,144,256]{2,1,0:T(8,128)} %copy-done.2, f32[8,144,256]{2,1,0:T(8,128)} %get-tuple-element.52.r_2_, f32[2,144,256]{2,1,0:T(8,128)} %slice.83.r_3_, f32[144,256]{1,0:T(8,128)} %and_convert_fusion.r_4_, ...), custom_call_target="tpu_custom_call" | custom-call | tf_op jit(solution)/shard_map/pallas_call | solution.py:222
  73.8 1.7 slice_bitcast_fusion.2
  76.8 5.9 %collective-permute-start.10 = (f32[144,256]{1,0:T(8,128)}, f32[144,256]{1,0:T(8,128)}, u32[]{:S(2)}, u32[]{:S(2)}) collective-permute-start(f32[144,256]{1,0:T(8,128)} %get-tuple-element.50), channel_id=1, source_target_pairs={{0,16},{1,17},{2,18},{3,19},{4,20},{5,21},{6,22},{7,23},{8,24},{9,... | collective-permute-start | bytes 442376 | tf_op jit(solution)/shard_map/ppermute | solution.py:236
  84.8 5.8 %shard_map.96 = (f32[16,144,256]{2,1,0:T(8,128)}, f32[2,144,256]{2,1,0:T(8,128)}, f32[2,144,256]{2,1,0:T(8,128)}) custom-call(f32[8]{0:T(128)} %add_divide_fusion.r_0_, f32[16,144,256]{2,1,0:T(8,128)} %get-tuple-element.19.r_1_, f32[8,144,256]{2,1,0:T(8,128)} %get-tuple-element.52.r_2_, f32[2,144,256]{2,1,0:T(8,128)} %slice.83.r_3_, ...), custom_call_target="tpu_custom_call" | custom-call | tf_op jit(solution)/shard_map/pallas_call | solution.py:222
  90.6 1.6 collective-permute-start.8
  93.7 1.8 copy.60.r_2_
  96.7 4.3 %collective-permute-done.9.r_6_ = f32[2,144,256]{2,1,0:T(8,128)S(1)} collective-permute-done((f32[2,144,256]{2,1,0:T(8,128)}, f32[2,144,256]{2,1,0:T(8,128)S(1)}, u32[]{:S(2)}, u32[]{:S(2)}) %collective-permute-start.9) | collective-permute-done | bytes 294944 | tf_op jit(solution)/shard_map/ppermute | solution.py:220
  101.8 5.9 %shard_map.97 = (f32[8,144,256]{2,1,0:T(8,128)}, f32[2,8,128,128]{3,2,1,0:T(8,128)}) custom-call(f32[8]{0:T(128)} %add_divide_fusion.r_0_, f32[16,144,256]{2,1,0:T(8,128)} %get-tuple-element.22.r_1_, f32[8,144,256]{2,1,0:T(8,128)} %get-tuple-element.52.r_2_, f32[2,144,256]{2,1,0:T(8,128)} %slice.83.r_3_, f32[144,256]{1,0:T(8,128)} %and_convert_fusion.r_4_, ...), custom_call_target="tpu_custom_call" | custom-call | tf_op jit(solution)/shard_map/pallas_call | solution.py:222
  107.7 6.5 %shard_map.98 = (f32[8,144,256]{2,1,0:T(8,128)}, f32[144,256]{1,0:T(8,128)}, f32[144,256]{1,0:T(8,128)}) custom-call(f32[8,144,256]{2,1,0:T(8,128)} %get-tuple-element.51.r_0_, f32[8,144,256]{2,1,0:T(8,128)} %get-tuple-element.26.r_1_, f32[10,144,256]{2,1,0:T(8,128)} %copy.60.r_2_, f32[144,256]{1,0:T(8,128)} %collective-permute-done.10.r_3_, ...), custom_call_target="tpu_custom_call" | custom-call | tf_op jit(solution)/shard_map/pallas_call | solution.py:239
  114.2 1.5 collective-permute-start.12
  118.7 4.3 %collective-permute-done.13.r_4_ = f32[144,256]{1,0:T(8,128)S(1)} collective-permute-done((f32[144,256]{1,0:T(8,128)}, f32[144,256]{1,0:T(8,128)S(1)}, u32[]{:S(2)}, u32[]{:S(2)}) %collective-permute-start.13) | collective-permute-done | bytes 147488 | tf_op jit(solution)/shard_map/ppermute | solution.py:237
  123.7 6.5 %shard_map.99 = (f32[8,144,256]{2,1,0:T(8,128)}, f32[144,256]{1,0:T(8,128)}, f32[144,256]{1,0:T(8,128)}) custom-call(f32[8,144,256]{2,1,0:T(8,128)} %get-tuple-element.27.r_0_, f32[8,144,256]{2,1,0:T(8,128)} %get-tuple-element.26.r_1_, f32[10,144,256]{2,1,0:T(8,128)} %copy.60.r_2_, f32[144,256]{1,0:T(8,128)} %copy-done.17, f32[144,256]{1,0:T(8,128)} %copy-done.20), custom_call_target="tpu_custom_call" | custom-call | tf_op jit(solution)/shard_map/pallas_call | solution.py:239
  130.1 1.6 collective-permute-start.14
  133.0 1.7 collective-permute-done.14.r_3_
  134.7 4.3 %collective-permute-done.15.r_4_ = f32[144,256]{1,0:T(8,128)S(1)} collective-permute-done((f32[144,256]{1,0:T(8,128)}, f32[144,256]{1,0:T(8,128)S(1)}, u32[]{:S(2)}, u32[]{:S(2)}) %collective-permute-start.15) | collective-permute-done | bytes 147488 | tf_op jit(solution)/shard_map/ppermute | solution.py:237
  139.6 6.5 %shard_map.100 = (f32[8,144,256]{2,1,0:T(8,128)}, f32[144,256]{1,0:T(8,128)}, f32[144,256]{1,0:T(8,128)}) custom-call(f32[8,144,256]{2,1,0:T(8,128)} %get-tuple-element.30.r_0_, f32[8,144,256]{2,1,0:T(8,128)} %get-tuple-element.26.r_1_, f32[10,144,256]{2,1,0:T(8,128)} %copy.60.r_2_, f32[144,256]{1,0:T(8,128)} %copy-done.18, f32[144,256]{1,0:T(8,128)} %copy-done.21), custom_call_target="tpu_custom_call" | custom-call | tf_op jit(solution)/shard_map/pallas_call | solution.py:239
  146.1 1.6 collective-permute-start.16
  149.0 1.7 collective-permute-done.16.r_3_
  150.7 4.3 %collective-permute-done.17.r_4_ = f32[144,256]{1,0:T(8,128)S(1)} collective-permute-done((f32[144,256]{1,0:T(8,128)}, f32[144,256]{1,0:T(8,128)S(1)}, u32[]{:S(2)}, u32[]{:S(2)}) %collective-permute-start.17) | collective-permute-done | bytes 147488 | tf_op jit(solution)/shard_map/ppermute | solution.py:237
  155.6 4.4 %shard_map.101 = f32[8,128,128]{2,1,0:T(8,128)} custom-call(f32[8,144,256]{2,1,0:T(8,128)} %get-tuple-element.33.r_0_, f32[8,144,256]{2,1,0:T(8,128)} %get-tuple-element.26.r_1_, f32[10,144,256]{2,1,0:T(8,128)} %copy.60.r_2_, f32[144,256]{1,0:T(8,128)} %copy-done.19, f32[144,256]{1,0:T(8,128)} %copy-done.22), custom_call_target="tpu_custom_call" | custom-call | tf_op jit(solution)/shard_map/pallas_call | solution.py:239
  164.0 17.5 %collective-permute-done.19 = f32[8,128,128]{2,1,0:T(8,128)S(1)} collective-permute-done((f32[8,128,128]{2,1,0:T(8,128)}, f32[8,128,128]{2,1,0:T(8,128)S(1)}, u32[]{:S(2)}, u32[]{:S(2)}) %collective-permute-start.19) | collective-permute-done | bytes 524320 | tf_op jit(solution)/shard_map/ppermute | solution.py:250
  181.5 4.1 %collective-permute-done.18 = f32[8,128,128]{2,1,0:T(8,128)S(1)} collective-permute-done((f32[8,128,128]{2,1,0:T(8,128)}, f32[8,128,128]{2,1,0:T(8,128)S(1)}, u32[]{:S(2)}, u32[]{:S(2)}) %collective-permute-start.18) | collective-permute-done | bytes 524320 | tf_op jit(solution)/shard_map/ppermute | solution.py:250
  (141 shorter events, 52.2 us)
Async XLA Ops:
  2.8 6.8 %copy-start.24 = (s32[32]{0:T(128)S(1)}, s32[32]{0:T(128)}, u32[]{:S(2)}) copy-start(s32[32]{0:T(128)} %constant.243.clone.1) | copy-start | bytes 388
  2.8 7.5 %copy-start.27 = (s32[32,1]{0,1:T(1,128)S(1)}, s32[32,1]{0,1:T(1,128)}, u32[]{:S(2)}) copy-start(s32[32,1]{0,1:T(1,128)} %constant.249.clone.1) | copy-start | bytes 388
  2.8 7.5 %copy-start.26 = (s32[18,1]{0,1:T(1,128)S(1)}, s32[18,1]{0,1:T(1,128)}, u32[]{:S(2)}) copy-start(s32[18,1]{0,1:T(1,128)} %constant.248.clone.1) | copy-start | bytes 220
  2.9 7.5 %copy-start.25 = (s32[18]{0:T(128)S(1)}, s32[18]{0:T(128)}, u32[]{:S(2)}) copy-start(s32[18]{0:T(128)} %constant.241.clone.1) | copy-start | bytes 220
  2.9 7.8 %copy-start.16 = (s32[2,64,64]{2,1,0:T(8,128)S(1)}, s32[2,64,64]{2,1,0:T(8,128)}, u32[]{:S(2)}) copy-start(s32[2,64,64]{2,1,0:T(8,128)} %param.12) | copy-start | bytes 98308
  4.0 11.2 %copy-start.5 = (f32[8,128,384]{2,1,0:T(8,128)S(1)}, f32[8,128,384]{2,1,0:T(8,128)}, u32[]{:S(2)}) copy-start(f32[8,128,384]{2,1,0:T(8,128)} %param.13) | copy-start | bytes 4718596
  4.0 15.7 %collective-permute-start.1 = (f32[26,8,128]{2,1,0:T(8,128)}, f32[26,8,128]{2,1,0:T(8,128)}, u32[]{:S(2)}, u32[]{:S(2)}) collective-permute-start(f32[26,8,128]{2,1,0:T(8,128)} %copy.50), channel_id=1, source_target_pairs={{0,1},{1,2},{2,3},{4,5},{5,6},{6,7},{8,9},{9,10},{10,11},{12,13},{... | collective-permute-start | bytes 319496 | tf_op jit(solution)/shard_map/ppermute | solution.py:174
  8.2 10.0 %collective-permute-start = (f32[26,8,128]{2,1,0:T(8,128)}, f32[26,8,128]{2,1,0:T(8,128)}, u32[]{:S(2)}, u32[]{:S(2)}) collective-permute-start(f32[26,8,128]{2,1,0:T(8,128)} %copy.48), channel_id=1, source_target_pairs={{1,0},{2,1},{3,2},{5,4},{6,5},{7,6},{9,8},{10,9},{11,10},{13,12},{... | collective-permute-start | bytes 319496 | tf_op jit(solution)/shard_map/ppermute | solution.py:175
  24.8 12.7 %collective-permute-start.2 = (f32[34,8,256]{2,1,0:T(8,128)}, f32[34,8,256]{2,1,0:T(8,128)}, u32[]{:S(2)}, u32[]{:S(2)}) collective-permute-start(f32[34,8,256]{2,1,0:T(8,128)} %get-tuple-element.47), channel_id=1, source_target_pairs={{4,0},{8,4},{12,8},{5,1},{9,5},{13,9},{6,2},{10,6},{14,10},{7,3},{... | collective-permute-start | bytes 835592 | tf_op jit(solution)/shard_map/ppermute | solution.py:190
  26.1 11.4 %collective-permute-start.3 = (f32[34,8,256]{2,1,0:T(8,128)}, f32[34,8,256]{2,1,0:T(8,128)}, u32[]{:S(2)}, u32[]{:S(2)}) collective-permute-start(f32[34,8,256]{2,1,0:T(8,128)} %get-tuple-element.48), channel_id=1, source_target_pairs={{0,4},{4,8},{8,12},{1,5},{5,9},{9,13},{2,6},{6,10},{10,14},{3,7},{... | collective-permute-start | bytes 835592 | tf_op jit(solution)/shard_map/ppermute | solution.py:189
  46.3 7.6 %copy-start.8 = (f32[144,256]{1,0:T(8,128)S(1)}, f32[144,256]{1,0:T(8,128)}, u32[]{:S(2)}) copy-start(f32[144,256]{1,0:T(8,128)} %copy.55) | copy-start | bytes 442372
  46.4 10.7 %copy-start.2 = (f32[16,144,256]{2,1,0:T(8,128)}, f32[16,144,256]{2,1,0:T(8,128)S(1)}, u32[]{:S(2)}) copy-start(f32[16,144,256]{2,1,0:T(8,128)S(1)} %slice.81.r_1_) | copy-start | bytes 7077892
  48.3 11.8 %collective-permute-start.4 = (f32[2,144,256]{2,1,0:T(8,128)}, f32[2,144,256]{2,1,0:T(8,128)S(1)}, u32[]{:S(2)}, u32[]{:S(2)}) collective-permute-start(f32[2,144,256]{2,1,0:T(8,128)} %gather_fusion.2), channel_id=1, source_target_pairs={{0,16},{1,17},{2,18},{3,19},{4,20},{5,21},{6,22},{7,23},{8,24},{9,... | collective-permute-start | bytes 884744 | tf_op jit(solution)/shard_map/ppermute | solution.py:219
  52.5 11.4 %collective-permute-start.5 = (f32[2,144,256]{2,1,0:T(8,128)S(1)}, f32[2,144,256]{2,1,0:T(8,128)S(1)}, u32[]{:S(2)}, u32[]{:S(2)}) collective-permute-start(f32[2,144,256]{2,1,0:T(8,128)S(1)} %gather_fusion.3), channel_id=1, source_target_pairs={{16,0},{17,1},{18,2},{19,3},{20,4},{21,5},{22,6},{23,7},{24,8},{25... | collective-permute-start | bytes 884744 | tf_op jit(solution)/shard_map/ppermute | solution.py:220
  64.6 8.7 %copy-start.9 = (f32[10,18,32]{2,1,0:T(8,128)S(1)}, f32[10,18,32]{2,1,0:T(8,128)}, u32[]{:S(2)}) copy-start(f32[10,18,32]{2,1,0:T(8,128)} %slice.85) | copy-start | bytes 69124
  70.6 12.1 %collective-permute-start.6 = (f32[2,144,256]{2,1,0:T(8,128)}, f32[2,144,256]{2,1,0:T(8,128)S(1)}, u32[]{:S(2)}, u32[]{:S(2)}) collective-permute-start(f32[2,144,256]{2,1,0:T(8,128)} %get-tuple-element.20), channel_id=1, source_target_pairs={{0,16},{1,17},{2,18},{3,19},{4,20},{5,21},{6,22},{7,23},{8,24},{9,... | collective-permute-start | bytes 884744 | tf_op jit(solution)/shard_map/ppermute | solution.py:219
  72.0 12.0 %collective-permute-start.7 = (f32[2,144,256]{2,1,0:T(8,128)}, f32[2,144,256]{2,1,0:T(8,128)S(1)}, u32[]{:S(2)}, u32[]{:S(2)}) collective-permute-start(f32[2,144,256]{2,1,0:T(8,128)} %get-tuple-element.21), channel_id=1, source_target_pairs={{16,0},{17,1},{18,2},{19,3},{20,4},{21,5},{22,6},{23,7},{24,8},{25... | collective-permute-start | bytes 884744 | tf_op jit(solution)/shard_map/ppermute | solution.py:220
  75.5 32.2 %collective-permute-start.11 = (f32[144,256]{1,0:T(8,128)}, f32[144,256]{1,0:T(8,128)}, u32[]{:S(2)}, u32[]{:S(2)}) collective-permute-start(f32[144,256]{1,0:T(8,128)} %get-tuple-element.49), channel_id=1, source_target_pairs={{16,0},{17,1},{18,2},{19,3},{20,4},{21,5},{22,6},{23,7},{24,8},{25... | collective-permute-start | bytes 442376 | tf_op jit(solution)/shard_map/ppermute | solution.py:237
  76.8 30.9 %collective-permute-start.10 = (f32[144,256]{1,0:T(8,128)}, f32[144,256]{1,0:T(8,128)}, u32[]{:S(2)}, u32[]{:S(2)}) collective-permute-start(f32[144,256]{1,0:T(8,128)} %get-tuple-element.50), channel_id=1, source_target_pairs={{0,16},{1,17},{2,18},{3,19},{4,20},{5,21},{6,22},{7,23},{8,24},{9,... | collective-permute-start | bytes 442376 | tf_op jit(solution)/shard_map/ppermute | solution.py:236
  90.6 6.1 %collective-permute-start.8 = (f32[2,144,256]{2,1,0:T(8,128)}, f32[2,144,256]{2,1,0:T(8,128)S(1)}, u32[]{:S(2)}, u32[]{:S(2)}) collective-permute-start(f32[2,144,256]{2,1,0:T(8,128)} %get-tuple-element.23), channel_id=1, source_target_pairs={{0,16},{1,17},{2,18},{3,19},{4,20},{5,21},{6,22},{7,23},{8,24},{9,... | collective-permute-start | bytes 884744 | tf_op jit(solution)/shard_map/ppermute | solution.py:219
  92.2 8.8 %collective-permute-start.9 = (f32[2,144,256]{2,1,0:T(8,128)}, f32[2,144,256]{2,1,0:T(8,128)S(1)}, u32[]{:S(2)}, u32[]{:S(2)}) collective-permute-start(f32[2,144,256]{2,1,0:T(8,128)} %get-tuple-element.24), channel_id=1, source_target_pairs={{16,0},{17,1},{18,2},{19,3},{20,4},{21,5},{22,6},{23,7},{24,8},{25... | collective-permute-start | bytes 884744 | tf_op jit(solution)/shard_map/ppermute | solution.py:220
  96.7 4.3 %copy-start.12 = (f32[2,144,256]{2,1,0:T(8,128)}, f32[2,144,256]{2,1,0:T(8,128)S(1)}, u32[]{:S(2)}) copy-start(f32[2,144,256]{2,1,0:T(8,128)S(1)} %collective-permute-done.8.r_5_) | copy-start | bytes 884740
  114.2 4.5 %collective-permute-start.12 = (f32[144,256]{1,0:T(8,128)}, f32[144,256]{1,0:T(8,128)S(1)}, u32[]{:S(2)}, u32[]{:S(2)}) collective-permute-start(f32[144,256]{1,0:T(8,128)} %get-tuple-element.28), channel_id=1, source_target_pairs={{0,16},{1,17},{2,18},{3,19},{4,20},{5,21},{6,22},{7,23},{8,24},{9,... | collective-permute-start | bytes 442376 | tf_op jit(solution)/shard_map/ppermute | solution.py:236
  115.8 7.2 %collective-permute-start.13 = (f32[144,256]{1,0:T(8,128)}, f32[144,256]{1,0:T(8,128)S(1)}, u32[]{:S(2)}, u32[]{:S(2)}) collective-permute-start(f32[144,256]{1,0:T(8,128)} %get-tuple-element.29), channel_id=1, source_target_pairs={{16,0},{17,1},{18,2},{19,3},{20,4},{21,5},{22,6},{23,7},{24,8},{25... | collective-permute-start | bytes 442376 | tf_op jit(solution)/shard_map/ppermute | solution.py:237
  118.7 4.3 %copy-start.17 = (f32[144,256]{1,0:T(8,128)}, f32[144,256]{1,0:T(8,128)S(1)}, u32[]{:S(2)}) copy-start(f32[144,256]{1,0:T(8,128)S(1)} %collective-permute-done.12.r_3_) | copy-start | bytes 442372
  130.1 4.5 %collective-permute-start.14 = (f32[144,256]{1,0:T(8,128)}, f32[144,256]{1,0:T(8,128)S(1)}, u32[]{:S(2)}, u32[]{:S(2)}) collective-permute-start(f32[144,256]{1,0:T(8,128)} %get-tuple-element.31), channel_id=1, source_target_pairs={{0,16},{1,17},{2,18},{3,19},{4,20},{5,21},{6,22},{7,23},{8,24},{9,... | collective-permute-start | bytes 442376 | tf_op jit(solution)/shard_map/ppermute | solution.py:236
  131.7 7.2 %collective-permute-start.15 = (f32[144,256]{1,0:T(8,128)}, f32[144,256]{1,0:T(8,128)S(1)}, u32[]{:S(2)}, u32[]{:S(2)}) collective-permute-start(f32[144,256]{1,0:T(8,128)} %get-tuple-element.32), channel_id=1, source_target_pairs={{16,0},{17,1},{18,2},{19,3},{20,4},{21,5},{22,6},{23,7},{24,8},{25... | collective-permute-start | bytes 442376 | tf_op jit(solution)/shard_map/ppermute | solution.py:237
  146.1 4.5 %collective-permute-start.16 = (f32[144,256]{1,0:T(8,128)}, f32[144,256]{1,0:T(8,128)S(1)}, u32[]{:S(2)}, u32[]{:S(2)}) collective-permute-start(f32[144,256]{1,0:T(8,128)} %get-tuple-element.34), channel_id=1, source_target_pairs={{0,16},{1,17},{2,18},{3,19},{4,20},{5,21},{6,22},{7,23},{8,24},{9,... | collective-permute-start | bytes 442376 | tf_op jit(solution)/shard_map/ppermute | solution.py:236
  147.7 7.2 %collective-permute-start.17 = (f32[144,256]{1,0:T(8,128)}, f32[144,256]{1,0:T(8,128)S(1)}, u32[]{:S(2)}, u32[]{:S(2)}) collective-permute-start(f32[144,256]{1,0:T(8,128)} %get-tuple-element.35), channel_id=1, source_target_pairs={{16,0},{17,1},{18,2},{19,3},{20,4},{21,5},{22,6},{23,7},{24,8},{25... | collective-permute-start | bytes 442376 | tf_op jit(solution)/shard_map/ppermute | solution.py:237
  160.0 4.0 %collective-permute-start.20 = (f32[8,128,128]{2,1,0:T(8,128)}, f32[8,128,128]{2,1,0:T(8,128)S(1)}, u32[]{:S(2)}, u32[]{:S(2)}) collective-permute-start(f32[8,128,128]{2,1,0:T(8,128)} %shard_map.101), channel_id=1, source_target_pairs={{1,0},{2,1},{3,2},{5,4},{6,5},{7,6},{9,8},{10,9},{11,10},{13,12},{... | collective-permute-start | bytes 1572872 | tf_op jit(solution)/shard_map/ppermute | solution.py:250
  161.3 20.2 %collective-permute-start.19 = (f32[8,128,128]{2,1,0:T(8,128)}, f32[8,128,128]{2,1,0:T(8,128)S(1)}, u32[]{:S(2)}, u32[]{:S(2)}) collective-permute-start(f32[8,128,128]{2,1,0:T(8,128)} %shard_map.101), channel_id=1, source_target_pairs={{1,3},{2,0},{3,1},{5,7},{6,4},{7,5},{9,11},{10,8},{11,9},{13,15},{... | collective-permute-start | bytes 1572872 | tf_op jit(solution)/shard_map/ppermute | solution.py:250
  162.6 23.0 %collective-permute-start.18 = (f32[8,128,128]{2,1,0:T(8,128)}, f32[8,128,128]{2,1,0:T(8,128)S(1)}, u32[]{:S(2)}, u32[]{:S(2)}) collective-permute-start(f32[8,128,128]{2,1,0:T(8,128)} %shard_map.101), channel_id=1, source_target_pairs={{1,2},{2,3},{3,0},{5,6},{6,7},{7,4},{9,10},{10,11},{11,8},{13,14},... | collective-permute-start | bytes 1572872 | tf_op jit(solution)/shard_map/ppermute | solution.py:250
  (17 other events, 33.8 us)

commit v3 on v2

--- a/solution.py
+++ b/solution.py
@@ -26,14 +26,45 @@
     )
 
 
-def _em_kernel(factor, last, depth, prof, f, cpl, w, inside, zlo, zhi, *outs):
+def _selectors(pos, rows, lanes, height, breadth, x_first_block):
+    shift = MB.bit_length() - 1
+    r = lax.shift_right_logical(lax.broadcasted_iota(jnp.int32, (rows, 128), 0), shift)
+    b = lax.broadcasted_iota(jnp.int32, (rows, 128), 1)
+    ty = pos[1] + jnp.where(r < (height + H) // MB, r, r - rows // MB)
+    sy = (b == ty).astype(jnp.float32)
+    l = lax.shift_right_logical(lax.broadcasted_iota(jnp.int32, (lanes, 128), 0), shift)
+    bx = lax.broadcasted_iota(jnp.int32, (lanes, 128), 1)
+    far = jnp.where(l >= (lanes - H) // MB, l - lanes // MB, -(10 ** 6))
+    tx = pos[2] + jnp.where(l < (breadth + H) // MB, l, far)
+    sx = ((bx == tx) & (bx >= x_first_block)).astype(jnp.float32)
+    return sy, sx
+
+
+def _cells(fl, zb, sy, sx):
+    a = jnp.dot(sy, fl[zb], preferred_element_type=jnp.float32)
+    return lax.dot_general(a, sx, (((1,), (1,)), ((), ())), preferred_element_type=jnp.float32)
+
+
+def _inside(pos, rows, lanes, height, breadth, y_total, x_total):
+    r = lax.broadcasted_iota(jnp.int32, (rows, lanes), 0)
+    l = lax.broadcasted_iota(jnp.int32, (rows, lanes), 1)
+    y = pos[1] * MB + jnp.where(r < height + H, r, r - rows)
+    far = jnp.where(l >= lanes - H, l - lanes, -(10 ** 6))
+    x = pos[2] * MB + jnp.where(l < breadth + H, l, far)
+    return (y >= 0) & (y < y_total) & (x >= 0) & (x < x_total)
+
+
+def _em_kernel(factor, last, depth, totals, pos, prof, fl, f, mat, w, zlo, zhi, *outs):
     diagonal = 6.0 + SHIFT
     if last:
         (heat, own) = outs
-        ny, nx = own.shape[2], own.shape[3]
     else:
         (o, oz0, oz1) = outs
-    keep = inside[...] > 0.0
+    height, breadth, y_total, x_total = totals
+    rows, lanes = f.shape[1], f.shape[2]
+    keep = _inside(pos, rows, lanes, height, breadth, y_total, x_total)
+    sy, sx = _selectors(pos, rows, lanes, height, breadth, 0)
+    masks = [_cells(fl, pos[0] + zo, sy, sx) for zo in range(depth // MB)]
     for z in range(depth):
         cur = [f[c * depth + z] for c in range(2)]
         beside = []
@@ -44,7 +75,7 @@
             total = z_up + z_dn
             total = total + y_up + y_dn
             beside.append(total + x_up + x_dn)
-        k = cpl[z]
+        k = masks[z // MB] * mat[z]
         s0 = prof[z] * w[0]
         s1 = prof[z] * w[1]
         real_res = s0 - (diagonal * cur[0] - k * cur[1] - beside[0])
@@ -54,8 +85,8 @@
         n1 = jnp.where(keep, cur[1] + scaled * (diagonal * imag_res - k * real_res), 0.0)
         if last:
             heat[z] = HEATING * k * (n0 * n0 + n1 * n1)
-            own[0, z] = n0[0:ny, 0:nx]
-            own[1, z] = n1[0:ny, 0:nx]
+            own[0, z] = n0[0:height, 0:breadth]
+            own[1, z] = n1[0:height, 0:breadth]
         else:
             o[z] = n0
             o[depth + z] = n1
@@ -67,29 +98,40 @@
                 oz1[1] = n1
 
 
-def _heat_kernel(last, depth, t, q, m, tzlo, tzhi, *outs):
+def _heat_kernel(last, depth, totals, pos, fl, t, q, tzlo, tzhi, *outs):
     if last:
         (own,) = outs
-        ny, nx = own.shape[1], own.shape[2]
     else:
         (o, oz0, oz1) = outs
+    height, breadth, x_first_block = totals
+    rows, lanes = t.shape[1], t.shape[2]
+    sy, sx = _selectors(pos, rows, lanes, height, breadth, x_first_block)
+    zb_total = fl.shape[0]
+    below = pos[0] - 1
+    above = pos[0] + depth // MB
+    m_below = _cells(fl, jnp.maximum(below, 0), sy, sx) * jnp.where(below >= 0, 1.0, 0.0)
+    m_above = _cells(fl, jnp.minimum(above, zb_total - 1), sy, sx) * jnp.where(
+        above < zb_total, 1.0, 0.0)
+    m_own = [_cells(fl, pos[0] + zo, sy, sx) for zo in range(depth // MB)]
+    planes = [m_below] + [m_own[z // MB] for z in range(depth)] + [m_above]
+    temps = [tzlo[...]] + [t[z] for z in range(depth)] + [tzhi[...]]
+    kaps = [1.0 / (1.0 + SOFTEN * v * v) for v in temps]
     for z in range(depth):
-        c = t[z]
-        z_up = t[z + 1] if z + 1 < depth else tzhi[...]
-        z_dn = t[z - 1] if z > 0 else tzlo[...]
+        c = temps[z + 1]
+        centre_kappa = kaps[z + 1]
         y_up, y_dn, x_up, x_dn = _rolls(c)
-        mc = m[z + 1]
+        ky_up, ky_dn, kx_up, kx_dn = _rolls(centre_kappa)
+        mc = planes[z + 1]
         my_up, my_dn, mx_up, mx_dn = _rolls(mc)
-        centre_kappa = 1.0 / (1.0 + SOFTEN * c * c)
         flux = jnp.zeros_like(c)
-        for other, other_mask in (
-            (z_up, m[z + 2]), (z_dn, m[z]), (y_up, my_up), (y_dn, my_dn), (x_up, mx_up), (x_dn, mx_dn)
+        for other, kappa, other_mask in (
+            (temps[z + 2], kaps[z + 2], planes[z + 2]), (temps[z], kaps[z], planes[z]),
+            (y_up, ky_up, my_up), (y_dn, ky_dn, my_dn), (x_up, kx_up, mx_up), (x_dn, kx_dn, mx_dn),
         ):
-            kappa = 1.0 / (1.0 + SOFTEN * other * other)
             flux = flux + other_mask * (centre_kappa + kappa) * (other - c)
         new = c + 0.5 * CONDUCT * mc * flux + q[z]
         if last:
-            own[z] = new[0:ny, 0:nx]
+            own[z] = new[0:height, 0:breadth]
         else:
             o[z] = new
             if z == 0:
@@ -98,10 +140,9 @@
                 oz1[...] = new
 
 
-def _vmem_call(kernel, out_shape, n_in, smem_first=False):
-    specs = [pl.BlockSpec(memory_space=pltpu.VMEM)] * n_in
-    if smem_first:
-        specs[0] = pl.BlockSpec(memory_space=pltpu.SMEM)
+def _vmem_call(kernel, out_shape, n_in, n_smem=0):
+    specs = [pl.BlockSpec(memory_space=pltpu.SMEM)] * n_smem
+    specs += [pl.BlockSpec(memory_space=pltpu.VMEM)] * (n_in - n_smem)
     return pl.pallas_call(
         kernel,
         out_shape=out_shape,
@@ -114,29 +155,6 @@
     up = [(i, i + 1) for i in range(first, n - 1)]
     down = [(j, i) for i, j in up]
     return up, down
-
-
-def _frame_index(start, own, total):
-    nb, tb, hb = own // MB, total // MB, H // MB
-    body = jnp.arange(nb + hb)
-    tail = jnp.arange(-hb, 0)
-    gap = jnp.full((tb - nb - 2 * hb,), -(10 ** 6), jnp.int32)
-    return start // MB + jnp.concatenate([body, gap, tail]).astype(jnp.int32)
-
-
-def _expand(blocks):
-    cells = jnp.repeat(blocks, MB, axis=0)
-    cells = jnp.repeat(cells, MB, axis=1)
-    return jnp.repeat(cells, MB, axis=2).astype(jnp.float32)
-
-
-def _pick(flags, zi, yi, xi):
-    ok = [(i >= 0) & (i < n) for i, n in zip((zi, yi, xi), flags.shape)]
-    sel = jnp.take(flags, jnp.clip(zi, 0, flags.shape[0] - 1), axis=0)
-    sel = jnp.take(sel, jnp.clip(yi, 0, flags.shape[1] - 1), axis=1)
-    sel = jnp.take(sel, jnp.clip(xi, 0, flags.shape[2] - 1), axis=2)
-    valid = ok[0][:, None, None] & ok[1][None, :, None] & ok[2][None, None, :]
-    return jnp.where(valid, sel, 0)
 
 
 def on_device(
@@ -194,18 +212,10 @@
     winding = frame[3 * depth: 3 * depth + 2]
     kelvin = frame[3 * depth + 2:]
 
-    yi = _frame_index(y_start, height, rows)
-    xi = _frame_index(x_start, breadth, lanes)
-    ycell = jnp.repeat(yi, MB) * MB + jnp.tile(jnp.arange(MB), rows // MB)
-    xcell = jnp.repeat(xi, MB) * MB + jnp.tile(jnp.arange(MB), lanes // MB)
-    inside = (((ycell >= 0) & (ycell < y_total))[:, None]
-              & ((xcell >= 0) & (xcell < x_total))[None, :]).astype(jnp.float32)
-    zb = z_start // MB + jnp.arange(depth // MB)
-    coupling = _expand(_pick(specimen_presence_flags, zb, yi, xi)) * material
-    tz = z_start // MB + jnp.arange(-1, depth // MB + 1)
-    tb = _pick(specimen_presence_flags, tz, yi, xi)
-    tb = jnp.where((xi >= offset // MB)[None, None, :], tb, 0)
-    t_mask = _expand(tb)[MB - 1: MB + 1 + depth]
+    fb = specimen_presence_flags.shape
+    flags = jnp.pad(specimen_presence_flags.astype(jnp.float32),
+                    ((0, 0), (0, 128 - fb[1]), (0, 128 - fb[2])))
+    pos = jnp.stack([z_start // MB, y_start // MB, x_start // MB]).astype(jnp.int32)
 
     up_z, down_z = _line_pairs(n_gz)
     fshape = jax.ShapeDtypeStruct((2 * depth, rows, lanes), jnp.float32)
@@ -220,8 +230,9 @@
         zhi = lax.ppermute(lo_plane, "gz", down_z)
         outs = (qshape, oshape) if last else (fshape, plane2, plane2)
         res = _vmem_call(
-            lambda *r, factor=factor, last=last: _em_kernel(factor, last, depth, *r), outs, 7, True
-        )(profile, field, coupling, winding, inside, zlo, zhi)
+            lambda *r, factor=factor, last=last: _em_kernel(
+                factor, last, depth, (height, breadth, y_total, x_total), *r), outs, 8, 2
+        )(pos, profile, flags, field, material, winding, zlo, zhi)
         if last:
             heat, field_out = res
         else:
@@ -237,8 +248,9 @@
         tzhi = lax.ppermute(lo_t, "gz", down_z)
         outs = (town,) if last else (tshape, tplane, tplane)
         res = _vmem_call(
-            lambda *r, last=last: _heat_kernel(last, depth, *r), outs, 5
-        )(kelvin, heat, t_mask, tzlo, tzhi)
+            lambda *r, last=last: _heat_kernel(
+                last, depth, (height, breadth, offset // MB), *r), outs, 6, 1
+        )(pos, flags, kelvin, heat, tzlo, tzhi)
         if last:
             (own_t,) = res
         else:

time: 189 us -> 174 us (0.921)
  local copies, waits for them, and re-layouts: 30.6 us -> 21.5 us
  other arithmetic: 18.9 us -> 10.2 us
  waiting for transfers between devices: 52.9 us -> 61.4 us
  Pallas kernels: 41.6 us -> 38.1 us
    ppermute x3, waiting for transfers between devices: 4.15 us -> 8.18 us  [on_device(): zlo = lax.ppermute(hi_plane, 'gz', up_z)]
    pallas_call x4, Pallas kernels: 23.8 us -> 19.9 us  [on_device(): _vmem_call(lambda *r, last=last: _heat_kernel(last, depth, (height, bread...]
    slice x1 -> x0, other arithmetic: 3.29 us -> none  [on_device(): kelvin = frame[3 * depth + 2:]]
    gather x7 -> x0, local copies, waits for them, and re-layouts: 3.08 us -> none  [the longest x4 1.36 us: _pick(): sel = jnp.take(sel, jnp.clip(xi, 0, flags.shape[2] - 1), axis=2)]
    concatenate x1, other arithmetic: 6.38 us -> 3.81 us  [on_device(): frame = jnp.concatenate([ystack, from_below, from_above], axis=1)]
    convert_element_type x4 -> x0, local copies, waits for them, and re-layouts: 2.53 us -> none  [_expand(): return jnp.repeat(cells, MB, axis=2).astype(jnp.float32)]
    ppermute x1, waiting for transfers between devices: 0.01 us -> 2.47 us  [on_device(): from_below = lax.ppermute(ystack[:, :H, :], 'gy', down_y)]
    convert_element_type x3 -> x1, other arithmetic: 2.11 us -> 0.01 us  [on_device(): specimen_presence_flags.astype(jnp.float32)]
  transfers between devices with their start and end apart: 21 -> 21, of which waited for: 13 -> 15; matrix products, arithmetic and copies ran while one was open for 13% -> 5% of each run, Pallas kernels for 6% -> 4%
where the time goes in v3:
time: 174 us; the launch traced here: 173 us
  waiting for transfers between devices  61.4 us (35%)
  starting transfers between devices  40.4 us (23%)
  Pallas kernels  38.1 us (22%)
  local copies, waits for them, and re-layouts  21.5 us (12%)
  other arithmetic  10.2 us (6%)
  between operations  1.83 us (1%)
    pallas_call x4, Pallas kernels, on_device(): _vmem_call(lambda *r, last=last: _heat_kernel(last, depth, (height, bread...  19.9 us
    ppermute x3, waiting for transfers between devices, on_device(): lax.ppermute(own_t, 'gx', [(k, (k + s) % n_gx) for k in owners])  19.9 us
    pallas_call x3, Pallas kernels, on_device(): _vmem_call(lambda *r, factor=factor, last=last: _em_kernel(factor, last,...  18.2 us
    ppermute x4, waiting for transfers between devices, on_device(): tzhi = lax.ppermute(lo_t, 'gz', down_z)  12.8 us
    ppermute x3, waiting for transfers between devices, on_device(): zhi = lax.ppermute(lo_plane, 'gz', down_z)  11.3 us
    ppermute x4, starting transfers between devices, on_device(): tzlo = lax.ppermute(hi_t, 'gz', up_z)  9.43 us
    ppermute x3, waiting for transfers between devices, on_device(): zlo = lax.ppermute(hi_plane, 'gz', up_z)  8.18 us
    unnamed x48, local copies, waits for them, and re-layouts  7.7 us
  transfers between devices with their start and end apart: 21, of which 15 were waited for; matrix products, arithmetic and copies ran while one was open for 5% of the time, Pallas kernels for 4%

profile of v3, /device:TPU:0, one launch (start us, length us, event | category | flops | bytes accessed | tf_op | source)
XLA Modules:
  0.0 173.4 jit_solution(17922729640712203331)
XLA Ops:
  0.6 1.6 pad_maximum_fusion.2
  3.9 3.1 %collective-permute-start.1 = (f32[26,8,128]{2,1,0:T(8,128)}, f32[26,8,128]{2,1,0:T(8,128)}, u32[]{:S(2)}, u32[]{:S(2)}) collective-permute-start(f32[26,8,128]{2,1,0:T(8,128)} %copy.12), channel_id=1, source_target_pairs={{0,1},{1,2},{2,3},{4,5},{5,6},{6,7},{8,9},{9,10},{10,11},{12,13},{... | collective-permute-start | bytes 319496 | tf_op jit(solution)/shard_map/ppermute | solution.py:192
  18.4 5.0 %collective-permute-start.3 = (f32[34,8,256]{2,1,0:T(8,128)S(1)}, f32[34,8,256]{2,1,0:T(8,128)S(1)}, u32[]{:S(2)}, u32[]{:S(2)}) collective-permute-start(f32[34,8,256]{2,1,0:T(8,128)S(1)} %get-tuple-element.37), channel_id=1, source_target_pairs={{0,4},{4,8},{8,12},{1,5},{5,9},{9,13},{2,6},{6,10},{10,14},{3,7},{... | collective-permute-start | bytes 835592 | tf_op jit(solution)/shard_map/ppermute | solution.py:207
  24.7 2.5 %collective-permute-done.2 = f32[34,8,256]{2,1,0:T(8,128)S(1)} collective-permute-done((f32[34,8,256]{2,1,0:T(8,128)S(1)}, f32[34,8,256]{2,1,0:T(8,128)S(1)}, u32[]{:S(2)}, u32[]{:S(2)}) %collective-permute-start.2) | collective-permute-done | bytes 278560 | tf_op jit(solution)/shard_map/ppermute | solution.py:208
  27.1 1.7 %collective-permute-done.3 = f32[34,8,256]{2,1,0:T(8,128)S(1)} collective-permute-done((f32[34,8,256]{2,1,0:T(8,128)S(1)}, f32[34,8,256]{2,1,0:T(8,128)S(1)}, u32[]{:S(2)}, u32[]{:S(2)}) %collective-permute-start.3) | collective-permute-done | bytes 278560 | tf_op jit(solution)/shard_map/ppermute | solution.py:207
  28.9 3.8 %pad_maximum_fusion = f32[34,144,256]{2,1,0:T(8,128)S(1)} fusion(f32[34,8,256]{2,1,0:T(8,128)S(1)} %collective-permute-done.3, f32[34,8,256]{2,1,0:T(8,128)S(1)} %collective-permute-done.2, f32[8,128,8]{2,1,0:T(8,128)S(1)} %copy-done.5, f32[8,128,112]{2,1,0:T(8,128)S(1)} %broadcast_in_dim.13, f32[8,128,136]{2,1,0:T(8,128)S(1)} %copy-done.3, ...), kind=kLoop, calls=%fused_computation.2 | loop fusion | flops 12533760 | bytes 10027008 | tf_op jit(solution)/shard_map/concatenate | solution.py:209
  36.4 4.4 %collective-permute-start.4 = (f32[2,144,256]{2,1,0:T(8,128)S(1)}, f32[2,144,256]{2,1,0:T(8,128)S(1)}, u32[]{:S(2)}, u32[]{:S(2)}) collective-permute-start(f32[2,144,256]{2,1,0:T(8,128)S(1)} %gather_fusion), channel_id=1, source_target_pairs={{0,16},{1,17},{2,18},{3,19},{4,20},{5,21},{6,22},{7,23},{8,24},{9,... | collective-permute-start | bytes 884744 | tf_op jit(solution)/shard_map/ppermute | solution.py:229
  42.0 3.2 %fusion.1 = (f32[8,144,256]{2,1,0:T(8,128)}, f32[8,144,256]{2,1,0:T(8,128)}) fusion(f32[34,144,256]{2,1,0:T(8,128)} %copy-done), kind=kLoop, calls=%fused_computation.29 | loop fusion | bytes 4718592 | tf_op jit(solution)/shard_map/slice | solution.py:213
  45.3 2.7 %collective-permute-done.4.r_6_ = f32[2,144,256]{2,1,0:T(8,128)S(1)} collective-permute-done((f32[2,144,256]{2,1,0:T(8,128)S(1)}, f32[2,144,256]{2,1,0:T(8,128)S(1)}, u32[]{:S(2)}, u32[]{:S(2)}) %collective-permute-start.4) | collective-permute-done | bytes 294944 | tf_op jit(solution)/shard_map/ppermute | solution.py:229
  48.0 4.4 %collective-permute-done.5.r_7_ = f32[2,144,256]{2,1,0:T(8,128)S(1)} collective-permute-done((f32[2,144,256]{2,1,0:T(8,128)S(1)}, f32[2,144,256]{2,1,0:T(8,128)S(1)}, u32[]{:S(2)}, u32[]{:S(2)}) %collective-permute-start.5) | collective-permute-done | bytes 294944 | tf_op jit(solution)/shard_map/ppermute | solution.py:230
  53.1 6.1 %shard_map.95 = (f32[16,144,256]{2,1,0:T(8,128)}, f32[2,144,256]{2,1,0:T(8,128)}, f32[2,144,256]{2,1,0:T(8,128)}) custom-call(s32[3]{0:T(128)} %pad_add_fusion.r_0_, f32[8]{0:T(128)} %add_divide_fusion.r_1_, f32[2,128,128]{2,1,0:T(8,128)} %pad.8.r_2_.r_1_, f32[16,144,256]{2,1,0:T(8,128)} %copy-done.1, f32[8,144,256]{2,1,0:T(8,128)} %get-tuple-element.41.r_4_, ...), custom_call_target="tpu_custom_call" | custom-call | tf_op jit(solution)/shard_map/pallas_call | solution.py:232
  61.9 5.5 %collective-permute-done.6.r_6_ = f32[2,144,256]{2,1,0:T(8,128)S(1)} collective-permute-done((f32[2,144,256]{2,1,0:T(8,128)}, f32[2,144,256]{2,1,0:T(8,128)S(1)}, u32[]{:S(2)}, u32[]{:S(2)}) %collective-permute-start.6) | collective-permute-done | bytes 294944 | tf_op jit(solution)/shard_map/ppermute | solution.py:229
  67.4 4.0 %collective-permute-done.7.r_7_ = f32[2,144,256]{2,1,0:T(8,128)S(1)} collective-permute-done((f32[2,144,256]{2,1,0:T(8,128)}, f32[2,144,256]{2,1,0:T(8,128)S(1)}, u32[]{:S(2)}, u32[]{:S(2)}) %collective-permute-start.7) | collective-permute-done | bytes 294944 | tf_op jit(solution)/shard_map/ppermute | solution.py:230
  72.2 6.0 %shard_map.96 = (f32[16,144,256]{2,1,0:T(8,128)}, f32[2,144,256]{2,1,0:T(8,128)}, f32[2,144,256]{2,1,0:T(8,128)}) custom-call(s32[3]{0:T(128)} %pad_add_fusion.r_0_, f32[8]{0:T(128)} %add_divide_fusion.r_1_, f32[2,128,128]{2,1,0:T(8,128)} %pad.8.r_2_.r_1_, f32[16,144,256]{2,1,0:T(8,128)} %get-tuple-element.19.r_3_, f32[8,144,256]{2,1,0:T(8,128)} %get-tuple-element.41.r_4_, ...), custom_call_target="tpu_custom_call" | custom-call | tf_op jit(solution)/shard_map/pallas_call | solution.py:232
  78.2 1.6 collective-permute-start.8
  83.4 4.8 %collective-permute-start.10 = (f32[144,256]{1,0:T(8,128)S(1)}, f32[144,256]{1,0:T(8,128)S(1)}, u32[]{:S(2)}, u32[]{:S(2)}) collective-permute-start(f32[144,256]{1,0:T(8,128)S(1)} %get-tuple-element.39), channel_id=1, source_target_pairs={{0,16},{1,17},{2,18},{3,19},{4,20},{5,21},{6,22},{7,23},{8,24},{9,... | collective-permute-start | bytes 442376 | tf_op jit(solution)/shard_map/ppermute | solution.py:247
  88.1 2.9 %collective-permute-done.9.r_7_ = f32[2,144,256]{2,1,0:T(8,128)S(1)} collective-permute-done((f32[2,144,256]{2,1,0:T(8,128)}, f32[2,144,256]{2,1,0:T(8,128)S(1)}, u32[]{:S(2)}, u32[]{:S(2)}) %collective-permute-start.9) | collective-permute-done | bytes 294944 | tf_op jit(solution)/shard_map/ppermute | solution.py:230
  91.8 6.1 %shard_map.97 = (f32[8,144,256]{2,1,0:T(8,128)}, f32[2,8,128,128]{3,2,1,0:T(8,128)}) custom-call(s32[3]{0:T(128)} %pad_add_fusion.r_0_, f32[8]{0:T(128)} %add_divide_fusion.r_1_, f32[2,128,128]{2,1,0:T(8,128)} %pad.8.r_2_.r_1_, f32[16,144,256]{2,1,0:T(8,128)} %get-tuple-element.22.r_3_, f32[8,144,256]{2,1,0:T(8,128)} %get-tuple-element.41.r_4_, ...), custom_call_target="tpu_custom_call" | custom-call | tf_op jit(solution)/shard_map/pallas_call | solution.py:232
  98.6 5.3 %shard_map.98 = (f32[8,144,256]{2,1,0:T(8,128)}, f32[144,256]{1,0:T(8,128)}, f32[144,256]{1,0:T(8,128)}) custom-call(s32[3]{0:T(128)} %pad_add_fusion.r_0_, f32[2,128,128]{2,1,0:T(8,128)} %pad.8.r_2_.r_1_, f32[8,144,256]{2,1,0:T(8,128)} %get-tuple-element.40.r_2_, f32[8,144,256]{2,1,0:T(8,128)} %get-tuple-element.26.r_3_, f32[144,256]{1,0:T(8,128)} %copy-done.15, ...), custom_call_target="tpu_custom_call" | custom-call | tf_op jit(solution)/shard_map/pallas_call | solution.py:250
  106.8 1.7 collective-permute-done.12.r_4_
  108.5 4.3 %collective-permute-done.13.r_5_ = f32[144,256]{1,0:T(8,128)S(1)} collective-permute-done((f32[144,256]{1,0:T(8,128)}, f32[144,256]{1,0:T(8,128)S(1)}, u32[]{:S(2)}, u32[]{:S(2)}) %collective-permute-start.13) | collective-permute-done | bytes 147488 | tf_op jit(solution)/shard_map/ppermute | solution.py:248
  113.4 5.3 %shard_map.99 = (f32[8,144,256]{2,1,0:T(8,128)}, f32[144,256]{1,0:T(8,128)}, f32[144,256]{1,0:T(8,128)}) custom-call(s32[3]{0:T(128)} %pad_add_fusion.r_0_, f32[2,128,128]{2,1,0:T(8,128)} %pad.8.r_2_.r_1_, f32[8,144,256]{2,1,0:T(8,128)} %get-tuple-element.27.r_2_, f32[8,144,256]{2,1,0:T(8,128)} %get-tuple-element.26.r_3_, f32[144,256]{1,0:T(8,128)} %copy-done.16, ...), custom_call_target="tpu_custom_call" | custom-call | tf_op jit(solution)/shard_map/pallas_call | solution.py:250
  118.7 1.6 collective-permute-start.14
  121.6 1.7 collective-permute-done.14.r_4_
  123.3 4.3 %collective-permute-done.15.r_5_ = f32[144,256]{1,0:T(8,128)S(1)} collective-permute-done((f32[144,256]{1,0:T(8,128)}, f32[144,256]{1,0:T(8,128)S(1)}, u32[]{:S(2)}, u32[]{:S(2)}) %collective-permute-start.15) | collective-permute-done | bytes 147488 | tf_op jit(solution)/shard_map/ppermute | solution.py:248
  128.2 5.3 %shard_map.100 = (f32[8,144,256]{2,1,0:T(8,128)}, f32[144,256]{1,0:T(8,128)}, f32[144,256]{1,0:T(8,128)}) custom-call(s32[3]{0:T(128)} %pad_add_fusion.r_0_, f32[2,128,128]{2,1,0:T(8,128)} %pad.8.r_2_.r_1_, f32[8,144,256]{2,1,0:T(8,128)} %get-tuple-element.30.r_2_, f32[8,144,256]{2,1,0:T(8,128)} %get-tuple-element.26.r_3_, f32[144,256]{1,0:T(8,128)} %copy-done.17, ...), custom_call_target="tpu_custom_call" | custom-call | tf_op jit(solution)/shard_map/pallas_call | solution.py:250
  133.5 1.6 collective-permute-start.16
  136.4 1.7 collective-permute-done.16.r_4_
  138.1 4.3 %collective-permute-done.17.r_5_ = f32[144,256]{1,0:T(8,128)S(1)} collective-permute-done((f32[144,256]{1,0:T(8,128)}, f32[144,256]{1,0:T(8,128)S(1)}, u32[]{:S(2)}, u32[]{:S(2)}) %collective-permute-start.17) | collective-permute-done | bytes 147488 | tf_op jit(solution)/shard_map/ppermute | solution.py:248
  143.0 3.9 %shard_map.101 = f32[8,128,128]{2,1,0:T(8,128)} custom-call(s32[3]{0:T(128)} %pad_add_fusion.r_0_, f32[2,128,128]{2,1,0:T(8,128)} %pad.8.r_2_.r_1_, f32[8,144,256]{2,1,0:T(8,128)} %get-tuple-element.33.r_2_, f32[8,144,256]{2,1,0:T(8,128)} %get-tuple-element.26.r_3_, f32[144,256]{1,0:T(8,128)} %copy-done.18, f32[144,256]{1,0:T(8,128)} %copy-done.21), custom_call_target="tpu_custom_call" | custom-call | tf_op jit(solution)/shard_map/pallas_call | solution.py:250
  151.0 14.0 %collective-permute-done.19 = f32[8,128,128]{2,1,0:T(8,128)S(1)} collective-permute-done((f32[8,128,128]{2,1,0:T(8,128)}, f32[8,128,128]{2,1,0:T(8,128)S(1)}, u32[]{:S(2)}, u32[]{:S(2)}) %collective-permute-start.19) | collective-permute-done | bytes 524320 | tf_op jit(solution)/shard_map/ppermute | solution.py:262
  165.0 5.8 %collective-permute-done.18 = f32[8,128,128]{2,1,0:T(8,128)S(1)} collective-permute-done((f32[8,128,128]{2,1,0:T(8,128)}, f32[8,128,128]{2,1,0:T(8,128)S(1)}, u32[]{:S(2)}, u32[]{:S(2)}) %collective-permute-start.18) | collective-permute-done | bytes 524320 | tf_op jit(solution)/shard_map/ppermute | solution.py:262
  (93 shorter events, 41.6 us)
Async XLA Ops:
  3.9 5.6 %copy-start.4 = (f32[8,128,384]{2,1,0:T(8,128)S(1)}, f32[8,128,384]{2,1,0:T(8,128)}, u32[]{:S(2)}) copy-start(f32[8,128,384]{2,1,0:T(8,128)} %param.13) | copy-start | bytes 4718596
  3.9 9.1 %collective-permute-start.1 = (f32[26,8,128]{2,1,0:T(8,128)}, f32[26,8,128]{2,1,0:T(8,128)}, u32[]{:S(2)}, u32[]{:S(2)}) collective-permute-start(f32[26,8,128]{2,1,0:T(8,128)} %copy.12), channel_id=1, source_target_pairs={{0,1},{1,2},{2,3},{4,5},{5,6},{6,7},{8,9},{9,10},{10,11},{12,13},{... | collective-permute-start | bytes 319496 | tf_op jit(solution)/shard_map/ppermute | solution.py:192
  7.5 4.9 %collective-permute-start = (f32[26,8,128]{2,1,0:T(8,128)S(1)}, f32[26,8,128]{2,1,0:T(8,128)S(1)}, u32[]{:S(2)}, u32[]{:S(2)}) collective-permute-start(f32[26,8,128]{2,1,0:T(8,128)S(1)} %copy.10), channel_id=1, source_target_pairs={{1,0},{2,1},{3,2},{5,4},{6,5},{7,6},{9,8},{10,9},{11,10},{13,12},{... | collective-permute-start | bytes 319496 | tf_op jit(solution)/shard_map/ppermute | solution.py:193
  16.0 8.0 %copy-start.22 = (s32[2,64,64]{2,1,0:T(8,128)S(1)}, s32[2,64,64]{2,1,0:T(8,128)}, u32[]{:S(2)}) copy-start(s32[2,64,64]{2,1,0:T(8,128)} %param.12) | copy-start | bytes 98308
  16.0 8.7 %copy-start.23 = (s32[2]{0:T(128)S(1)}, s32[2]{0:T(128)}, u32[]{:S(2)}) copy-start(s32[2]{0:T(128)} %constant.119) | copy-start | bytes 28
  16.0 12.9 %copy-start.5 = (f32[8,128,8]{2,1,0:T(8,128)S(1)}, f32[8,128,8]{2,1,0:T(8,128)}, u32[]{:S(2)}) copy-start(f32[8,128,8]{2,1,0:T(8,128)} %pad_dynamic-slice_fusion) | copy-start | bytes 98308
  16.0 12.9 %copy-start.6 = (f32[8,128,128]{2,1,0:T(8,128)S(1)}, f32[8,128,128]{2,1,0:T(8,128)}, u32[]{:S(2)}) copy-start(f32[8,128,128]{2,1,0:T(8,128)} %param.9) | copy-start | bytes 1572868
  17.1 10.0 %collective-permute-start.2 = (f32[34,8,256]{2,1,0:T(8,128)S(1)}, f32[34,8,256]{2,1,0:T(8,128)S(1)}, u32[]{:S(2)}, u32[]{:S(2)}) collective-permute-start(f32[34,8,256]{2,1,0:T(8,128)S(1)} %get-tuple-element.36), channel_id=1, source_target_pairs={{4,0},{8,4},{12,8},{5,1},{9,5},{13,9},{6,2},{10,6},{14,10},{7,3},{... | collective-permute-start | bytes 835592 | tf_op jit(solution)/shard_map/ppermute | solution.py:208
  18.4 10.5 %collective-permute-start.3 = (f32[34,8,256]{2,1,0:T(8,128)S(1)}, f32[34,8,256]{2,1,0:T(8,128)S(1)}, u32[]{:S(2)}, u32[]{:S(2)}) collective-permute-start(f32[34,8,256]{2,1,0:T(8,128)S(1)} %get-tuple-element.37), channel_id=1, source_target_pairs={{0,4},{4,8},{8,12},{1,5},{5,9},{9,13},{2,6},{6,10},{10,14},{3,7},{... | collective-permute-start | bytes 835592 | tf_op jit(solution)/shard_map/ppermute | solution.py:207
  35.2 10.1 %copy-start.1 = (f32[16,144,256]{2,1,0:T(8,128)}, f32[16,144,256]{2,1,0:T(8,128)S(1)}, u32[]{:S(2)}) copy-start(f32[16,144,256]{2,1,0:T(8,128)S(1)} %slice.48.r_3_) | copy-start | bytes 7077892
  36.4 11.6 %collective-permute-start.4 = (f32[2,144,256]{2,1,0:T(8,128)S(1)}, f32[2,144,256]{2,1,0:T(8,128)S(1)}, u32[]{:S(2)}, u32[]{:S(2)}) collective-permute-start(f32[2,144,256]{2,1,0:T(8,128)S(1)} %gather_fusion), channel_id=1, source_target_pairs={{0,16},{1,17},{2,18},{3,19},{4,20},{5,21},{6,22},{7,23},{8,24},{9,... | collective-permute-start | bytes 884744 | tf_op jit(solution)/shard_map/ppermute | solution.py:229
  40.7 11.6 %collective-permute-start.5 = (f32[2,144,256]{2,1,0:T(8,128)S(1)}, f32[2,144,256]{2,1,0:T(8,128)S(1)}, u32[]{:S(2)}, u32[]{:S(2)}) collective-permute-start(f32[2,144,256]{2,1,0:T(8,128)S(1)} %gather_fusion.1), channel_id=1, source_target_pairs={{16,0},{17,1},{18,2},{19,3},{20,4},{21,5},{22,6},{23,7},{24,8},{25... | collective-permute-start | bytes 884744 | tf_op jit(solution)/shard_map/ppermute | solution.py:230
  48.0 4.4 %copy-start.10 = (f32[2,144,256]{2,1,0:T(8,128)}, f32[2,144,256]{2,1,0:T(8,128)S(1)}, u32[]{:S(2)}) copy-start(f32[2,144,256]{2,1,0:T(8,128)S(1)} %collective-permute-done.4.r_6_) | copy-start | bytes 884740
  59.2 8.3 %collective-permute-start.6 = (f32[2,144,256]{2,1,0:T(8,128)}, f32[2,144,256]{2,1,0:T(8,128)S(1)}, u32[]{:S(2)}, u32[]{:S(2)}) collective-permute-start(f32[2,144,256]{2,1,0:T(8,128)} %get-tuple-element.20), channel_id=1, source_target_pairs={{0,16},{1,17},{2,18},{3,19},{4,20},{5,21},{6,22},{7,23},{8,24},{9,... | collective-permute-start | bytes 884744 | tf_op jit(solution)/shard_map/ppermute | solution.py:229
  60.6 10.8 %collective-permute-start.7 = (f32[2,144,256]{2,1,0:T(8,128)}, f32[2,144,256]{2,1,0:T(8,128)S(1)}, u32[]{:S(2)}, u32[]{:S(2)}) collective-permute-start(f32[2,144,256]{2,1,0:T(8,128)} %get-tuple-element.21), channel_id=1, source_target_pairs={{16,0},{17,1},{18,2},{19,3},{20,4},{21,5},{22,6},{23,7},{24,8},{25... | collective-permute-start | bytes 884744 | tf_op jit(solution)/shard_map/ppermute | solution.py:230
  67.4 4.0 %copy-start.11 = (f32[2,144,256]{2,1,0:T(8,128)}, f32[2,144,256]{2,1,0:T(8,128)S(1)}, u32[]{:S(2)}) copy-start(f32[2,144,256]{2,1,0:T(8,128)S(1)} %collective-permute-done.6.r_6_) | copy-start | bytes 884740
  78.2 9.9 %collective-permute-start.8 = (f32[2,144,256]{2,1,0:T(8,128)}, f32[2,144,256]{2,1,0:T(8,128)S(1)}, u32[]{:S(2)}, u32[]{:S(2)}) collective-permute-start(f32[2,144,256]{2,1,0:T(8,128)} %get-tuple-element.23), channel_id=1, source_target_pairs={{0,16},{1,17},{2,18},{3,19},{4,20},{5,21},{6,22},{7,23},{8,24},{9,... | collective-permute-start | bytes 884744 | tf_op jit(solution)/shard_map/ppermute | solution.py:229
  79.8 11.3 %collective-permute-start.9 = (f32[2,144,256]{2,1,0:T(8,128)}, f32[2,144,256]{2,1,0:T(8,128)S(1)}, u32[]{:S(2)}, u32[]{:S(2)}) collective-permute-start(f32[2,144,256]{2,1,0:T(8,128)} %get-tuple-element.24), channel_id=1, source_target_pairs={{16,0},{17,1},{18,2},{19,3},{20,4},{21,5},{22,6},{23,7},{24,8},{25... | collective-permute-start | bytes 884744 | tf_op jit(solution)/shard_map/ppermute | solution.py:230
  82.1 15.8 %collective-permute-start.11 = (f32[144,256]{1,0:T(8,128)S(1)}, f32[144,256]{1,0:T(8,128)S(1)}, u32[]{:S(2)}, u32[]{:S(2)}) collective-permute-start(f32[144,256]{1,0:T(8,128)S(1)} %get-tuple-element.38), channel_id=1, source_target_pairs={{16,0},{17,1},{18,2},{19,3},{20,4},{21,5},{22,6},{23,7},{24,8},{25... | collective-permute-start | bytes 442376 | tf_op jit(solution)/shard_map/ppermute | solution.py:248
  83.4 14.6 %collective-permute-start.10 = (f32[144,256]{1,0:T(8,128)S(1)}, f32[144,256]{1,0:T(8,128)S(1)}, u32[]{:S(2)}, u32[]{:S(2)}) collective-permute-start(f32[144,256]{1,0:T(8,128)S(1)} %get-tuple-element.39), channel_id=1, source_target_pairs={{0,16},{1,17},{2,18},{3,19},{4,20},{5,21},{6,22},{7,23},{8,24},{9,... | collective-permute-start | bytes 442376 | tf_op jit(solution)/shard_map/ppermute | solution.py:247
  104.0 4.5 %collective-permute-start.12 = (f32[144,256]{1,0:T(8,128)}, f32[144,256]{1,0:T(8,128)S(1)}, u32[]{:S(2)}, u32[]{:S(2)}) collective-permute-start(f32[144,256]{1,0:T(8,128)} %get-tuple-element.28), channel_id=1, source_target_pairs={{0,16},{1,17},{2,18},{3,19},{4,20},{5,21},{6,22},{7,23},{8,24},{9,... | collective-permute-start | bytes 442376 | tf_op jit(solution)/shard_map/ppermute | solution.py:247
  105.5 7.2 %collective-permute-start.13 = (f32[144,256]{1,0:T(8,128)}, f32[144,256]{1,0:T(8,128)S(1)}, u32[]{:S(2)}, u32[]{:S(2)}) collective-permute-start(f32[144,256]{1,0:T(8,128)} %get-tuple-element.29), channel_id=1, source_target_pairs={{16,0},{17,1},{18,2},{19,3},{20,4},{21,5},{22,6},{23,7},{24,8},{25... | collective-permute-start | bytes 442376 | tf_op jit(solution)/shard_map/ppermute | solution.py:248
  108.5 4.3 %copy-start.16 = (f32[144,256]{1,0:T(8,128)}, f32[144,256]{1,0:T(8,128)S(1)}, u32[]{:S(2)}) copy-start(f32[144,256]{1,0:T(8,128)S(1)} %collective-permute-done.12.r_4_) | copy-start | bytes 442372
  118.7 4.5 %collective-permute-start.14 = (f32[144,256]{1,0:T(8,128)}, f32[144,256]{1,0:T(8,128)S(1)}, u32[]{:S(2)}, u32[]{:S(2)}) collective-permute-start(f32[144,256]{1,0:T(8,128)} %get-tuple-element.31), channel_id=1, source_target_pairs={{0,16},{1,17},{2,18},{3,19},{4,20},{5,21},{6,22},{7,23},{8,24},{9,... | collective-permute-start | bytes 442376 | tf_op jit(solution)/shard_map/ppermute | solution.py:247
  120.3 7.2 %collective-permute-start.15 = (f32[144,256]{1,0:T(8,128)}, f32[144,256]{1,0:T(8,128)S(1)}, u32[]{:S(2)}, u32[]{:S(2)}) collective-permute-start(f32[144,256]{1,0:T(8,128)} %get-tuple-element.32), channel_id=1, source_target_pairs={{16,0},{17,1},{18,2},{19,3},{20,4},{21,5},{22,6},{23,7},{24,8},{25... | collective-permute-start | bytes 442376 | tf_op jit(solution)/shard_map/ppermute | solution.py:248
  123.3 4.3 %copy-start.17 = (f32[144,256]{1,0:T(8,128)}, f32[144,256]{1,0:T(8,128)S(1)}, u32[]{:S(2)}) copy-start(f32[144,256]{1,0:T(8,128)S(1)} %collective-permute-done.14.r_4_) | copy-start | bytes 442372
  133.5 4.5 %collective-permute-start.16 = (f32[144,256]{1,0:T(8,128)}, f32[144,256]{1,0:T(8,128)S(1)}, u32[]{:S(2)}, u32[]{:S(2)}) collective-permute-start(f32[144,256]{1,0:T(8,128)} %get-tuple-element.34), channel_id=1, source_target_pairs={{0,16},{1,17},{2,18},{3,19},{4,20},{5,21},{6,22},{7,23},{8,24},{9,... | collective-permute-start | bytes 442376 | tf_op jit(solution)/shard_map/ppermute | solution.py:247
  135.1 7.2 %collective-permute-start.17 = (f32[144,256]{1,0:T(8,128)}, f32[144,256]{1,0:T(8,128)S(1)}, u32[]{:S(2)}, u32[]{:S(2)}) collective-permute-start(f32[144,256]{1,0:T(8,128)} %get-tuple-element.35), channel_id=1, source_target_pairs={{16,0},{17,1},{18,2},{19,3},{20,4},{21,5},{22,6},{23,7},{24,8},{25... | collective-permute-start | bytes 442376 | tf_op jit(solution)/shard_map/ppermute | solution.py:248
  138.1 4.3 %copy-start.18 = (f32[144,256]{1,0:T(8,128)}, f32[144,256]{1,0:T(8,128)S(1)}, u32[]{:S(2)}) copy-start(f32[144,256]{1,0:T(8,128)S(1)} %collective-permute-done.16.r_4_) | copy-start | bytes 442372
  146.9 4.0 %collective-permute-start.20 = (f32[8,128,128]{2,1,0:T(8,128)}, f32[8,128,128]{2,1,0:T(8,128)S(1)}, u32[]{:S(2)}, u32[]{:S(2)}) collective-permute-start(f32[8,128,128]{2,1,0:T(8,128)} %shard_map.101), channel_id=1, source_target_pairs={{1,0},{2,1},{3,2},{5,4},{6,5},{7,6},{9,8},{10,9},{11,10},{13,12},{... | collective-permute-start | bytes 1572872 | tf_op jit(solution)/shard_map/ppermute | solution.py:262
  148.2 16.7 %collective-permute-start.19 = (f32[8,128,128]{2,1,0:T(8,128)}, f32[8,128,128]{2,1,0:T(8,128)S(1)}, u32[]{:S(2)}, u32[]{:S(2)}) collective-permute-start(f32[8,128,128]{2,1,0:T(8,128)} %shard_map.101), channel_id=1, source_target_pairs={{1,3},{2,0},{3,1},{5,7},{6,4},{7,5},{9,11},{10,8},{11,9},{13,15},{... | collective-permute-start | bytes 1572872 | tf_op jit(solution)/shard_map/ppermute | solution.py:262
  149.5 21.2 %collective-permute-start.18 = (f32[8,128,128]{2,1,0:T(8,128)}, f32[8,128,128]{2,1,0:T(8,128)S(1)}, u32[]{:S(2)}, u32[]{:S(2)}) collective-permute-start(f32[8,128,128]{2,1,0:T(8,128)} %shard_map.101), channel_id=1, source_target_pairs={{1,2},{2,3},{3,0},{5,6},{6,7},{7,4},{9,10},{10,11},{11,8},{13,14},... | collective-permute-start | bytes 1572872 | tf_op jit(solution)/shard_map/ppermute | solution.py:262
  (13 other events, 15.2 us)

commit v4 on v3

--- a/solution.py
+++ b/solution.py
@@ -157,6 +157,25 @@
     return up, down
 
 
+def _broadcast_blocks(own, me, n, first):
+    if (n, first) == (4, 1):
+        r1 = lax.ppermute(own, "gx", [(2, 0), (3, 1), (1, 2)])
+        a = jnp.where((me == 0) | (me == 2), r1, own)
+        b = jnp.where((me == 1) | (me == 0), r1, own)
+        r2 = lax.ppermute(jnp.stack([a, b]), "gx", [(0, 1), (1, 0), (2, 3), (3, 2)])
+        b1 = jnp.where(me == 1, own, jnp.where(me == 2, r1, r2[0]))
+        b2 = jnp.where(me == 0, r1, jnp.where(me == 1, r2[0], jnp.where(me == 2, own, r2[1])))
+        b3 = jnp.where(me == 0, r2[1], jnp.where(me == 1, r1, jnp.where(me == 2, r2[0], own)))
+        return jnp.concatenate([b1, b2, b3], axis=2)
+    owners = list(range(first, n))
+    held = [own]
+    for s in range(1, n):
+        held.append(lax.ppermute(own, "gx", [(k, (k + s) % n) for k in owners]))
+    held = jnp.stack(held)
+    pieces = [lax.dynamic_index_in_dim(held, (me - k) % n, 0, keepdims=False) for k in owners]
+    return jnp.concatenate(pieces, axis=2)
+
+
 def on_device(
     earlier_window_curl_state,
     material_resistivity_inverse,
@@ -256,13 +275,7 @@
         else:
             kelvin, lo_t, hi_t = res
 
-    owners = list(range(first_owner, n_gx))
-    held = [own_t]
-    for s in range(1, n_gx):
-        held.append(lax.ppermute(own_t, "gx", [(k, (k + s) % n_gx) for k in owners]))
-    held = jnp.stack(held)
-    pieces = [lax.dynamic_index_in_dim(held, (gx_i - k) % n_gx, 0, keepdims=False) for k in owners]
-    segment_kelvin = jnp.concatenate(pieces, axis=2)
+    segment_kelvin = _broadcast_blocks(own_t, gx_i, n_gx, first_owner)
     return (field_out, segment_kelvin)
 
 

time: 174 us -> 164 us (0.943)
  waiting for transfers between devices: 61.4 us -> 54.1 us
  starting transfers between devices: 40.4 us -> 37.9 us
    ppermute x3 -> x2, waiting for transfers between devices: 19.9 us -> 12.6 us  [the longest x1 9.96 us: _broadcast_blocks(): r1 = lax.ppermute(own, 'gx', [(2, 0), (3, 1), (1, 2)])]
    ppermute x3 -> x2, starting transfers between devices: 3.86 us -> 1.35 us  [the longest x1 1.28 us: _broadcast_blocks(): r1 = lax.ppermute(own, 'gx', [(2, 0), (3, 1), (1, 2)])]
    unnamed x48 -> x50, local copies, waits for them, and re-layouts: 7.7 us -> 7.72 us
  transfers between devices with their start and end apart: 21 -> 20, of which waited for: 15 -> 15; matrix products, arithmetic and copies ran while one was open for 5% -> 6% of each run, Pallas kernels for 4% -> 4%
where the time goes in v4:
time: 164 us
  waiting for transfers between devices  54.1 us (33%)
  Pallas kernels  38.1 us (23%)
  starting transfers between devices  37.9 us (23%)
  local copies, waits for them, and re-layouts  21.3 us (13%)
  other arithmetic  10.5 us (6%)
  between operations  1.78 us (1%)
    pallas_call x4, Pallas kernels, on_device(): _vmem_call(lambda *r, last=last: _heat_kernel(last, depth, (height, bread...  19.8 us
    pallas_call x3, Pallas kernels, on_device(): _vmem_call(lambda *r, factor=factor, last=last: _em_kernel(factor, last,...  18.3 us
    ppermute x4, waiting for transfers between devices, on_device(): tzhi = lax.ppermute(lo_t, 'gz', down_z)  12.8 us
    ppermute x3, waiting for transfers between devices, on_device(): zhi = lax.ppermute(lo_plane, 'gz', down_z)  11.3 us
    ppermute x1, waiting for transfers between devices, _broadcast_blocks(): r1 = lax.ppermute(own, 'gx', [(2, 0), (3, 1), (1, 2)])  9.96 us
    ppermute x4, starting transfers between devices, on_device(): tzlo = lax.ppermute(hi_t, 'gz', up_z)  9.43 us
    ppermute x3, waiting for transfers between devices, on_device(): zlo = lax.ppermute(hi_plane, 'gz', up_z)  8.19 us
    unnamed x50, local copies, waits for them, and re-layouts  7.72 us
  transfers between devices with their start and end apart: 20, of which 15 were waited for; matrix products, arithmetic and copies ran while one was open for 6% of the time, Pallas kernels for 4%

profile of v4, /device:TPU:0, one launch (start us, length us, event | category | flops | bytes accessed | tf_op | source)
XLA Modules:
  0.0 163.6 jit_solution(3863025145460540173)
XLA Ops:
  0.6 1.6 pad_maximum_fusion.1
  3.9 3.1 %collective-permute-start.1 = (f32[26,8,128]{2,1,0:T(8,128)}, f32[26,8,128]{2,1,0:T(8,128)}, u32[]{:S(2)}, u32[]{:S(2)}) collective-permute-start(f32[26,8,128]{2,1,0:T(8,128)} %copy.12), channel_id=1, source_target_pairs={{0,1},{1,2},{2,3},{4,5},{5,6},{6,7},{8,9},{9,10},{10,11},{12,13},{... | collective-permute-start | bytes 319496 | tf_op jit(solution)/shard_map/ppermute | solution.py:211
  18.4 5.0 %collective-permute-start.3 = (f32[34,8,256]{2,1,0:T(8,128)S(1)}, f32[34,8,256]{2,1,0:T(8,128)S(1)}, u32[]{:S(2)}, u32[]{:S(2)}) collective-permute-start(f32[34,8,256]{2,1,0:T(8,128)S(1)} %get-tuple-element.37), channel_id=1, source_target_pairs={{0,4},{4,8},{8,12},{1,5},{5,9},{9,13},{2,6},{6,10},{10,14},{3,7},{... | collective-permute-start | bytes 835592 | tf_op jit(solution)/shard_map/ppermute | solution.py:226
  24.8 2.4 %collective-permute-done.2 = f32[34,8,256]{2,1,0:T(8,128)S(1)} collective-permute-done((f32[34,8,256]{2,1,0:T(8,128)S(1)}, f32[34,8,256]{2,1,0:T(8,128)S(1)}, u32[]{:S(2)}, u32[]{:S(2)}) %collective-permute-start.2) | collective-permute-done | bytes 278560 | tf_op jit(solution)/shard_map/ppermute | solution.py:227
  27.2 1.8 %collective-permute-done.3 = f32[34,8,256]{2,1,0:T(8,128)S(1)} collective-permute-done((f32[34,8,256]{2,1,0:T(8,128)S(1)}, f32[34,8,256]{2,1,0:T(8,128)S(1)}, u32[]{:S(2)}, u32[]{:S(2)}) %collective-permute-start.3) | collective-permute-done | bytes 278560 | tf_op jit(solution)/shard_map/ppermute | solution.py:226
  29.0 3.8 %pad_maximum_fusion = f32[34,144,256]{2,1,0:T(8,128)S(1)} fusion(f32[34,8,256]{2,1,0:T(8,128)S(1)} %collective-permute-done.3, f32[34,8,256]{2,1,0:T(8,128)S(1)} %collective-permute-done.2, f32[8,128,8]{2,1,0:T(8,128)S(1)} %copy-done.5, f32[8,128,112]{2,1,0:T(8,128)S(1)} %broadcast_in_dim.13, f32[8,128,136]{2,1,0:T(8,128)S(1)} %copy-done.3, ...), kind=kLoop, calls=%fused_computation.2 | loop fusion | flops 12533760 | bytes 10027008 | tf_op jit(solution)/shard_map/concatenate | solution.py:228
  36.4 4.3 %collective-permute-start.4 = (f32[2,144,256]{2,1,0:T(8,128)S(1)}, f32[2,144,256]{2,1,0:T(8,128)S(1)}, u32[]{:S(2)}, u32[]{:S(2)}) collective-permute-start(f32[2,144,256]{2,1,0:T(8,128)S(1)} %gather_fusion), channel_id=1, source_target_pairs={{0,16},{1,17},{2,18},{3,19},{4,20},{5,21},{6,22},{7,23},{8,24},{9,... | collective-permute-start | bytes 884744 | tf_op jit(solution)/shard_map/ppermute | solution.py:248
  42.1 3.2 %fusion.1 = (f32[8,144,256]{2,1,0:T(8,128)}, f32[8,144,256]{2,1,0:T(8,128)}) fusion(f32[34,144,256]{2,1,0:T(8,128)} %copy-done), kind=kLoop, calls=%fused_computation.33 | loop fusion | bytes 4718592 | tf_op jit(solution)/shard_map/slice | solution.py:232
  45.3 2.7 %collective-permute-done.4.r_6_ = f32[2,144,256]{2,1,0:T(8,128)S(1)} collective-permute-done((f32[2,144,256]{2,1,0:T(8,128)S(1)}, f32[2,144,256]{2,1,0:T(8,128)S(1)}, u32[]{:S(2)}, u32[]{:S(2)}) %collective-permute-start.4) | collective-permute-done | bytes 294944 | tf_op jit(solution)/shard_map/ppermute | solution.py:248
  48.0 4.4 %collective-permute-done.5.r_7_ = f32[2,144,256]{2,1,0:T(8,128)S(1)} collective-permute-done((f32[2,144,256]{2,1,0:T(8,128)S(1)}, f32[2,144,256]{2,1,0:T(8,128)S(1)}, u32[]{:S(2)}, u32[]{:S(2)}) %collective-permute-start.5) | collective-permute-done | bytes 294944 | tf_op jit(solution)/shard_map/ppermute | solution.py:249
  53.1 6.1 %shard_map.95 = (f32[16,144,256]{2,1,0:T(8,128)}, f32[2,144,256]{2,1,0:T(8,128)}, f32[2,144,256]{2,1,0:T(8,128)}) custom-call(s32[3]{0:T(128)} %pad_add_fusion.r_0_, f32[8]{0:T(128)} %add_divide_fusion.r_1_, f32[2,128,128]{2,1,0:T(8,128)} %pad.8.r_2_.r_1_, f32[16,144,256]{2,1,0:T(8,128)} %copy-done.1, f32[8,144,256]{2,1,0:T(8,128)} %get-tuple-element.41.r_4_, ...), custom_call_target="tpu_custom_call" | custom-call | tf_op jit(solution)/shard_map/pallas_call | solution.py:251
  62.0 5.5 %collective-permute-done.6.r_6_ = f32[2,144,256]{2,1,0:T(8,128)S(1)} collective-permute-done((f32[2,144,256]{2,1,0:T(8,128)}, f32[2,144,256]{2,1,0:T(8,128)S(1)}, u32[]{:S(2)}, u32[]{:S(2)}) %collective-permute-start.6) | collective-permute-done | bytes 294944 | tf_op jit(solution)/shard_map/ppermute | solution.py:248
  67.5 4.0 %collective-permute-done.7.r_7_ = f32[2,144,256]{2,1,0:T(8,128)S(1)} collective-permute-done((f32[2,144,256]{2,1,0:T(8,128)}, f32[2,144,256]{2,1,0:T(8,128)S(1)}, u32[]{:S(2)}, u32[]{:S(2)}) %collective-permute-start.7) | collective-permute-done | bytes 294944 | tf_op jit(solution)/shard_map/ppermute | solution.py:249
  72.2 6.0 %shard_map.96 = (f32[16,144,256]{2,1,0:T(8,128)}, f32[2,144,256]{2,1,0:T(8,128)}, f32[2,144,256]{2,1,0:T(8,128)}) custom-call(s32[3]{0:T(128)} %pad_add_fusion.r_0_, f32[8]{0:T(128)} %add_divide_fusion.r_1_, f32[2,128,128]{2,1,0:T(8,128)} %pad.8.r_2_.r_1_, f32[16,144,256]{2,1,0:T(8,128)} %get-tuple-element.19.r_3_, f32[8,144,256]{2,1,0:T(8,128)} %get-tuple-element.41.r_4_, ...), custom_call_target="tpu_custom_call" | custom-call | tf_op jit(solution)/shard_map/pallas_call | solution.py:251
  78.2 1.6 collective-permute-start.8
  83.4 4.8 %collective-permute-start.10 = (f32[144,256]{1,0:T(8,128)S(1)}, f32[144,256]{1,0:T(8,128)S(1)}, u32[]{:S(2)}, u32[]{:S(2)}) collective-permute-start(f32[144,256]{1,0:T(8,128)S(1)} %get-tuple-element.39), channel_id=1, source_target_pairs={{0,16},{1,17},{2,18},{3,19},{4,20},{5,21},{6,22},{7,23},{8,24},{9,... | collective-permute-start | bytes 442376 | tf_op jit(solution)/shard_map/ppermute | solution.py:266
  88.2 2.9 %collective-permute-done.9.r_7_ = f32[2,144,256]{2,1,0:T(8,128)S(1)} collective-permute-done((f32[2,144,256]{2,1,0:T(8,128)}, f32[2,144,256]{2,1,0:T(8,128)S(1)}, u32[]{:S(2)}, u32[]{:S(2)}) %collective-permute-start.9) | collective-permute-done | bytes 294944 | tf_op jit(solution)/shard_map/ppermute | solution.py:249
  91.8 6.1 %shard_map.97 = (f32[8,144,256]{2,1,0:T(8,128)}, f32[2,8,128,128]{3,2,1,0:T(8,128)}) custom-call(s32[3]{0:T(128)} %pad_add_fusion.r_0_, f32[8]{0:T(128)} %add_divide_fusion.r_1_, f32[2,128,128]{2,1,0:T(8,128)} %pad.8.r_2_.r_1_, f32[16,144,256]{2,1,0:T(8,128)} %get-tuple-element.22.r_3_, f32[8,144,256]{2,1,0:T(8,128)} %get-tuple-element.41.r_4_, ...), custom_call_target="tpu_custom_call" | custom-call | tf_op jit(solution)/shard_map/pallas_call | solution.py:251
  98.7 5.3 %shard_map.98 = (f32[8,144,256]{2,1,0:T(8,128)}, f32[144,256]{1,0:T(8,128)}, f32[144,256]{1,0:T(8,128)}) custom-call(s32[3]{0:T(128)} %pad_add_fusion.r_0_, f32[2,128,128]{2,1,0:T(8,128)} %pad.8.r_2_.r_1_, f32[8,144,256]{2,1,0:T(8,128)} %get-tuple-element.40.r_2_, f32[8,144,256]{2,1,0:T(8,128)} %get-tuple-element.26.r_3_, f32[144,256]{1,0:T(8,128)} %copy-done.16, ...), custom_call_target="tpu_custom_call" | custom-call | tf_op jit(solution)/shard_map/pallas_call | solution.py:269
  106.8 1.7 %collective-permute-done.12.r_4_ = f32[144,256]{1,0:T(8,128)S(1)} collective-permute-done((f32[144,256]{1,0:T(8,128)}, f32[144,256]{1,0:T(8,128)S(1)}, u32[]{:S(2)}, u32[]{:S(2)}) %collective-permute-start.12) | collective-permute-done | bytes 147488 | tf_op jit(solution)/shard_map/ppermute | solution.py:266
  108.5 4.3 %collective-permute-done.13.r_5_ = f32[144,256]{1,0:T(8,128)S(1)} collective-permute-done((f32[144,256]{1,0:T(8,128)}, f32[144,256]{1,0:T(8,128)S(1)}, u32[]{:S(2)}, u32[]{:S(2)}) %collective-permute-start.13) | collective-permute-done | bytes 147488 | tf_op jit(solution)/shard_map/ppermute | solution.py:267
  113.4 5.3 %shard_map.99 = (f32[8,144,256]{2,1,0:T(8,128)}, f32[144,256]{1,0:T(8,128)}, f32[144,256]{1,0:T(8,128)}) custom-call(s32[3]{0:T(128)} %pad_add_fusion.r_0_, f32[2,128,128]{2,1,0:T(8,128)} %pad.8.r_2_.r_1_, f32[8,144,256]{2,1,0:T(8,128)} %get-tuple-element.27.r_2_, f32[8,144,256]{2,1,0:T(8,128)} %get-tuple-element.26.r_3_, f32[144,256]{1,0:T(8,128)} %copy-done.17, ...), custom_call_target="tpu_custom_call" | custom-call | tf_op jit(solution)/shard_map/pallas_call | solution.py:269
  118.7 1.6 collective-permute-start.14
  121.6 1.7 %collective-permute-done.14.r_4_ = f32[144,256]{1,0:T(8,128)S(1)} collective-permute-done((f32[144,256]{1,0:T(8,128)}, f32[144,256]{1,0:T(8,128)S(1)}, u32[]{:S(2)}, u32[]{:S(2)}) %collective-permute-start.14) | collective-permute-done | bytes 147488 | tf_op jit(solution)/shard_map/ppermute | solution.py:266
  123.3 4.3 %collective-permute-done.15.r_5_ = f32[144,256]{1,0:T(8,128)S(1)} collective-permute-done((f32[144,256]{1,0:T(8,128)}, f32[144,256]{1,0:T(8,128)S(1)}, u32[]{:S(2)}, u32[]{:S(2)}) %collective-permute-start.15) | collective-permute-done | bytes 147488 | tf_op jit(solution)/shard_map/ppermute | solution.py:267
  128.2 5.3 %shard_map.100 = (f32[8,144,256]{2,1,0:T(8,128)}, f32[144,256]{1,0:T(8,128)}, f32[144,256]{1,0:T(8,128)}) custom-call(s32[3]{0:T(128)} %pad_add_fusion.r_0_, f32[2,128,128]{2,1,0:T(8,128)} %pad.8.r_2_.r_1_, f32[8,144,256]{2,1,0:T(8,128)} %get-tuple-element.30.r_2_, f32[8,144,256]{2,1,0:T(8,128)} %get-tuple-element.26.r_3_, f32[144,256]{1,0:T(8,128)} %copy-done.18, ...), custom_call_target="tpu_custom_call" | custom-call | tf_op jit(solution)/shard_map/pallas_call | solution.py:269
  133.5 1.6 collective-permute-start.16
  136.4 1.7 %collective-permute-done.16.r_4_ = f32[144,256]{1,0:T(8,128)S(1)} collective-permute-done((f32[144,256]{1,0:T(8,128)}, f32[144,256]{1,0:T(8,128)S(1)}, u32[]{:S(2)}, u32[]{:S(2)}) %collective-permute-start.16) | collective-permute-done | bytes 147488 | tf_op jit(solution)/shard_map/ppermute | solution.py:266
  138.0 4.3 %collective-permute-done.17.r_5_ = f32[144,256]{1,0:T(8,128)S(1)} collective-permute-done((f32[144,256]{1,0:T(8,128)}, f32[144,256]{1,0:T(8,128)S(1)}, u32[]{:S(2)}, u32[]{:S(2)}) %collective-permute-start.17) | collective-permute-done | bytes 147488 | tf_op jit(solution)/shard_map/ppermute | solution.py:267
  143.0 3.9 %shard_map.101 = f32[8,128,128]{2,1,0:T(8,128)} custom-call(s32[3]{0:T(128)} %pad_add_fusion.r_0_, f32[2,128,128]{2,1,0:T(8,128)} %pad.8.r_2_.r_1_, f32[8,144,256]{2,1,0:T(8,128)} %get-tuple-element.33.r_2_, f32[8,144,256]{2,1,0:T(8,128)} %get-tuple-element.26.r_3_, f32[144,256]{1,0:T(8,128)} %copy-done.19, f32[144,256]{1,0:T(8,128)} %copy-done.22), custom_call_target="tpu_custom_call" | custom-call | tf_op jit(solution)/shard_map/pallas_call | solution.py:269
  148.2 10.0 %collective-permute-done.18 = f32[8,128,128]{2,1,0:T(8,128)S(1)} collective-permute-done((f32[8,128,128]{2,1,0:T(8,128)}, f32[8,128,128]{2,1,0:T(8,128)S(1)}, u32[]{:S(2)}, u32[]{:S(2)}) %collective-permute-start.18) | collective-permute-done | bytes 524320 | tf_op jit(solution)/shard_map/ppermute | solution.py:162
  159.5 2.6 %collective-permute-done.19 = f32[2,8,128,128]{3,2,1,0:T(8,128)S(1)} collective-permute-done((f32[2,8,128,128]{3,2,1,0:T(8,128)S(1)}, f32[2,8,128,128]{3,2,1,0:T(8,128)S(1)}, u32[]{:S(2)}, u32[]{:S(2)}) %collective-permute-start.19) | collective-permute-done | bytes 1048608 | tf_op jit(solution)/shard_map/ppermute | solution.py:165
  (94 shorter events, 39.2 us)
Async XLA Ops:
  3.9 5.6 %copy-start.4 = (f32[8,128,384]{2,1,0:T(8,128)S(1)}, f32[8,128,384]{2,1,0:T(8,128)}, u32[]{:S(2)}) copy-start(f32[8,128,384]{2,1,0:T(8,128)} %param.13) | copy-start | bytes 4718596
  3.9 9.1 %collective-permute-start.1 = (f32[26,8,128]{2,1,0:T(8,128)}, f32[26,8,128]{2,1,0:T(8,128)}, u32[]{:S(2)}, u32[]{:S(2)}) collective-permute-start(f32[26,8,128]{2,1,0:T(8,128)} %copy.12), channel_id=1, source_target_pairs={{0,1},{1,2},{2,3},{4,5},{5,6},{6,7},{8,9},{9,10},{10,11},{12,13},{... | collective-permute-start | bytes 319496 | tf_op jit(solution)/shard_map/ppermute | solution.py:211
  7.5 5.0 %collective-permute-start = (f32[26,8,128]{2,1,0:T(8,128)S(1)}, f32[26,8,128]{2,1,0:T(8,128)S(1)}, u32[]{:S(2)}, u32[]{:S(2)}) collective-permute-start(f32[26,8,128]{2,1,0:T(8,128)S(1)} %copy.10), channel_id=1, source_target_pairs={{1,0},{2,1},{3,2},{5,4},{6,5},{7,6},{9,8},{10,9},{11,10},{13,12},{... | collective-permute-start | bytes 319496 | tf_op jit(solution)/shard_map/ppermute | solution.py:212
  16.0 8.0 %copy-start.23 = (s32[2,64,64]{2,1,0:T(8,128)S(1)}, s32[2,64,64]{2,1,0:T(8,128)}, u32[]{:S(2)}) copy-start(s32[2,64,64]{2,1,0:T(8,128)} %param.12) | copy-start | bytes 98308
  16.0 8.7 %copy-start.24 = (s32[2]{0:T(128)S(1)}, s32[2]{0:T(128)}, u32[]{:S(2)}) copy-start(s32[2]{0:T(128)} %constant.87) | copy-start | bytes 28
  16.0 12.9 %copy-start.5 = (f32[8,128,8]{2,1,0:T(8,128)S(1)}, f32[8,128,8]{2,1,0:T(8,128)}, u32[]{:S(2)}) copy-start(f32[8,128,8]{2,1,0:T(8,128)} %pad_dynamic-slice_fusion) | copy-start | bytes 98308
  16.0 12.9 %copy-start.6 = (f32[8,128,128]{2,1,0:T(8,128)S(1)}, f32[8,128,128]{2,1,0:T(8,128)}, u32[]{:S(2)}) copy-start(f32[8,128,128]{2,1,0:T(8,128)} %param.9) | copy-start | bytes 1572868
  17.1 10.1 %collective-permute-start.2 = (f32[34,8,256]{2,1,0:T(8,128)S(1)}, f32[34,8,256]{2,1,0:T(8,128)S(1)}, u32[]{:S(2)}, u32[]{:S(2)}) collective-permute-start(f32[34,8,256]{2,1,0:T(8,128)S(1)} %get-tuple-element.36), channel_id=1, source_target_pairs={{4,0},{8,4},{12,8},{5,1},{9,5},{13,9},{6,2},{10,6},{14,10},{7,3},{... | collective-permute-start | bytes 835592 | tf_op jit(solution)/shard_map/ppermute | solution.py:227
  18.4 10.5 %collective-permute-start.3 = (f32[34,8,256]{2,1,0:T(8,128)S(1)}, f32[34,8,256]{2,1,0:T(8,128)S(1)}, u32[]{:S(2)}, u32[]{:S(2)}) collective-permute-start(f32[34,8,256]{2,1,0:T(8,128)S(1)} %get-tuple-element.37), channel_id=1, source_target_pairs={{0,4},{4,8},{8,12},{1,5},{5,9},{9,13},{2,6},{6,10},{10,14},{3,7},{... | collective-permute-start | bytes 835592 | tf_op jit(solution)/shard_map/ppermute | solution.py:226
  35.3 10.1 %copy-start.1 = (f32[16,144,256]{2,1,0:T(8,128)}, f32[16,144,256]{2,1,0:T(8,128)S(1)}, u32[]{:S(2)}) copy-start(f32[16,144,256]{2,1,0:T(8,128)S(1)} %slice.59.r_3_) | copy-start | bytes 7077892
  36.4 11.6 %collective-permute-start.4 = (f32[2,144,256]{2,1,0:T(8,128)S(1)}, f32[2,144,256]{2,1,0:T(8,128)S(1)}, u32[]{:S(2)}, u32[]{:S(2)}) collective-permute-start(f32[2,144,256]{2,1,0:T(8,128)S(1)} %gather_fusion), channel_id=1, source_target_pairs={{0,16},{1,17},{2,18},{3,19},{4,20},{5,21},{6,22},{7,23},{8,24},{9,... | collective-permute-start | bytes 884744 | tf_op jit(solution)/shard_map/ppermute | solution.py:248
  40.8 11.6 %collective-permute-start.5 = (f32[2,144,256]{2,1,0:T(8,128)S(1)}, f32[2,144,256]{2,1,0:T(8,128)S(1)}, u32[]{:S(2)}, u32[]{:S(2)}) collective-permute-start(f32[2,144,256]{2,1,0:T(8,128)S(1)} %gather_fusion.1), channel_id=1, source_target_pairs={{16,0},{17,1},{18,2},{19,3},{20,4},{21,5},{22,6},{23,7},{24,8},{25... | collective-permute-start | bytes 884744 | tf_op jit(solution)/shard_map/ppermute | solution.py:249
  48.0 4.4 %copy-start.11 = (f32[2,144,256]{2,1,0:T(8,128)}, f32[2,144,256]{2,1,0:T(8,128)S(1)}, u32[]{:S(2)}) copy-start(f32[2,144,256]{2,1,0:T(8,128)S(1)} %collective-permute-done.4.r_6_) | copy-start | bytes 884740
  59.2 8.3 %collective-permute-start.6 = (f32[2,144,256]{2,1,0:T(8,128)}, f32[2,144,256]{2,1,0:T(8,128)S(1)}, u32[]{:S(2)}, u32[]{:S(2)}) collective-permute-start(f32[2,144,256]{2,1,0:T(8,128)} %get-tuple-element.20), channel_id=1, source_target_pairs={{0,16},{1,17},{2,18},{3,19},{4,20},{5,21},{6,22},{7,23},{8,24},{9,... | collective-permute-start | bytes 884744 | tf_op jit(solution)/shard_map/ppermute | solution.py:248
  60.7 10.8 %collective-permute-start.7 = (f32[2,144,256]{2,1,0:T(8,128)}, f32[2,144,256]{2,1,0:T(8,128)S(1)}, u32[]{:S(2)}, u32[]{:S(2)}) collective-permute-start(f32[2,144,256]{2,1,0:T(8,128)} %get-tuple-element.21), channel_id=1, source_target_pairs={{16,0},{17,1},{18,2},{19,3},{20,4},{21,5},{22,6},{23,7},{24,8},{25... | collective-permute-start | bytes 884744 | tf_op jit(solution)/shard_map/ppermute | solution.py:249
  67.5 4.0 %copy-start.12 = (f32[2,144,256]{2,1,0:T(8,128)}, f32[2,144,256]{2,1,0:T(8,128)S(1)}, u32[]{:S(2)}) copy-start(f32[2,144,256]{2,1,0:T(8,128)S(1)} %collective-permute-done.6.r_6_) | copy-start | bytes 884740
  78.2 9.9 %collective-permute-start.8 = (f32[2,144,256]{2,1,0:T(8,128)}, f32[2,144,256]{2,1,0:T(8,128)S(1)}, u32[]{:S(2)}, u32[]{:S(2)}) collective-permute-start(f32[2,144,256]{2,1,0:T(8,128)} %get-tuple-element.23), channel_id=1, source_target_pairs={{0,16},{1,17},{2,18},{3,19},{4,20},{5,21},{6,22},{7,23},{8,24},{9,... | collective-permute-start | bytes 884744 | tf_op jit(solution)/shard_map/ppermute | solution.py:248
  79.8 11.3 %collective-permute-start.9 = (f32[2,144,256]{2,1,0:T(8,128)}, f32[2,144,256]{2,1,0:T(8,128)S(1)}, u32[]{:S(2)}, u32[]{:S(2)}) collective-permute-start(f32[2,144,256]{2,1,0:T(8,128)} %get-tuple-element.24), channel_id=1, source_target_pairs={{16,0},{17,1},{18,2},{19,3},{20,4},{21,5},{22,6},{23,7},{24,8},{25... | collective-permute-start | bytes 884744 | tf_op jit(solution)/shard_map/ppermute | solution.py:249
  82.1 15.8 %collective-permute-start.11 = (f32[144,256]{1,0:T(8,128)S(1)}, f32[144,256]{1,0:T(8,128)S(1)}, u32[]{:S(2)}, u32[]{:S(2)}) collective-permute-start(f32[144,256]{1,0:T(8,128)S(1)} %get-tuple-element.38), channel_id=1, source_target_pairs={{16,0},{17,1},{18,2},{19,3},{20,4},{21,5},{22,6},{23,7},{24,8},{25... | collective-permute-start | bytes 442376 | tf_op jit(solution)/shard_map/ppermute | solution.py:267
  83.4 14.5 %collective-permute-start.10 = (f32[144,256]{1,0:T(8,128)S(1)}, f32[144,256]{1,0:T(8,128)S(1)}, u32[]{:S(2)}, u32[]{:S(2)}) collective-permute-start(f32[144,256]{1,0:T(8,128)S(1)} %get-tuple-element.39), channel_id=1, source_target_pairs={{0,16},{1,17},{2,18},{3,19},{4,20},{5,21},{6,22},{7,23},{8,24},{9,... | collective-permute-start | bytes 442376 | tf_op jit(solution)/shard_map/ppermute | solution.py:266
  104.0 4.5 %collective-permute-start.12 = (f32[144,256]{1,0:T(8,128)}, f32[144,256]{1,0:T(8,128)S(1)}, u32[]{:S(2)}, u32[]{:S(2)}) collective-permute-start(f32[144,256]{1,0:T(8,128)} %get-tuple-element.28), channel_id=1, source_target_pairs={{0,16},{1,17},{2,18},{3,19},{4,20},{5,21},{6,22},{7,23},{8,24},{9,... | collective-permute-start | bytes 442376 | tf_op jit(solution)/shard_map/ppermute | solution.py:266
  105.5 7.2 %collective-permute-start.13 = (f32[144,256]{1,0:T(8,128)}, f32[144,256]{1,0:T(8,128)S(1)}, u32[]{:S(2)}, u32[]{:S(2)}) collective-permute-start(f32[144,256]{1,0:T(8,128)} %get-tuple-element.29), channel_id=1, source_target_pairs={{16,0},{17,1},{18,2},{19,3},{20,4},{21,5},{22,6},{23,7},{24,8},{25... | collective-permute-start | bytes 442376 | tf_op jit(solution)/shard_map/ppermute | solution.py:267
  108.5 4.3 %copy-start.17 = (f32[144,256]{1,0:T(8,128)}, f32[144,256]{1,0:T(8,128)S(1)}, u32[]{:S(2)}) copy-start(f32[144,256]{1,0:T(8,128)S(1)} %collective-permute-done.12.r_4_) | copy-start | bytes 442372
  118.7 4.5 %collective-permute-start.14 = (f32[144,256]{1,0:T(8,128)}, f32[144,256]{1,0:T(8,128)S(1)}, u32[]{:S(2)}, u32[]{:S(2)}) collective-permute-start(f32[144,256]{1,0:T(8,128)} %get-tuple-element.31), channel_id=1, source_target_pairs={{0,16},{1,17},{2,18},{3,19},{4,20},{5,21},{6,22},{7,23},{8,24},{9,... | collective-permute-start | bytes 442376 | tf_op jit(solution)/shard_map/ppermute | solution.py:266
  120.3 7.2 %collective-permute-start.15 = (f32[144,256]{1,0:T(8,128)}, f32[144,256]{1,0:T(8,128)S(1)}, u32[]{:S(2)}, u32[]{:S(2)}) collective-permute-start(f32[144,256]{1,0:T(8,128)} %get-tuple-element.32), channel_id=1, source_target_pairs={{16,0},{17,1},{18,2},{19,3},{20,4},{21,5},{22,6},{23,7},{24,8},{25... | collective-permute-start | bytes 442376 | tf_op jit(solution)/shard_map/ppermute | solution.py:267
  123.2 4.3 %copy-start.18 = (f32[144,256]{1,0:T(8,128)}, f32[144,256]{1,0:T(8,128)S(1)}, u32[]{:S(2)}) copy-start(f32[144,256]{1,0:T(8,128)S(1)} %collective-permute-done.14.r_4_) | copy-start | bytes 442372
  133.5 4.5 %collective-permute-start.16 = (f32[144,256]{1,0:T(8,128)}, f32[144,256]{1,0:T(8,128)S(1)}, u32[]{:S(2)}, u32[]{:S(2)}) collective-permute-start(f32[144,256]{1,0:T(8,128)} %get-tuple-element.34), channel_id=1, source_target_pairs={{0,16},{1,17},{2,18},{3,19},{4,20},{5,21},{6,22},{7,23},{8,24},{9,... | collective-permute-start | bytes 442376 | tf_op jit(solution)/shard_map/ppermute | solution.py:266
  135.1 7.2 %collective-permute-start.17 = (f32[144,256]{1,0:T(8,128)}, f32[144,256]{1,0:T(8,128)S(1)}, u32[]{:S(2)}, u32[]{:S(2)}) collective-permute-start(f32[144,256]{1,0:T(8,128)} %get-tuple-element.35), channel_id=1, source_target_pairs={{16,0},{17,1},{18,2},{19,3},{20,4},{21,5},{22,6},{23,7},{24,8},{25... | collective-permute-start | bytes 442376 | tf_op jit(solution)/shard_map/ppermute | solution.py:267
  138.0 4.3 %copy-start.19 = (f32[144,256]{1,0:T(8,128)}, f32[144,256]{1,0:T(8,128)S(1)}, u32[]{:S(2)}) copy-start(f32[144,256]{1,0:T(8,128)S(1)} %collective-permute-done.16.r_4_) | copy-start | bytes 442372
  146.9 11.3 %collective-permute-start.18 = (f32[8,128,128]{2,1,0:T(8,128)}, f32[8,128,128]{2,1,0:T(8,128)S(1)}, u32[]{:S(2)}, u32[]{:S(2)}) collective-permute-start(f32[8,128,128]{2,1,0:T(8,128)} %shard_map.101), channel_id=1, source_target_pairs={{2,0},{3,1},{1,2},{6,4},{7,5},{5,6},{10,8},{11,9},{9,10},{14,12},{... | collective-permute-start | bytes 1572872 | tf_op jit(solution)/shard_map/ppermute | solution.py:162
  148.2 13.9 %copy-start.7 = (f32[8,128,128]{2,1,0:T(8,128)S(1)}, f32[8,128,128]{2,1,0:T(8,128)}, u32[]{:S(2)}) copy-start(f32[8,128,128]{2,1,0:T(8,128)} %shard_map.101) | copy-start | bytes 1572868
  159.4 2.7 %collective-permute-start.19 = (f32[2,8,128,128]{3,2,1,0:T(8,128)S(1)}, f32[2,8,128,128]{3,2,1,0:T(8,128)S(1)}, u32[]{:S(2)}, u32[]{:S(2)}) collective-permute-start(f32[2,8,128,128]{3,2,1,0:T(8,128)S(1)} %pad_maximum_fusion.3), channel_id=1, source_target_pairs={{0,1},{1,0},{2,3},{3,2},{4,5},{5,4},{6,7},{7,6},{8,9},{9,8},{10,11... | collective-permute-start | bytes 3145736 | tf_op jit(solution)/shard_map/ppermute | solution.py:165
  (13 other events, 15.2 us)

commit v5 on v4

--- a/solution.py
+++ b/solution.py
@@ -54,28 +54,24 @@
     return (y >= 0) & (y < y_total) & (x >= 0) & (x < x_total)
 
 
-def _em_kernel(factor, last, depth, totals, pos, prof, fl, f, mat, w, zlo, zhi, *outs):
+def _em_planes(factor, zs, depth, totals, pos, prof, fl, get_f, mat_at, w, put):
     diagonal = 6.0 + SHIFT
-    if last:
-        (heat, own) = outs
-    else:
-        (o, oz0, oz1) = outs
     height, breadth, y_total, x_total = totals
-    rows, lanes = f.shape[1], f.shape[2]
+    rows, lanes = w.shape[1], w.shape[2]
     keep = _inside(pos, rows, lanes, height, breadth, y_total, x_total)
     sy, sx = _selectors(pos, rows, lanes, height, breadth, 0)
-    masks = [_cells(fl, pos[0] + zo, sy, sx) for zo in range(depth // MB)]
-    for z in range(depth):
-        cur = [f[c * depth + z] for c in range(2)]
+    masks = {}
+    for z in zs:
+        if z // MB not in masks:
+            masks[z // MB] = _cells(fl, pos[0] + z // MB, sy, sx)
+        cur = [get_f(c, z) for c in range(2)]
         beside = []
         for c in range(2):
-            z_up = f[c * depth + z + 1] if z + 1 < depth else zhi[c]
-            z_dn = f[c * depth + z - 1] if z > 0 else zlo[c]
             y_up, y_dn, x_up, x_dn = _rolls(cur[c])
-            total = z_up + z_dn
+            total = get_f(c, z + 1) + get_f(c, z - 1)
             total = total + y_up + y_dn
             beside.append(total + x_up + x_dn)
-        k = masks[z // MB] * mat[z]
+        k = masks[z // MB] * mat_at(z)
         s0 = prof[z] * w[0]
         s1 = prof[z] * w[1]
         real_res = s0 - (diagonal * cur[0] - k * cur[1] - beside[0])
@@ -83,71 +79,161 @@
         scaled = factor / (diagonal * diagonal + k * k)
         n0 = jnp.where(keep, cur[0] + scaled * (diagonal * real_res + k * imag_res), 0.0)
         n1 = jnp.where(keep, cur[1] + scaled * (diagonal * imag_res - k * real_res), 0.0)
-        if last:
-            heat[z] = HEATING * k * (n0 * n0 + n1 * n1)
-            own[0, z] = n0[0:height, 0:breadth]
-            own[1, z] = n1[0:height, 0:breadth]
-        else:
-            o[z] = n0
-            o[depth + z] = n1
-            if z == 0:
-                oz0[0] = n0
-                oz0[1] = n1
-            if z == depth - 1:
-                oz1[0] = n0
-                oz1[1] = n1
-
-
-def _heat_kernel(last, depth, totals, pos, fl, t, q, tzlo, tzhi, *outs):
-    if last:
-        (own,) = outs
-    else:
-        (o, oz0, oz1) = outs
+        put(z, n0, n1, HEATING * k * (n0 * n0 + n1 * n1))
+
+
+def _em_inner(factor, last, depth, totals, pos, prof, fl, f, p0, p7, mat, w, *outs):
+    height, breadth = totals[0], totals[1]
+
+    def get_f(c, z):
+        if z == 0:
+            return p0[c]
+        if z == depth - 1:
+            return p7[c]
+        return f[c * depth + z]
+
+    def put(z, n0, n1, q):
+        if last:
+            outs[0][z] = q
+            outs[1][0, z] = n0[0:height, 0:breadth]
+            outs[1][1, z] = n1[0:height, 0:breadth]
+        else:
+            outs[0][z] = n0
+            outs[0][depth + z] = n1
+
+    if not last:
+        zero = jnp.zeros(w.shape[1:], jnp.float32)
+        for c in range(2):
+            outs[0][c * depth] = zero
+            outs[0][c * depth + depth - 1] = zero
+    _em_planes(factor, range(1, depth - 1), depth, totals, pos, prof, fl, get_f,
+               lambda z: mat[z], w, put)
+
+
+def _em_outer(factor, last, depth, totals, pos, prof, fl, f1, f9, f6, f14, p0, p7, m0, m7, w,
+              zlo, zhi, *outs):
+    height, breadth = totals[0], totals[1]
+    near = {(0, 1): f1, (1, 1): f9, (0, depth - 2): f6, (1, depth - 2): f14}
+
+    def get_f(c, z):
+        if z == -1:
+            return zlo[c]
+        if z == depth:
+            return zhi[c]
+        if z == 0:
+            return p0[c]
+        if z == depth - 1:
+            return p7[c]
+        return near[(c, z)][0]
+
+    def put(z, n0, n1, q):
+        j = 0 if z == 0 else 1
+        if last:
+            outs[0][j] = q
+            outs[1][0, j] = n0[0:height, 0:breadth]
+            outs[1][1, j] = n1[0:height, 0:breadth]
+        else:
+            outs[j][0] = n0
+            outs[j][1] = n1
+
+    _em_planes(factor, (0, depth - 1), depth, totals, pos, prof, fl, get_f,
+               lambda z: (m0 if z == 0 else m7)[0], w, put)
+
+
+def _heat_planes(zs, depth, totals, pos, fl, get_t, heat_at, put):
     height, breadth, x_first_block = totals
-    rows, lanes = t.shape[1], t.shape[2]
+    rows, lanes = get_t(zs[0]).shape
     sy, sx = _selectors(pos, rows, lanes, height, breadth, x_first_block)
     zb_total = fl.shape[0]
-    below = pos[0] - 1
-    above = pos[0] + depth // MB
-    m_below = _cells(fl, jnp.maximum(below, 0), sy, sx) * jnp.where(below >= 0, 1.0, 0.0)
-    m_above = _cells(fl, jnp.minimum(above, zb_total - 1), sy, sx) * jnp.where(
-        above < zb_total, 1.0, 0.0)
-    m_own = [_cells(fl, pos[0] + zo, sy, sx) for zo in range(depth // MB)]
-    planes = [m_below] + [m_own[z // MB] for z in range(depth)] + [m_above]
-    temps = [tzlo[...]] + [t[z] for z in range(depth)] + [tzhi[...]]
-    kaps = [1.0 / (1.0 + SOFTEN * v * v) for v in temps]
-    for z in range(depth):
-        c = temps[z + 1]
-        centre_kappa = kaps[z + 1]
+    cache = {}
+
+    def mask(z):
+        blk = -1 if z < 0 else z // MB
+        if blk not in cache:
+            zb = pos[0] + blk
+            ok = jnp.where((zb >= 0) & (zb < zb_total), 1.0, 0.0)
+            cache[blk] = _cells(fl, jnp.clip(zb, 0, zb_total - 1), sy, sx) * ok
+        return cache[blk]
+
+    kap_cache = {}
+
+    def kap(z):
+        if z not in kap_cache:
+            v = get_t(z)
+            kap_cache[z] = 1.0 / (1.0 + SOFTEN * v * v)
+        return kap_cache[z]
+
+    for z in zs:
+        c = get_t(z)
+        centre_kappa = kap(z)
         y_up, y_dn, x_up, x_dn = _rolls(c)
         ky_up, ky_dn, kx_up, kx_dn = _rolls(centre_kappa)
-        mc = planes[z + 1]
+        mc = mask(z)
         my_up, my_dn, mx_up, mx_dn = _rolls(mc)
         flux = jnp.zeros_like(c)
         for other, kappa, other_mask in (
-            (temps[z + 2], kaps[z + 2], planes[z + 2]), (temps[z], kaps[z], planes[z]),
+            (get_t(z + 1), kap(z + 1), mask(z + 1)), (get_t(z - 1), kap(z - 1), mask(z - 1)),
             (y_up, ky_up, my_up), (y_dn, ky_dn, my_dn), (x_up, kx_up, mx_up), (x_dn, kx_dn, mx_dn),
         ):
             flux = flux + other_mask * (centre_kappa + kappa) * (other - c)
-        new = c + 0.5 * CONDUCT * mc * flux + q[z]
-        if last:
-            own[z] = new[0:height, 0:breadth]
-        else:
-            o[z] = new
-            if z == 0:
-                oz0[...] = new
-            if z == depth - 1:
-                oz1[...] = new
-
-
-def _vmem_call(kernel, out_shape, n_in, n_smem=0):
-    specs = [pl.BlockSpec(memory_space=pltpu.SMEM)] * n_smem
-    specs += [pl.BlockSpec(memory_space=pltpu.VMEM)] * (n_in - n_smem)
+        put(z, c + 0.5 * CONDUCT * mc * flux + heat_at(z))
+
+
+def _heat_inner(last, depth, totals, pos, fl, t, t0, t7, q, *outs):
+    height, breadth = totals[0], totals[1]
+
+    def get_t(z):
+        if z == 0:
+            return t0[...]
+        if z == depth - 1:
+            return t7[...]
+        return t[z]
+
+    def put(z, new):
+        if last:
+            outs[0][z] = new[0:height, 0:breadth]
+        else:
+            outs[0][z] = new
+
+    if not last:
+        zero = jnp.zeros(t0.shape, jnp.float32)
+        outs[0][0] = zero
+        outs[0][depth - 1] = zero
+    _heat_planes(list(range(1, depth - 1)), depth, totals, pos, fl, get_t, lambda z: q[z], put)
+
+
+def _heat_outer(last, depth, totals, pos, fl, t1, t6, t0, t7, qb, tzlo, tzhi, *outs):
+    height, breadth = totals[0], totals[1]
+
+    def get_t(z):
+        return {-1: tzlo, 0: t0, 1: t1, depth - 2: t6, depth - 1: t7, depth: tzhi}[z][...].reshape(
+            t0.shape)
+
+    def put(z, new):
+        j = 0 if z == 0 else 1
+        if last:
+            outs[0][j] = new[0:height, 0:breadth]
+        else:
+            outs[j][...] = new
+
+    _heat_planes([0, depth - 1], depth, totals, pos, fl, get_t,
+                 lambda z: qb[0 if z == 0 else 1], put)
+
+
+def _plane(idx, rows, lanes):
+    return pl.BlockSpec((1, rows, lanes), lambda i: (idx, 0, 0))
+
+
+def _call(kernel, out_shape, specs, flops, nbytes):
+    smem = pl.BlockSpec(memory_space=pltpu.SMEM)
+    vmem = pl.BlockSpec(memory_space=pltpu.VMEM)
     return pl.pallas_call(
         kernel,
         out_shape=out_shape,
-        in_specs=specs,
-        out_specs=[pl.BlockSpec(memory_space=pltpu.VMEM)] * len(out_shape),
+        grid=(1,),
+        in_specs=[smem if x == "s" else vmem if x == "v" else x for x in specs],
+        out_specs=[vmem] * len(out_shape),
+        cost_estimate=pl.CostEstimate(flops=flops, transcendentals=0, bytes_accessed=nbytes),
     )
 
 
@@ -236,44 +322,73 @@
                     ((0, 0), (0, 128 - fb[1]), (0, 128 - fb[2])))
     pos = jnp.stack([z_start // MB, y_start // MB, x_start // MB]).astype(jnp.int32)
 
+    assert depth >= 3
     up_z, down_z = _line_pairs(n_gz)
-    fshape = jax.ShapeDtypeStruct((2 * depth, rows, lanes), jnp.float32)
-    plane2 = jax.ShapeDtypeStruct((2, rows, lanes), jnp.float32)
-    qshape = jax.ShapeDtypeStruct((depth, rows, lanes), jnp.float32)
-    oshape = jax.ShapeDtypeStruct((2, depth, height, breadth), jnp.float32)
-    lo_plane = field[jnp.array([0, depth])]
-    hi_plane = field[jnp.array([depth - 1, 2 * depth - 1])]
+    f32 = jnp.float32
+    fshape = jax.ShapeDtypeStruct((2 * depth, rows, lanes), f32)
+    plane2 = jax.ShapeDtypeStruct((2, rows, lanes), f32)
+    qshape = jax.ShapeDtypeStruct((depth, rows, lanes), f32)
+    oshape = jax.ShapeDtypeStruct((2, depth, height, breadth), f32)
+    obshape = jax.ShapeDtypeStruct((2, 2, height, breadth), f32)
+    em_totals = (height, breadth, y_total, x_total)
+    cells = rows * lanes
+    near = [_plane(i, rows, lanes) for i in (1, depth + 1, depth - 2, 2 * depth - 2)]
+    mat_planes = [_plane(0, rows, lanes), _plane(depth - 1, rows, lanes)]
+    p0 = field[jnp.array([0, depth])]
+    p7 = field[jnp.array([depth - 1, 2 * depth - 1])]
     for i, factor in enumerate(WEIGHTS):
         last = i == len(WEIGHTS) - 1
-        zlo = lax.ppermute(hi_plane, "gz", up_z)
-        zhi = lax.ppermute(lo_plane, "gz", down_z)
-        outs = (qshape, oshape) if last else (fshape, plane2, plane2)
-        res = _vmem_call(
-            lambda *r, factor=factor, last=last: _em_kernel(
-                factor, last, depth, (height, breadth, y_total, x_total), *r), outs, 8, 2
-        )(pos, profile, flags, field, material, winding, zlo, zhi)
-        if last:
-            heat, field_out = res
-        else:
-            field, lo_plane, hi_plane = res
-
-    tshape = jax.ShapeDtypeStruct((depth, rows, lanes), jnp.float32)
-    tplane = jax.ShapeDtypeStruct((rows, lanes), jnp.float32)
-    town = jax.ShapeDtypeStruct((depth, height, breadth), jnp.float32)
-    lo_t, hi_t = kelvin[0], kelvin[depth - 1]
+        zlo = lax.ppermute(p7, "gz", up_z)
+        zhi = lax.ppermute(p0, "gz", down_z)
+        outs = (qshape, oshape) if last else (fshape,)
+        inner = _call(
+            lambda *r, factor=factor, last=last: _em_inner(factor, last, depth, em_totals, *r),
+            outs, ["s", "s", "v", "v", "v", "v", "v", "v"],
+            60 * 2 * (depth - 2) * cells, 4 * (5 * depth + 6) * cells,
+        )(pos, profile, flags, field, p0, p7, material, winding)
+        outs = (plane2, obshape) if last else (plane2, plane2)
+        outer = _call(
+            lambda *r, factor=factor, last=last: _em_outer(factor, last, depth, em_totals, *r),
+            outs, ["s", "s", "v"] + near + ["v", "v"] + mat_planes + ["v", "v", "v"],
+            60 * 2 * 2 * cells, 4 * 20 * cells,
+        )(pos, profile, flags, field, field, field, field, p0, p7, material, material, winding,
+          zlo, zhi)
+        if last:
+            heat, field_out = inner
+            heat_b, own_b = outer
+        else:
+            (field,) = inner
+            p0, p7 = outer
+    field_out = field_out.at[:, 0].set(own_b[:, 0]).at[:, depth - 1].set(own_b[:, 1])
+
+    tshape = jax.ShapeDtypeStruct((depth, rows, lanes), f32)
+    tplane = jax.ShapeDtypeStruct((rows, lanes), f32)
+    town = jax.ShapeDtypeStruct((depth, height, breadth), f32)
+    tbshape = jax.ShapeDtypeStruct((2, height, breadth), f32)
+    t_totals = (height, breadth, offset // MB)
+    t_near = [_plane(1, rows, lanes), _plane(depth - 2, rows, lanes)]
+    t0, t7 = kelvin[0], kelvin[depth - 1]
     for number in range(STEPS):
         last = number == STEPS - 1
-        tzlo = lax.ppermute(hi_t, "gz", up_z)
-        tzhi = lax.ppermute(lo_t, "gz", down_z)
-        outs = (town,) if last else (tshape, tplane, tplane)
-        res = _vmem_call(
-            lambda *r, last=last: _heat_kernel(
-                last, depth, (height, breadth, offset // MB), *r), outs, 6, 1
-        )(pos, flags, kelvin, heat, tzlo, tzhi)
-        if last:
-            (own_t,) = res
-        else:
-            kelvin, lo_t, hi_t = res
+        tzlo = lax.ppermute(t7, "gz", up_z)
+        tzhi = lax.ppermute(t0, "gz", down_z)
+        inner = _call(
+            lambda *r, last=last: _heat_inner(last, depth, t_totals, *r),
+            (town,) if last else (tshape,), ["s", "v", "v", "v", "v", "v"],
+            80 * (depth - 2) * cells, 4 * (3 * depth + 2) * cells,
+        )(pos, flags, kelvin, t0, t7, heat)
+        outer = _call(
+            lambda *r, last=last: _heat_outer(last, depth, t_totals, *r),
+            (tbshape,) if last else (tplane, tplane), ["s", "v"] + t_near + ["v"] * 5,
+            80 * 2 * cells, 4 * 12 * cells,
+        )(pos, flags, kelvin, kelvin, t0, t7, heat_b, tzlo, tzhi)
+        if last:
+            (own_t,) = inner
+            (own_tb,) = outer
+        else:
+            (kelvin,) = inner
+            t0, t7 = outer
+    own_t = own_t.at[0].set(own_tb[0]).at[depth - 1].set(own_tb[1])
 
     segment_kelvin = _broadcast_blocks(own_t, gx_i, n_gx, first_owner)
     return (field_out, segment_kelvin)

time: 164 us -> 166 us (1.012)
  waiting for transfers between devices: 54.1 us -> 22.2 us
  Pallas kernels: 38.1 us -> 54.5 us
  starting transfers between devices: 37.9 us -> 50.1 us
  local copies, waits for them, and re-layouts: 21.3 us -> 27 us
    ppermute x14, waiting for transfers between devices: 37.3 us -> 5.25 us  [the longest x3 3.09 us: on_device(): zlo = lax.ppermute(p7, 'gz', up_z)]
    pallas_call x7 -> x14, Pallas kernels: 38.1 us -> 54.5 us  [the longest x4 17.8 us: on_device(): _call(lambda *r, last=last: _heat_inner(last, depth, t_totals, *r), (town...]
    ppermute x14, starting transfers between devices: 25.8 us -> 38.1 us  [the longest x4 15.2 us: on_device(): tzlo = lax.ppermute(t7, 'gz', up_z)]
    scatter x0 -> x4, local copies, waits for them, and re-layouts: none -> 3.02 us  [the longest x2 1.69 us: on_device(): own_t = own_t.at[0].set(own_tb[0]).at[depth - 1].set(own_tb[1])]
    unnamed x50 -> x60, local copies, waits for them, and re-layouts: 7.72 us -> 10.3 us
  transfers between devices with their start and end apart: 20 -> 20, of which waited for: 15 -> 8; matrix products, arithmetic and copies ran while one was open for 6% -> 6% of each run, Pallas kernels for 4% -> 23%
where the time goes in v5:
time: 166 us; the launch traced here: 165 us
  Pallas kernels  54.5 us (33%)
  starting transfers between devices  50.1 us (30%)
  local copies, waits for them, and re-layouts  27 us (16%)
  waiting for transfers between devices  22.2 us (13%)
  other arithmetic  9.33 us (6%)
  between operations  1.87 us (1%)
    pallas_call x4, Pallas kernels, on_device(): _call(lambda *r, last=last: _heat_inner(last, depth, t_totals, *r), (town...  17.8 us
    pallas_call x3, Pallas kernels, on_device(): _call(lambda *r, factor=factor, last=last: _em_inner(factor, last, depth,...  16.4 us
    ppermute x4, starting transfers between devices, on_device(): tzlo = lax.ppermute(t7, 'gz', up_z)  15.2 us
    ppermute x3, starting transfers between devices, on_device(): zlo = lax.ppermute(p7, 'gz', up_z)  13.7 us
    ppermute x1, waiting for transfers between devices, _broadcast_blocks(): r1 = lax.ppermute(own, 'gx', [(2, 0), (3, 1), (1, 2)])  11.5 us
    pallas_call x4, Pallas kernels, on_device(): _call(lambda *r, last=last: _heat_outer(last, depth, t_totals, *r), (tbsh...  10.9 us
    unnamed x60, local copies, waits for them, and re-layouts  10.3 us
    pallas_call x3, Pallas kernels, on_device(): _call(lambda *r, factor=factor, last=last: _em_outer(factor, last, depth,...  9.48 us
  transfers between devices with their start and end apart: 20, of which 8 were waited for; matrix products, arithmetic and copies ran while one was open for 6% of the time, Pallas kernels for 23%

profile of v5, /device:TPU:0, one launch (start us, length us, event | category | flops | bytes accessed | tf_op | source)
XLA Modules:
  0.0 165.0 jit_solution(16449918024376837303)
XLA Ops:
  0.6 1.6 pad_maximum_fusion.1
  3.9 3.1 %collective-permute-start.1 = (f32[26,8,128]{2,1,0:T(8,128)}, f32[26,8,128]{2,1,0:T(8,128)}, u32[]{:S(2)}, u32[]{:S(2)}) collective-permute-start(f32[26,8,128]{2,1,0:T(8,128)} %copy.12), channel_id=1, source_target_pairs={{0,1},{1,2},{2,3},{4,5},{5,6},{6,7},{8,9},{9,10},{10,11},{12,13},{... | collective-permute-start | bytes 319496 | tf_op jit(solution)/shard_map/ppermute | solution.py:297
  18.4 5.0 %collective-permute-start.3 = (f32[34,8,256]{2,1,0:T(8,128)S(1)}, f32[34,8,256]{2,1,0:T(8,128)S(1)}, u32[]{:S(2)}, u32[]{:S(2)}) collective-permute-start(f32[34,8,256]{2,1,0:T(8,128)S(1)} %get-tuple-element.79), channel_id=1, source_target_pairs={{0,4},{4,8},{8,12},{1,5},{5,9},{9,13},{2,6},{6,10},{10,14},{3,7},{... | collective-permute-start | bytes 835592 | tf_op jit(solution)/shard_map/ppermute | solution.py:312
  24.7 2.4 %collective-permute-done.2 = f32[34,8,256]{2,1,0:T(8,128)S(1)} collective-permute-done((f32[34,8,256]{2,1,0:T(8,128)S(1)}, f32[34,8,256]{2,1,0:T(8,128)S(1)}, u32[]{:S(2)}, u32[]{:S(2)}) %collective-permute-start.2) | collective-permute-done | bytes 278560 | tf_op jit(solution)/shard_map/ppermute | solution.py:313
  27.1 1.7 %collective-permute-done.3 = f32[34,8,256]{2,1,0:T(8,128)S(1)} collective-permute-done((f32[34,8,256]{2,1,0:T(8,128)S(1)}, f32[34,8,256]{2,1,0:T(8,128)S(1)}, u32[]{:S(2)}, u32[]{:S(2)}) %collective-permute-start.3) | collective-permute-done | bytes 278560 | tf_op jit(solution)/shard_map/ppermute | solution.py:312
  28.8 3.8 %pad_maximum_fusion = f32[34,144,256]{2,1,0:T(8,128)S(1)} fusion(f32[34,8,256]{2,1,0:T(8,128)S(1)} %collective-permute-done.3, f32[34,8,256]{2,1,0:T(8,128)S(1)} %collective-permute-done.2, f32[8,128,8]{2,1,0:T(8,128)S(1)} %copy-done.5, f32[8,128,112]{2,1,0:T(8,128)S(1)} %broadcast_in_dim.13, f32[8,128,136]{2,1,0:T(8,128)S(1)} %copy-done.3, ...), kind=kLoop, calls=%fused_computation.2 | loop fusion | flops 12533760 | bytes 10027008 | tf_op jit(solution)/shard_map/concatenate | solution.py:314
  33.5 1.5 copy-done.1
  37.6 4.6 %collective-permute-start.4 = (f32[2,144,256]{2,1,0:T(8,128)S(1)}, f32[2,144,256]{2,1,0:T(8,128)S(1)}, u32[]{:S(2)}, u32[]{:S(2)}) collective-permute-start(f32[2,144,256]{2,1,0:T(8,128)S(1)} %gather_fusion.1), channel_id=1, source_target_pairs={{0,16},{1,17},{2,18},{3,19},{4,20},{5,21},{6,22},{7,23},{8,24},{9,... | collective-permute-start | bytes 884744 | tf_op jit(solution)/shard_map/ppermute | solution.py:341
  42.2 3.2 %fusion.1 = (f32[8,144,256]{2,1,0:T(8,128)}, f32[8,144,256]{2,1,0:T(8,128)}) fusion(f32[34,144,256]{2,1,0:T(8,128)} %copy-done.1), kind=kLoop, calls=%fused_computation.37 | loop fusion | bytes 4718592 | tf_op jit(solution)/shard_map/slice | solution.py:318
  45.5 2.0 %collective-permute-done.5.r_13_ = f32[2,144,256]{2,1,0:T(8,128)S(1)} collective-permute-done((f32[2,144,256]{2,1,0:T(8,128)S(1)}, f32[2,144,256]{2,1,0:T(8,128)S(1)}, u32[]{:S(2)}, u32[]{:S(2)}) %collective-permute-start.5) | collective-permute-done | bytes 294944 | tf_op jit(solution)/shard_map/ppermute | solution.py:342
  47.5 1.8 %collective-permute-done.4.r_12_ = f32[2,144,256]{2,1,0:T(8,128)S(1)} collective-permute-done((f32[2,144,256]{2,1,0:T(8,128)S(1)}, f32[2,144,256]{2,1,0:T(8,128)S(1)}, u32[]{:S(2)}, u32[]{:S(2)}) %collective-permute-start.4) | collective-permute-done | bytes 294944 | tf_op jit(solution)/shard_map/ppermute | solution.py:341
  50.0 3.1 %shard_map.96 = (f32[2,144,256]{2,1,0:T(8,128)}, f32[2,144,256]{2,1,0:T(8,128)}) custom-call(s32[3]{0:T(128)} %pad_add_fusion.r_0_, f32[8]{0:T(128)} %add_divide_fusion.r_1_, f32[2,128,128]{2,1,0:T(8,128)} %pad.16.r_2_.r_1_, f32[16,144,256]{2,1,0:T(8,128)} %copy-done, f32[16,144,256]{2,1,0:T(8,128)} %copy-done, f32[16,144,256]{2,1,0:T(8,128)} %copy-done, ...), custom_call_target="tpu_custom_call" | custom-call | flops 8847360 | bytes 2949120 | tf_op jit(solution)/shard_map/pallas_call | solution.py:350
  54.4 4.6 %collective-permute-start.6 = (f32[2,144,256]{2,1,0:T(8,128)}, f32[2,144,256]{2,1,0:T(8,128)S(1)}, u32[]{:S(2)}, u32[]{:S(2)}) collective-permute-start(f32[2,144,256]{2,1,0:T(8,128)} %get-tuple-element.65.r_5_.r_8_), channel_id=1, source_target_pairs={{0,16},{1,17},{2,18},{3,19},{4,20},{5,21},{6,22},{7,23},{8,24},{9,... | collective-permute-start | bytes 884744 | tf_op jit(solution)/shard_map/ppermute | solution.py:341
  59.0 5.5 %shard_map.95.r_3_.r_4_.r_5_.r_6_ = f32[16,144,256]{2,1,0:T(8,128)} custom-call(s32[3]{0:T(128)} %pad_add_fusion.r_0_, f32[8]{0:T(128)} %add_divide_fusion.r_1_, f32[2,128,128]{2,1,0:T(8,128)} %pad.16.r_2_.r_1_, f32[16,144,256]{2,1,0:T(8,128)} %copy-done, f32[2,144,256]{2,1,0:T(8,128)} %copy-done.9, f32[2,144,256]{2,1,0:T(8,128)} %copy-done.8, ...), custom_call_target="tpu_custom_call" | custom-call | flops 26542080 | bytes 6782976 | tf_op jit(solution)/shard_map/pallas_call | solution.py:344
  66.6 3.1 %shard_map.98 = (f32[2,144,256]{2,1,0:T(8,128)}, f32[2,144,256]{2,1,0:T(8,128)}) custom-call(s32[3]{0:T(128)} %pad_add_fusion.r_0_, f32[8]{0:T(128)} %add_divide_fusion.r_1_, f32[2,128,128]{2,1,0:T(8,128)} %pad.16.r_2_.r_1_, f32[16,144,256]{2,1,0:T(8,128)} %shard_map.95.r_3_.r_4_.r_5_.r_6_, f32[16,144,256]{2,1,0:T(8,128)} %shard_map.95.r_3_.r_4_.r_5_.r_6_, ...), custom_call_target="tpu_custom_call" | custom-call | flops 8847360 | bytes 2949120 | tf_op jit(solution)/shard_map/pallas_call | solution.py:350
  71.0 4.6 %collective-permute-start.8 = (f32[2,144,256]{2,1,0:T(8,128)}, f32[2,144,256]{2,1,0:T(8,128)S(1)}, u32[]{:S(2)}, u32[]{:S(2)}) collective-permute-start(f32[2,144,256]{2,1,0:T(8,128)} %get-tuple-element.67.r_5_.r_8_), channel_id=1, source_target_pairs={{0,16},{1,17},{2,18},{3,19},{4,20},{5,21},{6,22},{7,23},{8,24},{9,... | collective-permute-start | bytes 884744 | tf_op jit(solution)/shard_map/ppermute | solution.py:341
  77.9 1.5 collective-permute-start.11
  79.4 5.4 %shard_map.97.r_3_.r_4_.r_5_.r_6_ = f32[16,144,256]{2,1,0:T(8,128)} custom-call(s32[3]{0:T(128)} %pad_add_fusion.r_0_, f32[8]{0:T(128)} %add_divide_fusion.r_1_, f32[2,128,128]{2,1,0:T(8,128)} %pad.16.r_2_.r_1_, f32[16,144,256]{2,1,0:T(8,128)} %shard_map.95.r_3_.r_4_.r_5_.r_6_, f32[2,144,256]{2,1,0:T(8,128)} %get-tuple-element.64.r_4_.r_7_, ...), custom_call_target="tpu_custom_call" | custom-call | flops 26542080 | bytes 6782976 | tf_op jit(solution)/shard_map/pallas_call | solution.py:344
  86.3 3.3 %shard_map.100 = (f32[2,144,256]{2,1,0:T(8,128)}, f32[2,2,128,128]{3,2,1,0:T(8,128)}) custom-call(s32[3]{0:T(128)} %pad_add_fusion.r_0_, f32[8]{0:T(128)} %add_divide_fusion.r_1_, f32[2,128,128]{2,1,0:T(8,128)} %pad.16.r_2_.r_1_, f32[16,144,256]{2,1,0:T(8,128)} %shard_map.97.r_3_.r_4_.r_5_.r_6_, f32[16,144,256]{2,1,0:T(8,128)} %shard_map.97.r_3_.r_4_.r_5_.r_6_, ...), custom_call_target="tpu_custom_call" | custom-call | flops 8847360 | bytes 2949120 | tf_op jit(solution)/shard_map/pallas_call | solution.py:350
  90.2 2.8 %shard_map.102 = (f32[144,256]{1,0:T(8,128)}, f32[144,256]{1,0:T(8,128)}) custom-call(s32[3]{0:T(128)} %pad_add_fusion.r_0_, f32[2,128,128]{2,1,0:T(8,128)} %pad.16.r_2_.r_1_, f32[8,144,256]{2,1,0:T(8,128)} %get-tuple-element.82.r_2_.r_3_, f32[8,144,256]{2,1,0:T(8,128)} %get-tuple-element.82.r_2_.r_3_, f32[144,256]{1,0:T(8,128)} %copy-done.11, ...), custom_call_target="tpu_custom_call" | custom-call | flops 5898240 | bytes 1769472 | tf_op jit(solution)/shard_map/pallas_call | solution.py:380
  94.3 4.6 %collective-permute-start.12 = (f32[144,256]{1,0:T(8,128)}, f32[144,256]{1,0:T(8,128)S(1)}, u32[]{:S(2)}, u32[]{:S(2)}) collective-permute-start(f32[144,256]{1,0:T(8,128)} %get-tuple-element.73.r_4_.r_5_), channel_id=1, source_target_pairs={{0,16},{1,17},{2,18},{3,19},{4,20},{5,21},{6,22},{7,23},{8,24},{9,... | collective-permute-start | bytes 442376 | tf_op jit(solution)/shard_map/ppermute | solution.py:373
  98.9 5.5 %shard_map.99 = (f32[8,144,256]{2,1,0:T(8,128)}, f32[2,8,128,128]{3,2,1,0:T(8,128)}) custom-call(s32[3]{0:T(128)} %pad_add_fusion.r_0_, f32[8]{0:T(128)} %add_divide_fusion.r_1_, f32[2,128,128]{2,1,0:T(8,128)} %pad.16.r_2_.r_1_, f32[16,144,256]{2,1,0:T(8,128)} %shard_map.97.r_3_.r_4_.r_5_.r_6_, f32[2,144,256]{2,1,0:T(8,128)} %get-tuple-element.66.r_4_.r_7_, ...), custom_call_target="tpu_custom_call" | custom-call | flops 26542080 | bytes 6782976 | tf_op jit(solution)/shard_map/pallas_call | solution.py:344
  104.4 4.7 %shard_map.101.r_2_.r_3_ = f32[8,144,256]{2,1,0:T(8,128)} custom-call(s32[3]{0:T(128)} %pad_add_fusion.r_0_, f32[2,128,128]{2,1,0:T(8,128)} %pad.16.r_2_.r_1_, f32[8,144,256]{2,1,0:T(8,128)} %get-tuple-element.82.r_2_.r_3_, f32[144,256]{1,0:T(8,128)} %copy-done.11, f32[144,256]{1,0:T(8,128)} %copy-done.10, f32[8,144,256]{2,1,0:T(8,128)} %get-tuple-element.70.r_5_), custom_call_target="tpu_custom_call" | custom-call | flops 17694720 | bytes 3833856 | tf_op jit(solution)/shard_map/pallas_call | solution.py:375
  110.4 2.8 %shard_map.104 = (f32[144,256]{1,0:T(8,128)}, f32[144,256]{1,0:T(8,128)}) custom-call(s32[3]{0:T(128)} %pad_add_fusion.r_0_, f32[2,128,128]{2,1,0:T(8,128)} %pad.16.r_2_.r_1_, f32[8,144,256]{2,1,0:T(8,128)} %shard_map.101.r_2_.r_3_, f32[8,144,256]{2,1,0:T(8,128)} %shard_map.101.r_2_.r_3_, f32[144,256]{1,0:T(8,128)} %get-tuple-element.72.r_3_.r_4_, ...), custom_call_target="tpu_custom_call" | custom-call | flops 5898240 | bytes 1769472 | tf_op jit(solution)/shard_map/pallas_call | solution.py:380
  114.5 4.6 %collective-permute-start.14 = (f32[144,256]{1,0:T(8,128)}, f32[144,256]{1,0:T(8,128)S(1)}, u32[]{:S(2)}, u32[]{:S(2)}) collective-permute-start(f32[144,256]{1,0:T(8,128)} %get-tuple-element.75.r_4_.r_5_), channel_id=1, source_target_pairs={{0,16},{1,17},{2,18},{3,19},{4,20},{5,21},{6,22},{7,23},{8,24},{9,... | collective-permute-start | bytes 442376 | tf_op jit(solution)/shard_map/ppermute | solution.py:373
  119.1 4.7 %shard_map.103.r_2_.r_3_ = f32[8,144,256]{2,1,0:T(8,128)} custom-call(s32[3]{0:T(128)} %pad_add_fusion.r_0_, f32[2,128,128]{2,1,0:T(8,128)} %pad.16.r_2_.r_1_, f32[8,144,256]{2,1,0:T(8,128)} %shard_map.101.r_2_.r_3_, f32[144,256]{1,0:T(8,128)} %get-tuple-element.72.r_3_.r_4_, f32[144,256]{1,0:T(8,128)} %get-tuple-element.73.r_4_.r_5_, ...), custom_call_target="tpu_custom_call" | custom-call | flops 17694720 | bytes 3833856 | tf_op jit(solution)/shard_map/pallas_call | solution.py:375
  125.0 2.8 %shard_map.106 = (f32[144,256]{1,0:T(8,128)}, f32[144,256]{1,0:T(8,128)}) custom-call(s32[3]{0:T(128)} %pad_add_fusion.r_0_, f32[2,128,128]{2,1,0:T(8,128)} %pad.16.r_2_.r_1_, f32[8,144,256]{2,1,0:T(8,128)} %shard_map.103.r_2_.r_3_, f32[8,144,256]{2,1,0:T(8,128)} %shard_map.103.r_2_.r_3_, f32[144,256]{1,0:T(8,128)} %get-tuple-element.74.r_3_.r_4_, ...), custom_call_target="tpu_custom_call" | custom-call | flops 5898240 | bytes 1769472 | tf_op jit(solution)/shard_map/pallas_call | solution.py:380
  129.1 4.8 %collective-permute-start.16 = (f32[144,256]{1,0:T(8,128)}, f32[144,256]{1,0:T(8,128)S(1)}, u32[]{:S(2)}, u32[]{:S(2)}) collective-permute-start(f32[144,256]{1,0:T(8,128)} %get-tuple-element.77.r_4_.r_5_), channel_id=1, source_target_pairs={{0,16},{1,17},{2,18},{3,19},{4,20},{5,21},{6,22},{7,23},{8,24},{9,... | collective-permute-start | bytes 442376 | tf_op jit(solution)/shard_map/ppermute | solution.py:373
  133.9 4.7 %shard_map.105.r_2_.r_3_ = f32[8,144,256]{2,1,0:T(8,128)} custom-call(s32[3]{0:T(128)} %pad_add_fusion.r_0_, f32[2,128,128]{2,1,0:T(8,128)} %pad.16.r_2_.r_1_, f32[8,144,256]{2,1,0:T(8,128)} %shard_map.103.r_2_.r_3_, f32[144,256]{1,0:T(8,128)} %get-tuple-element.74.r_3_.r_4_, f32[144,256]{1,0:T(8,128)} %get-tuple-element.75.r_4_.r_5_, ...), custom_call_target="tpu_custom_call" | custom-call | flops 17694720 | bytes 3833856 | tf_op jit(solution)/shard_map/pallas_call | solution.py:375
  138.6 3.7 %shard_map.107 = f32[8,128,128]{2,1,0:T(8,128)} custom-call(s32[3]{0:T(128)} %pad_add_fusion.r_0_, f32[2,128,128]{2,1,0:T(8,128)} %pad.16.r_2_.r_1_, f32[8,144,256]{2,1,0:T(8,128)} %shard_map.105.r_2_.r_3_, f32[144,256]{1,0:T(8,128)} %get-tuple-element.76.r_3_.r_4_, f32[144,256]{1,0:T(8,128)} %get-tuple-element.77.r_4_.r_5_, ...), custom_call_target="tpu_custom_call" | custom-call | flops 17694720 | bytes 3833856 | tf_op jit(solution)/shard_map/pallas_call | solution.py:375
  143.6 2.5 %shard_map.108 = f32[2,128,128]{2,1,0:T(8,128)} custom-call(s32[3]{0:T(128)} %pad_add_fusion.r_0_, f32[2,128,128]{2,1,0:T(8,128)} %pad.16.r_2_.r_1_, f32[8,144,256]{2,1,0:T(8,128)} %shard_map.105.r_2_.r_3_, f32[8,144,256]{2,1,0:T(8,128)} %shard_map.105.r_2_.r_3_, f32[144,256]{1,0:T(8,128)} %get-tuple-element.76.r_3_.r_4_, ...), custom_call_target="tpu_custom_call" | custom-call | flops 5898240 | bytes 1769472 | tf_op jit(solution)/shard_map/pallas_call | solution.py:380
  149.1 11.5 %collective-permute-done.18 = f32[8,128,128]{2,1,0:T(8,128)S(1)} collective-permute-done((f32[8,128,128]{2,1,0:T(8,128)S(1)}, f32[8,128,128]{2,1,0:T(8,128)S(1)}, u32[]{:S(2)}, u32[]{:S(2)}) %collective-permute-start.18) | collective-permute-done | bytes 524320 | tf_op jit(solution)/shard_map/ppermute | solution.py:248
  (115 shorter events, 41.8 us)
Async XLA Ops:
  3.9 5.6 %copy-start.4 = (f32[8,128,384]{2,1,0:T(8,128)S(1)}, f32[8,128,384]{2,1,0:T(8,128)}, u32[]{:S(2)}) copy-start(f32[8,128,384]{2,1,0:T(8,128)} %param.21) | copy-start | bytes 4718596
  3.9 9.0 %collective-permute-start.1 = (f32[26,8,128]{2,1,0:T(8,128)}, f32[26,8,128]{2,1,0:T(8,128)}, u32[]{:S(2)}, u32[]{:S(2)}) collective-permute-start(f32[26,8,128]{2,1,0:T(8,128)} %copy.12), channel_id=1, source_target_pairs={{0,1},{1,2},{2,3},{4,5},{5,6},{6,7},{8,9},{9,10},{10,11},{12,13},{... | collective-permute-start | bytes 319496 | tf_op jit(solution)/shard_map/ppermute | solution.py:297
  7.5 4.9 %collective-permute-start = (f32[26,8,128]{2,1,0:T(8,128)S(1)}, f32[26,8,128]{2,1,0:T(8,128)S(1)}, u32[]{:S(2)}, u32[]{:S(2)}) collective-permute-start(f32[26,8,128]{2,1,0:T(8,128)S(1)} %copy.10), channel_id=1, source_target_pairs={{1,0},{2,1},{3,2},{5,4},{6,5},{7,6},{9,8},{10,9},{11,10},{13,12},{... | collective-permute-start | bytes 319496 | tf_op jit(solution)/shard_map/ppermute | solution.py:298
  15.9 8.0 %copy-start.28 = (s32[2,64,64]{2,1,0:T(8,128)S(1)}, s32[2,64,64]{2,1,0:T(8,128)}, u32[]{:S(2)}) copy-start(s32[2,64,64]{2,1,0:T(8,128)} %param.20) | copy-start | bytes 98308
  15.9 8.7 %copy-start.29 = (s32[2]{0:T(128)S(1)}, s32[2]{0:T(128)}, u32[]{:S(2)}) copy-start(s32[2]{0:T(128)} %constant.191) | copy-start | bytes 28
  16.0 12.9 %copy-start.5 = (f32[8,128,8]{2,1,0:T(8,128)S(1)}, f32[8,128,8]{2,1,0:T(8,128)}, u32[]{:S(2)}) copy-start(f32[8,128,8]{2,1,0:T(8,128)} %pad_dynamic-slice_fusion) | copy-start | bytes 98308
  16.0 12.9 %copy-start.6 = (f32[8,128,128]{2,1,0:T(8,128)S(1)}, f32[8,128,128]{2,1,0:T(8,128)}, u32[]{:S(2)}) copy-start(f32[8,128,128]{2,1,0:T(8,128)} %param.17) | copy-start | bytes 1572868
  17.1 10.0 %collective-permute-start.2 = (f32[34,8,256]{2,1,0:T(8,128)S(1)}, f32[34,8,256]{2,1,0:T(8,128)S(1)}, u32[]{:S(2)}, u32[]{:S(2)}) collective-permute-start(f32[34,8,256]{2,1,0:T(8,128)S(1)} %get-tuple-element.78), channel_id=1, source_target_pairs={{4,0},{8,4},{12,8},{5,1},{9,5},{13,9},{6,2},{10,6},{14,10},{7,3},{... | collective-permute-start | bytes 835592 | tf_op jit(solution)/shard_map/ppermute | solution.py:313
  18.4 10.4 %collective-permute-start.3 = (f32[34,8,256]{2,1,0:T(8,128)S(1)}, f32[34,8,256]{2,1,0:T(8,128)S(1)}, u32[]{:S(2)}, u32[]{:S(2)}) collective-permute-start(f32[34,8,256]{2,1,0:T(8,128)S(1)} %get-tuple-element.79), channel_id=1, source_target_pairs={{0,4},{4,8},{8,12},{1,5},{5,9},{9,13},{2,6},{6,10},{10,14},{3,7},{... | collective-permute-start | bytes 835592 | tf_op jit(solution)/shard_map/ppermute | solution.py:312
  35.2 10.3 %copy-start = (f32[16,144,256]{2,1,0:T(8,128)}, f32[16,144,256]{2,1,0:T(8,128)S(1)}, u32[]{:S(2)}) copy-start(f32[16,144,256]{2,1,0:T(8,128)S(1)} %slice.165.r_3_.r_4_.r_5_.r_6_) | copy-start | bytes 7077892
  35.7 9.7 %copy-start.8 = (f32[2,144,256]{2,1,0:T(8,128)}, f32[2,144,256]{2,1,0:T(8,128)S(1)}, u32[]{:S(2)}) copy-start(f32[2,144,256]{2,1,0:T(8,128)S(1)} %gather_fusion.1) | copy-start | bytes 884740
  36.3 9.1 %copy-start.9 = (f32[2,144,256]{2,1,0:T(8,128)}, f32[2,144,256]{2,1,0:T(8,128)S(1)}, u32[]{:S(2)}) copy-start(f32[2,144,256]{2,1,0:T(8,128)S(1)} %gather_fusion) | copy-start | bytes 884740
  36.3 11.1 %collective-permute-start.5 = (f32[2,144,256]{2,1,0:T(8,128)S(1)}, f32[2,144,256]{2,1,0:T(8,128)S(1)}, u32[]{:S(2)}, u32[]{:S(2)}) collective-permute-start(f32[2,144,256]{2,1,0:T(8,128)S(1)} %gather_fusion), channel_id=1, source_target_pairs={{16,0},{17,1},{18,2},{19,3},{20,4},{21,5},{22,6},{23,7},{24,8},{25... | collective-permute-start | bytes 884744 | tf_op jit(solution)/shard_map/ppermute | solution.py:342
  37.6 11.6 %collective-permute-start.4 = (f32[2,144,256]{2,1,0:T(8,128)S(1)}, f32[2,144,256]{2,1,0:T(8,128)S(1)}, u32[]{:S(2)}, u32[]{:S(2)}) collective-permute-start(f32[2,144,256]{2,1,0:T(8,128)S(1)} %gather_fusion.1), channel_id=1, source_target_pairs={{0,16},{1,17},{2,18},{3,19},{4,20},{5,21},{6,22},{7,23},{8,24},{9,... | collective-permute-start | bytes 884744 | tf_op jit(solution)/shard_map/ppermute | solution.py:341
  53.1 11.5 %collective-permute-start.7 = (f32[2,144,256]{2,1,0:T(8,128)}, f32[2,144,256]{2,1,0:T(8,128)S(1)}, u32[]{:S(2)}, u32[]{:S(2)}) collective-permute-start(f32[2,144,256]{2,1,0:T(8,128)} %get-tuple-element.64.r_4_.r_7_), channel_id=1, source_target_pairs={{16,0},{17,1},{18,2},{19,3},{20,4},{21,5},{22,6},{23,7},{24,8},{25... | collective-permute-start | bytes 884744 | tf_op jit(solution)/shard_map/ppermute | solution.py:342
  54.4 11.5 %collective-permute-start.6 = (f32[2,144,256]{2,1,0:T(8,128)}, f32[2,144,256]{2,1,0:T(8,128)S(1)}, u32[]{:S(2)}, u32[]{:S(2)}) collective-permute-start(f32[2,144,256]{2,1,0:T(8,128)} %get-tuple-element.65.r_5_.r_8_), channel_id=1, source_target_pairs={{0,16},{1,17},{2,18},{3,19},{4,20},{5,21},{6,22},{7,23},{8,24},{9,... | collective-permute-start | bytes 884744 | tf_op jit(solution)/shard_map/ppermute | solution.py:341
  69.7 15.1 %collective-permute-start.9 = (f32[2,144,256]{2,1,0:T(8,128)}, f32[2,144,256]{2,1,0:T(8,128)S(1)}, u32[]{:S(2)}, u32[]{:S(2)}) collective-permute-start(f32[2,144,256]{2,1,0:T(8,128)} %get-tuple-element.66.r_4_.r_7_), channel_id=1, source_target_pairs={{16,0},{17,1},{18,2},{19,3},{20,4},{21,5},{22,6},{23,7},{24,8},{25... | collective-permute-start | bytes 884744 | tf_op jit(solution)/shard_map/ppermute | solution.py:342
  71.0 13.8 %collective-permute-start.8 = (f32[2,144,256]{2,1,0:T(8,128)}, f32[2,144,256]{2,1,0:T(8,128)S(1)}, u32[]{:S(2)}, u32[]{:S(2)}) collective-permute-start(f32[2,144,256]{2,1,0:T(8,128)} %get-tuple-element.67.r_5_.r_8_), channel_id=1, source_target_pairs={{0,16},{1,17},{2,18},{3,19},{4,20},{5,21},{6,22},{7,23},{8,24},{9,... | collective-permute-start | bytes 884744 | tf_op jit(solution)/shard_map/ppermute | solution.py:341
  76.6 8.2 %copy-start.10 = (f32[144,256]{1,0:T(8,128)}, f32[144,256]{1,0:T(8,128)S(1)}, u32[]{:S(2)}) copy-start(f32[144,256]{1,0:T(8,128)S(1)} %get-tuple-element.80.r_4_.r_5_) | copy-start | bytes 442372
  76.6 8.2 %copy-start.11 = (f32[144,256]{1,0:T(8,128)}, f32[144,256]{1,0:T(8,128)S(1)}, u32[]{:S(2)}) copy-start(f32[144,256]{1,0:T(8,128)S(1)} %get-tuple-element.81.r_3_.r_4_) | copy-start | bytes 442372
  76.6 12.9 %collective-permute-start.10 = (f32[144,256]{1,0:T(8,128)S(1)}, f32[144,256]{1,0:T(8,128)S(1)}, u32[]{:S(2)}, u32[]{:S(2)}) collective-permute-start(f32[144,256]{1,0:T(8,128)S(1)} %get-tuple-element.80.r_4_.r_5_), channel_id=1, source_target_pairs={{0,16},{1,17},{2,18},{3,19},{4,20},{5,21},{6,22},{7,23},{8,24},{9,... | collective-permute-start | bytes 442376 | tf_op jit(solution)/shard_map/ppermute | solution.py:373
  77.9 11.6 %collective-permute-start.11 = (f32[144,256]{1,0:T(8,128)S(1)}, f32[144,256]{1,0:T(8,128)S(1)}, u32[]{:S(2)}, u32[]{:S(2)}) collective-permute-start(f32[144,256]{1,0:T(8,128)S(1)} %get-tuple-element.81.r_3_.r_4_), channel_id=1, source_target_pairs={{16,0},{17,1},{18,2},{19,3},{20,4},{21,5},{22,6},{23,7},{24,8},{25... | collective-permute-start | bytes 442376 | tf_op jit(solution)/shard_map/ppermute | solution.py:374
  93.0 16.1 %collective-permute-start.13 = (f32[144,256]{1,0:T(8,128)}, f32[144,256]{1,0:T(8,128)S(1)}, u32[]{:S(2)}, u32[]{:S(2)}) collective-permute-start(f32[144,256]{1,0:T(8,128)} %get-tuple-element.72.r_3_.r_4_), channel_id=1, source_target_pairs={{16,0},{17,1},{18,2},{19,3},{20,4},{21,5},{22,6},{23,7},{24,8},{25... | collective-permute-start | bytes 442376 | tf_op jit(solution)/shard_map/ppermute | solution.py:374
  94.3 14.8 %collective-permute-start.12 = (f32[144,256]{1,0:T(8,128)}, f32[144,256]{1,0:T(8,128)S(1)}, u32[]{:S(2)}, u32[]{:S(2)}) collective-permute-start(f32[144,256]{1,0:T(8,128)} %get-tuple-element.73.r_4_.r_5_), channel_id=1, source_target_pairs={{0,16},{1,17},{2,18},{3,19},{4,20},{5,21},{6,22},{7,23},{8,24},{9,... | collective-permute-start | bytes 442376 | tf_op jit(solution)/shard_map/ppermute | solution.py:373
  113.2 10.5 %collective-permute-start.15 = (f32[144,256]{1,0:T(8,128)}, f32[144,256]{1,0:T(8,128)S(1)}, u32[]{:S(2)}, u32[]{:S(2)}) collective-permute-start(f32[144,256]{1,0:T(8,128)} %get-tuple-element.74.r_3_.r_4_), channel_id=1, source_target_pairs={{16,0},{17,1},{18,2},{19,3},{20,4},{21,5},{22,6},{23,7},{24,8},{25... | collective-permute-start | bytes 442376 | tf_op jit(solution)/shard_map/ppermute | solution.py:374
  114.5 9.2 %collective-permute-start.14 = (f32[144,256]{1,0:T(8,128)}, f32[144,256]{1,0:T(8,128)S(1)}, u32[]{:S(2)}, u32[]{:S(2)}) collective-permute-start(f32[144,256]{1,0:T(8,128)} %get-tuple-element.75.r_4_.r_5_), channel_id=1, source_target_pairs={{0,16},{1,17},{2,18},{3,19},{4,20},{5,21},{6,22},{7,23},{8,24},{9,... | collective-permute-start | bytes 442376 | tf_op jit(solution)/shard_map/ppermute | solution.py:373
  127.8 14.5 %collective-permute-start.17 = (f32[144,256]{1,0:T(8,128)}, f32[144,256]{1,0:T(8,128)S(1)}, u32[]{:S(2)}, u32[]{:S(2)}) collective-permute-start(f32[144,256]{1,0:T(8,128)} %get-tuple-element.76.r_3_.r_4_), channel_id=1, source_target_pairs={{16,0},{17,1},{18,2},{19,3},{20,4},{21,5},{22,6},{23,7},{24,8},{25... | collective-permute-start | bytes 442376 | tf_op jit(solution)/shard_map/ppermute | solution.py:374
  129.1 13.2 %collective-permute-start.16 = (f32[144,256]{1,0:T(8,128)}, f32[144,256]{1,0:T(8,128)S(1)}, u32[]{:S(2)}, u32[]{:S(2)}) collective-permute-start(f32[144,256]{1,0:T(8,128)} %get-tuple-element.77.r_4_.r_5_), channel_id=1, source_target_pairs={{0,16},{1,17},{2,18},{3,19},{4,20},{5,21},{6,22},{7,23},{8,24},{9,... | collective-permute-start | bytes 442376 | tf_op jit(solution)/shard_map/ppermute | solution.py:373
  142.3 3.8 %copy-start.7 = (f32[8,128,128]{2,1,0:T(8,128)S(1)}, f32[8,128,128]{2,1,0:T(8,128)}, u32[]{:S(2)}) copy-start(f32[8,128,128]{2,1,0:T(8,128)} %shard_map.107) | copy-start | bytes 1572868
  147.8 12.8 %collective-permute-start.18 = (f32[8,128,128]{2,1,0:T(8,128)S(1)}, f32[8,128,128]{2,1,0:T(8,128)S(1)}, u32[]{:S(2)}, u32[]{:S(2)}) collective-permute-start(f32[8,128,128]{2,1,0:T(8,128)S(1)} %slice_dynamic-update-slice_fusion.2), channel_id=1, source_target_pairs={{2,0},{3,1},{1,2},{6,4},{7,5},{5,6},{10,8},{11,9},{9,10},{14,12},{... | collective-permute-start | bytes 1572872 | tf_op jit(solution)/shard_map/ppermute | solution.py:248
  149.1 11.8 %copy-start.19 = (f32[2,2,128,128]{3,2,1,0:T(8,128)S(1)}, f32[2,2,128,128]{3,2,1,0:T(8,128)}, u32[]{:S(2)}) copy-start(f32[2,2,128,128]{3,2,1,0:T(8,128)} %get-tuple-element.69) | copy-start | bytes 786436
  160.8 2.7 %collective-permute-start.19 = (f32[2,8,128,128]{3,2,1,0:T(8,128)S(1)}, f32[2,8,128,128]{3,2,1,0:T(8,128)S(1)}, u32[]{:S(2)}, u32[]{:S(2)}) collective-permute-start(f32[2,8,128,128]{3,2,1,0:T(8,128)S(1)} %pad_maximum_fusion.3), channel_id=1, source_target_pairs={{0,1},{1,0},{2,3},{3,2},{4,5},{5,4},{6,7},{7,6},{8,9},{9,8},{10,11... | collective-permute-start | bytes 3145736 | tf_op jit(solution)/shard_map/ppermute | solution.py:251
  (18 other events, 18.1 us)

commit v6 on v4

v6 whole, which is shorter than its diff:
```python
import jax
import jax.numpy as jnp
from jax import lax
from jax.experimental import pallas as pl
from jax.experimental.pallas import tpu as pltpu
from jax.sharding import PartitionSpec as P

MB = 8
STEPS = 4


WEIGHTS = (0.8, 1.0, 1.25)
SHIFT = 0.2
HEATING = 0.02
CONDUCT = 0.16
SOFTEN = 0.25

H = MB


def _rolls(a):
    rows, lanes = a.shape
    return (
        pltpu.roll(a, rows - 1, 0), pltpu.roll(a, 1, 0),
        pltpu.roll(a, lanes - 1, 1), pltpu.roll(a, 1, 1),
    )


def _selectors(pos, rows, lanes, height, breadth, x_first_block):
    shift = MB.bit_length() - 1
    r = lax.shift_right_logical(lax.broadcasted_iota(jnp.int32, (rows, 128), 0), shift)
    b = lax.broadcasted_iota(jnp.int32, (rows, 128), 1)
    ty = pos[1] + jnp.where(r < (height + H) // MB, r, r - rows // MB)
    sy = (b == ty).astype(jnp.float32)
    l = lax.shift_right_logical(lax.broadcasted_iota(jnp.int32, (lanes, 128), 0), shift)
    bx = lax.broadcasted_iota(jnp.int32, (lanes, 128), 1)
    far = jnp.where(l >= (lanes - H) // MB, l - lanes // MB, -(10 ** 6))
    tx = pos[2] + jnp.where(l < (breadth + H) // MB, l, far)
    sx = ((bx == tx) & (bx >= x_first_block)).astype(jnp.float32)
    return sy, sx


def _cells(fl, zb, sy, sx):
    a = jnp.dot(sy, fl[zb], preferred_element_type=jnp.float32)
    return lax.dot_general(a, sx, (((1,), (1,)), ((), ())), preferred_element_type=jnp.float32)


def _inside(pos, rows, lanes, height, breadth, y_total, x_total):
    r = lax.broadcasted_iota(jnp.int32, (rows, lanes), 0)
    l = lax.broadcasted_iota(jnp.int32, (rows, lanes), 1)
    y = pos[1] * MB + jnp.where(r < height + H, r, r - rows)
    far = jnp.where(l >= lanes - H, l - lanes, -(10 ** 6))
    x = pos[2] * MB + jnp.where(l < breadth + H, l, far)
    return (y >= 0) & (y < y_total) & (x >= 0) & (x < x_total)


def _em_kernel(factor, last, depth, totals, pos, prof, fl, fa0, f0, fb0, fa1, f1, fb1, mat,
               w0, w1, zlo, zhi, *rest):
    diagonal = 6.0 + SHIFT
    if last:
        (heat, own, mask_s, keep_s) = rest
    else:
        (o0, o1, oz0, oz1, mask_s, keep_s) = rest
    height, breadth, y_total, x_total = totals
    rows, lanes = keep_s.shape
    z = pl.program_id(0)

    @pl.when(z == 0)
    def _():
        keep_s[...] = _inside(pos, rows, lanes, height, breadth, y_total, x_total).astype(
            jnp.float32)
        sy, sx = _selectors(pos, rows, lanes, height, breadth, 0)
        for zo in range(depth // MB):
            mask_s[zo] = _cells(fl, pos[0] + zo, sy, sx)

    planes = ((fa0, f0, fb0), (fa1, f1, fb1))
    cur = [planes[c][1][0] for c in range(2)]
    beside = []
    for c in range(2):
        z_up = jnp.where(z == depth - 1, zhi[c], planes[c][2][0])
        z_dn = jnp.where(z == 0, zlo[c], planes[c][0][0])
        y_up, y_dn, x_up, x_dn = _rolls(cur[c])
        total = z_up + z_dn
        total = total + y_up + y_dn
        beside.append(total + x_up + x_dn)
    k = mask_s[lax.shift_right_logical(z, MB.bit_length() - 1)] * mat[0]
    s0 = prof[z] * w0[0]
    s1 = prof[z] * w1[0]
    real_res = s0 - (diagonal * cur[0] - k * cur[1] - beside[0])
    imag_res = s1 - (diagonal * cur[1] + k * cur[0] - beside[1])
    scaled = factor / (diagonal * diagonal + k * k)
    keep = keep_s[...] > 0.0
    n0 = jnp.where(keep, cur[0] + scaled * (diagonal * real_res + k * imag_res), 0.0)
    n1 = jnp.where(keep, cur[1] + scaled * (diagonal * imag_res - k * real_res), 0.0)
    if last:
        heat[0] = HEATING * k * (n0 * n0 + n1 * n1)
        own[0, 0] = n0[0:height, 0:breadth]
        own[1, 0] = n1[0:height, 0:breadth]
    else:
        o0[0] = n0
        o1[0] = n1

        @pl.when(z == 0)
        def _():
            oz0[0] = n0
            oz0[1] = n1

        @pl.when(z == depth - 1)
        def _():
            oz1[0] = n0
            oz1[1] = n1


def _heat_kernel(last, depth, totals, pos, fl, ta, t, tb, q, tzlo, tzhi, *rest):
    if last:
        (own, mask_s) = rest
    else:
        (o, oz0, oz1, mask_s) = rest
    height, breadth, x_first_block = totals
    rows, lanes = tzlo.shape
    z = pl.program_id(0)
    shift = MB.bit_length() - 1

    @pl.when(z == 0)
    def _():
        sy, sx = _selectors(pos, rows, lanes, height, breadth, x_first_block)
        zb_total = fl.shape[0]
        for j in range(depth // MB + 2):
            zb = pos[0] + j - 1
            ok = jnp.where((zb >= 0) & (zb < zb_total), 1.0, 0.0)
            mask_s[j] = _cells(fl, jnp.clip(zb, 0, zb_total - 1), sy, sx) * ok

    c = t[0]
    up = jnp.where(z == depth - 1, tzhi[...], tb[0])
    dn = jnp.where(z == 0, tzlo[...], ta[0])
    centre_kappa = 1.0 / (1.0 + SOFTEN * c * c)
    y_up, y_dn, x_up, x_dn = _rolls(c)
    ky_up, ky_dn, kx_up, kx_dn = _rolls(centre_kappa)
    mc = mask_s[lax.shift_right_logical(z + MB, shift)]
    my_up, my_dn, mx_up, mx_dn = _rolls(mc)
    flux = jnp.zeros_like(c)
    for other, kappa, other_mask in (
        (up, 1.0 / (1.0 + SOFTEN * up * up), mask_s[lax.shift_right_logical(z + 1 + MB, shift)]),
        (dn, 1.0 / (1.0 + SOFTEN * dn * dn), mask_s[lax.shift_right_logical(z - 1 + MB, shift)]),
        (y_up, ky_up, my_up), (y_dn, ky_dn, my_dn), (x_up, kx_up, mx_up), (x_dn, kx_dn, mx_dn),
    ):
        flux = flux + other_mask * (centre_kappa + kappa) * (other - c)
    new = c + 0.5 * CONDUCT * mc * flux + q[0]
    if last:
        own[0] = new[0:height, 0:breadth]
    else:
        o[0] = new

        @pl.when(z == 0)
        def _():
            oz0[...] = new

        @pl.when(z == depth - 1)
        def _():
            oz1[...] = new


def _plane_specs(base, depth, rows, lanes):
    def at(d):
        return pl.BlockSpec(
            (1, rows, lanes), lambda z: (base + jnp.clip(z + d, 0, depth - 1), 0, 0))
    return [at(-1), at(0), at(1)]


def _fixed(shape, idx=None):
    n = len(shape)
    if idx is None:
        return pl.BlockSpec(shape, lambda z: (0,) * n)
    return pl.BlockSpec(shape, lambda z: (idx,) + (0,) * (n - 1))


def _line_pairs(n, first=0):
    up = [(i, i + 1) for i in range(first, n - 1)]
    down = [(j, i) for i, j in up]
    return up, down


def _broadcast_blocks(own, me, n, first):
    if (n, first) == (4, 1):
        r1 = lax.ppermute(own, "gx", [(2, 0), (3, 1), (1, 2)])
        a = jnp.where((me == 0) | (me == 2), r1, own)
        b = jnp.where((me == 1) | (me == 0), r1, own)
        r2 = lax.ppermute(jnp.stack([a, b]), "gx", [(0, 1), (1, 0), (2, 3), (3, 2)])
        b1 = jnp.where(me == 1, own, jnp.where(me == 2, r1, r2[0]))
        b2 = jnp.where(me == 0, r1, jnp.where(me == 1, r2[0], jnp.where(me == 2, own, r2[1])))
        b3 = jnp.where(me == 0, r2[1], jnp.where(me == 1, r1, jnp.where(me == 2, r2[0], own)))
        return jnp.concatenate([b1, b2, b3], axis=2)
    owners = list(range(first, n))
    held = [own]
    for s in range(1, n):
        held.append(lax.ppermute(own, "gx", [(k, (k + s) % n) for k in owners]))
    held = jnp.stack(held)
    pieces = [lax.dynamic_index_in_dim(held, (me - k) % n, 0, keepdims=False) for k in owners]
    return jnp.concatenate(pieces, axis=2)


def on_device(
    earlier_window_curl_state,
    material_resistivity_inverse,
    winding_current_pattern,
    winding_axial_centre,
    specimen_presence_flags,
    specimen_kelvin_values,
):
    depth, height, breadth = material_resistivity_inverse.shape
    n_gz, n_gy, n_gx = lax.axis_size("gz"), lax.axis_size("gy"), lax.axis_size("gx")
    z_total, y_total, x_total = depth * n_gz, height * n_gy, breadth * n_gx
    gz_i, gy_i, gx_i = lax.axis_index("gz"), lax.axis_index("gy"), lax.axis_index("gx")
    z_start, y_start, x_start = gz_i * depth, gy_i * height, gx_i * breadth
    rows = height + 2 * H
    lanes = -(-(breadth + 2 * H) // 128) * 128
    gap = lanes - breadth - 2 * H
    specimen_columns = specimen_kelvin_values.shape[2]
    offset = x_total - specimen_columns
    assert offset % breadth == 0 and depth % MB == 0 and height % MB == 0 and breadth % MB == 0
    first_owner = offset // breadth

    coil_width = z_total // 4
    axial = (
        (z_start + jnp.arange(depth)).astype(jnp.float32)
        - winding_axial_centre[0].astype(jnp.float32)
    ) / coil_width
    profile = 1.0 / (1.0 + axial * axial)

    stack = jnp.concatenate(
        [earlier_window_curl_state.reshape(2 * depth, height, breadth), material_resistivity_inverse,
         winding_current_pattern], axis=0)
    up_x, down_x = _line_pairs(n_gx)
    from_left = lax.ppermute(jnp.swapaxes(stack[:, :, breadth - H:], 1, 2), "gx", up_x)
    from_right = lax.ppermute(jnp.swapaxes(stack[:, :, :H], 1, 2), "gx", down_x)
    nch = stack.shape[0]
    xext = jnp.concatenate(
        [stack, jnp.swapaxes(from_right, 1, 2), jnp.zeros((nch, height, gap), jnp.float32),
         jnp.swapaxes(from_left, 1, 2)], axis=2)

    j_start = x_start - offset
    kpad = jnp.pad(specimen_kelvin_values, ((0, 0), (0, 0), (H, H)))
    t_body = lax.dynamic_slice_in_dim(kpad, j_start + H, breadth + H, 2)
    t_tail = lax.dynamic_slice_in_dim(kpad, j_start, H, 2)
    t_x = jnp.concatenate([t_body, jnp.zeros((depth, height, gap), jnp.float32), t_tail], axis=2)

    ystack = jnp.concatenate([xext, t_x], axis=0)
    up_y, down_y = _line_pairs(n_gy)
    from_above = lax.ppermute(ystack[:, height - H:, :], "gy", up_y)
    from_below = lax.ppermute(ystack[:, :H, :], "gy", down_y)
    frame = jnp.concatenate([ystack, from_below, from_above], axis=1)

    fb = specimen_presence_flags.shape
    flags = jnp.pad(specimen_presence_flags.astype(jnp.float32),
                    ((0, 0), (0, 128 - fb[1]), (0, 128 - fb[2])))
    pos = jnp.stack([z_start // MB, y_start // MB, x_start // MB]).astype(jnp.int32)

    up_z, down_z = _line_pairs(n_gz)
    f32 = jnp.float32
    smem = pl.BlockSpec(memory_space=pltpu.SMEM)
    plane = jax.ShapeDtypeStruct((depth, rows, lanes), f32)
    plane2 = jax.ShapeDtypeStruct((2, rows, lanes), f32)
    oshape = jax.ShapeDtypeStruct((2, depth, height, breadth), f32)
    at_z = pl.BlockSpec((1, rows, lanes), lambda z: (z, 0, 0))
    fl_spec = _fixed(flags.shape)
    em_totals = (height, breadth, y_total, x_total)
    arrays = (frame, frame)
    bases = (0, depth)
    lo_plane = frame[jnp.array([0, depth])]
    hi_plane = frame[jnp.array([depth - 1, 2 * depth - 1])]
    for i, factor in enumerate(WEIGHTS):
        last = i == len(WEIGHTS) - 1
        zlo = lax.ppermute(hi_plane, "gz", up_z)
        zhi = lax.ppermute(lo_plane, "gz", down_z)
        if last:
            outs = (plane, oshape)
            out_specs = [at_z, pl.BlockSpec((2, 1, height, breadth), lambda z: (0, z, 0, 0))]
        else:
            outs = (plane, plane, plane2, plane2)
            out_specs = [at_z, at_z, _fixed((2, rows, lanes)), _fixed((2, rows, lanes))]
        in_specs = ([smem, smem, fl_spec] + _plane_specs(bases[0], depth, rows, lanes)
                    + _plane_specs(bases[1], depth, rows, lanes)
                    + [pl.BlockSpec((1, rows, lanes), lambda z: (2 * depth + z, 0, 0)),
                       _fixed((1, rows, lanes), 3 * depth), _fixed((1, rows, lanes), 3 * depth + 1),
                       _fixed((2, rows, lanes)), _fixed((2, rows, lanes))])
        res = pl.pallas_call(
            lambda *r, factor=factor, last=last: _em_kernel(factor, last, depth, em_totals, *r),
            out_shape=outs,
            grid=(depth,),
            in_specs=in_specs,
            out_specs=out_specs,
            scratch_shapes=[pltpu.VMEM((depth // MB, rows, lanes), f32),
                            pltpu.VMEM((rows, lanes), f32)],
        )(pos, profile, flags, arrays[0], arrays[0], arrays[0], arrays[1], arrays[1], arrays[1],
          frame, frame, frame, zlo, zhi)
        if last:
            heat, field_out = res
        else:
            f0, f1, lo_plane, hi_plane = res
            arrays, bases = (f0, f1), (0, 0)

    tplane = jax.ShapeDtypeStruct((rows, lanes), f32)
    town = jax.ShapeDtypeStruct((depth, height, breadth), f32)
    t_totals = (height, breadth, offset // MB)
    kelvin, t_base = frame, 3 * depth + 2
    lo_t, hi_t = frame[t_base], frame[t_base + depth - 1]
    for number in range(STEPS):
        last = number == STEPS - 1
        tzlo = lax.ppermute(hi_t, "gz", up_z)
        tzhi = lax.ppermute(lo_t, "gz", down_z)
        if last:
            outs = (town,)
            out_specs = [pl.BlockSpec((1, height, breadth), lambda z: (z, 0, 0))]
        else:
            outs = (plane, tplane, tplane)
            out_specs = [at_z, _fixed((rows, lanes)), _fixed((rows, lanes))]
        res = pl.pallas_call(
            lambda *r, last=last: _heat_kernel(last, depth, t_totals, *r),
            out_shape=outs,
            grid=(depth,),
            in_specs=[smem, fl_spec] + _plane_specs(t_base, depth, rows, lanes)
            + [at_z, _fixed((rows, lanes)), _fixed((rows, lanes))],
            out_specs=out_specs,
            scratch_shapes=[pltpu.VMEM((depth // MB + 2, rows, lanes), f32)],
        )(pos, flags, kelvin, kelvin, kelvin, heat, tzlo, tzhi)
        if last:
            (own_t,) = res
        else:
            kelvin, lo_t, hi_t = res
            t_base = 0

    segment_kelvin = _broadcast_blocks(own_t, gx_i, n_gx, first_owner)
    return (field_out, segment_kelvin)


def solution(mesh):
    placed = (
        P(None, "gz", "gy", "gx"),
        P("gz", "gy", "gx"),
        P(None, "gy", "gx"),
        P(),
        P(),
        P("gz", "gy", None),
    )
    return jax.shard_map(
        on_device,
        mesh=mesh,
        in_specs=placed,
        out_specs=(P(None, "gz", "gy", "gx"), P("gz", "gy", None)),
        check_vma=False,
    )
```

time: 164 us -> 191 us (1.16)
  Pallas kernels: 38.1 us -> 61.2 us
  starting transfers between devices: 37.9 us -> 43.9 us
  waiting for transfers between devices: 54.1 us -> 49.2 us
    pallas_call x7, Pallas kernels: 38.1 us -> 61.2 us  [the longest x4 34 us: on_device(): pl.pallas_call(lambda *r, last=last: _heat_kernel(last, depth, t_totals,...]
    ppermute x3, waiting for transfers between devices: 11.3 us -> 5.42 us  [on_device(): zhi = lax.ppermute(lo_plane, 'gz', down_z)]
    gather x2, local copies, waits for them, and re-layouts: 1.14 us -> 5.97 us  [the longest x1 2.99 us: on_device(): hi_plane = frame[jnp.array([depth - 1, 2 * depth - 1])]]
    slice x3 -> x0, local copies, waits for them, and re-layouts: 4.17 us -> none  [the longest x1 3.24 us: on_device(): kelvin = frame[3 * depth + 2:]]
    ppermute x3, starting transfers between devices: 7.36 us -> 10.6 us  [on_device(): zlo = lax.ppermute(hi_plane, 'gz', up_z)]
    ppermute x1, waiting for transfers between devices: 2.44 us -> 5.5 us  [on_device(): from_below = lax.ppermute(ystack[:, :H, :], 'gy', down_y)]
    unnamed x50 -> x44, local copies, waits for them, and re-layouts: 7.72 us -> 6.13 us
  transfers between devices with their start and end apart: 20 -> 20, of which waited for: 15 -> 14; matrix products, arithmetic and copies ran while one was open for 6% -> 6% of each run, Pallas kernels for 4% -> 5%
where the time goes in v6:
time: 191 us; the launch traced here: 189 us
  Pallas kernels  61.2 us (32%)
  waiting for transfers between devices  49.2 us (26%)
  starting transfers between devices  43.9 us (23%)
  local copies, waits for them, and re-layouts  20.4 us (11%)
  other arithmetic  12.4 us (6%)
    pallas_call x4, Pallas kernels, on_device(): pl.pallas_call(lambda *r, last=last: _heat_kernel(last, depth, t_totals,...  34 us
    pallas_call x3, Pallas kernels, on_device(): pl.pallas_call(lambda *r, factor=factor, last=last: _em_kernel(factor, la...  27.2 us
    ppermute x4, waiting for transfers between devices, on_device(): tzhi = lax.ppermute(lo_t, 'gz', down_z)  12.8 us
    ppermute x4, starting transfers between devices, on_device(): tzlo = lax.ppermute(hi_t, 'gz', up_z)  11 us
    ppermute x3, starting transfers between devices, on_device(): zlo = lax.ppermute(hi_plane, 'gz', up_z)  10.6 us
    ppermute x1, waiting for transfers between devices, _broadcast_blocks(): r1 = lax.ppermute(own, 'gx', [(2, 0), (3, 1), (1, 2)])  9.96 us
    ppermute x3, waiting for transfers between devices, on_device(): zlo = lax.ppermute(hi_plane, 'gz', up_z)  6.64 us
    unnamed x44, local copies, waits for them, and re-layouts  6.13 us
  transfers between devices with their start and end apart: 20, of which 14 were waited for; matrix products, arithmetic and copies ran while one was open for 6% of the time, Pallas kernels for 5%

profile of v6, /device:TPU:0, one launch (start us, length us, event | category | flops | bytes accessed | tf_op | source)
XLA Modules:
  0.0 188.8 jit_solution(2633709184315827295)
XLA Ops:
  0.6 1.6 pad_maximum_fusion.1
  5.8 3.7 %collective-permute-start.1 = (f32[26,8,128]{2,1,0:T(8,128)}, f32[26,8,128]{2,1,0:T(8,128)}, u32[]{:S(2)}, u32[]{:S(2)}) collective-permute-start(f32[26,8,128]{2,1,0:T(8,128)} %copy.12), channel_id=1, source_target_pairs={{0,1},{1,2},{2,3},{4,5},{5,6},{6,7},{8,9},{9,10},{10,11},{12,13},{... | collective-permute-start | bytes 319496 | tf_op jit(solution)/shard_map/ppermute | solution.py:234
  17.7 5.6 %collective-permute-start.3 = (f32[34,8,256]{2,1,0:T(8,128)S(1)}, f32[34,8,256]{2,1,0:T(8,128)S(1)}, u32[]{:S(2)}, u32[]{:S(2)}) collective-permute-start(f32[34,8,256]{2,1,0:T(8,128)S(1)} %get-tuple-element.41), channel_id=1, source_target_pairs={{0,4},{4,8},{8,12},{1,5},{5,9},{9,13},{2,6},{6,10},{10,14},{3,7},{... | collective-permute-start | bytes 835592 | tf_op jit(solution)/shard_map/ppermute | solution.py:249
  23.4 5.5 %collective-permute-done.2 = f32[34,8,256]{2,1,0:T(8,128)S(1)} collective-permute-done((f32[34,8,256]{2,1,0:T(8,128)S(1)}, f32[34,8,256]{2,1,0:T(8,128)S(1)}, u32[]{:S(2)}, u32[]{:S(2)}) %collective-permute-start.2) | collective-permute-done | bytes 278560 | tf_op jit(solution)/shard_map/ppermute | solution.py:250
  30.1 5.0 %pad_maximum_fusion.r_3_.r_4_.r_5_.r_6_.r_7_.r_8_.r_9_.r_10_.r_11_.r_2_ = f32[34,144,256]{2,1,0:T(8,128)} fusion(f32[34,8,256]{2,1,0:T(8,128)S(1)} %collective-permute-done.3, f32[34,8,256]{2,1,0:T(8,128)S(1)} %collective-permute-done.2, f32[8,128,8]{2,1,0:T(8,128)S(1)} %copy-done.3, f32[8,128,112]{2,1,0:T(8,128)S(1)} %broadcast_in_dim.13, ...), kind=kLoop, calls=%fused_computation.2 | loop fusion | flops 12533760 | bytes 10027008 | tf_op jit(solution)/shard_map/concatenate | solution.py:251
  35.0 3.0 %gather_fusion.1 = f32[2,144,256]{2,1,0:T(8,128)S(1)} fusion(f32[34,144,256]{2,1,0:T(8,128)} %pad_maximum_fusion.r_3_.r_4_.r_5_.r_6_.r_7_.r_8_.r_9_.r_10_.r_11_.r_2_, s32[1024]{0:T(1024)S(1)} %pad_clamp_fusion), kind=kCustom, calls=%fused_computation.1 | custom fusion | bytes 589832 | tf_op jit(solution)/shard_map/gather | solution.py:269
  39.3 3.0 %gather_fusion = f32[2,144,256]{2,1,0:T(8,128)S(1)} fusion(f32[34,144,256]{2,1,0:T(8,128)} %pad_maximum_fusion.r_3_.r_4_.r_5_.r_6_.r_7_.r_8_.r_9_.r_10_.r_11_.r_2_, s32[1024]{0:T(1024)S(1)} %pad_clamp_fusion.1), kind=kCustom, calls=%fused_computation | custom fusion | bytes 589832 | tf_op jit(solution)/shard_map/gather | solution.py:270
  42.3 4.6 %collective-permute-start.4 = (f32[2,144,256]{2,1,0:T(8,128)S(1)}, f32[2,144,256]{2,1,0:T(8,128)S(1)}, u32[]{:S(2)}, u32[]{:S(2)}) collective-permute-start(f32[2,144,256]{2,1,0:T(8,128)S(1)} %gather_fusion), channel_id=1, source_target_pairs={{0,16},{1,17},{2,18},{3,19},{4,20},{5,21},{6,22},{7,23},{8,24},{9,... | collective-permute-start | bytes 884744 | tf_op jit(solution)/shard_map/ppermute | solution.py:273
  50.3 2.6 %collective-permute-done.4.r_12_ = f32[2,144,256]{2,1,0:T(8,128)S(1)} collective-permute-done((f32[2,144,256]{2,1,0:T(8,128)S(1)}, f32[2,144,256]{2,1,0:T(8,128)S(1)}, u32[]{:S(2)}, u32[]{:S(2)}) %collective-permute-start.4) | collective-permute-done | bytes 294944 | tf_op jit(solution)/shard_map/ppermute | solution.py:273
  53.6 9.1 %shard_map.95 = (f32[8,144,256]{2,1,0:T(8,128)}, f32[8,144,256]{2,1,0:T(8,128)}, f32[2,144,256]{2,1,0:T(8,128)}, f32[2,144,256]{2,1,0:T(8,128)}) custom-call(s32[3]{0:T(128)} %pad_add_fusion.r_0_, f32[8]{0:T(128)} %add_divide_fusion.r_1_, f32[2,128,128]{2,1,0:T(8,128)} %pad.8.r_2_.r_1_, ...), custom_call_target="tpu_custom_call" | custom-call | tf_op jit(solution)/shard_map/pallas_call | solution.py:286
  62.7 4.4 %collective-permute-start.6 = (f32[2,144,256]{2,1,0:T(8,128)}, f32[2,144,256]{2,1,0:T(8,128)S(1)}, u32[]{:S(2)}, u32[]{:S(2)}) collective-permute-start(f32[2,144,256]{2,1,0:T(8,128)} %get-tuple-element.23), channel_id=1, source_target_pairs={{0,16},{1,17},{2,18},{3,19},{4,20},{5,21},{6,22},{7,23},{8,24},{9,... | collective-permute-start | bytes 884744 | tf_op jit(solution)/shard_map/ppermute | solution.py:273
  68.4 4.1 %collective-permute-done.6.r_12_ = f32[2,144,256]{2,1,0:T(8,128)S(1)} collective-permute-done((f32[2,144,256]{2,1,0:T(8,128)}, f32[2,144,256]{2,1,0:T(8,128)S(1)}, u32[]{:S(2)}, u32[]{:S(2)}) %collective-permute-start.6) | collective-permute-done | bytes 294944 | tf_op jit(solution)/shard_map/ppermute | solution.py:273
  72.4 4.0 %collective-permute-done.7.r_13_ = f32[2,144,256]{2,1,0:T(8,128)S(1)} collective-permute-done((f32[2,144,256]{2,1,0:T(8,128)}, f32[2,144,256]{2,1,0:T(8,128)S(1)}, u32[]{:S(2)}, u32[]{:S(2)}) %collective-permute-start.7) | collective-permute-done | bytes 294944 | tf_op jit(solution)/shard_map/ppermute | solution.py:274
  77.2 9.2 %shard_map.96 = (f32[8,144,256]{2,1,0:T(8,128)}, f32[8,144,256]{2,1,0:T(8,128)}, f32[2,144,256]{2,1,0:T(8,128)}, f32[2,144,256]{2,1,0:T(8,128)}) custom-call(s32[3]{0:T(128)} %pad_add_fusion.r_0_, f32[8]{0:T(128)} %add_divide_fusion.r_1_, f32[2,128,128]{2,1,0:T(8,128)} %pad.8.r_2_.r_1_, f32[8,144,256]{2,1,0:T(8,128)} %get-tuple-element.21.r_3_.r_4_.r_5_, ...), custom_call_target="tpu_custom_call" | custom-call | tf_op jit(solution)/shard_map/pallas_call | solution.py:286
  86.4 1.6 collective-permute-start.8
  90.3 4.6 %collective-permute-start.10 = (f32[144,256]{1,0:T(8,128)S(1)}, f32[144,256]{1,0:T(8,128)S(1)}, u32[]{:S(2)}, u32[]{:S(2)}) collective-permute-start(f32[144,256]{1,0:T(8,128)S(1)} %get-tuple-element.43), channel_id=1, source_target_pairs={{0,16},{1,17},{2,18},{3,19},{4,20},{5,21},{6,22},{7,23},{8,24},{9,... | collective-permute-start | bytes 442376 | tf_op jit(solution)/shard_map/ppermute | solution.py:309
  98.2 9.0 %shard_map.97 = (f32[8,144,256]{2,1,0:T(8,128)}, f32[2,8,128,128]{3,2,1,0:T(8,128)}) custom-call(s32[3]{0:T(128)} %pad_add_fusion.r_0_, f32[8]{0:T(128)} %add_divide_fusion.r_1_, f32[2,128,128]{2,1,0:T(8,128)} %pad.8.r_2_.r_1_, f32[8,144,256]{2,1,0:T(8,128)} %get-tuple-element.25.r_3_.r_4_.r_5_, f32[8,144,256]{2,1,0:T(8,128)} %get-tuple-element.25.r_3_.r_4_.r_5_, ...), custom_call_target="tpu_custom_call" | custom-call | tf_op jit(solution)/shard_map/pallas_call | solution.py:286
  108.0 8.8 %shard_map.98 = (f32[8,144,256]{2,1,0:T(8,128)}, f32[144,256]{1,0:T(8,128)}, f32[144,256]{1,0:T(8,128)}) custom-call(s32[3]{0:T(128)} %pad_add_fusion.r_0_, f32[2,128,128]{2,1,0:T(8,128)} %pad.8.r_2_.r_1_, f32[34,144,256]{2,1,0:T(8,128)} %pad_maximum_fusion.r_3_.r_4_.r_5_.r_6_.r_7_.r_8_.r_9_.r_10_.r_11_.r_2_, ...), custom_call_target="tpu_custom_call" | custom-call | tf_op jit(solution)/shard_map/pallas_call | solution.py:317
  116.7 3.3 %collective-permute-start.12 = (f32[144,256]{1,0:T(8,128)}, f32[144,256]{1,0:T(8,128)S(1)}, u32[]{:S(2)}, u32[]{:S(2)}) collective-permute-start(f32[144,256]{1,0:T(8,128)} %get-tuple-element.32), channel_id=1, source_target_pairs={{0,16},{1,17},{2,18},{3,19},{4,20},{5,21},{6,22},{7,23},{8,24},{9,... | collective-permute-start | bytes 442376 | tf_op jit(solution)/shard_map/ppermute | solution.py:309
  121.3 1.7 collective-permute-done.12.r_6_
  123.0 4.3 %collective-permute-done.13.r_7_ = f32[144,256]{1,0:T(8,128)S(1)} collective-permute-done((f32[144,256]{1,0:T(8,128)}, f32[144,256]{1,0:T(8,128)S(1)}, u32[]{:S(2)}, u32[]{:S(2)}) %collective-permute-start.13) | collective-permute-done | bytes 147488 | tf_op jit(solution)/shard_map/ppermute | solution.py:310
  127.9 8.8 %shard_map.99 = (f32[8,144,256]{2,1,0:T(8,128)}, f32[144,256]{1,0:T(8,128)}, f32[144,256]{1,0:T(8,128)}) custom-call(s32[3]{0:T(128)} %pad_add_fusion.r_0_, f32[2,128,128]{2,1,0:T(8,128)} %pad.8.r_2_.r_1_, f32[8,144,256]{2,1,0:T(8,128)} %get-tuple-element.31.r_2_.r_3_.r_4_, f32[8,144,256]{2,1,0:T(8,128)} %get-tuple-element.31.r_2_.r_3_.r_4_, ...), custom_call_target="tpu_custom_call" | custom-call | tf_op jit(solution)/shard_map/pallas_call | solution.py:317
  136.7 1.6 collective-permute-start.14
  139.6 1.7 collective-permute-done.14.r_6_
  141.2 4.3 %collective-permute-done.15.r_7_ = f32[144,256]{1,0:T(8,128)S(1)} collective-permute-done((f32[144,256]{1,0:T(8,128)}, f32[144,256]{1,0:T(8,128)S(1)}, u32[]{:S(2)}, u32[]{:S(2)}) %collective-permute-start.15) | collective-permute-done | bytes 147488 | tf_op jit(solution)/shard_map/ppermute | solution.py:310
  146.2 8.8 %shard_map.100 = (f32[8,144,256]{2,1,0:T(8,128)}, f32[144,256]{1,0:T(8,128)}, f32[144,256]{1,0:T(8,128)}) custom-call(s32[3]{0:T(128)} %pad_add_fusion.r_0_, f32[2,128,128]{2,1,0:T(8,128)} %pad.8.r_2_.r_1_, f32[8,144,256]{2,1,0:T(8,128)} %get-tuple-element.34.r_2_.r_3_.r_4_, f32[8,144,256]{2,1,0:T(8,128)} %get-tuple-element.34.r_2_.r_3_.r_4_, ...), custom_call_target="tpu_custom_call" | custom-call | tf_op jit(solution)/shard_map/pallas_call | solution.py:317
  155.0 1.6 collective-permute-start.16
  157.8 1.7 collective-permute-done.16.r_6_
  159.5 4.3 %collective-permute-done.17.r_7_ = f32[144,256]{1,0:T(8,128)S(1)} collective-permute-done((f32[144,256]{1,0:T(8,128)}, f32[144,256]{1,0:T(8,128)S(1)}, u32[]{:S(2)}, u32[]{:S(2)}) %collective-permute-start.17) | collective-permute-done | bytes 147488 | tf_op jit(solution)/shard_map/ppermute | solution.py:310
  164.5 7.6 %shard_map.101 = f32[8,128,128]{2,1,0:T(8,128)} custom-call(s32[3]{0:T(128)} %pad_add_fusion.r_0_, f32[2,128,128]{2,1,0:T(8,128)} %pad.8.r_2_.r_1_, f32[8,144,256]{2,1,0:T(8,128)} %get-tuple-element.37.r_2_.r_3_.r_4_, f32[8,144,256]{2,1,0:T(8,128)} %get-tuple-element.37.r_2_.r_3_.r_4_, f32[8,144,256]{2,1,0:T(8,128)} %get-tuple-element.37.r_2_.r_3_.r_4_, ...), custom_call_target="tpu_custom_call" | custom-call | tf_op jit(solution)/shard_map/pallas_call | solution.py:317
  173.4 10.0 %collective-permute-done.18 = f32[8,128,128]{2,1,0:T(8,128)S(1)} collective-permute-done((f32[8,128,128]{2,1,0:T(8,128)}, f32[8,128,128]{2,1,0:T(8,128)S(1)}, u32[]{:S(2)}, u32[]{:S(2)}) %collective-permute-start.18) | collective-permute-done | bytes 524320 | tf_op jit(solution)/shard_map/ppermute | solution.py:185
  184.7 2.6 %collective-permute-done.19 = f32[2,8,128,128]{3,2,1,0:T(8,128)S(1)} collective-permute-done((f32[2,8,128,128]{3,2,1,0:T(8,128)S(1)}, f32[2,8,128,128]{3,2,1,0:T(8,128)S(1)}, u32[]{:S(2)}, u32[]{:S(2)}) %collective-permute-start.19) | collective-permute-done | bytes 1048608 | tf_op jit(solution)/shard_map/ppermute | solution.py:188
  (85 shorter events, 35.9 us)
Async XLA Ops:
  3.3 6.2 %copy-start.2 = (f32[8,128,384]{2,1,0:T(8,128)S(1)}, f32[8,128,384]{2,1,0:T(8,128)}, u32[]{:S(2)}) copy-start(f32[8,128,384]{2,1,0:T(8,128)} %param.13) | copy-start | bytes 4718596
  3.3 8.5 %collective-permute-start = (f32[26,8,128]{2,1,0:T(8,128)S(1)}, f32[26,8,128]{2,1,0:T(8,128)S(1)}, u32[]{:S(2)}, u32[]{:S(2)}) collective-permute-start(f32[26,8,128]{2,1,0:T(8,128)S(1)} %copy.10), channel_id=1, source_target_pairs={{1,0},{2,1},{3,2},{5,4},{6,5},{7,6},{9,8},{10,9},{11,10},{13,12},{... | collective-permute-start | bytes 319496 | tf_op jit(solution)/shard_map/ppermute | solution.py:235
  5.8 6.5 %collective-permute-start.1 = (f32[26,8,128]{2,1,0:T(8,128)}, f32[26,8,128]{2,1,0:T(8,128)}, u32[]{:S(2)}, u32[]{:S(2)}) collective-permute-start(f32[26,8,128]{2,1,0:T(8,128)} %copy.12), channel_id=1, source_target_pairs={{0,1},{1,2},{2,3},{4,5},{5,6},{6,7},{8,9},{9,10},{10,11},{12,13},{... | collective-permute-start | bytes 319496 | tf_op jit(solution)/shard_map/ppermute | solution.py:234
  12.3 1.7 copy-start.6
  13.8 1.5 copy-start.1
  15.3 8.0 %copy-start.21 = (s32[2]{0:T(128)S(1)}, s32[2]{0:T(128)}, u32[]{:S(2)}) copy-start(s32[2]{0:T(128)} %constant.87) | copy-start | bytes 28
  15.3 14.7 %copy-start.3 = (f32[8,128,8]{2,1,0:T(8,128)S(1)}, f32[8,128,8]{2,1,0:T(8,128)}, u32[]{:S(2)}) copy-start(f32[8,128,8]{2,1,0:T(8,128)} %pad_dynamic-slice_fusion) | copy-start | bytes 98308
  15.3 14.7 %copy-start.4 = (f32[8,128,128]{2,1,0:T(8,128)S(1)}, f32[8,128,128]{2,1,0:T(8,128)}, u32[]{:S(2)}) copy-start(f32[8,128,128]{2,1,0:T(8,128)} %param.9) | copy-start | bytes 1572868
  16.4 12.4 %collective-permute-start.2 = (f32[34,8,256]{2,1,0:T(8,128)S(1)}, f32[34,8,256]{2,1,0:T(8,128)S(1)}, u32[]{:S(2)}, u32[]{:S(2)}) collective-permute-start(f32[34,8,256]{2,1,0:T(8,128)S(1)} %get-tuple-element.40), channel_id=1, source_target_pairs={{4,0},{8,4},{12,8},{5,1},{9,5},{13,9},{6,2},{10,6},{14,10},{7,3},{... | collective-permute-start | bytes 835592 | tf_op jit(solution)/shard_map/ppermute | solution.py:250
  17.7 12.3 %collective-permute-start.3 = (f32[34,8,256]{2,1,0:T(8,128)S(1)}, f32[34,8,256]{2,1,0:T(8,128)S(1)}, u32[]{:S(2)}, u32[]{:S(2)}) collective-permute-start(f32[34,8,256]{2,1,0:T(8,128)S(1)} %get-tuple-element.41), channel_id=1, source_target_pairs={{0,4},{4,8},{8,12},{1,5},{5,9},{9,13},{2,6},{6,10},{10,14},{3,7},{... | collective-permute-start | bytes 835592 | tf_op jit(solution)/shard_map/ppermute | solution.py:249
  38.0 12.3 %collective-permute-start.5 = (f32[2,144,256]{2,1,0:T(8,128)S(1)}, f32[2,144,256]{2,1,0:T(8,128)S(1)}, u32[]{:S(2)}, u32[]{:S(2)}) collective-permute-start(f32[2,144,256]{2,1,0:T(8,128)S(1)} %gather_fusion.1), channel_id=1, source_target_pairs={{16,0},{17,1},{18,2},{19,3},{20,4},{21,5},{22,6},{23,7},{24,8},{25... | collective-permute-start | bytes 884744 | tf_op jit(solution)/shard_map/ppermute | solution.py:274
  42.3 10.5 %collective-permute-start.4 = (f32[2,144,256]{2,1,0:T(8,128)S(1)}, f32[2,144,256]{2,1,0:T(8,128)S(1)}, u32[]{:S(2)}, u32[]{:S(2)}) collective-permute-start(f32[2,144,256]{2,1,0:T(8,128)S(1)} %gather_fusion), channel_id=1, source_target_pairs={{0,16},{1,17},{2,18},{3,19},{4,20},{5,21},{6,22},{7,23},{8,24},{9,... | collective-permute-start | bytes 884744 | tf_op jit(solution)/shard_map/ppermute | solution.py:273
  50.3 2.6 %copy-start.11 = (f32[2,144,256]{2,1,0:T(8,128)}, f32[2,144,256]{2,1,0:T(8,128)S(1)}, u32[]{:S(2)}) copy-start(f32[2,144,256]{2,1,0:T(8,128)S(1)} %collective-permute-done.5.r_13_) | copy-start | bytes 884740
  62.7 9.8 %collective-permute-start.6 = (f32[2,144,256]{2,1,0:T(8,128)}, f32[2,144,256]{2,1,0:T(8,128)S(1)}, u32[]{:S(2)}, u32[]{:S(2)}) collective-permute-start(f32[2,144,256]{2,1,0:T(8,128)} %get-tuple-element.23), channel_id=1, source_target_pairs={{0,16},{1,17},{2,18},{3,19},{4,20},{5,21},{6,22},{7,23},{8,24},{9,... | collective-permute-start | bytes 884744 | tf_op jit(solution)/shard_map/ppermute | solution.py:273
  67.1 9.4 %collective-permute-start.7 = (f32[2,144,256]{2,1,0:T(8,128)}, f32[2,144,256]{2,1,0:T(8,128)S(1)}, u32[]{:S(2)}, u32[]{:S(2)}) collective-permute-start(f32[2,144,256]{2,1,0:T(8,128)} %get-tuple-element.24), channel_id=1, source_target_pairs={{16,0},{17,1},{18,2},{19,3},{20,4},{21,5},{22,6},{23,7},{24,8},{25... | collective-permute-start | bytes 884744 | tf_op jit(solution)/shard_map/ppermute | solution.py:274
  72.4 4.0 %copy-start.9 = (f32[2,144,256]{2,1,0:T(8,128)}, f32[2,144,256]{2,1,0:T(8,128)S(1)}, u32[]{:S(2)}) copy-start(f32[2,144,256]{2,1,0:T(8,128)S(1)} %collective-permute-done.6.r_12_) | copy-start | bytes 884740
  86.4 9.8 %collective-permute-start.8 = (f32[2,144,256]{2,1,0:T(8,128)}, f32[2,144,256]{2,1,0:T(8,128)S(1)}, u32[]{:S(2)}, u32[]{:S(2)}) collective-permute-start(f32[2,144,256]{2,1,0:T(8,128)} %get-tuple-element.27), channel_id=1, source_target_pairs={{0,16},{1,17},{2,18},{3,19},{4,20},{5,21},{6,22},{7,23},{8,24},{9,... | collective-permute-start | bytes 884744 | tf_op jit(solution)/shard_map/ppermute | solution.py:273
  87.9 9.6 %collective-permute-start.9 = (f32[2,144,256]{2,1,0:T(8,128)}, f32[2,144,256]{2,1,0:T(8,128)S(1)}, u32[]{:S(2)}, u32[]{:S(2)}) collective-permute-start(f32[2,144,256]{2,1,0:T(8,128)} %get-tuple-element.28), channel_id=1, source_target_pairs={{16,0},{17,1},{18,2},{19,3},{20,4},{21,5},{22,6},{23,7},{24,8},{25... | collective-permute-start | bytes 884744 | tf_op jit(solution)/shard_map/ppermute | solution.py:274
  90.3 17.0 %collective-permute-start.10 = (f32[144,256]{1,0:T(8,128)S(1)}, f32[144,256]{1,0:T(8,128)S(1)}, u32[]{:S(2)}, u32[]{:S(2)}) collective-permute-start(f32[144,256]{1,0:T(8,128)S(1)} %get-tuple-element.43), channel_id=1, source_target_pairs={{0,16},{1,17},{2,18},{3,19},{4,20},{5,21},{6,22},{7,23},{8,24},{9,... | collective-permute-start | bytes 442376 | tf_op jit(solution)/shard_map/ppermute | solution.py:309
  94.8 12.4 %collective-permute-start.11 = (f32[144,256]{1,0:T(8,128)S(1)}, f32[144,256]{1,0:T(8,128)S(1)}, u32[]{:S(2)}, u32[]{:S(2)}) collective-permute-start(f32[144,256]{1,0:T(8,128)S(1)} %get-tuple-element.42), channel_id=1, source_target_pairs={{16,0},{17,1},{18,2},{19,3},{20,4},{21,5},{22,6},{23,7},{24,8},{25... | collective-permute-start | bytes 442376 | tf_op jit(solution)/shard_map/ppermute | solution.py:310
  116.7 6.2 %collective-permute-start.12 = (f32[144,256]{1,0:T(8,128)}, f32[144,256]{1,0:T(8,128)S(1)}, u32[]{:S(2)}, u32[]{:S(2)}) collective-permute-start(f32[144,256]{1,0:T(8,128)} %get-tuple-element.32), channel_id=1, source_target_pairs={{0,16},{1,17},{2,18},{3,19},{4,20},{5,21},{6,22},{7,23},{8,24},{9,... | collective-permute-start | bytes 442376 | tf_op jit(solution)/shard_map/ppermute | solution.py:309
  120.0 7.2 %collective-permute-start.13 = (f32[144,256]{1,0:T(8,128)}, f32[144,256]{1,0:T(8,128)S(1)}, u32[]{:S(2)}, u32[]{:S(2)}) collective-permute-start(f32[144,256]{1,0:T(8,128)} %get-tuple-element.33), channel_id=1, source_target_pairs={{16,0},{17,1},{18,2},{19,3},{20,4},{21,5},{22,6},{23,7},{24,8},{25... | collective-permute-start | bytes 442376 | tf_op jit(solution)/shard_map/ppermute | solution.py:310
  123.0 4.3 %copy-start.17 = (f32[144,256]{1,0:T(8,128)}, f32[144,256]{1,0:T(8,128)S(1)}, u32[]{:S(2)}) copy-start(f32[144,256]{1,0:T(8,128)S(1)} %collective-permute-done.12.r_6_) | copy-start | bytes 442372
  136.7 4.5 %collective-permute-start.14 = (f32[144,256]{1,0:T(8,128)}, f32[144,256]{1,0:T(8,128)S(1)}, u32[]{:S(2)}, u32[]{:S(2)}) collective-permute-start(f32[144,256]{1,0:T(8,128)} %get-tuple-element.35), channel_id=1, source_target_pairs={{0,16},{1,17},{2,18},{3,19},{4,20},{5,21},{6,22},{7,23},{8,24},{9,... | collective-permute-start | bytes 442376 | tf_op jit(solution)/shard_map/ppermute | solution.py:309
  138.3 7.2 %collective-permute-start.15 = (f32[144,256]{1,0:T(8,128)}, f32[144,256]{1,0:T(8,128)S(1)}, u32[]{:S(2)}, u32[]{:S(2)}) collective-permute-start(f32[144,256]{1,0:T(8,128)} %get-tuple-element.36), channel_id=1, source_target_pairs={{16,0},{17,1},{18,2},{19,3},{20,4},{21,5},{22,6},{23,7},{24,8},{25... | collective-permute-start | bytes 442376 | tf_op jit(solution)/shard_map/ppermute | solution.py:310
  141.2 4.3 %copy-start.18 = (f32[144,256]{1,0:T(8,128)}, f32[144,256]{1,0:T(8,128)S(1)}, u32[]{:S(2)}) copy-start(f32[144,256]{1,0:T(8,128)S(1)} %collective-permute-done.14.r_6_) | copy-start | bytes 442372
  155.0 4.5 %collective-permute-start.16 = (f32[144,256]{1,0:T(8,128)}, f32[144,256]{1,0:T(8,128)S(1)}, u32[]{:S(2)}, u32[]{:S(2)}) collective-permute-start(f32[144,256]{1,0:T(8,128)} %get-tuple-element.38), channel_id=1, source_target_pairs={{0,16},{1,17},{2,18},{3,19},{4,20},{5,21},{6,22},{7,23},{8,24},{9,... | collective-permute-start | bytes 442376 | tf_op jit(solution)/shard_map/ppermute | solution.py:309
  156.5 7.2 %collective-permute-start.17 = (f32[144,256]{1,0:T(8,128)}, f32[144,256]{1,0:T(8,128)S(1)}, u32[]{:S(2)}, u32[]{:S(2)}) collective-permute-start(f32[144,256]{1,0:T(8,128)} %get-tuple-element.39), channel_id=1, source_target_pairs={{16,0},{17,1},{18,2},{19,3},{20,4},{21,5},{22,6},{23,7},{24,8},{25... | collective-permute-start | bytes 442376 | tf_op jit(solution)/shard_map/ppermute | solution.py:310
  159.5 4.3 %copy-start.15 = (f32[144,256]{1,0:T(8,128)}, f32[144,256]{1,0:T(8,128)S(1)}, u32[]{:S(2)}) copy-start(f32[144,256]{1,0:T(8,128)S(1)} %collective-permute-done.16.r_6_) | copy-start | bytes 442372
  172.1 11.3 %collective-permute-start.18 = (f32[8,128,128]{2,1,0:T(8,128)}, f32[8,128,128]{2,1,0:T(8,128)S(1)}, u32[]{:S(2)}, u32[]{:S(2)}) collective-permute-start(f32[8,128,128]{2,1,0:T(8,128)} %shard_map.101), channel_id=1, source_target_pairs={{2,0},{3,1},{1,2},{6,4},{7,5},{5,6},{10,8},{11,9},{9,10},{14,12},{... | collective-permute-start | bytes 1572872 | tf_op jit(solution)/shard_map/ppermute | solution.py:185
  173.4 13.9 %copy-start.5 = (f32[8,128,128]{2,1,0:T(8,128)S(1)}, f32[8,128,128]{2,1,0:T(8,128)}, u32[]{:S(2)}) copy-start(f32[8,128,128]{2,1,0:T(8,128)} %shard_map.101) | copy-start | bytes 1572868
  184.6 2.7 %collective-permute-start.19 = (f32[2,8,128,128]{3,2,1,0:T(8,128)S(1)}, f32[2,8,128,128]{3,2,1,0:T(8,128)S(1)}, u32[]{:S(2)}, u32[]{:S(2)}) collective-permute-start(f32[2,8,128,128]{3,2,1,0:T(8,128)S(1)} %pad_maximum_fusion.3), channel_id=1, source_target_pairs={{0,1},{1,0},{2,3},{3,2},{4,5},{5,4},{6,7},{7,6},{8,9},{9,8},{10,11... | collective-permute-start | bytes 3145736 | tf_op jit(solution)/shard_map/ppermute | solution.py:188
  (10 other events, 8.1 us)

commit v7 on v4

--- a/solution.py
+++ b/solution.py
@@ -54,12 +54,16 @@
     return (y >= 0) & (y < y_total) & (x >= 0) & (x < x_total)
 
 
-def _em_kernel(factor, last, depth, totals, pos, prof, fl, f, mat, w, zlo, zhi, *outs):
+def _em_kernel(factor, last, pair, depth, totals, pos, prof, fl, f, mat, w, zlo, zhi, *outs):
     diagonal = 6.0 + SHIFT
     if last:
         (heat, own) = outs
+    elif pair:
+        (o, oz0) = outs
+        oz1 = None
     else:
         (o, oz0, oz1) = outs
+    bottom = pos[0] == 0
     height, breadth, y_total, x_total = totals
     rows, lanes = f.shape[1], f.shape[2]
     keep = _inside(pos, rows, lanes, height, breadth, y_total, x_total)
@@ -69,8 +73,14 @@
         cur = [f[c * depth + z] for c in range(2)]
         beside = []
         for c in range(2):
-            z_up = f[c * depth + z + 1] if z + 1 < depth else zhi[c]
-            z_dn = f[c * depth + z - 1] if z > 0 else zlo[c]
+            if z + 1 < depth:
+                z_up = f[c * depth + z + 1]
+            else:
+                z_up = jnp.where(bottom, zhi[c], 0.0) if pair else zhi[c]
+            if z > 0:
+                z_dn = f[c * depth + z - 1]
+            else:
+                z_dn = jnp.where(bottom, 0.0, zlo[c]) if pair else zlo[c]
             y_up, y_dn, x_up, x_dn = _rolls(cur[c])
             total = z_up + z_dn
             total = total + y_up + y_dn
@@ -93,16 +103,23 @@
             if z == 0:
                 oz0[0] = n0
                 oz0[1] = n1
-            if z == depth - 1:
+            if z == depth - 1 and pair:
+                oz0[0] = jnp.where(bottom, n0, oz0[0])
+                oz0[1] = jnp.where(bottom, n1, oz0[1])
+            elif z == depth - 1:
                 oz1[0] = n0
                 oz1[1] = n1
 
 
-def _heat_kernel(last, depth, totals, pos, fl, t, q, tzlo, tzhi, *outs):
+def _heat_kernel(last, pair, depth, totals, pos, fl, t, q, tzlo, tzhi, *outs):
     if last:
         (own,) = outs
+    elif pair:
+        (o, oz0) = outs
+        oz1 = None
     else:
         (o, oz0, oz1) = outs
+    bottom = pos[0] == 0
     height, breadth, x_first_block = totals
     rows, lanes = t.shape[1], t.shape[2]
     sy, sx = _selectors(pos, rows, lanes, height, breadth, x_first_block)
@@ -114,7 +131,12 @@
         above < zb_total, 1.0, 0.0)
     m_own = [_cells(fl, pos[0] + zo, sy, sx) for zo in range(depth // MB)]
     planes = [m_below] + [m_own[z // MB] for z in range(depth)] + [m_above]
-    temps = [tzlo[...]] + [t[z] for z in range(depth)] + [tzhi[...]]
+    if pair:
+        below_t = jnp.where(bottom, 0.0, tzlo[...])
+        above_t = jnp.where(bottom, tzhi[...], 0.0)
+    else:
+        below_t, above_t = tzlo[...], tzhi[...]
+    temps = [below_t] + [t[z] for z in range(depth)] + [above_t]
     kaps = [1.0 / (1.0 + SOFTEN * v * v) for v in temps]
     for z in range(depth):
         c = temps[z + 1]
@@ -136,7 +158,9 @@
             o[z] = new
             if z == 0:
                 oz0[...] = new
-            if z == depth - 1:
+            if z == depth - 1 and pair:
+                oz0[...] = jnp.where(bottom, new, oz0[...])
+            elif z == depth - 1:
                 oz1[...] = new
 
 
@@ -243,17 +267,26 @@
     oshape = jax.ShapeDtypeStruct((2, depth, height, breadth), jnp.float32)
     lo_plane = field[jnp.array([0, depth])]
     hi_plane = field[jnp.array([depth - 1, 2 * depth - 1])]
+    pair = n_gz == 2
+    both = [(0, 1), (1, 0)]
+    if pair:
+        send = jnp.where(gz_i == 0, hi_plane, lo_plane)
     for i, factor in enumerate(WEIGHTS):
         last = i == len(WEIGHTS) - 1
-        zlo = lax.ppermute(hi_plane, "gz", up_z)
-        zhi = lax.ppermute(lo_plane, "gz", down_z)
-        outs = (qshape, oshape) if last else (fshape, plane2, plane2)
+        if pair:
+            zlo = zhi = lax.ppermute(send, "gz", both)
+        else:
+            zlo = lax.ppermute(hi_plane, "gz", up_z)
+            zhi = lax.ppermute(lo_plane, "gz", down_z)
+        outs = (qshape, oshape) if last else (fshape, plane2) if pair else (fshape, plane2, plane2)
         res = _vmem_call(
             lambda *r, factor=factor, last=last: _em_kernel(
-                factor, last, depth, (height, breadth, y_total, x_total), *r), outs, 8, 2
+                factor, last, pair, depth, (height, breadth, y_total, x_total), *r), outs, 8, 2
         )(pos, profile, flags, field, material, winding, zlo, zhi)
         if last:
             heat, field_out = res
+        elif pair:
+            field, send = res
         else:
             field, lo_plane, hi_plane = res
 
@@ -261,17 +294,24 @@
     tplane = jax.ShapeDtypeStruct((rows, lanes), jnp.float32)
     town = jax.ShapeDtypeStruct((depth, height, breadth), jnp.float32)
     lo_t, hi_t = kelvin[0], kelvin[depth - 1]
+    if pair:
+        send_t = jnp.where(gz_i == 0, hi_t, lo_t)
     for number in range(STEPS):
         last = number == STEPS - 1
-        tzlo = lax.ppermute(hi_t, "gz", up_z)
-        tzhi = lax.ppermute(lo_t, "gz", down_z)
-        outs = (town,) if last else (tshape, tplane, tplane)
+        if pair:
+            tzlo = tzhi = lax.ppermute(send_t, "gz", both)
+        else:
+            tzlo = lax.ppermute(hi_t, "gz", up_z)
+            tzhi = lax.ppermute(lo_t, "gz", down_z)
+        outs = (town,) if last else (tshape, tplane) if pair else (tshape, tplane, tplane)
         res = _vmem_call(
             lambda *r, last=last: _heat_kernel(
-                last, depth, (height, breadth, offset // MB), *r), outs, 6, 1
+                last, pair, depth, (height, breadth, offset // MB), *r), outs, 6, 1
         )(pos, flags, kelvin, heat, tzlo, tzhi)
         if last:
             (own_t,) = res
+        elif pair:
+            kelvin, send_t = res
         else:
             kelvin, lo_t, hi_t = res
 

time: 164 us -> 147 us (0.90)
  starting transfers between devices: 37.9 us -> 24.3 us
  waiting for transfers between devices: 54.1 us -> 45.8 us
  other arithmetic: 10.5 us -> 15.9 us
    ppermute x14 -> x7, starting transfers between devices: 25.8 us -> 11.6 us  [the longest x3 6.45 us: on_device(): zlo = zhi = lax.ppermute(send, 'gz', both)]
    ppermute x14 -> x7, waiting for transfers between devices: 37.3 us -> 30.2 us  [the longest x3 18.9 us: on_device(): zlo = zhi = lax.ppermute(send, 'gz', both)]
    concatenate x1, other arithmetic: 3.81 us -> 6.55 us  [on_device(): frame = jnp.concatenate([ystack, from_below, from_above], axis=1)]
    unnamed x50 -> x34, local copies, waits for them, and re-layouts: 7.72 us -> 7.89 us
  transfers between devices with their start and end apart: 20 -> 13, of which waited for: 15 -> 10; matrix products, arithmetic and copies ran while one was open for 6% -> 7% of each run, Pallas kernels for 4% -> 4%
where the time goes in v7:
time: 147 us; the launch traced here: 146 us
  waiting for transfers between devices  45.8 us (31%)
  Pallas kernels  38.2 us (26%)
  starting transfers between devices  24.3 us (17%)
  local copies, waits for them, and re-layouts  20.5 us (14%)
  other arithmetic  15.9 us (11%)
  between operations  1.63 us (1%)
    pallas_call x4, Pallas kernels, on_device(): _vmem_call(lambda *r, last=last: _heat_kernel(last, pair, depth, (height,...  20 us
    ppermute x3, waiting for transfers between devices, on_device(): zlo = zhi = lax.ppermute(send, 'gz', both)  18.9 us
    pallas_call x3, Pallas kernels, on_device(): _vmem_call(lambda *r, factor=factor, last=last: _em_kernel(factor, last,...  18.2 us
    ppermute x4, waiting for transfers between devices, on_device(): tzlo = tzhi = lax.ppermute(send_t, 'gz', both)  11.3 us
    ppermute x1, waiting for transfers between devices, _broadcast_blocks(): r1 = lax.ppermute(own, 'gx', [(2, 0), (3, 1), (1, 2)])  9.96 us
    unnamed x34, local copies, waits for them, and re-layouts  7.89 us
    concatenate x1, other arithmetic, on_device(): frame = jnp.concatenate([ystack, from_below, from_above], axis=1)  6.55 us
    ppermute x3, starting transfers between devices, on_device(): zlo = zhi = lax.ppermute(send, 'gz', both)  6.45 us
  transfers between devices with their start and end apart: 13, of which 10 were waited for; matrix products, arithmetic and copies ran while one was open for 7% of the time, Pallas kernels for 4%

profile of v7, /device:TPU:0, one launch (start us, length us, event | category | flops | bytes accessed | tf_op | source)
XLA Modules:
  0.0 146.3 jit_solution(8592252550138625134)
XLA Ops:
  0.6 1.6 %pad_maximum_fusion.1 = f32[26,128,128]{2,1,0:T(8,128)S(1)} fusion(f32[2,128,128]{2,1,0:T(8,128)} %param.10, f32[8,128,128]{2,1,0:T(8,128)} %param.9, f32[16,128,128]{2,1,0:T(8,128)} %bitcast.35), kind=kLoop, calls=%fused_computation.7 | loop fusion | flops 851968 | bytes 3407872 | tf_op jit(solution)/shard_map/concatenate | solution.py:231
  3.9 3.1 %collective-permute-start.1 = (f32[26,8,128]{2,1,0:T(8,128)}, f32[26,8,128]{2,1,0:T(8,128)}, u32[]{:S(2)}, u32[]{:S(2)}) collective-permute-start(f32[26,8,128]{2,1,0:T(8,128)} %copy.12), channel_id=1, source_target_pairs={{0,1},{1,2},{2,3},{4,5},{5,6},{6,7},{8,9},{9,10},{10,11},{12,13},{... | collective-permute-start | bytes 319496 | tf_op jit(solution)/shard_map/ppermute | solution.py:235
  7.5 1.3 collective-permute-start
  10.6 1.3 pad_dynamic-slice_fusion.1
  13.0 1.4 copy.13
  16.2 2.0 %maximum_maximum_fusion = (f32[34,8,256]{2,1,0:T(8,128)}, f32[34,8,256]{2,1,0:T(8,128)}) fusion(f32[8,128,8]{2,1,0:T(8,128)} %pad_dynamic-slice_fusion, f32[26,128,8]{2,1,0:T(8,128)S(1)} %bitcast.33, f32[8,128,112]{2,1,0:T(8,128)S(1)} %broadcast_in_dim.13, f32[8,128,136]{2,1,0:T(8,128)S(1)} %copy-done.4, f32[26,128,112]{2,1,0:T(8,128)S(1)} %broadcast_in_dim.12, ...), kind=kLoop, calls=%fused_computation.25 | loop fusion | flops 1114112 | bytes 5013504 | tf_op jit(solution)/shard_map/slice | solution.py:251
  19.5 5.7 %collective-permute-start.3 = (f32[34,8,256]{2,1,0:T(8,128)}, f32[34,8,256]{2,1,0:T(8,128)}, u32[]{:S(2)}, u32[]{:S(2)}) collective-permute-start(f32[34,8,256]{2,1,0:T(8,128)} %get-tuple-element.27), channel_id=1, source_target_pairs={{0,4},{4,8},{8,12},{1,5},{5,9},{9,13},{2,6},{6,10},{10,14},{3,7},{... | collective-permute-start | bytes 835592 | tf_op jit(solution)/shard_map/ppermute | solution.py:250
  28.5 1.8 %collective-permute-done.3 = f32[34,8,256]{2,1,0:T(8,128)} collective-permute-done((f32[34,8,256]{2,1,0:T(8,128)}, f32[34,8,256]{2,1,0:T(8,128)}, u32[]{:S(2)}, u32[]{:S(2)}) %collective-permute-start.3) | collective-permute-done | bytes 278560 | tf_op jit(solution)/shard_map/ppermute | solution.py:250
  30.3 6.5 %pad_maximum_fusion = f32[34,144,256]{2,1,0:T(8,128)S(1)} fusion(f32[34,8,256]{2,1,0:T(8,128)} %collective-permute-done.3, f32[34,8,256]{2,1,0:T(8,128)} %collective-permute-done.2, f32[8,128,8]{2,1,0:T(8,128)} %pad_dynamic-slice_fusion, f32[8,128,112]{2,1,0:T(8,128)} %copy-done.6, f32[8,128,136]{2,1,0:T(8,128)} %pad_dynamic-slice_fusion.1, ...), kind=kLoop, calls=%fused_computation.2 | loop fusion | flops 12533760 | bytes 10027008 | tf_op jit(solution)/shard_map/concatenate | solution.py:252
  37.6 1.6 %copy-done = f32[34,144,256]{2,1,0:T(8,128)} copy-done((f32[34,144,256]{2,1,0:T(8,128)}, f32[34,144,256]{2,1,0:T(8,128)S(1)}, u32[]{:S(2)}) %copy-start) | copy-done | bytes 5013528
  40.6 2.5 %collective-permute-start.4 = (f32[2,144,256]{2,1,0:T(8,128)S(1)}, f32[2,144,256]{2,1,0:T(8,128)S(1)}, u32[]{:S(2)}, u32[]{:S(2)}) collective-permute-start(f32[2,144,256]{2,1,0:T(8,128)S(1)} %broadcast_select_fusion), channel_id=1, source_target_pairs={{0,16},{16,0},{1,17},{17,1},{2,18},{18,2},{3,19},{19,3},{4,20},{20... | collective-permute-start | bytes 884744 | tf_op jit(solution)/shard_map/ppermute | solution.py:277
  43.1 3.2 %fusion.2 = (f32[8,144,256]{2,1,0:T(8,128)}, f32[8,144,256]{2,1,0:T(8,128)}) fusion(f32[34,144,256]{2,1,0:T(8,128)} %copy-done), kind=kLoop, calls=%fused_computation.34 | loop fusion | bytes 4718592 | tf_op jit(solution)/shard_map/slice | solution.py:256
  46.3 4.3 %collective-permute-done.4.r_6_.r_7_ = f32[2,144,256]{2,1,0:T(8,128)S(1)} collective-permute-done((f32[2,144,256]{2,1,0:T(8,128)S(1)}, f32[2,144,256]{2,1,0:T(8,128)S(1)}, u32[]{:S(2)}, u32[]{:S(2)}) %collective-permute-start.4) | collective-permute-done | bytes 294944 | tf_op jit(solution)/shard_map/ppermute | solution.py:277
  51.3 6.1 %shard_map.95 = (f32[16,144,256]{2,1,0:T(8,128)}, f32[2,144,256]{2,1,0:T(8,128)}) custom-call(s32[3]{0:T(128)} %pad_add_fusion.r_0_, f32[8]{0:T(128)} %add_divide_fusion.r_1_, f32[2,128,128]{2,1,0:T(8,128)} %pad.8.r_2_.r_1_, f32[16,144,256]{2,1,0:T(8,128)} %copy-done.2, f32[8,144,256]{2,1,0:T(8,128)} %get-tuple-element.29.r_4_, f32[2,144,256]{2,1,0:T(8,128)} %slice.61.r_5_, ...), custom_call_target="tpu_custom_call" | custom-call | tf_op jit(solution)/shard_map/pallas_call | solution.py:282
  57.4 2.2 %collective-permute-start.5 = (f32[2,144,256]{2,1,0:T(8,128)}, f32[2,144,256]{2,1,0:T(8,128)S(1)}, u32[]{:S(2)}, u32[]{:S(2)}) collective-permute-start(f32[2,144,256]{2,1,0:T(8,128)} %get-tuple-element.15), channel_id=1, source_target_pairs={{0,16},{16,0},{1,17},{17,1},{2,18},{18,2},{3,19},{19,3},{4,20},{20... | collective-permute-start | bytes 884744 | tf_op jit(solution)/shard_map/ppermute | solution.py:277
  59.6 7.5 %collective-permute-done.5.r_6_.r_7_ = f32[2,144,256]{2,1,0:T(8,128)S(1)} collective-permute-done((f32[2,144,256]{2,1,0:T(8,128)}, f32[2,144,256]{2,1,0:T(8,128)S(1)}, u32[]{:S(2)}, u32[]{:S(2)}) %collective-permute-start.5) | collective-permute-done | bytes 294944 | tf_op jit(solution)/shard_map/ppermute | solution.py:277
  67.8 6.0 %shard_map.96 = (f32[16,144,256]{2,1,0:T(8,128)}, f32[2,144,256]{2,1,0:T(8,128)}) custom-call(s32[3]{0:T(128)} %pad_add_fusion.r_0_, f32[8]{0:T(128)} %add_divide_fusion.r_1_, f32[2,128,128]{2,1,0:T(8,128)} %pad.8.r_2_.r_1_, f32[16,144,256]{2,1,0:T(8,128)} %get-tuple-element.14.r_3_, f32[8,144,256]{2,1,0:T(8,128)} %get-tuple-element.29.r_4_, ...), custom_call_target="tpu_custom_call" | custom-call | tf_op jit(solution)/shard_map/pallas_call | solution.py:282
  73.9 1.7 %collective-permute-start.6 = (f32[2,144,256]{2,1,0:T(8,128)}, f32[2,144,256]{2,1,0:T(8,128)S(1)}, u32[]{:S(2)}, u32[]{:S(2)}) collective-permute-start(f32[2,144,256]{2,1,0:T(8,128)} %get-tuple-element.17), channel_id=1, source_target_pairs={{0,16},{16,0},{1,17},{17,1},{2,18},{18,2},{3,19},{19,3},{4,20},{20... | collective-permute-start | bytes 884744 | tf_op jit(solution)/shard_map/ppermute | solution.py:277
  77.0 7.0 %collective-permute-done.6.r_6_.r_7_ = f32[2,144,256]{2,1,0:T(8,128)S(1)} collective-permute-done((f32[2,144,256]{2,1,0:T(8,128)}, f32[2,144,256]{2,1,0:T(8,128)S(1)}, u32[]{:S(2)}, u32[]{:S(2)}) %collective-permute-start.6) | collective-permute-done | bytes 294944 | tf_op jit(solution)/shard_map/ppermute | solution.py:277
  84.8 6.1 %shard_map.97 = (f32[8,144,256]{2,1,0:T(8,128)}, f32[2,8,128,128]{3,2,1,0:T(8,128)}) custom-call(s32[3]{0:T(128)} %pad_add_fusion.r_0_, f32[8]{0:T(128)} %add_divide_fusion.r_1_, f32[2,128,128]{2,1,0:T(8,128)} %pad.8.r_2_.r_1_, f32[16,144,256]{2,1,0:T(8,128)} %get-tuple-element.16.r_3_, f32[8,144,256]{2,1,0:T(8,128)} %get-tuple-element.29.r_4_, ...), custom_call_target="tpu_custom_call" | custom-call | tf_op jit(solution)/shard_map/pallas_call | solution.py:282
  91.5 5.3 %shard_map.98 = (f32[8,144,256]{2,1,0:T(8,128)}, f32[144,256]{1,0:T(8,128)}) custom-call(s32[3]{0:T(128)} %pad_add_fusion.r_0_, f32[2,128,128]{2,1,0:T(8,128)} %pad.8.r_2_.r_1_, f32[8,144,256]{2,1,0:T(8,128)} %get-tuple-element.28.r_2_, f32[8,144,256]{2,1,0:T(8,128)} %get-tuple-element.19.r_3_, f32[144,256]{1,0:T(8,128)} %copy-done.12, f32[144,256]{1,0:T(8,128)} %copy-done.12), custom_call_target="tpu_custom_call" | custom-call | tf_op jit(solution)/shard_map/pallas_call | solution.py:307
  96.8 1.6 %collective-permute-start.8 = (f32[144,256]{1,0:T(8,128)}, f32[144,256]{1,0:T(8,128)S(1)}, u32[]{:S(2)}, u32[]{:S(2)}) collective-permute-start(f32[144,256]{1,0:T(8,128)} %get-tuple-element.21), channel_id=1, source_target_pairs={{0,16},{16,0},{1,17},{17,1},{2,18},{18,2},{3,19},{19,3},{4,20},{20... | collective-permute-start | bytes 442376 | tf_op jit(solution)/shard_map/ppermute | solution.py:302
  98.4 3.8 %collective-permute-done.8.r_4_.r_5_ = f32[144,256]{1,0:T(8,128)S(1)} collective-permute-done((f32[144,256]{1,0:T(8,128)}, f32[144,256]{1,0:T(8,128)S(1)}, u32[]{:S(2)}, u32[]{:S(2)}) %collective-permute-start.8) | collective-permute-done | bytes 147488 | tf_op jit(solution)/shard_map/ppermute | solution.py:302
  102.8 5.5 %shard_map.99 = (f32[8,144,256]{2,1,0:T(8,128)}, f32[144,256]{1,0:T(8,128)}) custom-call(s32[3]{0:T(128)} %pad_add_fusion.r_0_, f32[2,128,128]{2,1,0:T(8,128)} %pad.8.r_2_.r_1_, f32[8,144,256]{2,1,0:T(8,128)} %get-tuple-element.20.r_2_, f32[8,144,256]{2,1,0:T(8,128)} %get-tuple-element.19.r_3_, f32[144,256]{1,0:T(8,128)} %copy-done.14, f32[144,256]{1,0:T(8,128)} %copy-done.14), custom_call_target="tpu_custom_call" | custom-call | tf_op jit(solution)/shard_map/pallas_call | solution.py:307
  108.3 1.6 %collective-permute-start.9 = (f32[144,256]{1,0:T(8,128)}, f32[144,256]{1,0:T(8,128)S(1)}, u32[]{:S(2)}, u32[]{:S(2)}) collective-permute-start(f32[144,256]{1,0:T(8,128)} %get-tuple-element.23), channel_id=1, source_target_pairs={{0,16},{16,0},{1,17},{17,1},{2,18},{18,2},{3,19},{19,3},{4,20},{20... | collective-permute-start | bytes 442376 | tf_op jit(solution)/shard_map/ppermute | solution.py:302
  109.9 3.8 %collective-permute-done.9.r_4_.r_5_ = f32[144,256]{1,0:T(8,128)S(1)} collective-permute-done((f32[144,256]{1,0:T(8,128)}, f32[144,256]{1,0:T(8,128)S(1)}, u32[]{:S(2)}, u32[]{:S(2)}) %collective-permute-start.9) | collective-permute-done | bytes 147488 | tf_op jit(solution)/shard_map/ppermute | solution.py:302
  114.3 5.3 %shard_map.100 = (f32[8,144,256]{2,1,0:T(8,128)}, f32[144,256]{1,0:T(8,128)}) custom-call(s32[3]{0:T(128)} %pad_add_fusion.r_0_, f32[2,128,128]{2,1,0:T(8,128)} %pad.8.r_2_.r_1_, f32[8,144,256]{2,1,0:T(8,128)} %get-tuple-element.22.r_2_, f32[8,144,256]{2,1,0:T(8,128)} %get-tuple-element.19.r_3_, f32[144,256]{1,0:T(8,128)} %copy-done.15, f32[144,256]{1,0:T(8,128)} %copy-done.15), custom_call_target="tpu_custom_call" | custom-call | tf_op jit(solution)/shard_map/pallas_call | solution.py:307
  119.6 1.6 %collective-permute-start.10 = (f32[144,256]{1,0:T(8,128)}, f32[144,256]{1,0:T(8,128)S(1)}, u32[]{:S(2)}, u32[]{:S(2)}) collective-permute-start(f32[144,256]{1,0:T(8,128)} %get-tuple-element.25), channel_id=1, source_target_pairs={{0,16},{16,0},{1,17},{17,1},{2,18},{18,2},{3,19},{19,3},{4,20},{20... | collective-permute-start | bytes 442376 | tf_op jit(solution)/shard_map/ppermute | solution.py:302
  121.2 3.8 %collective-permute-done.10.r_4_.r_5_ = f32[144,256]{1,0:T(8,128)S(1)} collective-permute-done((f32[144,256]{1,0:T(8,128)}, f32[144,256]{1,0:T(8,128)S(1)}, u32[]{:S(2)}, u32[]{:S(2)}) %collective-permute-start.10) | collective-permute-done | bytes 147488 | tf_op jit(solution)/shard_map/ppermute | solution.py:302
  125.7 3.9 %shard_map.101 = f32[8,128,128]{2,1,0:T(8,128)} custom-call(s32[3]{0:T(128)} %pad_add_fusion.r_0_, f32[2,128,128]{2,1,0:T(8,128)} %pad.8.r_2_.r_1_, f32[8,144,256]{2,1,0:T(8,128)} %get-tuple-element.24.r_2_, f32[8,144,256]{2,1,0:T(8,128)} %get-tuple-element.19.r_3_, f32[144,256]{1,0:T(8,128)} %copy-done.13, f32[144,256]{1,0:T(8,128)} %copy-done.13), custom_call_target="tpu_custom_call" | custom-call | tf_op jit(solution)/shard_map/pallas_call | solution.py:307
  130.9 10.0 %collective-permute-done.11 = f32[8,128,128]{2,1,0:T(8,128)S(1)} collective-permute-done((f32[8,128,128]{2,1,0:T(8,128)}, f32[8,128,128]{2,1,0:T(8,128)S(1)}, u32[]{:S(2)}, u32[]{:S(2)}) %collective-permute-start.11) | collective-permute-done | bytes 524320 | tf_op jit(solution)/shard_map/ppermute | solution.py:186
  142.2 2.6 %collective-permute-done.12 = f32[2,8,128,128]{3,2,1,0:T(8,128)S(1)} collective-permute-done((f32[2,8,128,128]{3,2,1,0:T(8,128)S(1)}, f32[2,8,128,128]{3,2,1,0:T(8,128)S(1)}, u32[]{:S(2)}, u32[]{:S(2)}) %collective-permute-start.12) | collective-permute-done | bytes 1048608 | tf_op jit(solution)/shard_map/ppermute | solution.py:189
  (65 shorter events, 23.0 us)
Async XLA Ops:
  3.9 5.6 %copy-start.5 = (f32[8,128,384]{2,1,0:T(8,128)S(1)}, f32[8,128,384]{2,1,0:T(8,128)}, u32[]{:S(2)}) copy-start(f32[8,128,384]{2,1,0:T(8,128)} %param.13) | copy-start | bytes 4718596
  3.9 9.1 %collective-permute-start.1 = (f32[26,8,128]{2,1,0:T(8,128)}, f32[26,8,128]{2,1,0:T(8,128)}, u32[]{:S(2)}, u32[]{:S(2)}) collective-permute-start(f32[26,8,128]{2,1,0:T(8,128)} %copy.12), channel_id=1, source_target_pairs={{0,1},{1,2},{2,3},{4,5},{5,6},{6,7},{8,9},{9,10},{10,11},{12,13},{... | collective-permute-start | bytes 319496 | tf_op jit(solution)/shard_map/ppermute | solution.py:235
  7.5 5.0 %collective-permute-start = (f32[26,8,128]{2,1,0:T(8,128)S(1)}, f32[26,8,128]{2,1,0:T(8,128)S(1)}, u32[]{:S(2)}, u32[]{:S(2)}) collective-permute-start(f32[26,8,128]{2,1,0:T(8,128)S(1)} %copy.10), channel_id=1, source_target_pairs={{1,0},{2,1},{3,2},{5,4},{6,5},{7,6},{9,8},{10,9},{11,10},{13,12},{... | collective-permute-start | bytes 319496 | tf_op jit(solution)/shard_map/ppermute | solution.py:236
  13.0 1.7 %copy-start.8 = (f32[2,128,128]{2,1,0:T(8,128)S(1)}, f32[2,128,128]{2,1,0:T(8,128)}, u32[]{:S(2)}) copy-start(f32[2,128,128]{2,1,0:T(8,128)} %param.10) | copy-start | bytes 393220
  14.4 1.4 copy-start.3
  14.4 1.7 %copy-start.4 = (f32[8,128,136]{2,1,0:T(8,128)S(1)}, f32[8,128,136]{2,1,0:T(8,128)}, u32[]{:S(2)}) copy-start(f32[8,128,136]{2,1,0:T(8,128)} %pad_dynamic-slice_fusion.1) | copy-start | bytes 1671172
  14.5 3.7 %copy-start.6 = (f32[8,128,112]{2,1,0:T(8,128)}, f32[8,128,112]{2,1,0:T(8,128)S(1)}, u32[]{:S(2)}) copy-start(f32[8,128,112]{2,1,0:T(8,128)S(1)} %broadcast_in_dim.13) | copy-start | bytes 1376260
  16.2 2.0 %copy-start.1 = (f32[26,128,112]{2,1,0:T(8,128)}, f32[26,128,112]{2,1,0:T(8,128)S(1)}, u32[]{:S(2)}) copy-start(f32[26,128,112]{2,1,0:T(8,128)S(1)} %broadcast_in_dim.12) | copy-start | bytes 4472836
  16.2 11.1 %copy-start.16 = (s32[2]{0:T(128)S(1)}, s32[2]{0:T(128)}, u32[]{:S(2)}) copy-start(s32[2]{0:T(128)} %constant.87) | copy-start | bytes 28
  18.2 10.4 %collective-permute-start.2 = (f32[34,8,256]{2,1,0:T(8,128)}, f32[34,8,256]{2,1,0:T(8,128)}, u32[]{:S(2)}, u32[]{:S(2)}) collective-permute-start(f32[34,8,256]{2,1,0:T(8,128)} %get-tuple-element.26), channel_id=1, source_target_pairs={{4,0},{8,4},{12,8},{5,1},{9,5},{13,9},{6,2},{10,6},{14,10},{7,3},{... | collective-permute-start | bytes 835592 | tf_op jit(solution)/shard_map/ppermute | solution.py:251
  19.5 10.8 %collective-permute-start.3 = (f32[34,8,256]{2,1,0:T(8,128)}, f32[34,8,256]{2,1,0:T(8,128)}, u32[]{:S(2)}, u32[]{:S(2)}) collective-permute-start(f32[34,8,256]{2,1,0:T(8,128)} %get-tuple-element.27), channel_id=1, source_target_pairs={{0,4},{4,8},{8,12},{1,5},{5,9},{9,13},{2,6},{6,10},{10,14},{3,7},{... | collective-permute-start | bytes 835592 | tf_op jit(solution)/shard_map/ppermute | solution.py:250
  36.8 2.4 %copy-start = (f32[34,144,256]{2,1,0:T(8,128)}, f32[34,144,256]{2,1,0:T(8,128)S(1)}, u32[]{:S(2)}) copy-start(f32[34,144,256]{2,1,0:T(8,128)S(1)} %pad_maximum_fusion) | copy-start | bytes 15040516
  39.4 6.9 %copy-start.2 = (f32[16,144,256]{2,1,0:T(8,128)}, f32[16,144,256]{2,1,0:T(8,128)S(1)}, u32[]{:S(2)}) copy-start(f32[16,144,256]{2,1,0:T(8,128)S(1)} %slice.59.r_3_) | copy-start | bytes 7077892
  40.6 10.0 %collective-permute-start.4 = (f32[2,144,256]{2,1,0:T(8,128)S(1)}, f32[2,144,256]{2,1,0:T(8,128)S(1)}, u32[]{:S(2)}, u32[]{:S(2)}) collective-permute-start(f32[2,144,256]{2,1,0:T(8,128)S(1)} %broadcast_select_fusion), channel_id=1, source_target_pairs={{0,16},{16,0},{1,17},{17,1},{2,18},{18,2},{3,19},{19,3},{4,20},{20... | collective-permute-start | bytes 884744 | tf_op jit(solution)/shard_map/ppermute | solution.py:277
  50.6 0.7 copy-start.10
  57.4 9.7 %collective-permute-start.5 = (f32[2,144,256]{2,1,0:T(8,128)}, f32[2,144,256]{2,1,0:T(8,128)S(1)}, u32[]{:S(2)}, u32[]{:S(2)}) collective-permute-start(f32[2,144,256]{2,1,0:T(8,128)} %get-tuple-element.15), channel_id=1, source_target_pairs={{0,16},{16,0},{1,17},{17,1},{2,18},{18,2},{3,19},{19,3},{4,20},{20... | collective-permute-start | bytes 884744 | tf_op jit(solution)/shard_map/ppermute | solution.py:277
  67.1 0.7 copy-start.11
  73.9 10.1 %collective-permute-start.6 = (f32[2,144,256]{2,1,0:T(8,128)}, f32[2,144,256]{2,1,0:T(8,128)S(1)}, u32[]{:S(2)}, u32[]{:S(2)}) collective-permute-start(f32[2,144,256]{2,1,0:T(8,128)} %get-tuple-element.17), channel_id=1, source_target_pairs={{0,16},{16,0},{1,17},{17,1},{2,18},{18,2},{3,19},{19,3},{4,20},{20... | collective-permute-start | bytes 884744 | tf_op jit(solution)/shard_map/ppermute | solution.py:277
  76.6 14.2 %collective-permute-start.7 = (f32[144,256]{1,0:T(8,128)S(1)}, f32[144,256]{1,0:T(8,128)S(1)}, u32[]{:S(2)}, u32[]{:S(2)}) collective-permute-start(f32[144,256]{1,0:T(8,128)S(1)} %fusion.1), channel_id=1, source_target_pairs={{0,16},{16,0},{1,17},{17,1},{2,18},{18,2},{3,19},{19,3},{4,20},{20... | collective-permute-start | bytes 442376 | tf_op jit(solution)/shard_map/ppermute | solution.py:302
  84.0 0.7 copy-start.9
  90.9 0.7 copy-start.12
  96.8 5.4 %collective-permute-start.8 = (f32[144,256]{1,0:T(8,128)}, f32[144,256]{1,0:T(8,128)S(1)}, u32[]{:S(2)}, u32[]{:S(2)}) collective-permute-start(f32[144,256]{1,0:T(8,128)} %get-tuple-element.21), channel_id=1, source_target_pairs={{0,16},{16,0},{1,17},{17,1},{2,18},{18,2},{3,19},{19,3},{4,20},{20... | collective-permute-start | bytes 442376 | tf_op jit(solution)/shard_map/ppermute | solution.py:302
  102.2 0.7 copy-start.14
  108.3 5.4 %collective-permute-start.9 = (f32[144,256]{1,0:T(8,128)}, f32[144,256]{1,0:T(8,128)S(1)}, u32[]{:S(2)}, u32[]{:S(2)}) collective-permute-start(f32[144,256]{1,0:T(8,128)} %get-tuple-element.23), channel_id=1, source_target_pairs={{0,16},{16,0},{1,17},{17,1},{2,18},{18,2},{3,19},{19,3},{4,20},{20... | collective-permute-start | bytes 442376 | tf_op jit(solution)/shard_map/ppermute | solution.py:302
  113.7 0.7 copy-start.15
  119.6 5.4 %collective-permute-start.10 = (f32[144,256]{1,0:T(8,128)}, f32[144,256]{1,0:T(8,128)S(1)}, u32[]{:S(2)}, u32[]{:S(2)}) collective-permute-start(f32[144,256]{1,0:T(8,128)} %get-tuple-element.25), channel_id=1, source_target_pairs={{0,16},{16,0},{1,17},{17,1},{2,18},{18,2},{3,19},{19,3},{4,20},{20... | collective-permute-start | bytes 442376 | tf_op jit(solution)/shard_map/ppermute | solution.py:302
  125.0 0.7 copy-start.13
  129.6 11.3 %collective-permute-start.11 = (f32[8,128,128]{2,1,0:T(8,128)}, f32[8,128,128]{2,1,0:T(8,128)S(1)}, u32[]{:S(2)}, u32[]{:S(2)}) collective-permute-start(f32[8,128,128]{2,1,0:T(8,128)} %shard_map.101), channel_id=1, source_target_pairs={{2,0},{3,1},{1,2},{6,4},{7,5},{5,6},{10,8},{11,9},{9,10},{14,12},{... | collective-permute-start | bytes 1572872 | tf_op jit(solution)/shard_map/ppermute | solution.py:186
  130.9 13.9 %copy-start.7 = (f32[8,128,128]{2,1,0:T(8,128)S(1)}, f32[8,128,128]{2,1,0:T(8,128)}, u32[]{:S(2)}) copy-start(f32[8,128,128]{2,1,0:T(8,128)} %shard_map.101) | copy-start | bytes 1572868
  142.1 2.7 %collective-permute-start.12 = (f32[2,8,128,128]{3,2,1,0:T(8,128)S(1)}, f32[2,8,128,128]{3,2,1,0:T(8,128)S(1)}, u32[]{:S(2)}, u32[]{:S(2)}) collective-permute-start(f32[2,8,128,128]{3,2,1,0:T(8,128)S(1)} %pad_maximum_fusion.3), channel_id=1, source_target_pairs={{0,1},{1,0},{2,3},{3,2},{4,5},{5,4},{6,7},{7,6},{8,9},{9,8},{10,11... | collective-permute-start | bytes 3145736 | tf_op jit(solution)/shard_map/ppermute | solution.py:189

commit v8 on v7

--- a/solution.py
+++ b/solution.py
@@ -269,15 +269,32 @@
     hi_plane = field[jnp.array([depth - 1, 2 * depth - 1])]
     pair = n_gz == 2
     both = [(0, 1), (1, 0)]
+
+    used = breadth + 2 * H
+    dense = (rows * used) % 128 == 0
+
+    def squeeze(p):
+        q = jnp.concatenate([p[..., : breadth + H], p[..., lanes - H:]], axis=-1)
+        return q.reshape(q.shape[:-2] + (rows * used // 128, 128)) if dense else q
+
+    def unsqueeze(p):
+        if dense:
+            p = p.reshape(p.shape[:-2] + (rows, used))
+        filler = jnp.zeros(p.shape[:-1] + (gap,), jnp.float32)
+        return jnp.concatenate([p[..., : breadth + H], filler, p[..., breadth + H:]], axis=-1)
+
+    def exchange(hi, lo, sent):
+        if pair:
+            got = unsqueeze(lax.ppermute(squeeze(sent), "gz", both))
+            return got, got
+        return (unsqueeze(lax.ppermute(squeeze(hi), "gz", up_z)),
+                unsqueeze(lax.ppermute(squeeze(lo), "gz", down_z)))
+
     if pair:
         send = jnp.where(gz_i == 0, hi_plane, lo_plane)
     for i, factor in enumerate(WEIGHTS):
         last = i == len(WEIGHTS) - 1
-        if pair:
-            zlo = zhi = lax.ppermute(send, "gz", both)
-        else:
-            zlo = lax.ppermute(hi_plane, "gz", up_z)
-            zhi = lax.ppermute(lo_plane, "gz", down_z)
+        zlo, zhi = exchange(hi_plane, lo_plane, send if pair else None)
         outs = (qshape, oshape) if last else (fshape, plane2) if pair else (fshape, plane2, plane2)
         res = _vmem_call(
             lambda *r, factor=factor, last=last: _em_kernel(
@@ -298,11 +315,7 @@
         send_t = jnp.where(gz_i == 0, hi_t, lo_t)
     for number in range(STEPS):
         last = number == STEPS - 1
-        if pair:
-            tzlo = tzhi = lax.ppermute(send_t, "gz", both)
-        else:
-            tzlo = lax.ppermute(hi_t, "gz", up_z)
-            tzhi = lax.ppermute(lo_t, "gz", down_z)
+        tzlo, tzhi = exchange(hi_t, lo_t, send_t if pair else None)
         outs = (town,) if last else (tshape, tplane) if pair else (tshape, tplane, tplane)
         res = _vmem_call(
             lambda *r, last=last: _heat_kernel(

time: 147 us -> 150 us (1.020)
  other arithmetic: 15.9 us -> 25.8 us
  waiting for transfers between devices: 45.8 us -> 38.4 us
  starting transfers between devices: 24.3 us -> 20.6 us
  local copies, waits for them, and re-layouts: 20.5 us -> 24.1 us
    concatenate x0 -> x14, other arithmetic: none -> 10.8 us  [the longest x7 5.5 us: unsqueeze(): jnp.concatenate([p[..., :breadth + H], filler, p[..., breadth + H:]], axi...]
    ppermute x7, waiting for transfers between devices: 30.2 us -> 21.6 us  [exchange(): got = unsqueeze(lax.ppermute(squeeze(sent), 'gz', both))]
    slice x0 -> x14, local copies, waits for them, and re-layouts: none -> 5.67 us  [the longest x7 5.06 us: squeeze(): q = jnp.concatenate([p[..., :breadth + H], p[..., lanes - H:]], axis=-1)]
    ppermute x7, starting transfers between devices: 11.6 us -> 6.6 us  [exchange(): got = unsqueeze(lax.ppermute(squeeze(sent), 'gz', both))]
    unnamed x34 -> x20, local copies, waits for them, and re-layouts: 7.89 us -> 3.2 us
    reshape x0 -> x14, local copies, waits for them, and re-layouts: none -> 2.35 us  [the longest x7 1.26 us: squeeze(): return q.reshape(q.shape[:-2] + (rows * used // 128, 128)) if dense else q]
    ppermute x1, waiting for transfers between devices: 1.24 us -> 2.97 us  [on_device(): from_below = lax.ppermute(ystack[:, :H, :], 'gy', down_y)]
  transfers between devices with their start and end apart: 13 -> 13, of which waited for: 10 -> 10; matrix products, arithmetic and copies ran while one was open for 7% -> 8% of each run, Pallas kernels for 4% -> 0%
where the time goes in v8:
time: 150 us; the launch traced here: 149 us
  waiting for transfers between devices  38.4 us (26%)
  Pallas kernels  38.4 us (26%)
  other arithmetic  25.8 us (17%)
  local copies, waits for them, and re-layouts  24.1 us (16%)
  starting transfers between devices  20.6 us (14%)
  between operations  1.77 us (1%)
    ppermute x7, waiting for transfers between devices, exchange(): got = unsqueeze(lax.ppermute(squeeze(sent), 'gz', both))  21.6 us
    pallas_call x4, Pallas kernels, on_device(): _vmem_call(lambda *r, last=last: _heat_kernel(last, pair, depth, (height,...  20.1 us
    pallas_call x3, Pallas kernels, on_device(): _vmem_call(lambda *r, factor=factor, last=last: _em_kernel(factor, last,...  18.3 us
    ppermute x1, waiting for transfers between devices, _broadcast_blocks(): r1 = lax.ppermute(own, 'gx', [(2, 0), (3, 1), (1, 2)])  9.96 us
    ppermute x7, starting transfers between devices, exchange(): got = unsqueeze(lax.ppermute(squeeze(sent), 'gz', both))  6.6 us
    concatenate x1, other arithmetic, on_device(): frame = jnp.concatenate([ystack, from_below, from_above], axis=1)  6.55 us
    ppermute x1, starting transfers between devices, on_device(): from_above = lax.ppermute(ystack[:, height - H:, :], 'gy', up_y)  6.27 us
    concatenate x7, other arithmetic, unsqueeze(): jnp.concatenate([p[..., :breadth + H], filler, p[..., breadth + H:]], axi...  5.5 us
  transfers between devices with their start and end apart: 13, of which 10 were waited for; matrix products, arithmetic and copies ran while one was open for 8% of the time, Pallas kernels for 0%

profile of v8, /device:TPU:0, one launch (start us, length us, event | category | flops | bytes accessed | tf_op | source)
XLA Modules:
  0.0 149.1 jit_solution(2960915034522945833)
XLA Ops:
  0.6 1.6 %pad_maximum_fusion.1 = f32[26,128,128]{2,1,0:T(8,128)S(1)} fusion(f32[2,128,128]{2,1,0:T(8,128)} %param.10, f32[8,128,128]{2,1,0:T(8,128)} %param.9, f32[16,128,128]{2,1,0:T(8,128)} %bitcast.49), kind=kLoop, calls=%fused_computation.7 | loop fusion | flops 851968 | bytes 3407872 | tf_op jit(solution)/shard_map/concatenate | solution.py:231
  3.3 1.4 collective-permute-start
  5.8 3.7 %collective-permute-start.1 = (f32[26,8,128]{2,1,0:T(8,128)}, f32[26,8,128]{2,1,0:T(8,128)}, u32[]{:S(2)}, u32[]{:S(2)}) collective-permute-start(f32[26,8,128]{2,1,0:T(8,128)} %copy.12), channel_id=1, source_target_pairs={{0,1},{1,2},{2,3},{4,5},{5,6},{6,7},{8,9},{9,10},{10,11},{12,13},{... | collective-permute-start | bytes 319496 | tf_op jit(solution)/shard_map/ppermute | solution.py:235
  9.5 1.3 pad_dynamic-slice_fusion.1
  13.6 1.4 copy.13
  15.3 1.2 copy-done.3
  17.2 2.0 %maximum_maximum_fusion = (f32[34,8,256]{2,1,0:T(8,128)}, f32[34,8,256]{2,1,0:T(8,128)}) fusion(f32[8,128,8]{2,1,0:T(8,128)} %pad_dynamic-slice_fusion, f32[26,128,8]{2,1,0:T(8,128)S(1)} %bitcast.47, f32[8,128,112]{2,1,0:T(8,128)S(1)} %broadcast_in_dim.13, f32[8,128,136]{2,1,0:T(8,128)S(1)} %copy-done.4, f32[26,128,112]{2,1,0:T(8,128)S(1)} %broadcast_in_dim.12, ...), kind=kLoop, calls=%fused_computation.31 | loop fusion | flops 1114112 | bytes 5013504 | tf_op jit(solution)/shard_map/slice | solution.py:251
  19.2 1.3 collective-permute-start.2
  20.5 6.3 %collective-permute-start.3 = (f32[34,8,256]{2,1,0:T(8,128)}, f32[34,8,256]{2,1,0:T(8,128)}, u32[]{:S(2)}, u32[]{:S(2)}) collective-permute-start(f32[34,8,256]{2,1,0:T(8,128)} %get-tuple-element.27), channel_id=1, source_target_pairs={{0,4},{4,8},{8,12},{1,5},{5,9},{9,13},{2,6},{6,10},{10,14},{3,7},{... | collective-permute-start | bytes 835592 | tf_op jit(solution)/shard_map/ppermute | solution.py:250
  29.0 3.0 %collective-permute-done.2 = f32[34,8,256]{2,1,0:T(8,128)} collective-permute-done((f32[34,8,256]{2,1,0:T(8,128)}, f32[34,8,256]{2,1,0:T(8,128)}, u32[]{:S(2)}, u32[]{:S(2)}) %collective-permute-start.2) | collective-permute-done | bytes 278560 | tf_op jit(solution)/shard_map/ppermute | solution.py:251
  31.9 1.2 collective-permute-done.3
  33.2 6.5 %pad_maximum_fusion = f32[34,144,256]{2,1,0:T(8,128)S(1)} fusion(f32[34,8,256]{2,1,0:T(8,128)} %collective-permute-done.3, f32[34,8,256]{2,1,0:T(8,128)} %collective-permute-done.2, f32[8,128,8]{2,1,0:T(8,128)} %pad_dynamic-slice_fusion, f32[8,128,112]{2,1,0:T(8,128)} %copy-done.6, f32[8,128,136]{2,1,0:T(8,128)} %pad_dynamic-slice_fusion.1, ...), kind=kLoop, calls=%fused_computation.2 | loop fusion | flops 12533760 | bytes 10027008 | tf_op jit(solution)/shard_map/concatenate | solution.py:252
  40.9 1.3 copy-done
  43.9 1.6 %collective-permute-start.4 = (f32[2,162,128]{2,1,0:T(8,128)S(1)}, f32[2,162,128]{2,1,0:T(8,128)S(1)}, u32[]{:S(2)}, u32[]{:S(2)}) collective-permute-start(f32[2,162,128]{2,1,0:T(8,128)S(1)} %reshape.53), channel_id=1, source_target_pairs={{0,16},{16,0},{1,17},{17,1},{2,18},{18,2},{3,19},{19,3},{4,20},{20... | collective-permute-start | bytes 497672 | tf_op jit(solution)/shard_map/ppermute | solution.py:288
  45.5 3.3 %fusion.2 = (f32[8,144,256]{2,1,0:T(8,128)}, f32[8,144,256]{2,1,0:T(8,128)}) fusion(f32[34,144,256]{2,1,0:T(8,128)} %copy-done), kind=kLoop, calls=%fused_computation.48 | loop fusion | bytes 4718592 | tf_op jit(solution)/shard_map/slice | solution.py:256
  48.8 1.3 collective-permute-done.4
  51.3 6.1 %shard_map.95 = (f32[16,144,256]{2,1,0:T(8,128)}, f32[2,144,256]{2,1,0:T(8,128)}) custom-call(s32[3]{0:T(128)} %pad_add_fusion.r_0_, f32[8]{0:T(128)} %add_divide_fusion.r_1_, f32[2,128,128]{2,1,0:T(8,128)} %pad.8.r_2_.r_1_, f32[16,144,256]{2,1,0:T(8,128)} %copy-done.2, f32[8,144,256]{2,1,0:T(8,128)} %get-tuple-element.29.r_4_, f32[2,144,256]{2,1,0:T(8,128)} %slice.173.r_5_, ...), custom_call_target="tpu_custom_call" | custom-call | tf_op jit(solution)/shard_map/pallas_call | solution.py:299
  62.1 4.8 %collective-permute-done.7 = f32[162,128]{1,0:T(8,128)S(1)} collective-permute-done((f32[162,128]{1,0:T(8,128)S(1)}, f32[162,128]{1,0:T(8,128)S(1)}, u32[]{:S(2)}, u32[]{:S(2)}) %collective-permute-start.7) | collective-permute-done | bytes 82976 | tf_op jit(solution)/shard_map/ppermute | solution.py:288
  68.3 6.1 %shard_map.96 = (f32[16,144,256]{2,1,0:T(8,128)}, f32[2,144,256]{2,1,0:T(8,128)}) custom-call(s32[3]{0:T(128)} %pad_add_fusion.r_0_, f32[8]{0:T(128)} %add_divide_fusion.r_1_, f32[2,128,128]{2,1,0:T(8,128)} %pad.8.r_2_.r_1_, f32[16,144,256]{2,1,0:T(8,128)} %get-tuple-element.14.r_3_, f32[8,144,256]{2,1,0:T(8,128)} %get-tuple-element.29.r_4_, ...), custom_call_target="tpu_custom_call" | custom-call | tf_op jit(solution)/shard_map/pallas_call | solution.py:299
  78.2 4.0 %collective-permute-done.6 = f32[2,162,128]{2,1,0:T(8,128)S(1)} collective-permute-done((f32[2,162,128]{2,1,0:T(8,128)S(1)}, f32[2,162,128]{2,1,0:T(8,128)S(1)}, u32[]{:S(2)}, u32[]{:S(2)}) %collective-permute-start.6) | collective-permute-done | bytes 165920 | tf_op jit(solution)/shard_map/ppermute | solution.py:288
  83.3 6.1 %shard_map.97 = (f32[8,144,256]{2,1,0:T(8,128)}, f32[2,8,128,128]{3,2,1,0:T(8,128)}) custom-call(s32[3]{0:T(128)} %pad_add_fusion.r_0_, f32[8]{0:T(128)} %add_divide_fusion.r_1_, f32[2,128,128]{2,1,0:T(8,128)} %pad.8.r_2_.r_1_, f32[16,144,256]{2,1,0:T(8,128)} %get-tuple-element.16.r_3_, f32[8,144,256]{2,1,0:T(8,128)} %get-tuple-element.29.r_4_, ...), custom_call_target="tpu_custom_call" | custom-call | tf_op jit(solution)/shard_map/pallas_call | solution.py:299
  89.4 5.5 %shard_map.98 = (f32[8,144,256]{2,1,0:T(8,128)}, f32[144,256]{1,0:T(8,128)}) custom-call(s32[3]{0:T(128)} %pad_add_fusion.r_0_, f32[2,128,128]{2,1,0:T(8,128)} %pad.8.r_2_.r_1_, f32[8,144,256]{2,1,0:T(8,128)} %get-tuple-element.28.r_2_, f32[8,144,256]{2,1,0:T(8,128)} %get-tuple-element.19.r_3_, f32[144,256]{1,0:T(8,128)} %pad_maximum_fusion.18.r_4_.r_5_, ...), custom_call_target="tpu_custom_call" | custom-call | tf_op jit(solution)/shard_map/pallas_call | solution.py:320
  97.7 3.8 %collective-permute-done.8 = f32[162,128]{1,0:T(8,128)S(1)} collective-permute-done((f32[162,128]{1,0:T(8,128)S(1)}, f32[162,128]{1,0:T(8,128)S(1)}, u32[]{:S(2)}, u32[]{:S(2)}) %collective-permute-start.8) | collective-permute-done | bytes 82976 | tf_op jit(solution)/shard_map/ppermute | solution.py:288
  102.5 5.3 %shard_map.99 = (f32[8,144,256]{2,1,0:T(8,128)}, f32[144,256]{1,0:T(8,128)}) custom-call(s32[3]{0:T(128)} %pad_add_fusion.r_0_, f32[2,128,128]{2,1,0:T(8,128)} %pad.8.r_2_.r_1_, f32[8,144,256]{2,1,0:T(8,128)} %get-tuple-element.20.r_2_, f32[8,144,256]{2,1,0:T(8,128)} %get-tuple-element.19.r_3_, f32[144,256]{1,0:T(8,128)} %pad_maximum_fusion.20.r_4_.r_5_, ...), custom_call_target="tpu_custom_call" | custom-call | tf_op jit(solution)/shard_map/pallas_call | solution.py:320
  110.6 3.8 %collective-permute-done.9 = f32[162,128]{1,0:T(8,128)S(1)} collective-permute-done((f32[162,128]{1,0:T(8,128)S(1)}, f32[162,128]{1,0:T(8,128)S(1)}, u32[]{:S(2)}, u32[]{:S(2)}) %collective-permute-start.9) | collective-permute-done | bytes 82976 | tf_op jit(solution)/shard_map/ppermute | solution.py:288
  115.4 5.3 %shard_map.100 = (f32[8,144,256]{2,1,0:T(8,128)}, f32[144,256]{1,0:T(8,128)}) custom-call(s32[3]{0:T(128)} %pad_add_fusion.r_0_, f32[2,128,128]{2,1,0:T(8,128)} %pad.8.r_2_.r_1_, f32[8,144,256]{2,1,0:T(8,128)} %get-tuple-element.22.r_2_, f32[8,144,256]{2,1,0:T(8,128)} %get-tuple-element.19.r_3_, f32[144,256]{1,0:T(8,128)} %pad_maximum_fusion.22.r_4_.r_5_, ...), custom_call_target="tpu_custom_call" | custom-call | tf_op jit(solution)/shard_map/pallas_call | solution.py:320
  123.6 3.8 %collective-permute-done.10 = f32[162,128]{1,0:T(8,128)S(1)} collective-permute-done((f32[162,128]{1,0:T(8,128)S(1)}, f32[162,128]{1,0:T(8,128)S(1)}, u32[]{:S(2)}, u32[]{:S(2)}) %collective-permute-start.10) | collective-permute-done | bytes 82976 | tf_op jit(solution)/shard_map/ppermute | solution.py:288
  128.4 3.9 %shard_map.101 = f32[8,128,128]{2,1,0:T(8,128)} custom-call(s32[3]{0:T(128)} %pad_add_fusion.r_0_, f32[2,128,128]{2,1,0:T(8,128)} %pad.8.r_2_.r_1_, f32[8,144,256]{2,1,0:T(8,128)} %get-tuple-element.24.r_2_, f32[8,144,256]{2,1,0:T(8,128)} %get-tuple-element.19.r_3_, f32[144,256]{1,0:T(8,128)} %pad_maximum_fusion.24.r_4_.r_5_, ...), custom_call_target="tpu_custom_call" | custom-call | tf_op jit(solution)/shard_map/pallas_call | solution.py:320
  132.3 1.3 collective-permute-start.11
  133.7 10.0 %collective-permute-done.11 = f32[8,128,128]{2,1,0:T(8,128)S(1)} collective-permute-done((f32[8,128,128]{2,1,0:T(8,128)}, f32[8,128,128]{2,1,0:T(8,128)S(1)}, u32[]{:S(2)}, u32[]{:S(2)}) %collective-permute-start.11) | collective-permute-done | bytes 524320 | tf_op jit(solution)/shard_map/ppermute | solution.py:186
  144.9 2.6 %collective-permute-done.12 = f32[2,8,128,128]{3,2,1,0:T(8,128)S(1)} collective-permute-done((f32[2,8,128,128]{3,2,1,0:T(8,128)S(1)}, f32[2,8,128,128]{3,2,1,0:T(8,128)S(1)}, u32[]{:S(2)}, u32[]{:S(2)}) %collective-permute-start.12) | collective-permute-done | bytes 1048608 | tf_op jit(solution)/shard_map/ppermute | solution.py:189
  147.8 1.3 pad_maximum_fusion.2
  (95 shorter events, 35.1 us)
Async XLA Ops:
  3.3 6.2 %copy-start.5 = (f32[8,128,384]{2,1,0:T(8,128)S(1)}, f32[8,128,384]{2,1,0:T(8,128)}, u32[]{:S(2)}) copy-start(f32[8,128,384]{2,1,0:T(8,128)} %param.13) | copy-start | bytes 4718596
  3.3 9.8 %collective-permute-start = (f32[26,8,128]{2,1,0:T(8,128)S(1)}, f32[26,8,128]{2,1,0:T(8,128)S(1)}, u32[]{:S(2)}, u32[]{:S(2)}) collective-permute-start(f32[26,8,128]{2,1,0:T(8,128)S(1)} %copy.10), channel_id=1, source_target_pairs={{1,0},{2,1},{3,2},{5,4},{6,5},{7,6},{9,8},{10,9},{11,10},{13,12},{... | collective-permute-start | bytes 319496 | tf_op jit(solution)/shard_map/ppermute | solution.py:236
  5.8 7.8 %collective-permute-start.1 = (f32[26,8,128]{2,1,0:T(8,128)}, f32[26,8,128]{2,1,0:T(8,128)}, u32[]{:S(2)}, u32[]{:S(2)}) collective-permute-start(f32[26,8,128]{2,1,0:T(8,128)} %copy.12), channel_id=1, source_target_pairs={{0,1},{1,2},{2,3},{4,5},{5,6},{6,7},{8,9},{9,10},{10,11},{12,13},{... | collective-permute-start | bytes 319496 | tf_op jit(solution)/shard_map/ppermute | solution.py:235
  13.6 1.7 %copy-start.8 = (f32[2,128,128]{2,1,0:T(8,128)S(1)}, f32[2,128,128]{2,1,0:T(8,128)}, u32[]{:S(2)}) copy-start(f32[2,128,128]{2,1,0:T(8,128)} %param.10) | copy-start | bytes 393220
  15.0 1.5 copy-start.3
  15.0 2.2 %copy-start.4 = (f32[8,128,136]{2,1,0:T(8,128)S(1)}, f32[8,128,136]{2,1,0:T(8,128)}, u32[]{:S(2)}) copy-start(f32[8,128,136]{2,1,0:T(8,128)} %pad_dynamic-slice_fusion.1) | copy-start | bytes 1671172
  15.2 4.0 %copy-start.1 = (f32[26,128,112]{2,1,0:T(8,128)}, f32[26,128,112]{2,1,0:T(8,128)S(1)}, u32[]{:S(2)}) copy-start(f32[26,128,112]{2,1,0:T(8,128)S(1)} %broadcast_in_dim.12) | copy-start | bytes 4472836
  17.2 2.0 %copy-start.6 = (f32[8,128,112]{2,1,0:T(8,128)}, f32[8,128,112]{2,1,0:T(8,128)S(1)}, u32[]{:S(2)}) copy-start(f32[8,128,112]{2,1,0:T(8,128)S(1)} %broadcast_in_dim.13) | copy-start | bytes 1376260
  17.2 11.8 %copy-start.9 = (s32[2]{0:T(128)S(1)}, s32[2]{0:T(128)}, u32[]{:S(2)}) copy-start(s32[2]{0:T(128)} %constant.89) | copy-start | bytes 28
  19.2 12.7 %collective-permute-start.2 = (f32[34,8,256]{2,1,0:T(8,128)}, f32[34,8,256]{2,1,0:T(8,128)}, u32[]{:S(2)}, u32[]{:S(2)}) collective-permute-start(f32[34,8,256]{2,1,0:T(8,128)} %get-tuple-element.26), channel_id=1, source_target_pairs={{4,0},{8,4},{12,8},{5,1},{9,5},{13,9},{6,2},{10,6},{14,10},{7,3},{... | collective-permute-start | bytes 835592 | tf_op jit(solution)/shard_map/ppermute | solution.py:251
  20.5 12.7 %collective-permute-start.3 = (f32[34,8,256]{2,1,0:T(8,128)}, f32[34,8,256]{2,1,0:T(8,128)}, u32[]{:S(2)}, u32[]{:S(2)}) collective-permute-start(f32[34,8,256]{2,1,0:T(8,128)} %get-tuple-element.27), channel_id=1, source_target_pairs={{0,4},{4,8},{8,12},{1,5},{5,9},{9,13},{2,6},{6,10},{10,14},{3,7},{... | collective-permute-start | bytes 835592 | tf_op jit(solution)/shard_map/ppermute | solution.py:250
  39.7 2.4 %copy-start = (f32[34,144,256]{2,1,0:T(8,128)}, f32[34,144,256]{2,1,0:T(8,128)S(1)}, u32[]{:S(2)}) copy-start(f32[34,144,256]{2,1,0:T(8,128)S(1)} %pad_maximum_fusion) | copy-start | bytes 15040516
  39.9 3.6 %copy-start.2 = (f32[16,144,256]{2,1,0:T(8,128)}, f32[16,144,256]{2,1,0:T(8,128)S(1)}, u32[]{:S(2)}) copy-start(f32[16,144,256]{2,1,0:T(8,128)S(1)} %slice.171.r_3_) | copy-start | bytes 7077892
  43.9 6.2 %collective-permute-start.4 = (f32[2,162,128]{2,1,0:T(8,128)S(1)}, f32[2,162,128]{2,1,0:T(8,128)S(1)}, u32[]{:S(2)}, u32[]{:S(2)}) collective-permute-start(f32[2,162,128]{2,1,0:T(8,128)S(1)} %reshape.53), channel_id=1, source_target_pairs={{0,16},{16,0},{1,17},{17,1},{2,18},{18,2},{3,19},{19,3},{4,20},{20... | collective-permute-start | bytes 497672 | tf_op jit(solution)/shard_map/ppermute | solution.py:288
  59.7 7.4 %collective-permute-start.5 = (f32[2,162,128]{2,1,0:T(8,128)S(1)}, f32[2,162,128]{2,1,0:T(8,128)S(1)}, u32[]{:S(2)}, u32[]{:S(2)}) collective-permute-start(f32[2,162,128]{2,1,0:T(8,128)S(1)} %reshape.55), channel_id=1, source_target_pairs={{0,16},{16,0},{1,17},{17,1},{2,18},{18,2},{3,19},{19,3},{4,20},{20... | collective-permute-start | bytes 497672 | tf_op jit(solution)/shard_map/ppermute | solution.py:288
  61.1 5.8 %collective-permute-start.7 = (f32[162,128]{1,0:T(8,128)S(1)}, f32[162,128]{1,0:T(8,128)S(1)}, u32[]{:S(2)}, u32[]{:S(2)}) collective-permute-start(f32[162,128]{1,0:T(8,128)S(1)} %reshape.59), channel_id=1, source_target_pairs={{0,16},{16,0},{1,17},{17,1},{2,18},{18,2},{3,19},{19,3},{4,20},{20... | collective-permute-start | bytes 248840 | tf_op jit(solution)/shard_map/ppermute | solution.py:288
  76.7 5.5 %collective-permute-start.6 = (f32[2,162,128]{2,1,0:T(8,128)S(1)}, f32[2,162,128]{2,1,0:T(8,128)S(1)}, u32[]{:S(2)}, u32[]{:S(2)}) collective-permute-start(f32[2,162,128]{2,1,0:T(8,128)S(1)} %reshape.57), channel_id=1, source_target_pairs={{0,16},{16,0},{1,17},{17,1},{2,18},{18,2},{3,19},{19,3},{4,20},{20... | collective-permute-start | bytes 497672 | tf_op jit(solution)/shard_map/ppermute | solution.py:288
  97.0 4.6 %collective-permute-start.8 = (f32[162,128]{1,0:T(8,128)S(1)}, f32[162,128]{1,0:T(8,128)S(1)}, u32[]{:S(2)}, u32[]{:S(2)}) collective-permute-start(f32[162,128]{1,0:T(8,128)S(1)} %reshape.61), channel_id=1, source_target_pairs={{0,16},{16,0},{1,17},{17,1},{2,18},{18,2},{3,19},{19,3},{4,20},{20... | collective-permute-start | bytes 248840 | tf_op jit(solution)/shard_map/ppermute | solution.py:288
  109.9 4.6 %collective-permute-start.9 = (f32[162,128]{1,0:T(8,128)S(1)}, f32[162,128]{1,0:T(8,128)S(1)}, u32[]{:S(2)}, u32[]{:S(2)}) collective-permute-start(f32[162,128]{1,0:T(8,128)S(1)} %reshape.63), channel_id=1, source_target_pairs={{0,16},{16,0},{1,17},{17,1},{2,18},{18,2},{3,19},{19,3},{4,20},{20... | collective-permute-start | bytes 248840 | tf_op jit(solution)/shard_map/ppermute | solution.py:288
  122.9 4.6 %collective-permute-start.10 = (f32[162,128]{1,0:T(8,128)S(1)}, f32[162,128]{1,0:T(8,128)S(1)}, u32[]{:S(2)}, u32[]{:S(2)}) collective-permute-start(f32[162,128]{1,0:T(8,128)S(1)} %reshape.65), channel_id=1, source_target_pairs={{0,16},{16,0},{1,17},{17,1},{2,18},{18,2},{3,19},{19,3},{4,20},{20... | collective-permute-start | bytes 248840 | tf_op jit(solution)/shard_map/ppermute | solution.py:288
  132.3 11.3 %collective-permute-start.11 = (f32[8,128,128]{2,1,0:T(8,128)}, f32[8,128,128]{2,1,0:T(8,128)S(1)}, u32[]{:S(2)}, u32[]{:S(2)}) collective-permute-start(f32[8,128,128]{2,1,0:T(8,128)} %shard_map.101), channel_id=1, source_target_pairs={{2,0},{3,1},{1,2},{6,4},{7,5},{5,6},{10,8},{11,9},{9,10},{14,12},{... | collective-permute-start | bytes 1572872 | tf_op jit(solution)/shard_map/ppermute | solution.py:186
  133.6 13.9 %copy-start.7 = (f32[8,128,128]{2,1,0:T(8,128)S(1)}, f32[8,128,128]{2,1,0:T(8,128)}, u32[]{:S(2)}) copy-start(f32[8,128,128]{2,1,0:T(8,128)} %shard_map.101) | copy-start | bytes 1572868
  144.8 2.7 %collective-permute-start.12 = (f32[2,8,128,128]{3,2,1,0:T(8,128)S(1)}, f32[2,8,128,128]{3,2,1,0:T(8,128)S(1)}, u32[]{:S(2)}, u32[]{:S(2)}) collective-permute-start(f32[2,8,128,128]{3,2,1,0:T(8,128)S(1)} %pad_maximum_fusion.3), channel_id=1, source_target_pairs={{0,1},{1,0},{2,3},{3,2},{4,5},{5,4},{6,7},{7,6},{8,9},{9,8},{10,11... | collective-permute-start | bytes 3145736 | tf_op jit(solution)/shard_map/ppermute | solution.py:189

commit v9 on v7

--- a/solution.py
+++ b/solution.py
@@ -265,38 +265,70 @@
     plane2 = jax.ShapeDtypeStruct((2, rows, lanes), jnp.float32)
     qshape = jax.ShapeDtypeStruct((depth, rows, lanes), jnp.float32)
     oshape = jax.ShapeDtypeStruct((2, depth, height, breadth), jnp.float32)
-    lo_plane = field[jnp.array([0, depth])]
-    hi_plane = field[jnp.array([depth - 1, 2 * depth - 1])]
+    tshape = jax.ShapeDtypeStruct((depth, rows, lanes), jnp.float32)
+    tplane = jax.ShapeDtypeStruct((rows, lanes), jnp.float32)
+    town = jax.ShapeDtypeStruct((depth, height, breadth), jnp.float32)
+    em_totals = (height, breadth, y_total, x_total)
+    t_totals = (height, breadth, offset // MB)
+    lo_idx = jnp.array([0, depth])
+    hi_idx = jnp.array([depth - 1, 2 * depth - 1])
     pair = n_gz == 2
     both = [(0, 1), (1, 0)]
     if pair:
-        send = jnp.where(gz_i == 0, hi_plane, lo_plane)
+        top = gz_i == 0
+        first = jnp.concatenate(
+            [jnp.where(top, field[hi_idx], field[lo_idx]),
+             jnp.where(top, kelvin[depth - 1], kelvin[0])[None]], axis=0)
+        got = lax.ppermute(first, "gz", both)
+    else:
+        lo_plane, hi_plane = field[lo_idx], field[hi_idx]
+        tzlo0 = lax.ppermute(kelvin[depth - 1], "gz", up_z)
+        tzhi0 = lax.ppermute(kelvin[0], "gz", down_z)
     for i, factor in enumerate(WEIGHTS):
         last = i == len(WEIGHTS) - 1
         if pair:
-            zlo = zhi = lax.ppermute(send, "gz", both)
+            zlo = zhi = got if i == 0 else lax.ppermute(send, "gz", both)
         else:
             zlo = lax.ppermute(hi_plane, "gz", up_z)
             zhi = lax.ppermute(lo_plane, "gz", down_z)
-        outs = (qshape, oshape) if last else (fshape, plane2) if pair else (fshape, plane2, plane2)
-        res = _vmem_call(
-            lambda *r, factor=factor, last=last: _em_kernel(
-                factor, last, pair, depth, (height, breadth, y_total, x_total), *r), outs, 8, 2
-        )(pos, profile, flags, field, material, winding, zlo, zhi)
         if last:
-            heat, field_out = res
-        elif pair:
-            field, send = res
-        else:
-            field, lo_plane, hi_plane = res
-
-    tshape = jax.ShapeDtypeStruct((depth, rows, lanes), jnp.float32)
-    tplane = jax.ShapeDtypeStruct((rows, lanes), jnp.float32)
-    town = jax.ShapeDtypeStruct((depth, height, breadth), jnp.float32)
-    lo_t, hi_t = kelvin[0], kelvin[depth - 1]
-    if pair:
-        send_t = jnp.where(gz_i == 0, hi_t, lo_t)
-    for number in range(STEPS):
+            outs = (qshape, oshape, tshape, tplane) if pair else (
+                qshape, oshape, tshape, tplane, tplane)
+
+            def fused(pos_r, prof_r, fl_r, f_r, mat_r, w_r, zlo_r, zhi_r, t_r, *rest,
+                      factor=factor):
+                if pair:
+                    tzlo_r = tzhi_r = rest[0].at[2]
+                    outs_r = rest[1:]
+                else:
+                    tzlo_r, tzhi_r = rest[0], rest[1]
+                    outs_r = rest[2:]
+                q_r, own_r = outs_r[0], outs_r[1]
+                _em_kernel(factor, True, pair, depth, em_totals, pos_r, prof_r, fl_r, f_r, mat_r,
+                           w_r, zlo_r, zhi_r, q_r, own_r)
+                _heat_kernel(False, pair, depth, t_totals, pos_r, fl_r, t_r, q_r, tzlo_r, tzhi_r,
+                             *outs_r[2:])
+
+            extra = (got,) if pair else (tzlo0, tzhi0)
+            res = _vmem_call(fused, outs, 9 + len(extra), 2)(
+                pos, profile, flags, field, material, winding, zlo, zhi, kelvin, *extra)
+            heat, field_out, kelvin = res[0], res[1], res[2]
+            if pair:
+                send_t = res[3]
+            else:
+                lo_t, hi_t = res[3], res[4]
+        else:
+            outs = (fshape, plane2) if pair else (fshape, plane2, plane2)
+            res = _vmem_call(
+                lambda *r, factor=factor: _em_kernel(
+                    factor, False, pair, depth, em_totals, *r), outs, 8, 2
+            )(pos, profile, flags, field, material, winding, zlo, zhi)
+            if pair:
+                field, send = res
+            else:
+                field, lo_plane, hi_plane = res
+
+    for number in range(1, STEPS):
         last = number == STEPS - 1
         if pair:
             tzlo = tzhi = lax.ppermute(send_t, "gz", both)
@@ -305,8 +337,7 @@
             tzhi = lax.ppermute(lo_t, "gz", down_z)
         outs = (town,) if last else (tshape, tplane) if pair else (tshape, tplane, tplane)
         res = _vmem_call(
-            lambda *r, last=last: _heat_kernel(
-                last, pair, depth, (height, breadth, offset // MB), *r), outs, 6, 1
+            lambda *r, last=last: _heat_kernel(last, pair, depth, t_totals, *r), outs, 6, 1
         )(pos, flags, kelvin, heat, tzlo, tzhi)
         if last:
             (own_t,) = res

time: 147 us -> 144 us (0.980)
  starting transfers between devices: 24.3 us -> 18.6 us
  waiting for transfers between devices: 45.8 us -> 50.1 us
  Pallas kernels: 38.2 us -> 36 us
  local copies, waits for them, and re-layouts: 20.5 us -> 22 us
    ppermute x4 -> x3, starting transfers between devices: 5.11 us -> 1.27 us  [on_device(): tzlo = tzhi = lax.ppermute(send_t, 'gz', both)]
    ppermute x4 -> x3, waiting for transfers between devices: 11.3 us -> 14.8 us  [on_device(): tzlo = tzhi = lax.ppermute(send_t, 'gz', both)]
    ppermute x1, waiting for transfers between devices: 1.24 us -> 4.47 us  [on_device(): from_below = lax.ppermute(ystack[:, :H, :], 'gy', down_y)]
    ppermute x3, starting transfers between devices: 6.45 us -> 3.3 us  [the longest x2 1.75 us: on_device(): zlo = zhi = got if i == 0 else lax.ppermute(send, 'gz', both)]
    pallas_call x7 -> x6, Pallas kernels: 38.2 us -> 36 us  [the longest x3 14.8 us: on_device(): _vmem_call(lambda *r, last=last: _heat_kernel(last, pair, depth, t_totals...]
    ppermute x3, waiting for transfers between devices: 18.9 us -> 17.1 us  [the longest x2 13.5 us: on_device(): zlo = zhi = got if i == 0 else lax.ppermute(send, 'gz', both)]
  transfers between devices with their start and end apart: 13 -> 12, of which waited for: 10 -> 10; matrix products, arithmetic and copies ran while one was open for 7% -> 7% of each run, Pallas kernels for 4% -> 0%
where the time goes in v9:
time: 144 us; the launch traced here: 143 us
  waiting for transfers between devices  50.1 us (35%)
  Pallas kernels  36 us (25%)
  local copies, waits for them, and re-layouts  22 us (15%)
  starting transfers between devices  18.6 us (13%)
  other arithmetic  15 us (10%)
  between operations  1.58 us (1%)
    pallas_call x3, Pallas kernels, on_device(): _vmem_call(lambda *r, last=last: _heat_kernel(last, pair, depth, t_totals...  14.8 us
    ppermute x3, waiting for transfers between devices, on_device(): tzlo = tzhi = lax.ppermute(send_t, 'gz', both)  14.8 us
    ppermute x2, waiting for transfers between devices, on_device(): zlo = zhi = got if i == 0 else lax.ppermute(send, 'gz', both)  13.5 us
    pallas_call x2, Pallas kernels, on_device(): _vmem_call(lambda *r, factor=factor: _em_kernel(factor, False, pair, dept...  12.3 us
    ppermute x1, waiting for transfers between devices, _broadcast_blocks(): r1 = lax.ppermute(own, 'gx', [(2, 0), (3, 1), (1, 2)])  9.96 us
    pallas_call x1, Pallas kernels, on_device(): _vmem_call(fused, outs, 9 + len(extra), 2)  8.94 us
    unnamed x34, local copies, waits for them, and re-layouts  8.4 us
    concatenate x1, other arithmetic, on_device(): frame = jnp.concatenate([ystack, from_below, from_above], axis=1)  6.55 us
  transfers between devices with their start and end apart: 12, of which 10 were waited for; matrix products, arithmetic and copies ran while one was open for 7% of the time, Pallas kernels for 0%

profile of v9, /device:TPU:0, one launch (start us, length us, event | category | flops | bytes accessed | tf_op | source)
XLA Modules:
  0.0 143.3 jit_solution(2320631485242146328)
XLA Ops:
  0.6 1.6 %pad_maximum_fusion.1 = f32[26,128,128]{2,1,0:T(8,128)S(1)} fusion(f32[2,128,128]{2,1,0:T(8,128)} %param.10, f32[8,128,128]{2,1,0:T(8,128)} %param.9, f32[16,128,128]{2,1,0:T(8,128)} %bitcast.33), kind=kLoop, calls=%fused_computation.7 | loop fusion | flops 851968 | bytes 3407872 | tf_op jit(solution)/shard_map/concatenate | solution.py:231
  3.3 1.4 collective-permute-start
  5.8 3.7 %collective-permute-start.1 = (f32[26,8,128]{2,1,0:T(8,128)}, f32[26,8,128]{2,1,0:T(8,128)}, u32[]{:S(2)}, u32[]{:S(2)}) collective-permute-start(f32[26,8,128]{2,1,0:T(8,128)} %copy.12), channel_id=1, source_target_pairs={{0,1},{1,2},{2,3},{4,5},{5,6},{6,7},{8,9},{9,10},{10,11},{12,13},{... | collective-permute-start | bytes 319496 | tf_op jit(solution)/shard_map/ppermute | solution.py:235
  9.5 1.3 pad_dynamic-slice_fusion.1
  12.3 1.4 copy.13
  14.0 1.2 copy-done.3
  15.9 2.0 %maximum_maximum_fusion = (f32[34,8,256]{2,1,0:T(8,128)}, f32[34,8,256]{2,1,0:T(8,128)}) fusion(f32[8,128,8]{2,1,0:T(8,128)} %pad_dynamic-slice_fusion, f32[26,128,8]{2,1,0:T(8,128)S(1)} %bitcast.31, f32[8,128,112]{2,1,0:T(8,128)S(1)} %broadcast_in_dim.14, f32[8,128,136]{2,1,0:T(8,128)S(1)} %copy-done.4, f32[26,128,112]{2,1,0:T(8,128)S(1)} %broadcast_in_dim.13, ...), kind=kLoop, calls=%fused_computation.26 | loop fusion | flops 1114112 | bytes 5013504 | tf_op jit(solution)/shard_map/slice | solution.py:251
  18.0 1.3 collective-permute-start.2
  19.2 6.3 %collective-permute-start.3 = (f32[34,8,256]{2,1,0:T(8,128)}, f32[34,8,256]{2,1,0:T(8,128)}, u32[]{:S(2)}, u32[]{:S(2)}) collective-permute-start(f32[34,8,256]{2,1,0:T(8,128)} %get-tuple-element.27), channel_id=1, source_target_pairs={{0,4},{4,8},{8,12},{1,5},{5,9},{9,13},{2,6},{6,10},{10,14},{3,7},{... | collective-permute-start | bytes 835592 | tf_op jit(solution)/shard_map/ppermute | solution.py:250
  26.2 4.5 %collective-permute-done.2 = f32[34,8,256]{2,1,0:T(8,128)} collective-permute-done((f32[34,8,256]{2,1,0:T(8,128)}, f32[34,8,256]{2,1,0:T(8,128)}, u32[]{:S(2)}, u32[]{:S(2)}) %collective-permute-start.2) | collective-permute-done | bytes 278560 | tf_op jit(solution)/shard_map/ppermute | solution.py:251
  30.7 1.2 collective-permute-done.3
  31.9 6.5 %pad_maximum_fusion = f32[34,144,256]{2,1,0:T(8,128)S(1)} fusion(f32[34,8,256]{2,1,0:T(8,128)} %collective-permute-done.3, f32[34,8,256]{2,1,0:T(8,128)} %collective-permute-done.2, f32[8,128,8]{2,1,0:T(8,128)} %pad_dynamic-slice_fusion, f32[8,128,112]{2,1,0:T(8,128)} %copy-done.6, f32[8,128,136]{2,1,0:T(8,128)} %pad_dynamic-slice_fusion.1, ...), kind=kLoop, calls=%fused_computation.2 | loop fusion | flops 12533760 | bytes 10027008 | tf_op jit(solution)/shard_map/concatenate | solution.py:252
  38.4 2.3 %copy-done = f32[34,144,256]{2,1,0:T(8,128)} copy-done((f32[34,144,256]{2,1,0:T(8,128)}, f32[34,144,256]{2,1,0:T(8,128)S(1)}, u32[]{:S(2)}) %copy-start) | copy-done | bytes 5013528
  43.1 1.6 %collective-permute-start.4 = (f32[3,144,256]{2,1,0:T(8,128)S(1)}, f32[3,144,256]{2,1,0:T(8,128)S(1)}, u32[]{:S(2)}, u32[]{:S(2)}) collective-permute-start(f32[3,144,256]{2,1,0:T(8,128)S(1)} %pad_maximum_fusion.4), channel_id=1, source_target_pairs={{0,16},{16,0},{1,17},{17,1},{2,18},{18,2},{3,19},{19,3},{4,20},{20... | collective-permute-start | bytes 1327112 | tf_op jit(solution)/shard_map/ppermute | solution.py:282
  46.5 1.7 %slice.61.r_5_.w_r = f32[2,144,256]{2,1,0:T(8,128)} slice(f32[34,144,256]{2,1,0:T(8,128)} %copy-done), slice={[24:26], [0:144], [0:256]} | slice | bytes 589824 | tf_op jit(solution)/shard_map/slice | solution.py:255
  48.2 3.3 %fusion.1 = (f32[8,144,256]{2,1,0:T(8,128)}, f32[8,144,256]{2,1,0:T(8,128)}) fusion(f32[34,144,256]{2,1,0:T(8,128)} %copy-done), kind=kLoop, calls=%fused_computation.34 | loop fusion | bytes 4718592 | tf_op jit(solution)/shard_map/slice | solution.py:256
  51.5 3.6 %collective-permute-done.4.r_6_.r_7_.rest_0_ = f32[3,144,256]{2,1,0:T(8,128)S(1)} collective-permute-done((f32[3,144,256]{2,1,0:T(8,128)S(1)}, f32[3,144,256]{2,1,0:T(8,128)S(1)}, u32[]{:S(2)}, u32[]{:S(2)}) %collective-permute-start.4) | collective-permute-done | bytes 442400 | tf_op jit(solution)/shard_map/ppermute | solution.py:282
  55.9 6.2 %shard_map.95 = (f32[16,144,256]{2,1,0:T(8,128)}, f32[2,144,256]{2,1,0:T(8,128)}) custom-call(s32[3]{0:T(128)} %pad_add_fusion.r_0_.pos_r, f32[8]{0:T(128)} %add_divide_fusion.r_1_.prof_r, f32[2,128,128]{2,1,0:T(8,128)} %pad.8.r_2_.fl_r.r_1_, f32[16,144,256]{2,1,0:T(8,128)} %copy-done.2, f32[8,144,256]{2,1,0:T(8,128)} %get-tuple-element.29.r_4_.mat_r, ...), custom_call_target="tpu_custom_call" | custom-call | tf_op jit(solution)/shard_map/pallas_call | solution.py:322
  63.2 7.0 %collective-permute-done.5.r_6_.r_7_ = f32[2,144,256]{2,1,0:T(8,128)S(1)} collective-permute-done((f32[2,144,256]{2,1,0:T(8,128)}, f32[2,144,256]{2,1,0:T(8,128)S(1)}, u32[]{:S(2)}, u32[]{:S(2)}) %collective-permute-start.5) | collective-permute-done | bytes 294944 | tf_op jit(solution)/shard_map/ppermute | solution.py:290
  70.9 6.1 %shard_map.96 = (f32[16,144,256]{2,1,0:T(8,128)}, f32[2,144,256]{2,1,0:T(8,128)}) custom-call(s32[3]{0:T(128)} %pad_add_fusion.r_0_.pos_r, f32[8]{0:T(128)} %add_divide_fusion.r_1_.prof_r, f32[2,128,128]{2,1,0:T(8,128)} %pad.8.r_2_.fl_r.r_1_, f32[16,144,256]{2,1,0:T(8,128)} %get-tuple-element.14.r_3_, f32[8,144,256]{2,1,0:T(8,128)} %get-tuple-element.29.r_4_.mat_r, ...), custom_call_target="tpu_custom_call" | custom-call | tf_op jit(solution)/shard_map/pallas_call | solution.py:322
  77.6 6.5 %collective-permute-done.6.zlo_r.zhi_r = f32[2,144,256]{2,1,0:T(8,128)S(1)} collective-permute-done((f32[2,144,256]{2,1,0:T(8,128)}, f32[2,144,256]{2,1,0:T(8,128)S(1)}, u32[]{:S(2)}, u32[]{:S(2)}) %collective-permute-start.6) | collective-permute-done | bytes 294944 | tf_op jit(solution)/shard_map/ppermute | solution.py:290
  84.9 8.9 %shard_map.97 = (f32[8,144,256]{2,1,0:T(8,128)}, f32[2,8,128,128]{3,2,1,0:T(8,128)}, f32[8,144,256]{2,1,0:T(8,128)}, f32[144,256]{1,0:T(8,128)}) custom-call(s32[3]{0:T(128)} %pad_add_fusion.r_0_.pos_r, f32[8]{0:T(128)} %add_divide_fusion.r_1_.prof_r, f32[2,128,128]{2,1,0:T(8,128)} %pad.8.r_2_.fl_r.r_1_, f32[16,144,256]{2,1,0:T(8,128)} %get-tuple-element.16.f_r, ...), custom_call_target="tpu_custom_call" | custom-call | tf_op jit(solution)/shard_map/pallas_call | solution.py:313
  94.2 4.9 %collective-permute-done.7.r_4_.r_5_ = f32[144,256]{1,0:T(8,128)S(1)} collective-permute-done((f32[144,256]{1,0:T(8,128)}, f32[144,256]{1,0:T(8,128)S(1)}, u32[]{:S(2)}, u32[]{:S(2)}) %collective-permute-start.7) | collective-permute-done | bytes 147488 | tf_op jit(solution)/shard_map/ppermute | solution.py:334
  99.8 5.5 %shard_map.98 = (f32[8,144,256]{2,1,0:T(8,128)}, f32[144,256]{1,0:T(8,128)}) custom-call(s32[3]{0:T(128)} %pad_add_fusion.r_0_.pos_r, f32[2,128,128]{2,1,0:T(8,128)} %pad.8.r_2_.fl_r.r_1_, f32[8,144,256]{2,1,0:T(8,128)} %get-tuple-element.19.r_2_, f32[8,144,256]{2,1,0:T(8,128)} %get-tuple-element.20.r_3_, f32[144,256]{1,0:T(8,128)} %copy-done.14, ...), custom_call_target="tpu_custom_call" | custom-call | tf_op jit(solution)/shard_map/pallas_call | solution.py:339
  105.7 4.9 %collective-permute-done.8.r_4_.r_5_ = f32[144,256]{1,0:T(8,128)S(1)} collective-permute-done((f32[144,256]{1,0:T(8,128)}, f32[144,256]{1,0:T(8,128)S(1)}, u32[]{:S(2)}, u32[]{:S(2)}) %collective-permute-start.8) | collective-permute-done | bytes 147488 | tf_op jit(solution)/shard_map/ppermute | solution.py:334
  111.3 5.4 %shard_map.99 = (f32[8,144,256]{2,1,0:T(8,128)}, f32[144,256]{1,0:T(8,128)}) custom-call(s32[3]{0:T(128)} %pad_add_fusion.r_0_.pos_r, f32[2,128,128]{2,1,0:T(8,128)} %pad.8.r_2_.fl_r.r_1_, f32[8,144,256]{2,1,0:T(8,128)} %get-tuple-element.22.r_2_, f32[8,144,256]{2,1,0:T(8,128)} %get-tuple-element.20.r_3_, f32[144,256]{1,0:T(8,128)} %copy-done.13, ...), custom_call_target="tpu_custom_call" | custom-call | tf_op jit(solution)/shard_map/pallas_call | solution.py:339
  117.1 4.9 %collective-permute-done.9.r_4_.r_5_ = f32[144,256]{1,0:T(8,128)S(1)} collective-permute-done((f32[144,256]{1,0:T(8,128)}, f32[144,256]{1,0:T(8,128)S(1)}, u32[]{:S(2)}, u32[]{:S(2)}) %collective-permute-start.9) | collective-permute-done | bytes 147488 | tf_op jit(solution)/shard_map/ppermute | solution.py:334
  122.7 3.9 %shard_map.100 = f32[8,128,128]{2,1,0:T(8,128)} custom-call(s32[3]{0:T(128)} %pad_add_fusion.r_0_.pos_r, f32[2,128,128]{2,1,0:T(8,128)} %pad.8.r_2_.fl_r.r_1_, f32[8,144,256]{2,1,0:T(8,128)} %get-tuple-element.24.r_2_, f32[8,144,256]{2,1,0:T(8,128)} %get-tuple-element.20.r_3_, f32[144,256]{1,0:T(8,128)} %copy-done.12, f32[144,256]{1,0:T(8,128)} %copy-done.12), custom_call_target="tpu_custom_call" | custom-call | tf_op jit(solution)/shard_map/pallas_call | solution.py:339
  126.6 1.3 collective-permute-start.10
  127.9 10.0 %collective-permute-done.10 = f32[8,128,128]{2,1,0:T(8,128)S(1)} collective-permute-done((f32[8,128,128]{2,1,0:T(8,128)}, f32[8,128,128]{2,1,0:T(8,128)S(1)}, u32[]{:S(2)}, u32[]{:S(2)}) %collective-permute-start.10) | collective-permute-done | bytes 524320 | tf_op jit(solution)/shard_map/ppermute | solution.py:186
  139.2 2.6 %collective-permute-done.11 = f32[2,8,128,128]{3,2,1,0:T(8,128)S(1)} collective-permute-done((f32[2,8,128,128]{3,2,1,0:T(8,128)S(1)}, f32[2,8,128,128]{3,2,1,0:T(8,128)S(1)}, u32[]{:S(2)}, u32[]{:S(2)}) %collective-permute-start.11) | collective-permute-done | bytes 1048608 | tf_op jit(solution)/shard_map/ppermute | solution.py:189
  142.1 1.3 pad_maximum_fusion.2
  (63 shorter events, 17.5 us)
Async XLA Ops:
  3.3 6.2 %copy-start.5 = (f32[8,128,384]{2,1,0:T(8,128)S(1)}, f32[8,128,384]{2,1,0:T(8,128)}, u32[]{:S(2)}) copy-start(f32[8,128,384]{2,1,0:T(8,128)} %param.13) | copy-start | bytes 4718596
  3.3 8.5 %collective-permute-start = (f32[26,8,128]{2,1,0:T(8,128)S(1)}, f32[26,8,128]{2,1,0:T(8,128)S(1)}, u32[]{:S(2)}, u32[]{:S(2)}) collective-permute-start(f32[26,8,128]{2,1,0:T(8,128)S(1)} %copy.10), channel_id=1, source_target_pairs={{1,0},{2,1},{3,2},{5,4},{6,5},{7,6},{9,8},{10,9},{11,10},{13,12},{... | collective-permute-start | bytes 319496 | tf_op jit(solution)/shard_map/ppermute | solution.py:236
  5.8 6.5 %collective-permute-start.1 = (f32[26,8,128]{2,1,0:T(8,128)}, f32[26,8,128]{2,1,0:T(8,128)}, u32[]{:S(2)}, u32[]{:S(2)}) collective-permute-start(f32[26,8,128]{2,1,0:T(8,128)} %copy.12), channel_id=1, source_target_pairs={{0,1},{1,2},{2,3},{4,5},{5,6},{6,7},{8,9},{9,10},{10,11},{12,13},{... | collective-permute-start | bytes 319496 | tf_op jit(solution)/shard_map/ppermute | solution.py:235
  12.3 1.7 %copy-start.9 = (f32[2,128,128]{2,1,0:T(8,128)S(1)}, f32[2,128,128]{2,1,0:T(8,128)}, u32[]{:S(2)}) copy-start(f32[2,128,128]{2,1,0:T(8,128)} %param.10) | copy-start | bytes 393220
  13.8 1.5 %copy-start.3 = (f32[2,8,128,128]{3,2,1,0:T(8,128)S(1)}, f32[2,8,128,128]{3,2,1,0:T(8,128)}, u32[]{:S(2)}) copy-start(f32[2,8,128,128]{3,2,1,0:T(8,128)} %param.8) | copy-start | bytes 3145732
  13.8 2.2 %copy-start.4 = (f32[8,128,136]{2,1,0:T(8,128)S(1)}, f32[8,128,136]{2,1,0:T(8,128)}, u32[]{:S(2)}) copy-start(f32[8,128,136]{2,1,0:T(8,128)} %pad_dynamic-slice_fusion.1) | copy-start | bytes 1671172
  14.0 4.0 %copy-start.1 = (f32[26,128,112]{2,1,0:T(8,128)}, f32[26,128,112]{2,1,0:T(8,128)S(1)}, u32[]{:S(2)}) copy-start(f32[26,128,112]{2,1,0:T(8,128)S(1)} %broadcast_in_dim.13) | copy-start | bytes 4472836
  15.9 2.0 %copy-start.6 = (f32[8,128,112]{2,1,0:T(8,128)}, f32[8,128,112]{2,1,0:T(8,128)S(1)}, u32[]{:S(2)}) copy-start(f32[8,128,112]{2,1,0:T(8,128)S(1)} %broadcast_in_dim.14) | copy-start | bytes 1376260
  15.9 10.3 %copy-start.16 = (s32[2]{0:T(128)S(1)}, s32[2]{0:T(128)}, u32[]{:S(2)}) copy-start(s32[2]{0:T(128)} %constant.87) | copy-start | bytes 28
  18.0 12.7 %collective-permute-start.2 = (f32[34,8,256]{2,1,0:T(8,128)}, f32[34,8,256]{2,1,0:T(8,128)}, u32[]{:S(2)}, u32[]{:S(2)}) collective-permute-start(f32[34,8,256]{2,1,0:T(8,128)} %get-tuple-element.26), channel_id=1, source_target_pairs={{4,0},{8,4},{12,8},{5,1},{9,5},{13,9},{6,2},{10,6},{14,10},{7,3},{... | collective-permute-start | bytes 835592 | tf_op jit(solution)/shard_map/ppermute | solution.py:251
  19.2 12.6 %collective-permute-start.3 = (f32[34,8,256]{2,1,0:T(8,128)}, f32[34,8,256]{2,1,0:T(8,128)}, u32[]{:S(2)}, u32[]{:S(2)}) collective-permute-start(f32[34,8,256]{2,1,0:T(8,128)} %get-tuple-element.27), channel_id=1, source_target_pairs={{0,4},{4,8},{8,12},{1,5},{5,9},{9,13},{2,6},{6,10},{10,14},{3,7},{... | collective-permute-start | bytes 835592 | tf_op jit(solution)/shard_map/ppermute | solution.py:250
  38.4 2.3 %copy-start = (f32[34,144,256]{2,1,0:T(8,128)}, f32[34,144,256]{2,1,0:T(8,128)S(1)}, u32[]{:S(2)}) copy-start(f32[34,144,256]{2,1,0:T(8,128)S(1)} %pad_maximum_fusion) | copy-start | bytes 15040516
  40.9 4.4 %copy-start.2 = (f32[16,144,256]{2,1,0:T(8,128)}, f32[16,144,256]{2,1,0:T(8,128)S(1)}, u32[]{:S(2)}) copy-start(f32[16,144,256]{2,1,0:T(8,128)S(1)} %slice.59.r_3_) | copy-start | bytes 7077892
  40.9 4.4 %copy-start.15 = (s32[2,64,64]{2,1,0:T(8,128)S(1)}, s32[2,64,64]{2,1,0:T(8,128)}, u32[]{:S(2)}) copy-start(s32[2,64,64]{2,1,0:T(8,128)} %param.12) | copy-start | bytes 98308
  43.1 12.0 %collective-permute-start.4 = (f32[3,144,256]{2,1,0:T(8,128)S(1)}, f32[3,144,256]{2,1,0:T(8,128)S(1)}, u32[]{:S(2)}, u32[]{:S(2)}) collective-permute-start(f32[3,144,256]{2,1,0:T(8,128)S(1)} %pad_maximum_fusion.4), channel_id=1, source_target_pairs={{0,16},{16,0},{1,17},{17,1},{2,18},{18,2},{3,19},{19,3},{4,20},{20... | collective-permute-start | bytes 1327112 | tf_op jit(solution)/shard_map/ppermute | solution.py:282
  55.1 0.8 copy-start.8
  62.1 8.1 %collective-permute-start.5 = (f32[2,144,256]{2,1,0:T(8,128)}, f32[2,144,256]{2,1,0:T(8,128)S(1)}, u32[]{:S(2)}, u32[]{:S(2)}) collective-permute-start(f32[2,144,256]{2,1,0:T(8,128)} %get-tuple-element.15), channel_id=1, source_target_pairs={{0,16},{16,0},{1,17},{17,1},{2,18},{18,2},{3,19},{19,3},{4,20},{20... | collective-permute-start | bytes 884744 | tf_op jit(solution)/shard_map/ppermute | solution.py:290
  70.2 0.7 copy-start.11
  77.0 7.2 %collective-permute-start.6 = (f32[2,144,256]{2,1,0:T(8,128)}, f32[2,144,256]{2,1,0:T(8,128)S(1)}, u32[]{:S(2)}, u32[]{:S(2)}) collective-permute-start(f32[2,144,256]{2,1,0:T(8,128)} %get-tuple-element.17), channel_id=1, source_target_pairs={{0,16},{16,0},{1,17},{17,1},{2,18},{18,2},{3,19},{19,3},{4,20},{20... | collective-permute-start | bytes 884744 | tf_op jit(solution)/shard_map/ppermute | solution.py:290
  84.1 0.7 copy-start.10
  93.8 5.4 %collective-permute-start.7 = (f32[144,256]{1,0:T(8,128)}, f32[144,256]{1,0:T(8,128)S(1)}, u32[]{:S(2)}, u32[]{:S(2)}) collective-permute-start(f32[144,256]{1,0:T(8,128)} %get-tuple-element.21), channel_id=1, source_target_pairs={{0,16},{16,0},{1,17},{17,1},{2,18},{18,2},{3,19},{19,3},{4,20},{20... | collective-permute-start | bytes 442376 | tf_op jit(solution)/shard_map/ppermute | solution.py:334
  99.2 0.6 copy-start.14
  105.3 5.4 %collective-permute-start.8 = (f32[144,256]{1,0:T(8,128)}, f32[144,256]{1,0:T(8,128)S(1)}, u32[]{:S(2)}, u32[]{:S(2)}) collective-permute-start(f32[144,256]{1,0:T(8,128)} %get-tuple-element.23), channel_id=1, source_target_pairs={{0,16},{16,0},{1,17},{17,1},{2,18},{18,2},{3,19},{19,3},{4,20},{20... | collective-permute-start | bytes 442376 | tf_op jit(solution)/shard_map/ppermute | solution.py:334
  110.7 0.6 copy-start.13
  116.7 5.4 %collective-permute-start.9 = (f32[144,256]{1,0:T(8,128)}, f32[144,256]{1,0:T(8,128)S(1)}, u32[]{:S(2)}, u32[]{:S(2)}) collective-permute-start(f32[144,256]{1,0:T(8,128)} %get-tuple-element.25), channel_id=1, source_target_pairs={{0,16},{16,0},{1,17},{17,1},{2,18},{18,2},{3,19},{19,3},{4,20},{20... | collective-permute-start | bytes 442376 | tf_op jit(solution)/shard_map/ppermute | solution.py:334
  122.0 0.6 copy-start.12
  126.6 11.3 %collective-permute-start.10 = (f32[8,128,128]{2,1,0:T(8,128)}, f32[8,128,128]{2,1,0:T(8,128)S(1)}, u32[]{:S(2)}, u32[]{:S(2)}) collective-permute-start(f32[8,128,128]{2,1,0:T(8,128)} %shard_map.100), channel_id=1, source_target_pairs={{2,0},{3,1},{1,2},{6,4},{7,5},{5,6},{10,8},{11,9},{9,10},{14,12},{... | collective-permute-start | bytes 1572872 | tf_op jit(solution)/shard_map/ppermute | solution.py:186
  127.9 13.9 %copy-start.7 = (f32[8,128,128]{2,1,0:T(8,128)S(1)}, f32[8,128,128]{2,1,0:T(8,128)}, u32[]{:S(2)}) copy-start(f32[8,128,128]{2,1,0:T(8,128)} %shard_map.100) | copy-start | bytes 1572868
  139.1 2.7 %collective-permute-start.11 = (f32[2,8,128,128]{3,2,1,0:T(8,128)S(1)}, f32[2,8,128,128]{3,2,1,0:T(8,128)S(1)}, u32[]{:S(2)}, u32[]{:S(2)}) collective-permute-start(f32[2,8,128,128]{3,2,1,0:T(8,128)S(1)} %pad_maximum_fusion.3), channel_id=1, source_target_pairs={{0,1},{1,0},{2,3},{3,2},{4,5},{5,4},{6,7},{7,6},{8,9},{9,8},{10,11... | collective-permute-start | bytes 3145736 | tf_op jit(solution)/shard_map/ppermute | solution.py:189

commit v10 on v9

--- a/solution.py
+++ b/solution.py
@@ -16,6 +16,15 @@
 SOFTEN = 0.25
 
 H = MB
+
+
+class _Rows:
+    def __init__(self, main, after, before, base, count):
+        self.parts, self.base = (main, after, before), base
+        self.shape = (count, main.shape[1] + after.shape[1] + before.shape[1], main.shape[2])
+
+    def __getitem__(self, i):
+        return jnp.concatenate([p[self.base + i] for p in self.parts], axis=0)
 
 
 def _rolls(a):
@@ -249,11 +258,10 @@
     up_y, down_y = _line_pairs(n_gy)
     from_above = lax.ppermute(ystack[:, height - H:, :], "gy", up_y)
     from_below = lax.ppermute(ystack[:, :H, :], "gy", down_y)
-    frame = jnp.concatenate([ystack, from_below, from_above], axis=1)
-    field = frame[: 2 * depth]
-    material = frame[2 * depth: 3 * depth]
-    winding = frame[3 * depth: 3 * depth + 2]
-    kelvin = frame[3 * depth + 2:]
+    pieces = (ystack, from_below, from_above)
+
+    def planes_of(idx):
+        return jnp.concatenate([p[idx] for p in pieces], axis=-2)
 
     fb = specimen_presence_flags.shape
     flags = jnp.pad(specimen_presence_flags.astype(jnp.float32),
@@ -276,14 +284,14 @@
     both = [(0, 1), (1, 0)]
     if pair:
         top = gz_i == 0
-        first = jnp.concatenate(
-            [jnp.where(top, field[hi_idx], field[lo_idx]),
-             jnp.where(top, kelvin[depth - 1], kelvin[0])[None]], axis=0)
+        first = planes_of(jnp.where(
+            top, jnp.array([depth - 1, 2 * depth - 1, 3 * depth + 2 + depth - 1]),
+            jnp.array([0, depth, 3 * depth + 2])))
         got = lax.ppermute(first, "gz", both)
     else:
-        lo_plane, hi_plane = field[lo_idx], field[hi_idx]
-        tzlo0 = lax.ppermute(kelvin[depth - 1], "gz", up_z)
-        tzhi0 = lax.ppermute(kelvin[0], "gz", down_z)
+        lo_plane, hi_plane = planes_of(lo_idx), planes_of(hi_idx)
+        tzlo0 = lax.ppermute(planes_of(3 * depth + 2 + depth - 1), "gz", up_z)
+        tzhi0 = lax.ppermute(planes_of(3 * depth + 2), "gz", down_z)
     for i, factor in enumerate(WEIGHTS):
         last = i == len(WEIGHTS) - 1
         if pair:
@@ -295,8 +303,11 @@
             outs = (qshape, oshape, tshape, tplane) if pair else (
                 qshape, oshape, tshape, tplane, tplane)
 
-            def fused(pos_r, prof_r, fl_r, f_r, mat_r, w_r, zlo_r, zhi_r, t_r, *rest,
+            def fused(pos_r, prof_r, fl_r, f_r, ys_r, yb_r, ya_r, zlo_r, zhi_r, *rest,
                       factor=factor):
+                mat_r = _Rows(ys_r, yb_r, ya_r, 2 * depth, depth)
+                w_r = _Rows(ys_r, yb_r, ya_r, 3 * depth, 2)
+                t_r = _Rows(ys_r, yb_r, ya_r, 3 * depth + 2, depth)
                 if pair:
                     tzlo_r = tzhi_r = rest[0].at[2]
                     outs_r = rest[1:]
@@ -311,7 +322,7 @@
 
             extra = (got,) if pair else (tzlo0, tzhi0)
             res = _vmem_call(fused, outs, 9 + len(extra), 2)(
-                pos, profile, flags, field, material, winding, zlo, zhi, kelvin, *extra)
+                pos, profile, flags, field, *pieces, zlo, zhi, *extra)
             heat, field_out, kelvin = res[0], res[1], res[2]
             if pair:
                 send_t = res[3]
@@ -319,10 +330,22 @@
                 lo_t, hi_t = res[3], res[4]
         else:
             outs = (fshape, plane2) if pair else (fshape, plane2, plane2)
-            res = _vmem_call(
-                lambda *r, factor=factor: _em_kernel(
-                    factor, False, pair, depth, em_totals, *r), outs, 8, 2
-            )(pos, profile, flags, field, material, winding, zlo, zhi)
+            def sweep(pos_r, prof_r, fl_r, *rest, factor=factor, i=i):
+                if i == 0:
+                    ys_r, yb_r, ya_r = rest[:3]
+                    f_r = _Rows(ys_r, yb_r, ya_r, 0, 2 * depth)
+                    rest = rest[3:]
+                else:
+                    f_r, ys_r, yb_r, ya_r = rest[:4]
+                    rest = rest[4:]
+                mat_r = _Rows(ys_r, yb_r, ya_r, 2 * depth, depth)
+                w_r = _Rows(ys_r, yb_r, ya_r, 3 * depth, 2)
+                _em_kernel(factor, False, pair, depth, em_totals, pos_r, prof_r, fl_r, f_r, mat_r,
+                           w_r, *rest)
+
+            fargs = () if i == 0 else (field,)
+            res = _vmem_call(sweep, outs, 8 + len(fargs), 2)(
+                pos, profile, flags, *fargs, *pieces, zlo, zhi)
             if pair:
                 field, send = res
             else:

time: 144 us -> 138 us (0.958)
  other arithmetic: 15 us -> 8.4 us
  local copies, waits for them, and re-layouts: 22 us -> 19.3 us
  Pallas kernels: 36 us -> 37.9 us
  waiting for transfers between devices: 50.1 us -> 51.9 us
    slice x3 -> x1, local copies, waits for them, and re-layouts: 5.16 us -> 0.04 us  [on_device(): from_above = lax.ppermute(ystack[:, height - H:, :], 'gy', up_y)]
    ppermute x1, waiting for transfers between devices: 3.6 us -> 7.85 us  [on_device(): got = lax.ppermute(first, 'gz', both)]
    concatenate x2, other arithmetic: 6.58 us -> 2.91 us  [the longest x1 2.88 us: on_device(): ystack = jnp.concatenate([xext, t_x], axis=0)]
    gather x2 -> x3, local copies, waits for them, and re-layouts: 1.14 us -> 3.93 us  [planes_of(): return jnp.concatenate([p[idx] for p in pieces], axis=-2)]
    unnamed x34 -> x30, local copies, waits for them, and re-layouts: 8.4 us -> 6.26 us
    slice x1 -> x0, other arithmetic: 2.01 us -> none  [on_device(): from_below = lax.ppermute(ystack[:, :H, :], 'gy', down_y)]
    ppermute x1, waiting for transfers between devices: 4.47 us -> 2.48 us  [on_device(): from_below = lax.ppermute(ystack[:, :H, :], 'gy', down_y)]
  transfers between devices with their start and end apart: 12 -> 12, of which waited for: 10 -> 10; matrix products, arithmetic and copies ran while one was open for 7% -> 8% of each run, Pallas kernels for 0% -> 0%
where the time goes in v10:
time: 138 us; the launch traced here: 137 us
  waiting for transfers between devices  51.9 us (38%)
  Pallas kernels  37.9 us (27%)
  local copies, waits for them, and re-layouts  19.3 us (14%)
  starting transfers between devices  18 us (13%)
  other arithmetic  8.4 us (6%)
  between operations  1.55 us (1%)
    ppermute x3, waiting for transfers between devices, on_device(): tzlo = tzhi = lax.ppermute(send_t, 'gz', both)  14.8 us
    pallas_call x3, Pallas kernels, on_device(): _vmem_call(lambda *r, last=last: _heat_kernel(last, pair, depth, t_totals...  14.8 us
    pallas_call x2, Pallas kernels, on_device(): _vmem_call(sweep, outs, 8 + len(fargs), 2)  13.6 us
    ppermute x2, waiting for transfers between devices, on_device(): zlo = zhi = got if i == 0 else lax.ppermute(send, 'gz', both)  13.5 us
    ppermute x1, waiting for transfers between devices, _broadcast_blocks(): r1 = lax.ppermute(own, 'gx', [(2, 0), (3, 1), (1, 2)])  9.96 us
    pallas_call x1, Pallas kernels, on_device(): _vmem_call(fused, outs, 9 + len(extra), 2)  9.58 us
    ppermute x1, waiting for transfers between devices, on_device(): got = lax.ppermute(first, 'gz', both)  7.85 us
    unnamed x30, local copies, waits for them, and re-layouts  6.26 us
  transfers between devices with their start and end apart: 12, of which 10 were waited for; matrix products, arithmetic and copies ran while one was open for 8% of the time, Pallas kernels for 0%

profile of v10, /device:TPU:0, one launch (start us, length us, event | category | flops | bytes accessed | tf_op | source)
XLA Modules:
  0.0 137.1 jit_solution(1443036892153013780)
XLA Ops:
  0.6 1.6 %pad_maximum_fusion = f32[26,128,128]{2,1,0:T(8,128)S(1)} fusion(f32[2,128,128]{2,1,0:T(8,128)} %param.10, f32[8,128,128]{2,1,0:T(8,128)} %param.9, f32[16,128,128]{2,1,0:T(8,128)} %bitcast.31), kind=kLoop, calls=%fused_computation.8 | loop fusion | flops 851968 | bytes 3407872 | tf_op jit(solution)/shard_map/concatenate | solution.py:240
  2.8 1.1 copy.10
  3.9 1.4 %collective-permute-start = (f32[26,8,128]{2,1,0:T(8,128)}, f32[26,8,128]{2,1,0:T(8,128)S(1)}, u32[]{:S(2)}, u32[]{:S(2)}) collective-permute-start(f32[26,8,128]{2,1,0:T(8,128)} %copy.10), channel_id=1, source_target_pairs={{1,0},{2,1},{3,2},{5,4},{6,5},{7,6},{9,8},{10,9},{11,10},{13,12},{... | collective-permute-start | bytes 319496 | tf_op jit(solution)/shard_map/ppermute | solution.py:245
  5.4 1.1 copy.12
  6.5 3.7 %collective-permute-start.1 = (f32[26,8,128]{2,1,0:T(8,128)}, f32[26,8,128]{2,1,0:T(8,128)}, u32[]{:S(2)}, u32[]{:S(2)}) collective-permute-start(f32[26,8,128]{2,1,0:T(8,128)} %copy.12), channel_id=1, source_target_pairs={{0,1},{1,2},{2,3},{4,5},{5,6},{6,7},{8,9},{9,10},{10,11},{12,13},{... | collective-permute-start | bytes 319496 | tf_op jit(solution)/shard_map/ppermute | solution.py:244
  11.5 1.3 pad_dynamic-slice_fusion.1
  14.4 1.4 %copy.13 = f32[26,8,128]{1,2,0:T(8,128)S(1)} copy(f32[26,8,128]{2,1,0:T(8,128)} %collective-permute-done.1) | data formatting | bytes 212992 | tf_op jit(solution)/shard_map/ppermute | solution.py:244
  15.8 2.9 %maximum_maximum_fusion.rest_0_.rest_1_.ys_r = f32[34,128,256]{2,1,0:T(8,128)S(1)} fusion(f32[8,128,8]{2,1,0:T(8,128)} %pad_dynamic-slice_fusion, f32[8,128,136]{2,1,0:T(8,128)} %pad_dynamic-slice_fusion.1, f32[26,128,8]{2,1,0:T(8,128)S(1)} %bitcast.30, f32[26,128,8]{2,1,0:T(8,128)S(1)} %bitcast.29, f32[2,128,128]{2,1,0:T(8,128)S(1)} %copy-done.11, ...), kind=kLoop, calls=%fused_computation.3 | loop fusion | flops 8912896 | bytes 7032832 | tf_op jit(solution)/shard_map/concatenate | solution.py:257
  18.7 2.0 %copy-done = f32[34,128,256]{2,1,0:T(8,128)} copy-done((f32[34,128,256]{2,1,0:T(8,128)}, f32[34,128,256]{2,1,0:T(8,128)S(1)}, u32[]{:S(2)}) %copy-start) | copy-done | bytes 4456472
  20.8 1.3 collective-permute-start.2
  22.1 5.8 %collective-permute-start.3 = (f32[34,8,256]{2,1,0:T(8,128)S(1)}, f32[34,8,256]{2,1,0:T(8,128)S(1)}, u32[]{:S(2)}, u32[]{:S(2)}) collective-permute-start(f32[34,8,256]{2,1,0:T(8,128)S(1)} %get-tuple-element.26), channel_id=1, source_target_pairs={{0,4},{4,8},{8,12},{1,5},{5,9},{9,13},{2,6},{6,10},{10,14},{3,7},{... | collective-permute-start | bytes 835592 | tf_op jit(solution)/shard_map/ppermute | solution.py:259
  27.9 2.8 %gather_fusion = f32[3,128,256]{2,1,0:T(8,128)S(1)} fusion(f32[34,128,256]{2,1,0:T(8,128)} %copy-done, s32[1024]{0:T(1024)S(1)} %pad_clamp_fusion), kind=kCustom, calls=%fused_computation | custom fusion | bytes 786444 | tf_op jit(solution)/shard_map/gather | solution.py:264
  30.7 2.5 %collective-permute-done.2.rest_1_.rest_2_.yb_r = f32[34,8,256]{2,1,0:T(8,128)S(1)} collective-permute-done((f32[34,8,256]{2,1,0:T(8,128)S(1)}, f32[34,8,256]{2,1,0:T(8,128)S(1)}, u32[]{:S(2)}, u32[]{:S(2)}) %collective-permute-start.2) | collective-permute-done | bytes 278560 | tf_op jit(solution)/shard_map/ppermute | solution.py:260
  35.0 1.6 %collective-permute-start.4 = (f32[3,144,256]{2,1,0:T(8,128)S(1)}, f32[3,144,256]{2,1,0:T(8,128)S(1)}, u32[]{:S(2)}, u32[]{:S(2)}) collective-permute-start(f32[3,144,256]{2,1,0:T(8,128)S(1)} %pad_maximum_fusion.3), channel_id=1, source_target_pairs={{0,16},{16,0},{1,17},{17,1},{2,18},{18,2},{3,19},{19,3},{4,20},{20... | collective-permute-start | bytes 1327112 | tf_op jit(solution)/shard_map/ppermute | solution.py:290
  39.1 7.8 %collective-permute-done.4.rest_3_.rest_4_.rest_0_ = f32[3,144,256]{2,1,0:T(8,128)S(1)} collective-permute-done((f32[3,144,256]{2,1,0:T(8,128)S(1)}, f32[3,144,256]{2,1,0:T(8,128)S(1)}, u32[]{:S(2)}, u32[]{:S(2)}) %collective-permute-start.4) | collective-permute-done | bytes 442400 | tf_op jit(solution)/shard_map/ppermute | solution.py:290
  47.7 6.5 %shard_map.95 = (f32[16,144,256]{2,1,0:T(8,128)}, f32[2,144,256]{2,1,0:T(8,128)}) custom-call(s32[3]{0:T(128)} %pad_add_fusion.pos_r.r_0_, f32[8]{0:T(128)} %add_divide_fusion.prof_r, f32[2,128,128]{2,1,0:T(8,128)} %pad.8.fl_r.r_1_, f32[34,128,256]{2,1,0:T(8,128)} %copy-done, f32[34,8,256]{2,1,0:T(8,128)} %copy-done.4, f32[34,8,256]{2,1,0:T(8,128)} %copy-done.5, ...), custom_call_target="tpu_custom_call" | custom-call | tf_op jit(solution)/shard_map/pallas_call | solution.py:347
  54.3 1.1 collective-permute-start.5
  55.3 7.0 %collective-permute-done.5.rest_4_.rest_5_ = f32[2,144,256]{2,1,0:T(8,128)S(1)} collective-permute-done((f32[2,144,256]{2,1,0:T(8,128)}, f32[2,144,256]{2,1,0:T(8,128)S(1)}, u32[]{:S(2)}, u32[]{:S(2)}) %collective-permute-start.5) | collective-permute-done | bytes 294944 | tf_op jit(solution)/shard_map/ppermute | solution.py:298
  63.0 7.0 %shard_map.96 = (f32[16,144,256]{2,1,0:T(8,128)}, f32[2,144,256]{2,1,0:T(8,128)}) custom-call(s32[3]{0:T(128)} %pad_add_fusion.pos_r.r_0_, f32[8]{0:T(128)} %add_divide_fusion.prof_r, f32[2,128,128]{2,1,0:T(8,128)} %pad.8.fl_r.r_1_, f32[16,144,256]{2,1,0:T(8,128)} %get-tuple-element.14.rest_0_, f32[34,128,256]{2,1,0:T(8,128)} %copy-done, ...), custom_call_target="tpu_custom_call" | custom-call | tf_op jit(solution)/shard_map/pallas_call | solution.py:347
  70.7 6.5 %collective-permute-done.6.zlo_r.zhi_r = f32[2,144,256]{2,1,0:T(8,128)S(1)} collective-permute-done((f32[2,144,256]{2,1,0:T(8,128)}, f32[2,144,256]{2,1,0:T(8,128)S(1)}, u32[]{:S(2)}, u32[]{:S(2)}) %collective-permute-start.6) | collective-permute-done | bytes 294944 | tf_op jit(solution)/shard_map/ppermute | solution.py:298
  78.0 9.6 %shard_map.97 = (f32[8,144,256]{2,1,0:T(8,128)}, f32[2,8,128,128]{3,2,1,0:T(8,128)}, f32[8,144,256]{2,1,0:T(8,128)}, f32[144,256]{1,0:T(8,128)}) custom-call(s32[3]{0:T(128)} %pad_add_fusion.pos_r.r_0_, f32[8]{0:T(128)} %add_divide_fusion.prof_r, f32[2,128,128]{2,1,0:T(8,128)} %pad.8.fl_r.r_1_, f32[16,144,256]{2,1,0:T(8,128)} %get-tuple-element.16.f_r, ...), custom_call_target="tpu_custom_call" | custom-call | tf_op jit(solution)/shard_map/pallas_call | solution.py:324
  88.0 4.9 %collective-permute-done.7.r_4_.r_5_ = f32[144,256]{1,0:T(8,128)S(1)} collective-permute-done((f32[144,256]{1,0:T(8,128)}, f32[144,256]{1,0:T(8,128)S(1)}, u32[]{:S(2)}, u32[]{:S(2)}) %collective-permute-start.7) | collective-permute-done | bytes 147488 | tf_op jit(solution)/shard_map/ppermute | solution.py:357
  93.6 5.5 %shard_map.98 = (f32[8,144,256]{2,1,0:T(8,128)}, f32[144,256]{1,0:T(8,128)}) custom-call(s32[3]{0:T(128)} %pad_add_fusion.pos_r.r_0_, f32[2,128,128]{2,1,0:T(8,128)} %pad.8.fl_r.r_1_, f32[8,144,256]{2,1,0:T(8,128)} %get-tuple-element.19.r_2_, f32[8,144,256]{2,1,0:T(8,128)} %get-tuple-element.20.r_3_, f32[144,256]{1,0:T(8,128)} %copy-done.10, ...), custom_call_target="tpu_custom_call" | custom-call | tf_op jit(solution)/shard_map/pallas_call | solution.py:362
  99.5 4.9 %collective-permute-done.8.r_4_.r_5_ = f32[144,256]{1,0:T(8,128)S(1)} collective-permute-done((f32[144,256]{1,0:T(8,128)}, f32[144,256]{1,0:T(8,128)S(1)}, u32[]{:S(2)}, u32[]{:S(2)}) %collective-permute-start.8) | collective-permute-done | bytes 147488 | tf_op jit(solution)/shard_map/ppermute | solution.py:357
  105.1 5.3 %shard_map.99 = (f32[8,144,256]{2,1,0:T(8,128)}, f32[144,256]{1,0:T(8,128)}) custom-call(s32[3]{0:T(128)} %pad_add_fusion.pos_r.r_0_, f32[2,128,128]{2,1,0:T(8,128)} %pad.8.fl_r.r_1_, f32[8,144,256]{2,1,0:T(8,128)} %get-tuple-element.22.r_2_, f32[8,144,256]{2,1,0:T(8,128)} %get-tuple-element.20.r_3_, f32[144,256]{1,0:T(8,128)} %copy-done.9, f32[144,256]{1,0:T(8,128)} %copy-done.9), custom_call_target="tpu_custom_call" | custom-call | tf_op jit(solution)/shard_map/pallas_call | solution.py:362
  110.8 4.9 %collective-permute-done.9.r_4_.r_5_ = f32[144,256]{1,0:T(8,128)S(1)} collective-permute-done((f32[144,256]{1,0:T(8,128)}, f32[144,256]{1,0:T(8,128)S(1)}, u32[]{:S(2)}, u32[]{:S(2)}) %collective-permute-start.9) | collective-permute-done | bytes 147488 | tf_op jit(solution)/shard_map/ppermute | solution.py:357
  116.4 3.9 %shard_map.100 = f32[8,128,128]{2,1,0:T(8,128)} custom-call(s32[3]{0:T(128)} %pad_add_fusion.pos_r.r_0_, f32[2,128,128]{2,1,0:T(8,128)} %pad.8.fl_r.r_1_, f32[8,144,256]{2,1,0:T(8,128)} %get-tuple-element.24.r_2_, f32[8,144,256]{2,1,0:T(8,128)} %get-tuple-element.20.r_3_, f32[144,256]{1,0:T(8,128)} %copy-done.8, f32[144,256]{1,0:T(8,128)} %copy-done.8), custom_call_target="tpu_custom_call" | custom-call | tf_op jit(solution)/shard_map/pallas_call | solution.py:362
  120.4 1.3 collective-permute-start.10
  121.7 10.0 %collective-permute-done.10 = f32[8,128,128]{2,1,0:T(8,128)S(1)} collective-permute-done((f32[8,128,128]{2,1,0:T(8,128)}, f32[8,128,128]{2,1,0:T(8,128)S(1)}, u32[]{:S(2)}, u32[]{:S(2)}) %collective-permute-start.10) | collective-permute-done | bytes 524320 | tf_op jit(solution)/shard_map/ppermute | solution.py:195
  131.6 1.1 select_bitcast_fusion.1
  132.9 2.6 %collective-permute-done.11 = f32[2,8,128,128]{3,2,1,0:T(8,128)S(1)} collective-permute-done((f32[2,8,128,128]{3,2,1,0:T(8,128)S(1)}, f32[2,8,128,128]{3,2,1,0:T(8,128)S(1)}, u32[]{:S(2)}, u32[]{:S(2)}) %collective-permute-start.11) | collective-permute-done | bytes 1048608 | tf_op jit(solution)/shard_map/ppermute | solution.py:198
  135.8 1.3 pad_maximum_fusion.1
  (56 shorter events, 13.7 us)
Async XLA Ops:
  3.9 7.6 %copy-start.1 = (f32[8,128,384]{2,1,0:T(8,128)S(1)}, f32[8,128,384]{2,1,0:T(8,128)}, u32[]{:S(2)}) copy-start(f32[8,128,384]{2,1,0:T(8,128)} %param.13) | copy-start | bytes 4718596
  3.9 9.9 %collective-permute-start = (f32[26,8,128]{2,1,0:T(8,128)}, f32[26,8,128]{2,1,0:T(8,128)S(1)}, u32[]{:S(2)}, u32[]{:S(2)}) collective-permute-start(f32[26,8,128]{2,1,0:T(8,128)} %copy.10), channel_id=1, source_target_pairs={{1,0},{2,1},{3,2},{5,4},{6,5},{7,6},{9,8},{10,9},{11,10},{13,12},{... | collective-permute-start | bytes 319496 | tf_op jit(solution)/shard_map/ppermute | solution.py:245
  6.5 7.9 %collective-permute-start.1 = (f32[26,8,128]{2,1,0:T(8,128)}, f32[26,8,128]{2,1,0:T(8,128)}, u32[]{:S(2)}, u32[]{:S(2)}) collective-permute-start(f32[26,8,128]{2,1,0:T(8,128)} %copy.12), channel_id=1, source_target_pairs={{0,1},{1,2},{2,3},{4,5},{5,6},{6,7},{8,9},{9,10},{10,11},{12,13},{... | collective-permute-start | bytes 319496 | tf_op jit(solution)/shard_map/ppermute | solution.py:244
  13.8 1.9 %copy-start.11 = (f32[2,128,128]{2,1,0:T(8,128)S(1)}, f32[2,128,128]{2,1,0:T(8,128)}, u32[]{:S(2)}) copy-start(f32[2,128,128]{2,1,0:T(8,128)} %param.10) | copy-start | bytes 393220
  15.8 12.1 %copy-start.13 = (s32[3]{0:T(128)S(1)}, s32[3]{0:T(128)}, u32[]{:S(2)}) copy-start(s32[3]{0:T(128)} %constant.76.clone) | copy-start | bytes 40
  15.8 12.1 %copy-start.14 = (s32[3]{0:T(128)S(1)}, s32[3]{0:T(128)}, u32[]{:S(2)}) copy-start(s32[3]{0:T(128)} %constant.77.clone) | copy-start | bytes 40
  18.7 2.0 %copy-start = (f32[34,128,256]{2,1,0:T(8,128)}, f32[34,128,256]{2,1,0:T(8,128)S(1)}, u32[]{:S(2)}) copy-start(f32[34,128,256]{2,1,0:T(8,128)S(1)} %maximum_maximum_fusion.rest_0_.rest_1_.ys_r) | copy-start | bytes 13369348
  20.7 16.5 %copy-start.12 = (s32[2,64,64]{2,1,0:T(8,128)S(1)}, s32[2,64,64]{2,1,0:T(8,128)}, u32[]{:S(2)}) copy-start(s32[2,64,64]{2,1,0:T(8,128)} %param.12) | copy-start | bytes 98308
  20.8 12.4 %collective-permute-start.2 = (f32[34,8,256]{2,1,0:T(8,128)S(1)}, f32[34,8,256]{2,1,0:T(8,128)S(1)}, u32[]{:S(2)}, u32[]{:S(2)}) collective-permute-start(f32[34,8,256]{2,1,0:T(8,128)S(1)} %get-tuple-element.27), channel_id=1, source_target_pairs={{4,0},{8,4},{12,8},{5,1},{9,5},{13,9},{6,2},{10,6},{14,10},{7,3},{... | collective-permute-start | bytes 835592 | tf_op jit(solution)/shard_map/ppermute | solution.py:260
  22.1 12.3 %collective-permute-start.3 = (f32[34,8,256]{2,1,0:T(8,128)S(1)}, f32[34,8,256]{2,1,0:T(8,128)S(1)}, u32[]{:S(2)}, u32[]{:S(2)}) collective-permute-start(f32[34,8,256]{2,1,0:T(8,128)S(1)} %get-tuple-element.26), channel_id=1, source_target_pairs={{0,4},{4,8},{8,12},{1,5},{5,9},{9,13},{2,6},{6,10},{10,14},{3,7},{... | collective-permute-start | bytes 835592 | tf_op jit(solution)/shard_map/ppermute | solution.py:259
  33.2 13.7 %copy-start.4 = (f32[34,8,256]{2,1,0:T(8,128)}, f32[34,8,256]{2,1,0:T(8,128)S(1)}, u32[]{:S(2)}) copy-start(f32[34,8,256]{2,1,0:T(8,128)S(1)} %collective-permute-done.2.rest_1_.rest_2_.yb_r) | copy-start | bytes 835588
  34.4 12.6 %copy-start.5 = (f32[34,8,256]{2,1,0:T(8,128)}, f32[34,8,256]{2,1,0:T(8,128)S(1)}, u32[]{:S(2)}) copy-start(f32[34,8,256]{2,1,0:T(8,128)S(1)} %collective-permute-done.3.rest_2_.rest_3_.ya_r) | copy-start | bytes 835588
  35.0 12.0 %collective-permute-start.4 = (f32[3,144,256]{2,1,0:T(8,128)S(1)}, f32[3,144,256]{2,1,0:T(8,128)S(1)}, u32[]{:S(2)}, u32[]{:S(2)}) collective-permute-start(f32[3,144,256]{2,1,0:T(8,128)S(1)} %pad_maximum_fusion.3), channel_id=1, source_target_pairs={{0,16},{16,0},{1,17},{17,1},{2,18},{18,2},{3,19},{19,3},{4,20},{20... | collective-permute-start | bytes 1327112 | tf_op jit(solution)/shard_map/ppermute | solution.py:290
  47.0 0.8 copy-start.3
  54.3 8.1 %collective-permute-start.5 = (f32[2,144,256]{2,1,0:T(8,128)}, f32[2,144,256]{2,1,0:T(8,128)S(1)}, u32[]{:S(2)}, u32[]{:S(2)}) collective-permute-start(f32[2,144,256]{2,1,0:T(8,128)} %get-tuple-element.15), channel_id=1, source_target_pairs={{0,16},{16,0},{1,17},{17,1},{2,18},{18,2},{3,19},{19,3},{4,20},{20... | collective-permute-start | bytes 884744 | tf_op jit(solution)/shard_map/ppermute | solution.py:298
  62.3 0.7 copy-start.7
  70.1 7.2 %collective-permute-start.6 = (f32[2,144,256]{2,1,0:T(8,128)}, f32[2,144,256]{2,1,0:T(8,128)S(1)}, u32[]{:S(2)}, u32[]{:S(2)}) collective-permute-start(f32[2,144,256]{2,1,0:T(8,128)} %get-tuple-element.17), channel_id=1, source_target_pairs={{0,16},{16,0},{1,17},{17,1},{2,18},{18,2},{3,19},{19,3},{4,20},{20... | collective-permute-start | bytes 884744 | tf_op jit(solution)/shard_map/ppermute | solution.py:298
  77.2 0.7 copy-start.6
  87.6 5.4 %collective-permute-start.7 = (f32[144,256]{1,0:T(8,128)}, f32[144,256]{1,0:T(8,128)S(1)}, u32[]{:S(2)}, u32[]{:S(2)}) collective-permute-start(f32[144,256]{1,0:T(8,128)} %get-tuple-element.21), channel_id=1, source_target_pairs={{0,16},{16,0},{1,17},{17,1},{2,18},{18,2},{3,19},{19,3},{4,20},{20... | collective-permute-start | bytes 442376 | tf_op jit(solution)/shard_map/ppermute | solution.py:357
  92.9 0.7 copy-start.10
  99.1 5.4 %collective-permute-start.8 = (f32[144,256]{1,0:T(8,128)}, f32[144,256]{1,0:T(8,128)S(1)}, u32[]{:S(2)}, u32[]{:S(2)}) collective-permute-start(f32[144,256]{1,0:T(8,128)} %get-tuple-element.23), channel_id=1, source_target_pairs={{0,16},{16,0},{1,17},{17,1},{2,18},{18,2},{3,19},{19,3},{4,20},{20... | collective-permute-start | bytes 442376 | tf_op jit(solution)/shard_map/ppermute | solution.py:357
  104.4 0.7 copy-start.9
  110.4 5.4 %collective-permute-start.9 = (f32[144,256]{1,0:T(8,128)}, f32[144,256]{1,0:T(8,128)S(1)}, u32[]{:S(2)}, u32[]{:S(2)}) collective-permute-start(f32[144,256]{1,0:T(8,128)} %get-tuple-element.25), channel_id=1, source_target_pairs={{0,16},{16,0},{1,17},{17,1},{2,18},{18,2},{3,19},{19,3},{4,20},{20... | collective-permute-start | bytes 442376 | tf_op jit(solution)/shard_map/ppermute | solution.py:357
  115.8 0.7 copy-start.8
  120.4 11.3 %collective-permute-start.10 = (f32[8,128,128]{2,1,0:T(8,128)}, f32[8,128,128]{2,1,0:T(8,128)S(1)}, u32[]{:S(2)}, u32[]{:S(2)}) collective-permute-start(f32[8,128,128]{2,1,0:T(8,128)} %shard_map.100), channel_id=1, source_target_pairs={{2,0},{3,1},{1,2},{6,4},{7,5},{5,6},{10,8},{11,9},{9,10},{14,12},{... | collective-permute-start | bytes 1572872 | tf_op jit(solution)/shard_map/ppermute | solution.py:195
  121.7 13.9 %copy-start.2 = (f32[8,128,128]{2,1,0:T(8,128)S(1)}, f32[8,128,128]{2,1,0:T(8,128)}, u32[]{:S(2)}) copy-start(f32[8,128,128]{2,1,0:T(8,128)} %shard_map.100) | copy-start | bytes 1572868
  132.9 2.7 %collective-permute-start.11 = (f32[2,8,128,128]{3,2,1,0:T(8,128)S(1)}, f32[2,8,128,128]{3,2,1,0:T(8,128)S(1)}, u32[]{:S(2)}, u32[]{:S(2)}) collective-permute-start(f32[2,8,128,128]{3,2,1,0:T(8,128)S(1)} %pad_maximum_fusion.2), channel_id=1, source_target_pairs={{0,1},{1,0},{2,3},{3,2},{4,5},{5,4},{6,7},{7,6},{8,9},{9,8},{10,11... | collective-permute-start | bytes 3145736 | tf_op jit(solution)/shard_map/ppermute | solution.py:198

commit v11 on v10

--- a/solution.py
+++ b/solution.py
@@ -261,7 +261,9 @@
     pieces = (ystack, from_below, from_above)
 
     def planes_of(idx):
-        return jnp.concatenate([p[idx] for p in pieces], axis=-2)
+        if isinstance(idx, int):
+            return jnp.concatenate([p[idx] for p in pieces], axis=0)
+        return jnp.stack([planes_of(i) for i in idx])
 
     fb = specimen_presence_flags.shape
     flags = jnp.pad(specimen_presence_flags.astype(jnp.float32),
@@ -284,12 +286,11 @@
     both = [(0, 1), (1, 0)]
     if pair:
         top = gz_i == 0
-        first = planes_of(jnp.where(
-            top, jnp.array([depth - 1, 2 * depth - 1, 3 * depth + 2 + depth - 1]),
-            jnp.array([0, depth, 3 * depth + 2])))
+        first = jnp.where(top, planes_of([depth - 1, 2 * depth - 1, 3 * depth + 2 + depth - 1]),
+                          planes_of([0, depth, 3 * depth + 2]))
         got = lax.ppermute(first, "gz", both)
     else:
-        lo_plane, hi_plane = planes_of(lo_idx), planes_of(hi_idx)
+        lo_plane, hi_plane = planes_of([0, depth]), planes_of([depth - 1, 2 * depth - 1])
         tzlo0 = lax.ppermute(planes_of(3 * depth + 2 + depth - 1), "gz", up_z)
         tzhi0 = lax.ppermute(planes_of(3 * depth + 2), "gz", down_z)
     for i, factor in enumerate(WEIGHTS):

time: 138 us -> 141 us (1.022)
  other arithmetic: 8.4 us -> 11.5 us
  waiting for transfers between devices: 51.9 us -> 53.6 us
  local copies, waits for them, and re-layouts: 19.3 us -> 17.7 us
    gather x3 -> x0, local copies, waits for them, and re-layouts: 3.93 us -> none  [planes_of(): return jnp.concatenate([p[idx] for p in pieces], axis=-2)]
    unnamed x30 -> x42, local copies, waits for them, and re-layouts: 6.26 us -> 8.81 us
    squeeze x0 -> x3, other arithmetic: none -> 2.11 us  [planes_of(): return jnp.concatenate([p[idx] for p in pieces], axis=0)]
  transfers between devices with their start and end apart: 12 -> 12, of which waited for: 10 -> 10; matrix products, arithmetic and copies ran while one was open for 8% -> 6% of each run, Pallas kernels for 0% -> 0%
where the time goes in v11:
time: 141 us
  waiting for transfers between devices  53.6 us (38%)
  Pallas kernels  38 us (27%)
  starting transfers between devices  18.3 us (13%)
  local copies, waits for them, and re-layouts  17.7 us (13%)
  other arithmetic  11.5 us (8%)
  between operations  1.63 us (1%)
    ppermute x3, waiting for transfers between devices, on_device(): tzlo = tzhi = lax.ppermute(send_t, 'gz', both)  14.8 us
    pallas_call x3, Pallas kernels, on_device(): _vmem_call(lambda *r, last=last: _heat_kernel(last, pair, depth, t_totals...  14.8 us
    pallas_call x2, Pallas kernels, on_device(): _vmem_call(sweep, outs, 8 + len(fargs), 2)  13.6 us
    ppermute x2, waiting for transfers between devices, on_device(): zlo = zhi = got if i == 0 else lax.ppermute(send, 'gz', both)  13.5 us
    ppermute x1, waiting for transfers between devices, _broadcast_blocks(): r1 = lax.ppermute(own, 'gx', [(2, 0), (3, 1), (1, 2)])  9.96 us
    pallas_call x1, Pallas kernels, on_device(): _vmem_call(fused, outs, 9 + len(extra), 2)  9.62 us
    unnamed x42, local copies, waits for them, and re-layouts  8.81 us
    ppermute x1, waiting for transfers between devices, on_device(): got = lax.ppermute(first, 'gz', both)  7.95 us
  transfers between devices with their start and end apart: 12, of which 10 were waited for; matrix products, arithmetic and copies ran while one was open for 6% of the time, Pallas kernels for 0%

profile of v11, /device:TPU:0, one launch (start us, length us, event | category | flops | bytes accessed | tf_op | source)
XLA Modules:
  0.0 140.7 jit_solution(10420544641528178152)
XLA Ops:
  0.6 1.6 %pad_maximum_fusion = f32[26,128,128]{2,1,0:T(8,128)S(1)} fusion(f32[2,128,128]{2,1,0:T(8,128)} %param.8, f32[8,128,128]{2,1,0:T(8,128)} %param.7, f32[16,128,128]{2,1,0:T(8,128)} %bitcast.83), kind=kLoop, calls=%fused_computation.5 | loop fusion | flops 851968 | bytes 3407872 | tf_op jit(solution)/shard_map/concatenate | solution.py:240
  3.3 1.4 %collective-permute-start = (f32[26,8,128]{2,1,0:T(8,128)S(1)}, f32[26,8,128]{2,1,0:T(8,128)S(1)}, u32[]{:S(2)}, u32[]{:S(2)}) collective-permute-start(f32[26,8,128]{2,1,0:T(8,128)S(1)} %copy.8), channel_id=1, source_target_pairs={{1,0},{2,1},{3,2},{5,4},{6,5},{7,6},{9,8},{10,9},{11,10},{13,12},{... | collective-permute-start | bytes 319496 | tf_op jit(solution)/shard_map/ppermute | solution.py:245
  4.7 1.1 copy.10
  5.8 3.7 %collective-permute-start.1 = (f32[26,8,128]{2,1,0:T(8,128)}, f32[26,8,128]{2,1,0:T(8,128)}, u32[]{:S(2)}, u32[]{:S(2)}) collective-permute-start(f32[26,8,128]{2,1,0:T(8,128)} %copy.10), channel_id=1, source_target_pairs={{0,1},{1,2},{2,3},{4,5},{5,6},{6,7},{8,9},{9,10},{10,11},{12,13},{... | collective-permute-start | bytes 319496 | tf_op jit(solution)/shard_map/ppermute | solution.py:244
  9.5 1.3 pad_dynamic-slice_fusion.1
  12.3 1.4 %copy.11 = f32[26,8,128]{1,2,0:T(8,128)S(1)} copy(f32[26,8,128]{2,1,0:T(8,128)} %collective-permute-done.1) | data formatting | bytes 212992 | tf_op jit(solution)/shard_map/ppermute | solution.py:244
  14.1 1.2 copy-done.3
  15.9 3.8 %maximum_maximum_fusion.rest_0_.rest_1_.ys_r = f32[34,128,256]{2,1,0:T(8,128)S(1)} fusion(f32[8,128,8]{2,1,0:T(8,128)} %pad_dynamic-slice_fusion, f32[8,128,112]{2,1,0:T(8,128)S(1)} %broadcast_in_dim.7, f32[8,128,136]{2,1,0:T(8,128)S(1)} %copy-done.5, f32[26,128,8]{2,1,0:T(8,128)S(1)} %bitcast.80, f32[26,128,112]{2,1,0:T(8,128)S(1)} %broadcast_in_dim.6, ...), kind=kLoop, calls=%fused_computation | loop fusion | flops 8912896 | bytes 8912896 | tf_op jit(solution)/shard_map/concatenate | solution.py:257
  19.8 2.1 %copy-done = f32[34,128,256]{2,1,0:T(8,128)} copy-done((f32[34,128,256]{2,1,0:T(8,128)}, f32[34,128,256]{2,1,0:T(8,128)S(1)}, u32[]{:S(2)}) %copy-start) | copy-done | bytes 4456472
  22.7 1.3 collective-permute-start.2
  24.9 6.0 %collective-permute-start.3 = (f32[34,8,256]{2,1,0:T(8,128)}, f32[34,8,256]{2,1,0:T(8,128)S(1)}, u32[]{:S(2)}, u32[]{:S(2)}) collective-permute-start(f32[34,8,256]{2,1,0:T(8,128)} %get-tuple-element.29), channel_id=1, source_target_pairs={{0,4},{4,8},{8,12},{1,5},{5,9},{9,13},{2,6},{6,10},{10,14},{3,7},{... | collective-permute-start | bytes 835592 | tf_op jit(solution)/shard_map/ppermute | solution.py:259
  30.9 1.2 maximum_bitcast_fusion.6
  32.2 3.2 %collective-permute-done.2.rest_1_.rest_2_.yb_r = f32[34,8,256]{2,1,0:T(8,128)} collective-permute-done((f32[34,8,256]{2,1,0:T(8,128)}, f32[34,8,256]{2,1,0:T(8,128)}, u32[]{:S(2)}, u32[]{:S(2)}) %collective-permute-start.2) | collective-permute-done | bytes 278560 | tf_op jit(solution)/shard_map/ppermute | solution.py:260
  36.3 1.5 %collective-permute-done.3.rest_2_.rest_3_.ya_r = f32[34,8,256]{2,1,0:T(8,128)S(1)} collective-permute-done((f32[34,8,256]{2,1,0:T(8,128)}, f32[34,8,256]{2,1,0:T(8,128)S(1)}, u32[]{:S(2)}, u32[]{:S(2)}) %collective-permute-start.3) | collective-permute-done | bytes 278560 | tf_op jit(solution)/shard_map/ppermute | solution.py:259
  38.5 1.6 %collective-permute-start.4 = (f32[3,144,256]{2,1,0:T(8,128)S(1)}, f32[3,144,256]{2,1,0:T(8,128)S(1)}, u32[]{:S(2)}, u32[]{:S(2)}) collective-permute-start(f32[3,144,256]{2,1,0:T(8,128)S(1)} %maximum_select_fusion), channel_id=1, source_target_pairs={{0,16},{16,0},{1,17},{17,1},{2,18},{18,2},{3,19},{19,3},{4,20},{20... | collective-permute-start | bytes 1327112 | tf_op jit(solution)/shard_map/ppermute | solution.py:291
  42.6 7.9 %collective-permute-done.4.rest_3_.rest_4_.rest_0_ = f32[3,144,256]{2,1,0:T(8,128)S(1)} collective-permute-done((f32[3,144,256]{2,1,0:T(8,128)S(1)}, f32[3,144,256]{2,1,0:T(8,128)S(1)}, u32[]{:S(2)}, u32[]{:S(2)}) %collective-permute-start.4) | collective-permute-done | bytes 442400 | tf_op jit(solution)/shard_map/ppermute | solution.py:291
  51.3 6.5 %shard_map.77 = (f32[16,144,256]{2,1,0:T(8,128)}, f32[2,144,256]{2,1,0:T(8,128)}) custom-call(s32[3]{0:T(128)} %pad_add_fusion.pos_r.r_0_, f32[8]{0:T(128)} %add_divide_fusion.prof_r, f32[2,128,128]{2,1,0:T(8,128)} %pad.8.fl_r.r_1_, f32[34,128,256]{2,1,0:T(8,128)} %copy-done, f32[34,8,256]{2,1,0:T(8,128)} %collective-permute-done.2.rest_1_.rest_2_.yb_r, ...), custom_call_target="tpu_custom_call" | custom-call | tf_op jit(solution)/shard_map/pallas_call | solution.py:348
  58.9 7.0 %collective-permute-done.5.rest_4_.rest_5_ = f32[2,144,256]{2,1,0:T(8,128)S(1)} collective-permute-done((f32[2,144,256]{2,1,0:T(8,128)}, f32[2,144,256]{2,1,0:T(8,128)S(1)}, u32[]{:S(2)}, u32[]{:S(2)}) %collective-permute-start.5) | collective-permute-done | bytes 294944 | tf_op jit(solution)/shard_map/ppermute | solution.py:299
  66.6 7.1 %shard_map.78 = (f32[16,144,256]{2,1,0:T(8,128)}, f32[2,144,256]{2,1,0:T(8,128)}) custom-call(s32[3]{0:T(128)} %pad_add_fusion.pos_r.r_0_, f32[8]{0:T(128)} %add_divide_fusion.prof_r, f32[2,128,128]{2,1,0:T(8,128)} %pad.8.fl_r.r_1_, f32[16,144,256]{2,1,0:T(8,128)} %get-tuple-element.14.rest_0_, f32[34,128,256]{2,1,0:T(8,128)} %copy-done, ...), custom_call_target="tpu_custom_call" | custom-call | tf_op jit(solution)/shard_map/pallas_call | solution.py:348
  74.3 6.5 %collective-permute-done.6.zlo_r.zhi_r = f32[2,144,256]{2,1,0:T(8,128)S(1)} collective-permute-done((f32[2,144,256]{2,1,0:T(8,128)}, f32[2,144,256]{2,1,0:T(8,128)S(1)}, u32[]{:S(2)}, u32[]{:S(2)}) %collective-permute-start.6) | collective-permute-done | bytes 294944 | tf_op jit(solution)/shard_map/ppermute | solution.py:299
  81.6 9.6 %shard_map.79 = (f32[8,144,256]{2,1,0:T(8,128)}, f32[2,8,128,128]{3,2,1,0:T(8,128)}, f32[8,144,256]{2,1,0:T(8,128)}, f32[144,256]{1,0:T(8,128)}) custom-call(s32[3]{0:T(128)} %pad_add_fusion.pos_r.r_0_, f32[8]{0:T(128)} %add_divide_fusion.prof_r, f32[2,128,128]{2,1,0:T(8,128)} %pad.8.fl_r.r_1_, f32[16,144,256]{2,1,0:T(8,128)} %get-tuple-element.16.f_r, ...), custom_call_target="tpu_custom_call" | custom-call | tf_op jit(solution)/shard_map/pallas_call | solution.py:325
  91.6 4.9 %collective-permute-done.7.r_4_.r_5_ = f32[144,256]{1,0:T(8,128)S(1)} collective-permute-done((f32[144,256]{1,0:T(8,128)}, f32[144,256]{1,0:T(8,128)S(1)}, u32[]{:S(2)}, u32[]{:S(2)}) %collective-permute-start.7) | collective-permute-done | bytes 147488 | tf_op jit(solution)/shard_map/ppermute | solution.py:358
  97.2 5.5 %shard_map.80 = (f32[8,144,256]{2,1,0:T(8,128)}, f32[144,256]{1,0:T(8,128)}) custom-call(s32[3]{0:T(128)} %pad_add_fusion.pos_r.r_0_, f32[2,128,128]{2,1,0:T(8,128)} %pad.8.fl_r.r_1_, f32[8,144,256]{2,1,0:T(8,128)} %get-tuple-element.19.r_2_, f32[8,144,256]{2,1,0:T(8,128)} %get-tuple-element.20.r_3_, f32[144,256]{1,0:T(8,128)} %copy-done.17, ...), custom_call_target="tpu_custom_call" | custom-call | tf_op jit(solution)/shard_map/pallas_call | solution.py:363
  103.1 4.9 %collective-permute-done.8.r_4_.r_5_ = f32[144,256]{1,0:T(8,128)S(1)} collective-permute-done((f32[144,256]{1,0:T(8,128)}, f32[144,256]{1,0:T(8,128)S(1)}, u32[]{:S(2)}, u32[]{:S(2)}) %collective-permute-start.8) | collective-permute-done | bytes 147488 | tf_op jit(solution)/shard_map/ppermute | solution.py:358
  108.7 5.3 %shard_map.81 = (f32[8,144,256]{2,1,0:T(8,128)}, f32[144,256]{1,0:T(8,128)}) custom-call(s32[3]{0:T(128)} %pad_add_fusion.pos_r.r_0_, f32[2,128,128]{2,1,0:T(8,128)} %pad.8.fl_r.r_1_, f32[8,144,256]{2,1,0:T(8,128)} %get-tuple-element.22.r_2_, f32[8,144,256]{2,1,0:T(8,128)} %get-tuple-element.20.r_3_, f32[144,256]{1,0:T(8,128)} %copy-done.16, ...), custom_call_target="tpu_custom_call" | custom-call | tf_op jit(solution)/shard_map/pallas_call | solution.py:363
  114.5 4.9 %collective-permute-done.9.r_4_.r_5_ = f32[144,256]{1,0:T(8,128)S(1)} collective-permute-done((f32[144,256]{1,0:T(8,128)}, f32[144,256]{1,0:T(8,128)S(1)}, u32[]{:S(2)}, u32[]{:S(2)}) %collective-permute-start.9) | collective-permute-done | bytes 147488 | tf_op jit(solution)/shard_map/ppermute | solution.py:358
  120.1 4.0 %shard_map.82 = f32[8,128,128]{2,1,0:T(8,128)} custom-call(s32[3]{0:T(128)} %pad_add_fusion.pos_r.r_0_, f32[2,128,128]{2,1,0:T(8,128)} %pad.8.fl_r.r_1_, f32[8,144,256]{2,1,0:T(8,128)} %get-tuple-element.24.r_2_, f32[8,144,256]{2,1,0:T(8,128)} %get-tuple-element.20.r_3_, f32[144,256]{1,0:T(8,128)} %copy-done.15, f32[144,256]{1,0:T(8,128)} %copy-done.15), custom_call_target="tpu_custom_call" | custom-call | tf_op jit(solution)/shard_map/pallas_call | solution.py:363
  124.0 1.3 collective-permute-start.10
  125.3 10.0 %collective-permute-done.10 = f32[8,128,128]{2,1,0:T(8,128)S(1)} collective-permute-done((f32[8,128,128]{2,1,0:T(8,128)}, f32[8,128,128]{2,1,0:T(8,128)S(1)}, u32[]{:S(2)}, u32[]{:S(2)}) %collective-permute-start.10) | collective-permute-done | bytes 524320 | tf_op jit(solution)/shard_map/ppermute | solution.py:195
  135.3 1.1 select_bitcast_fusion.1
  136.6 2.6 %collective-permute-done.11 = f32[2,8,128,128]{3,2,1,0:T(8,128)S(1)} collective-permute-done((f32[2,8,128,128]{3,2,1,0:T(8,128)S(1)}, f32[2,8,128,128]{3,2,1,0:T(8,128)S(1)}, u32[]{:S(2)}, u32[]{:S(2)}) %collective-permute-start.11) | collective-permute-done | bytes 1048608 | tf_op jit(solution)/shard_map/ppermute | solution.py:198
  139.5 1.3 pad_maximum_fusion.1
  (69 shorter events, 16.2 us)
Async XLA Ops:
  3.3 6.2 %copy-start.7 = (f32[8,128,384]{2,1,0:T(8,128)S(1)}, f32[8,128,384]{2,1,0:T(8,128)}, u32[]{:S(2)}) copy-start(f32[8,128,384]{2,1,0:T(8,128)} %param.11) | copy-start | bytes 4718596
  3.3 8.5 %collective-permute-start = (f32[26,8,128]{2,1,0:T(8,128)S(1)}, f32[26,8,128]{2,1,0:T(8,128)S(1)}, u32[]{:S(2)}, u32[]{:S(2)}) collective-permute-start(f32[26,8,128]{2,1,0:T(8,128)S(1)} %copy.8), channel_id=1, source_target_pairs={{1,0},{2,1},{3,2},{5,4},{6,5},{7,6},{9,8},{10,9},{11,10},{13,12},{... | collective-permute-start | bytes 319496 | tf_op jit(solution)/shard_map/ppermute | solution.py:245
  5.8 6.5 %collective-permute-start.1 = (f32[26,8,128]{2,1,0:T(8,128)}, f32[26,8,128]{2,1,0:T(8,128)}, u32[]{:S(2)}, u32[]{:S(2)}) collective-permute-start(f32[26,8,128]{2,1,0:T(8,128)} %copy.10), channel_id=1, source_target_pairs={{0,1},{1,2},{2,3},{4,5},{5,6},{6,7},{8,9},{9,10},{10,11},{12,13},{... | collective-permute-start | bytes 319496 | tf_op jit(solution)/shard_map/ppermute | solution.py:244
  12.3 1.7 %copy-start.12 = (f32[2,128,128]{2,1,0:T(8,128)S(1)}, f32[2,128,128]{2,1,0:T(8,128)}, u32[]{:S(2)}) copy-start(f32[2,128,128]{2,1,0:T(8,128)} %param.8) | copy-start | bytes 393220
  13.8 1.5 %copy-start.3 = (f32[2,8,128,128]{3,2,1,0:T(8,128)S(1)}, f32[2,8,128,128]{3,2,1,0:T(8,128)}, u32[]{:S(2)}) copy-start(f32[2,8,128,128]{3,2,1,0:T(8,128)} %param.6) | copy-start | bytes 3145732
  13.8 2.2 %copy-start.5 = (f32[8,128,136]{2,1,0:T(8,128)S(1)}, f32[8,128,136]{2,1,0:T(8,128)}, u32[]{:S(2)}) copy-start(f32[8,128,136]{2,1,0:T(8,128)} %pad_dynamic-slice_fusion.1) | copy-start | bytes 1671172
  14.0 5.8 %copy-start.1 = (f32[26,128,112]{2,1,0:T(8,128)}, f32[26,128,112]{2,1,0:T(8,128)S(1)}, u32[]{:S(2)}) copy-start(f32[26,128,112]{2,1,0:T(8,128)S(1)} %broadcast_in_dim.6) | copy-start | bytes 4472836
  15.9 8.1 %copy-start.8 = (f32[8,128,8]{2,1,0:T(8,128)S(1)}, f32[8,128,8]{2,1,0:T(8,128)}, u32[]{:S(2)}) copy-start(f32[8,128,8]{2,1,0:T(8,128)} %pad_dynamic-slice_fusion) | copy-start | bytes 98308
  19.8 2.1 %copy-start = (f32[34,128,256]{2,1,0:T(8,128)}, f32[34,128,256]{2,1,0:T(8,128)S(1)}, u32[]{:S(2)}) copy-start(f32[34,128,256]{2,1,0:T(8,128)S(1)} %maximum_maximum_fusion.rest_0_.rest_1_.ys_r) | copy-start | bytes 13369348
  22.7 12.7 %collective-permute-start.2 = (f32[34,8,256]{2,1,0:T(8,128)}, f32[34,8,256]{2,1,0:T(8,128)}, u32[]{:S(2)}, u32[]{:S(2)}) collective-permute-start(f32[34,8,256]{2,1,0:T(8,128)} %get-tuple-element.30), channel_id=1, source_target_pairs={{4,0},{8,4},{12,8},{5,1},{9,5},{13,9},{6,2},{10,6},{14,10},{7,3},{... | collective-permute-start | bytes 835592 | tf_op jit(solution)/shard_map/ppermute | solution.py:260
  24.9 7.2 %copy-start.2 = (f32[26,128,112]{2,1,0:T(8,128)S(1)}, f32[26,128,112]{2,1,0:T(8,128)}, u32[]{:S(2)}) copy-start(f32[26,128,112]{2,1,0:T(8,128)} %copy-done.1) | copy-start | bytes 4472836
  24.9 7.2 %copy-start.4 = (f32[2,8,128,128]{3,2,1,0:T(8,128)S(1)}, f32[2,8,128,128]{3,2,1,0:T(8,128)}, u32[]{:S(2)}) copy-start(f32[2,8,128,128]{3,2,1,0:T(8,128)} %param.6) | copy-start | bytes 3145732
  24.9 7.2 %copy-start.6 = (f32[8,128,128]{2,1,0:T(8,128)S(1)}, f32[8,128,128]{2,1,0:T(8,128)}, u32[]{:S(2)}) copy-start(f32[8,128,128]{2,1,0:T(8,128)} %param.7) | copy-start | bytes 1572868
  24.9 12.9 %collective-permute-start.3 = (f32[34,8,256]{2,1,0:T(8,128)}, f32[34,8,256]{2,1,0:T(8,128)S(1)}, u32[]{:S(2)}, u32[]{:S(2)}) collective-permute-start(f32[34,8,256]{2,1,0:T(8,128)} %get-tuple-element.29), channel_id=1, source_target_pairs={{0,4},{4,8},{8,12},{1,5},{5,9},{9,13},{2,6},{6,10},{10,14},{3,7},{... | collective-permute-start | bytes 835592 | tf_op jit(solution)/shard_map/ppermute | solution.py:259
  32.1 5.7 %copy-start.19 = (f32[128,256]{1,0:T(8,128)S(1)}, f32[128,256]{1,0:T(8,128)}, u32[]{:S(2)}) copy-start(f32[128,256]{1,0:T(8,128)} %get-tuple-element.34) | copy-start | bytes 393220
  32.1 5.7 %copy-start.18 = (f32[128,256]{1,0:T(8,128)S(1)}, f32[128,256]{1,0:T(8,128)}, u32[]{:S(2)}) copy-start(f32[128,256]{1,0:T(8,128)} %get-tuple-element.35) | copy-start | bytes 393220
  32.2 8.5 %copy-start.20 = (s32[2,64,64]{2,1,0:T(8,128)S(1)}, s32[2,64,64]{2,1,0:T(8,128)}, u32[]{:S(2)}) copy-start(s32[2,64,64]{2,1,0:T(8,128)} %param.10) | copy-start | bytes 98308
  37.8 0.7 copy-start.11
  38.5 12.0 %collective-permute-start.4 = (f32[3,144,256]{2,1,0:T(8,128)S(1)}, f32[3,144,256]{2,1,0:T(8,128)S(1)}, u32[]{:S(2)}, u32[]{:S(2)}) collective-permute-start(f32[3,144,256]{2,1,0:T(8,128)S(1)} %maximum_select_fusion), channel_id=1, source_target_pairs={{0,16},{16,0},{1,17},{17,1},{2,18},{18,2},{3,19},{19,3},{4,20},{20... | collective-permute-start | bytes 1327112 | tf_op jit(solution)/shard_map/ppermute | solution.py:291
  50.5 0.8 copy-start.10
  57.8 8.1 %collective-permute-start.5 = (f32[2,144,256]{2,1,0:T(8,128)}, f32[2,144,256]{2,1,0:T(8,128)S(1)}, u32[]{:S(2)}, u32[]{:S(2)}) collective-permute-start(f32[2,144,256]{2,1,0:T(8,128)} %get-tuple-element.15), channel_id=1, source_target_pairs={{0,16},{16,0},{1,17},{17,1},{2,18},{18,2},{3,19},{19,3},{4,20},{20... | collective-permute-start | bytes 884744 | tf_op jit(solution)/shard_map/ppermute | solution.py:299
  65.9 0.7 copy-start.14
  73.7 7.2 %collective-permute-start.6 = (f32[2,144,256]{2,1,0:T(8,128)}, f32[2,144,256]{2,1,0:T(8,128)S(1)}, u32[]{:S(2)}, u32[]{:S(2)}) collective-permute-start(f32[2,144,256]{2,1,0:T(8,128)} %get-tuple-element.17), channel_id=1, source_target_pairs={{0,16},{16,0},{1,17},{17,1},{2,18},{18,2},{3,19},{19,3},{4,20},{20... | collective-permute-start | bytes 884744 | tf_op jit(solution)/shard_map/ppermute | solution.py:299
  80.9 0.7 copy-start.13
  91.2 5.4 %collective-permute-start.7 = (f32[144,256]{1,0:T(8,128)}, f32[144,256]{1,0:T(8,128)S(1)}, u32[]{:S(2)}, u32[]{:S(2)}) collective-permute-start(f32[144,256]{1,0:T(8,128)} %get-tuple-element.21), channel_id=1, source_target_pairs={{0,16},{16,0},{1,17},{17,1},{2,18},{18,2},{3,19},{19,3},{4,20},{20... | collective-permute-start | bytes 442376 | tf_op jit(solution)/shard_map/ppermute | solution.py:358
  96.6 0.7 copy-start.17
  102.7 5.4 %collective-permute-start.8 = (f32[144,256]{1,0:T(8,128)}, f32[144,256]{1,0:T(8,128)S(1)}, u32[]{:S(2)}, u32[]{:S(2)}) collective-permute-start(f32[144,256]{1,0:T(8,128)} %get-tuple-element.23), channel_id=1, source_target_pairs={{0,16},{16,0},{1,17},{17,1},{2,18},{18,2},{3,19},{19,3},{4,20},{20... | collective-permute-start | bytes 442376 | tf_op jit(solution)/shard_map/ppermute | solution.py:358
  114.1 5.4 %collective-permute-start.9 = (f32[144,256]{1,0:T(8,128)}, f32[144,256]{1,0:T(8,128)S(1)}, u32[]{:S(2)}, u32[]{:S(2)}) collective-permute-start(f32[144,256]{1,0:T(8,128)} %get-tuple-element.25), channel_id=1, source_target_pairs={{0,16},{16,0},{1,17},{17,1},{2,18},{18,2},{3,19},{19,3},{4,20},{20... | collective-permute-start | bytes 442376 | tf_op jit(solution)/shard_map/ppermute | solution.py:358
  119.4 0.7 copy-start.15
  124.0 11.3 %collective-permute-start.10 = (f32[8,128,128]{2,1,0:T(8,128)}, f32[8,128,128]{2,1,0:T(8,128)S(1)}, u32[]{:S(2)}, u32[]{:S(2)}) collective-permute-start(f32[8,128,128]{2,1,0:T(8,128)} %shard_map.82), channel_id=1, source_target_pairs={{2,0},{3,1},{1,2},{6,4},{7,5},{5,6},{10,8},{11,9},{9,10},{14,12},{... | collective-permute-start | bytes 1572872 | tf_op jit(solution)/shard_map/ppermute | solution.py:195
  125.3 13.9 %copy-start.9 = (f32[8,128,128]{2,1,0:T(8,128)S(1)}, f32[8,128,128]{2,1,0:T(8,128)}, u32[]{:S(2)}) copy-start(f32[8,128,128]{2,1,0:T(8,128)} %shard_map.82) | copy-start | bytes 1572868
  136.5 2.7 %collective-permute-start.11 = (f32[2,8,128,128]{3,2,1,0:T(8,128)S(1)}, f32[2,8,128,128]{3,2,1,0:T(8,128)S(1)}, u32[]{:S(2)}, u32[]{:S(2)}) collective-permute-start(f32[2,8,128,128]{3,2,1,0:T(8,128)S(1)} %pad_maximum_fusion.2), channel_id=1, source_target_pairs={{0,1},{1,0},{2,3},{3,2},{4,5},{5,4},{6,7},{7,6},{8,9},{9,8},{10,11... | collective-permute-start | bytes 3145736 | tf_op jit(solution)/shard_map/ppermute | solution.py:198
  (1 other events, 0.7 us)

commit v12 on v10

--- a/solution.py
+++ b/solution.py
@@ -287,7 +287,8 @@
         first = planes_of(jnp.where(
             top, jnp.array([depth - 1, 2 * depth - 1, 3 * depth + 2 + depth - 1]),
             jnp.array([0, depth, 3 * depth + 2])))
-        got = lax.ppermute(first, "gz", both)
+        got = lax.ppermute(first[:2], "gz", both)
+        got_t = lax.ppermute(first[2:], "gz", both)
     else:
         lo_plane, hi_plane = planes_of(lo_idx), planes_of(hi_idx)
         tzlo0 = lax.ppermute(planes_of(3 * depth + 2 + depth - 1), "gz", up_z)
@@ -309,7 +310,7 @@
                 w_r = _Rows(ys_r, yb_r, ya_r, 3 * depth, 2)
                 t_r = _Rows(ys_r, yb_r, ya_r, 3 * depth + 2, depth)
                 if pair:
-                    tzlo_r = tzhi_r = rest[0].at[2]
+                    tzlo_r = tzhi_r = rest[0].at[0]
                     outs_r = rest[1:]
                 else:
                     tzlo_r, tzhi_r = rest[0], rest[1]
@@ -320,7 +321,7 @@
                 _heat_kernel(False, pair, depth, t_totals, pos_r, fl_r, t_r, q_r, tzlo_r, tzhi_r,
                              *outs_r[2:])
 
-            extra = (got,) if pair else (tzlo0, tzhi0)
+            extra = (got_t,) if pair else (tzlo0, tzhi0)
             res = _vmem_call(fused, outs, 9 + len(extra), 2)(
                 pos, profile, flags, field, *pieces, zlo, zhi, *extra)
             heat, field_out, kelvin = res[0], res[1], res[2]

time: 138 us -> 137 us (level)
    ppermute x2, waiting for transfers between devices: 13.5 us -> 6.99 us  [on_device(): zlo = zhi = got if i == 0 else lax.ppermute(send, 'gz', both)]
    ppermute x1 -> x2, waiting for transfers between devices: 7.85 us -> 13 us  [the longest x1 8.21 us: on_device(): got_t = lax.ppermute(first[2:], 'gz', both)]
    ppermute x1 -> x2, starting transfers between devices: 1.56 us -> 3.01 us  [the longest x1 1.56 us: on_device(): got = lax.ppermute(first[:2], 'gz', both)]
    unnamed x30 -> x34, local copies, waits for them, and re-layouts: 6.26 us -> 6.27 us
  transfers between devices with their start and end apart: 12 -> 13, of which waited for: 10 -> 10; matrix products, arithmetic and copies ran while one was open for 8% -> 8% of each run, Pallas kernels for 0% -> 0%
where the time goes in v12:
time: 137 us
  waiting for transfers between devices  50.9 us (37%)
  Pallas kernels  37.7 us (28%)
  local copies, waits for them, and re-layouts  19.3 us (14%)
  starting transfers between devices  19.1 us (14%)
  other arithmetic  8.3 us (6%)
  between operations  1.58 us (1%)
    ppermute x3, waiting for transfers between devices, on_device(): tzlo = tzhi = lax.ppermute(send_t, 'gz', both)  15.2 us
    pallas_call x3, Pallas kernels, on_device(): _vmem_call(lambda *r, last=last: _heat_kernel(last, pair, depth, t_totals...  14.8 us
    pallas_call x2, Pallas kernels, on_device(): _vmem_call(sweep, outs, 8 + len(fargs), 2)  13.5 us
    ppermute x1, waiting for transfers between devices, _broadcast_blocks(): r1 = lax.ppermute(own, 'gx', [(2, 0), (3, 1), (1, 2)])  9.96 us
    pallas_call x1, Pallas kernels, on_device(): _vmem_call(fused, outs, 9 + len(extra), 2)  9.47 us
    ppermute x1, waiting for transfers between devices, on_device(): got_t = lax.ppermute(first[2:], 'gz', both)  8.21 us
    ppermute x2, waiting for transfers between devices, on_device(): zlo = zhi = got if i == 0 else lax.ppermute(send, 'gz', both)  6.99 us
    unnamed x34, local copies, waits for them, and re-layouts  6.27 us
  transfers between devices with their start and end apart: 13, of which 10 were waited for; matrix products, arithmetic and copies ran while one was open for 8% of the time, Pallas kernels for 0%

profile of v12, /device:TPU:0, one launch (start us, length us, event | category | flops | bytes accessed | tf_op | source)
XLA Modules:
  0.0 136.9 jit_solution(11739205194102934894)
XLA Ops:
  0.6 1.6 %pad_maximum_fusion = f32[26,128,128]{2,1,0:T(8,128)S(1)} fusion(f32[2,128,128]{2,1,0:T(8,128)} %param.10, f32[8,128,128]{2,1,0:T(8,128)} %param.9, f32[16,128,128]{2,1,0:T(8,128)} %bitcast.31), kind=kLoop, calls=%fused_computation.8 | loop fusion | flops 851968 | bytes 3407872 | tf_op jit(solution)/shard_map/concatenate | solution.py:240
  2.8 1.1 copy.10
  3.9 1.4 %collective-permute-start = (f32[26,8,128]{2,1,0:T(8,128)}, f32[26,8,128]{2,1,0:T(8,128)S(1)}, u32[]{:S(2)}, u32[]{:S(2)}) collective-permute-start(f32[26,8,128]{2,1,0:T(8,128)} %copy.10), channel_id=1, source_target_pairs={{1,0},{2,1},{3,2},{5,4},{6,5},{7,6},{9,8},{10,9},{11,10},{13,12},{... | collective-permute-start | bytes 319496 | tf_op jit(solution)/shard_map/ppermute | solution.py:245
  5.3 1.1 copy.12
  6.5 3.7 %collective-permute-start.1 = (f32[26,8,128]{2,1,0:T(8,128)}, f32[26,8,128]{2,1,0:T(8,128)}, u32[]{:S(2)}, u32[]{:S(2)}) collective-permute-start(f32[26,8,128]{2,1,0:T(8,128)} %copy.12), channel_id=1, source_target_pairs={{0,1},{1,2},{2,3},{4,5},{5,6},{6,7},{8,9},{9,10},{10,11},{12,13},{... | collective-permute-start | bytes 319496 | tf_op jit(solution)/shard_map/ppermute | solution.py:244
  11.5 1.3 pad_dynamic-slice_fusion.1
  14.3 1.4 %copy.13 = f32[26,8,128]{1,2,0:T(8,128)S(1)} copy(f32[26,8,128]{2,1,0:T(8,128)} %collective-permute-done.1) | data formatting | bytes 212992 | tf_op jit(solution)/shard_map/ppermute | solution.py:244
  15.8 2.9 %maximum_maximum_fusion.rest_0_.rest_1_.ys_r = f32[34,128,256]{2,1,0:T(8,128)S(1)} fusion(f32[8,128,8]{2,1,0:T(8,128)} %pad_dynamic-slice_fusion, f32[8,128,136]{2,1,0:T(8,128)} %pad_dynamic-slice_fusion.1, f32[26,128,8]{2,1,0:T(8,128)S(1)} %bitcast.30, f32[26,128,8]{2,1,0:T(8,128)S(1)} %bitcast.29, f32[2,128,128]{2,1,0:T(8,128)S(1)} %copy-done.11, ...), kind=kLoop, calls=%fused_computation.3 | loop fusion | flops 8912896 | bytes 7032832 | tf_op jit(solution)/shard_map/concatenate | solution.py:257
  18.7 2.0 %copy-done = f32[34,128,256]{2,1,0:T(8,128)} copy-done((f32[34,128,256]{2,1,0:T(8,128)}, f32[34,128,256]{2,1,0:T(8,128)S(1)}, u32[]{:S(2)}) %copy-start) | copy-done | bytes 4456472
  20.7 1.3 collective-permute-start.2
  22.1 5.8 %collective-permute-start.3 = (f32[34,8,256]{2,1,0:T(8,128)S(1)}, f32[34,8,256]{2,1,0:T(8,128)S(1)}, u32[]{:S(2)}, u32[]{:S(2)}) collective-permute-start(f32[34,8,256]{2,1,0:T(8,128)S(1)} %get-tuple-element.26), channel_id=1, source_target_pairs={{0,4},{4,8},{8,12},{1,5},{5,9},{9,13},{2,6},{6,10},{10,14},{3,7},{... | collective-permute-start | bytes 835592 | tf_op jit(solution)/shard_map/ppermute | solution.py:259
  27.9 2.8 %gather_fusion = f32[3,128,256]{2,1,0:T(8,128)S(1)} fusion(f32[34,128,256]{2,1,0:T(8,128)} %copy-done, s32[1024]{0:T(1024)S(1)} %pad_clamp_fusion), kind=kCustom, calls=%fused_computation | custom fusion | bytes 786444 | tf_op jit(solution)/shard_map/gather | solution.py:264
  30.7 2.4 %collective-permute-done.2.rest_1_.rest_2_.yb_r = f32[34,8,256]{2,1,0:T(8,128)S(1)} collective-permute-done((f32[34,8,256]{2,1,0:T(8,128)S(1)}, f32[34,8,256]{2,1,0:T(8,128)S(1)}, u32[]{:S(2)}, u32[]{:S(2)}) %collective-permute-start.2) | collective-permute-done | bytes 278560 | tf_op jit(solution)/shard_map/ppermute | solution.py:260
  35.0 1.6 %collective-permute-start.4 = (f32[2,144,256]{2,1,0:T(8,128)S(1)}, f32[2,144,256]{2,1,0:T(8,128)S(1)}, u32[]{:S(2)}, u32[]{:S(2)}) collective-permute-start(f32[2,144,256]{2,1,0:T(8,128)S(1)} %slice.45), channel_id=1, source_target_pairs={{0,16},{16,0},{1,17},{17,1},{2,18},{18,2},{3,19},{19,3},{4,20},{20... | collective-permute-start | bytes 884744 | tf_op jit(solution)/shard_map/ppermute | solution.py:290
  39.0 4.8 %collective-permute-done.4.rest_3_.rest_4_ = f32[2,144,256]{2,1,0:T(8,128)S(1)} collective-permute-done((f32[2,144,256]{2,1,0:T(8,128)S(1)}, f32[2,144,256]{2,1,0:T(8,128)S(1)}, u32[]{:S(2)}, u32[]{:S(2)}) %collective-permute-start.4) | collective-permute-done | bytes 294944 | tf_op jit(solution)/shard_map/ppermute | solution.py:290
  44.5 6.4 %shard_map.95 = (f32[16,144,256]{2,1,0:T(8,128)}, f32[2,144,256]{2,1,0:T(8,128)}) custom-call(s32[3]{0:T(128)} %pad_add_fusion.pos_r.r_0_, f32[8]{0:T(128)} %add_divide_fusion.prof_r, f32[2,128,128]{2,1,0:T(8,128)} %pad.8.fl_r.r_1_, f32[34,128,256]{2,1,0:T(8,128)} %copy-done, f32[34,8,256]{2,1,0:T(8,128)} %copy-done.3, f32[34,8,256]{2,1,0:T(8,128)} %copy-done.4, ...), custom_call_target="tpu_custom_call" | custom-call | tf_op jit(solution)/shard_map/pallas_call | solution.py:348
  52.0 7.0 %collective-permute-done.5.rest_4_.rest_5_ = f32[2,144,256]{2,1,0:T(8,128)S(1)} collective-permute-done((f32[2,144,256]{2,1,0:T(8,128)}, f32[2,144,256]{2,1,0:T(8,128)S(1)}, u32[]{:S(2)}, u32[]{:S(2)}) %collective-permute-start.5) | collective-permute-done | bytes 294944 | tf_op jit(solution)/shard_map/ppermute | solution.py:299
  59.7 7.1 %shard_map.96 = (f32[16,144,256]{2,1,0:T(8,128)}, f32[2,144,256]{2,1,0:T(8,128)}) custom-call(s32[3]{0:T(128)} %pad_add_fusion.pos_r.r_0_, f32[8]{0:T(128)} %add_divide_fusion.prof_r, f32[2,128,128]{2,1,0:T(8,128)} %pad.8.fl_r.r_1_, f32[16,144,256]{2,1,0:T(8,128)} %get-tuple-element.14.rest_0_, f32[34,128,256]{2,1,0:T(8,128)} %copy-done, ...), custom_call_target="tpu_custom_call" | custom-call | tf_op jit(solution)/shard_map/pallas_call | solution.py:348
  67.5 1.5 %collective-permute-start.7 = (f32[1,144,256]{2,1,0:T(8,128)S(1)}, f32[1,144,256]{2,1,0:T(8,128)S(1)}, u32[]{:S(2)}, u32[]{:S(2)}) collective-permute-start(f32[1,144,256]{2,1,0:T(8,128)S(1)} %slice.46), channel_id=1, source_target_pairs={{0,16},{16,0},{1,17},{17,1},{2,18},{18,2},{3,19},{19,3},{4,20},{20... | collective-permute-start | bytes 442376 | tf_op jit(solution)/shard_map/ppermute | solution.py:291
  68.9 8.2 %collective-permute-done.7.rest_0_ = f32[1,144,256]{2,1,0:T(8,128)S(1)} collective-permute-done((f32[1,144,256]{2,1,0:T(8,128)S(1)}, f32[1,144,256]{2,1,0:T(8,128)S(1)}, u32[]{:S(2)}, u32[]{:S(2)}) %collective-permute-start.7) | collective-permute-done | bytes 147488 | tf_op jit(solution)/shard_map/ppermute | solution.py:291
  77.9 9.5 %shard_map.97 = (f32[8,144,256]{2,1,0:T(8,128)}, f32[2,8,128,128]{3,2,1,0:T(8,128)}, f32[8,144,256]{2,1,0:T(8,128)}, f32[144,256]{1,0:T(8,128)}) custom-call(s32[3]{0:T(128)} %pad_add_fusion.pos_r.r_0_, f32[8]{0:T(128)} %add_divide_fusion.prof_r, f32[2,128,128]{2,1,0:T(8,128)} %pad.8.fl_r.r_1_, f32[16,144,256]{2,1,0:T(8,128)} %get-tuple-element.16.f_r, ...), custom_call_target="tpu_custom_call" | custom-call | tf_op jit(solution)/shard_map/pallas_call | solution.py:325
  87.7 5.1 %collective-permute-done.8.r_4_.r_5_ = f32[144,256]{1,0:T(8,128)S(1)} collective-permute-done((f32[144,256]{1,0:T(8,128)}, f32[144,256]{1,0:T(8,128)S(1)}, u32[]{:S(2)}, u32[]{:S(2)}) %collective-permute-start.8) | collective-permute-done | bytes 147488 | tf_op jit(solution)/shard_map/ppermute | solution.py:358
  93.4 5.5 %shard_map.98 = (f32[8,144,256]{2,1,0:T(8,128)}, f32[144,256]{1,0:T(8,128)}) custom-call(s32[3]{0:T(128)} %pad_add_fusion.pos_r.r_0_, f32[2,128,128]{2,1,0:T(8,128)} %pad.8.fl_r.r_1_, f32[8,144,256]{2,1,0:T(8,128)} %get-tuple-element.19.r_2_, f32[8,144,256]{2,1,0:T(8,128)} %get-tuple-element.20.r_3_, f32[144,256]{1,0:T(8,128)} %copy-done.10, ...), custom_call_target="tpu_custom_call" | custom-call | tf_op jit(solution)/shard_map/pallas_call | solution.py:363
  99.2 5.1 %collective-permute-done.9.r_4_.r_5_ = f32[144,256]{1,0:T(8,128)S(1)} collective-permute-done((f32[144,256]{1,0:T(8,128)}, f32[144,256]{1,0:T(8,128)S(1)}, u32[]{:S(2)}, u32[]{:S(2)}) %collective-permute-start.9) | collective-permute-done | bytes 147488 | tf_op jit(solution)/shard_map/ppermute | solution.py:358
  104.9 5.3 %shard_map.99 = (f32[8,144,256]{2,1,0:T(8,128)}, f32[144,256]{1,0:T(8,128)}) custom-call(s32[3]{0:T(128)} %pad_add_fusion.pos_r.r_0_, f32[2,128,128]{2,1,0:T(8,128)} %pad.8.fl_r.r_1_, f32[8,144,256]{2,1,0:T(8,128)} %get-tuple-element.22.r_2_, f32[8,144,256]{2,1,0:T(8,128)} %get-tuple-element.20.r_3_, f32[144,256]{1,0:T(8,128)} %copy-done.9, f32[144,256]{1,0:T(8,128)} %copy-done.9), custom_call_target="tpu_custom_call" | custom-call | tf_op jit(solution)/shard_map/pallas_call | solution.py:363
  110.5 5.1 %collective-permute-done.10.r_4_.r_5_ = f32[144,256]{1,0:T(8,128)S(1)} collective-permute-done((f32[144,256]{1,0:T(8,128)}, f32[144,256]{1,0:T(8,128)S(1)}, u32[]{:S(2)}, u32[]{:S(2)}) %collective-permute-start.10) | collective-permute-done | bytes 147488 | tf_op jit(solution)/shard_map/ppermute | solution.py:358
  116.2 3.9 %shard_map.100 = f32[8,128,128]{2,1,0:T(8,128)} custom-call(s32[3]{0:T(128)} %pad_add_fusion.pos_r.r_0_, f32[2,128,128]{2,1,0:T(8,128)} %pad.8.fl_r.r_1_, f32[8,144,256]{2,1,0:T(8,128)} %get-tuple-element.24.r_2_, f32[8,144,256]{2,1,0:T(8,128)} %get-tuple-element.20.r_3_, f32[144,256]{1,0:T(8,128)} %copy-done.8, f32[144,256]{1,0:T(8,128)} %copy-done.8), custom_call_target="tpu_custom_call" | custom-call | tf_op jit(solution)/shard_map/pallas_call | solution.py:363
  120.2 1.3 collective-permute-start.11
  121.5 10.0 %collective-permute-done.11 = f32[8,128,128]{2,1,0:T(8,128)S(1)} collective-permute-done((f32[8,128,128]{2,1,0:T(8,128)}, f32[8,128,128]{2,1,0:T(8,128)S(1)}, u32[]{:S(2)}, u32[]{:S(2)}) %collective-permute-start.11) | collective-permute-done | bytes 524320 | tf_op jit(solution)/shard_map/ppermute | solution.py:195
  131.4 1.1 select_bitcast_fusion.1
  132.7 2.6 %collective-permute-done.12 = f32[2,8,128,128]{3,2,1,0:T(8,128)S(1)} collective-permute-done((f32[2,8,128,128]{3,2,1,0:T(8,128)S(1)}, f32[2,8,128,128]{3,2,1,0:T(8,128)S(1)}, u32[]{:S(2)}, u32[]{:S(2)}) %collective-permute-start.12) | collective-permute-done | bytes 1048608 | tf_op jit(solution)/shard_map/ppermute | solution.py:198
  135.6 1.3 pad_maximum_fusion.1
  (64 shorter events, 14.3 us)
Async XLA Ops:
  3.9 7.6 %copy-start.1 = (f32[8,128,384]{2,1,0:T(8,128)S(1)}, f32[8,128,384]{2,1,0:T(8,128)}, u32[]{:S(2)}) copy-start(f32[8,128,384]{2,1,0:T(8,128)} %param.13) | copy-start | bytes 4718596
  3.9 9.9 %collective-permute-start = (f32[26,8,128]{2,1,0:T(8,128)}, f32[26,8,128]{2,1,0:T(8,128)S(1)}, u32[]{:S(2)}, u32[]{:S(2)}) collective-permute-start(f32[26,8,128]{2,1,0:T(8,128)} %copy.10), channel_id=1, source_target_pairs={{1,0},{2,1},{3,2},{5,4},{6,5},{7,6},{9,8},{10,9},{11,10},{13,12},{... | collective-permute-start | bytes 319496 | tf_op jit(solution)/shard_map/ppermute | solution.py:245
  6.5 7.9 %collective-permute-start.1 = (f32[26,8,128]{2,1,0:T(8,128)}, f32[26,8,128]{2,1,0:T(8,128)}, u32[]{:S(2)}, u32[]{:S(2)}) collective-permute-start(f32[26,8,128]{2,1,0:T(8,128)} %copy.12), channel_id=1, source_target_pairs={{0,1},{1,2},{2,3},{4,5},{5,6},{6,7},{8,9},{9,10},{10,11},{12,13},{... | collective-permute-start | bytes 319496 | tf_op jit(solution)/shard_map/ppermute | solution.py:244
  13.8 1.9 %copy-start.11 = (f32[2,128,128]{2,1,0:T(8,128)S(1)}, f32[2,128,128]{2,1,0:T(8,128)}, u32[]{:S(2)}) copy-start(f32[2,128,128]{2,1,0:T(8,128)} %param.10) | copy-start | bytes 393220
  15.7 6.3 %copy-start.14 = (s32[3]{0:T(128)S(1)}, s32[3]{0:T(128)}, u32[]{:S(2)}) copy-start(s32[3]{0:T(128)} %constant.76.clone) | copy-start | bytes 40
  15.7 6.3 %copy-start.15 = (s32[3]{0:T(128)S(1)}, s32[3]{0:T(128)}, u32[]{:S(2)}) copy-start(s32[3]{0:T(128)} %constant.77.clone) | copy-start | bytes 40
  18.6 2.1 %copy-start = (f32[34,128,256]{2,1,0:T(8,128)}, f32[34,128,256]{2,1,0:T(8,128)S(1)}, u32[]{:S(2)}) copy-start(f32[34,128,256]{2,1,0:T(8,128)S(1)} %maximum_maximum_fusion.rest_0_.rest_1_.ys_r) | copy-start | bytes 13369348
  20.7 16.5 %copy-start.13 = (s32[2,64,64]{2,1,0:T(8,128)S(1)}, s32[2,64,64]{2,1,0:T(8,128)}, u32[]{:S(2)}) copy-start(s32[2,64,64]{2,1,0:T(8,128)} %param.12) | copy-start | bytes 98308
  20.7 12.4 %collective-permute-start.2 = (f32[34,8,256]{2,1,0:T(8,128)S(1)}, f32[34,8,256]{2,1,0:T(8,128)S(1)}, u32[]{:S(2)}, u32[]{:S(2)}) collective-permute-start(f32[34,8,256]{2,1,0:T(8,128)S(1)} %get-tuple-element.27), channel_id=1, source_target_pairs={{4,0},{8,4},{12,8},{5,1},{9,5},{13,9},{6,2},{10,6},{14,10},{7,3},{... | collective-permute-start | bytes 835592 | tf_op jit(solution)/shard_map/ppermute | solution.py:260
  22.1 12.3 %collective-permute-start.3 = (f32[34,8,256]{2,1,0:T(8,128)S(1)}, f32[34,8,256]{2,1,0:T(8,128)S(1)}, u32[]{:S(2)}, u32[]{:S(2)}) collective-permute-start(f32[34,8,256]{2,1,0:T(8,128)S(1)} %get-tuple-element.26), channel_id=1, source_target_pairs={{0,4},{4,8},{8,12},{1,5},{5,9},{9,13},{2,6},{6,10},{10,14},{3,7},{... | collective-permute-start | bytes 835592 | tf_op jit(solution)/shard_map/ppermute | solution.py:259
  33.2 10.6 %copy-start.3 = (f32[34,8,256]{2,1,0:T(8,128)}, f32[34,8,256]{2,1,0:T(8,128)S(1)}, u32[]{:S(2)}) copy-start(f32[34,8,256]{2,1,0:T(8,128)S(1)} %collective-permute-done.2.rest_1_.rest_2_.yb_r) | copy-start | bytes 835588
  34.4 9.4 %copy-start.4 = (f32[34,8,256]{2,1,0:T(8,128)}, f32[34,8,256]{2,1,0:T(8,128)S(1)}, u32[]{:S(2)}) copy-start(f32[34,8,256]{2,1,0:T(8,128)S(1)} %collective-permute-done.3.rest_2_.rest_3_.ya_r) | copy-start | bytes 835588
  35.0 8.8 %collective-permute-start.4 = (f32[2,144,256]{2,1,0:T(8,128)S(1)}, f32[2,144,256]{2,1,0:T(8,128)S(1)}, u32[]{:S(2)}, u32[]{:S(2)}) collective-permute-start(f32[2,144,256]{2,1,0:T(8,128)S(1)} %slice.45), channel_id=1, source_target_pairs={{0,16},{16,0},{1,17},{17,1},{2,18},{18,2},{3,19},{19,3},{4,20},{20... | collective-permute-start | bytes 884744 | tf_op jit(solution)/shard_map/ppermute | solution.py:290
  43.8 0.7 copy-start.5
  50.9 8.1 %collective-permute-start.5 = (f32[2,144,256]{2,1,0:T(8,128)}, f32[2,144,256]{2,1,0:T(8,128)S(1)}, u32[]{:S(2)}, u32[]{:S(2)}) collective-permute-start(f32[2,144,256]{2,1,0:T(8,128)} %get-tuple-element.15), channel_id=1, source_target_pairs={{0,16},{16,0},{1,17},{17,1},{2,18},{18,2},{3,19},{19,3},{4,20},{20... | collective-permute-start | bytes 884744 | tf_op jit(solution)/shard_map/ppermute | solution.py:299
  59.0 0.7 copy-start.7
  66.8 10.3 %collective-permute-start.6 = (f32[2,144,256]{2,1,0:T(8,128)}, f32[2,144,256]{2,1,0:T(8,128)S(1)}, u32[]{:S(2)}, u32[]{:S(2)}) collective-permute-start(f32[2,144,256]{2,1,0:T(8,128)} %get-tuple-element.17), channel_id=1, source_target_pairs={{0,16},{16,0},{1,17},{17,1},{2,18},{18,2},{3,19},{19,3},{4,20},{20... | collective-permute-start | bytes 884744 | tf_op jit(solution)/shard_map/ppermute | solution.py:299
  67.5 9.7 %collective-permute-start.7 = (f32[1,144,256]{2,1,0:T(8,128)S(1)}, f32[1,144,256]{2,1,0:T(8,128)S(1)}, u32[]{:S(2)}, u32[]{:S(2)}) collective-permute-start(f32[1,144,256]{2,1,0:T(8,128)S(1)} %slice.46), channel_id=1, source_target_pairs={{0,16},{16,0},{1,17},{17,1},{2,18},{18,2},{3,19},{19,3},{4,20},{20... | collective-permute-start | bytes 442376 | tf_op jit(solution)/shard_map/ppermute | solution.py:291
  77.1 0.7 copy-start.12
  77.1 0.8 copy-start.6
  87.4 5.4 %collective-permute-start.8 = (f32[144,256]{1,0:T(8,128)}, f32[144,256]{1,0:T(8,128)S(1)}, u32[]{:S(2)}, u32[]{:S(2)}) collective-permute-start(f32[144,256]{1,0:T(8,128)} %get-tuple-element.21), channel_id=1, source_target_pairs={{0,16},{16,0},{1,17},{17,1},{2,18},{18,2},{3,19},{19,3},{4,20},{20... | collective-permute-start | bytes 442376 | tf_op jit(solution)/shard_map/ppermute | solution.py:358
  92.7 0.7 copy-start.10
  98.9 5.4 %collective-permute-start.9 = (f32[144,256]{1,0:T(8,128)}, f32[144,256]{1,0:T(8,128)S(1)}, u32[]{:S(2)}, u32[]{:S(2)}) collective-permute-start(f32[144,256]{1,0:T(8,128)} %get-tuple-element.23), channel_id=1, source_target_pairs={{0,16},{16,0},{1,17},{17,1},{2,18},{18,2},{3,19},{19,3},{4,20},{20... | collective-permute-start | bytes 442376 | tf_op jit(solution)/shard_map/ppermute | solution.py:358
  104.3 0.7 copy-start.9
  110.2 5.4 %collective-permute-start.10 = (f32[144,256]{1,0:T(8,128)}, f32[144,256]{1,0:T(8,128)S(1)}, u32[]{:S(2)}, u32[]{:S(2)}) collective-permute-start(f32[144,256]{1,0:T(8,128)} %get-tuple-element.25), channel_id=1, source_target_pairs={{0,16},{16,0},{1,17},{17,1},{2,18},{18,2},{3,19},{19,3},{4,20},{20... | collective-permute-start | bytes 442376 | tf_op jit(solution)/shard_map/ppermute | solution.py:358
  115.6 0.6 copy-start.8
  120.2 11.3 %collective-permute-start.11 = (f32[8,128,128]{2,1,0:T(8,128)}, f32[8,128,128]{2,1,0:T(8,128)S(1)}, u32[]{:S(2)}, u32[]{:S(2)}) collective-permute-start(f32[8,128,128]{2,1,0:T(8,128)} %shard_map.100), channel_id=1, source_target_pairs={{2,0},{3,1},{1,2},{6,4},{7,5},{5,6},{10,8},{11,9},{9,10},{14,12},{... | collective-permute-start | bytes 1572872 | tf_op jit(solution)/shard_map/ppermute | solution.py:195
  121.5 13.9 %copy-start.2 = (f32[8,128,128]{2,1,0:T(8,128)S(1)}, f32[8,128,128]{2,1,0:T(8,128)}, u32[]{:S(2)}) copy-start(f32[8,128,128]{2,1,0:T(8,128)} %shard_map.100) | copy-start | bytes 1572868
  132.7 2.7 %collective-permute-start.12 = (f32[2,8,128,128]{3,2,1,0:T(8,128)S(1)}, f32[2,8,128,128]{3,2,1,0:T(8,128)S(1)}, u32[]{:S(2)}, u32[]{:S(2)}) collective-permute-start(f32[2,8,128,128]{3,2,1,0:T(8,128)S(1)} %pad_maximum_fusion.2), channel_id=1, source_target_pairs={{0,1},{1,0},{2,3},{3,2},{4,5},{5,4},{6,7},{7,6},{8,9},{9,8},{10,11... | collective-permute-start | bytes 3145736 | tf_op jit(solution)/shard_map/ppermute | solution.py:198

commit v13 on v12

--- a/solution.py
+++ b/solution.py
@@ -154,15 +154,17 @@
         ky_up, ky_dn, kx_up, kx_dn = _rolls(centre_kappa)
         mc = planes[z + 1]
         my_up, my_dn, mx_up, mx_dn = _rolls(mc)
+        cut = (lambda v: v[0:height, 0:breadth]) if last else (lambda v: v)
+        c, centre_kappa, mc = cut(c), cut(centre_kappa), cut(mc)
         flux = jnp.zeros_like(c)
         for other, kappa, other_mask in (
             (temps[z + 2], kaps[z + 2], planes[z + 2]), (temps[z], kaps[z], planes[z]),
             (y_up, ky_up, my_up), (y_dn, ky_dn, my_dn), (x_up, kx_up, mx_up), (x_dn, kx_dn, mx_dn),
         ):
-            flux = flux + other_mask * (centre_kappa + kappa) * (other - c)
-        new = c + 0.5 * CONDUCT * mc * flux + q[z]
+            flux = flux + cut(other_mask) * (centre_kappa + cut(kappa)) * (cut(other) - c)
+        new = c + 0.5 * CONDUCT * mc * flux + cut(q[z])
         if last:
-            own[z] = new[0:height, 0:breadth]
+            own[z] = new
         else:
             o[z] = new
             if z == 0:

time: 137 us -> 137 us (level)
  no operation moved by 1% of the time
where the time goes in v13:
time: 137 us
  waiting for transfers between devices  50.9 us (37%)
  Pallas kernels  37.7 us (28%)
  local copies, waits for them, and re-layouts  19.3 us (14%)
  starting transfers between devices  19.1 us (14%)
  other arithmetic  8.3 us (6%)
  between operations  1.58 us (1%)
    ppermute x3, waiting for transfers between devices, on_device(): tzlo = tzhi = lax.ppermute(send_t, 'gz', both)  15.2 us
    pallas_call x3, Pallas kernels, on_device(): _vmem_call(lambda *r, last=last: _heat_kernel(last, pair, depth, t_totals...  14.8 us
    pallas_call x2, Pallas kernels, on_device(): _vmem_call(sweep, outs, 8 + len(fargs), 2)  13.5 us
    ppermute x1, waiting for transfers between devices, _broadcast_blocks(): r1 = lax.ppermute(own, 'gx', [(2, 0), (3, 1), (1, 2)])  9.96 us
    pallas_call x1, Pallas kernels, on_device(): _vmem_call(fused, outs, 9 + len(extra), 2)  9.47 us
    ppermute x1, waiting for transfers between devices, on_device(): got_t = lax.ppermute(first[2:], 'gz', both)  8.21 us
    ppermute x2, waiting for transfers between devices, on_device(): zlo = zhi = got if i == 0 else lax.ppermute(send, 'gz', both)  6.99 us
    unnamed x34, local copies, waits for them, and re-layouts  6.27 us
  transfers between devices with their start and end apart: 13, of which 10 were waited for; matrix products, arithmetic and copies ran while one was open for 8% of the time, Pallas kernels for 0%

profile of v13, /device:TPU:0, one launch (start us, length us, event | category | flops | bytes accessed | tf_op | source)
XLA Modules:
  0.0 136.9 jit_solution(11739205194102934894)
XLA Ops:
  0.6 1.6 %pad_maximum_fusion = f32[26,128,128]{2,1,0:T(8,128)S(1)} fusion(f32[2,128,128]{2,1,0:T(8,128)} %param.10, f32[8,128,128]{2,1,0:T(8,128)} %param.9, f32[16,128,128]{2,1,0:T(8,128)} %bitcast.31), kind=kLoop, calls=%fused_computation.8 | loop fusion | flops 851968 | bytes 3407872 | tf_op jit(solution)/shard_map/concatenate | solution.py:242
  2.8 1.1 copy.10
  3.9 1.4 %collective-permute-start = (f32[26,8,128]{2,1,0:T(8,128)}, f32[26,8,128]{2,1,0:T(8,128)S(1)}, u32[]{:S(2)}, u32[]{:S(2)}) collective-permute-start(f32[26,8,128]{2,1,0:T(8,128)} %copy.10), channel_id=1, source_target_pairs={{1,0},{2,1},{3,2},{5,4},{6,5},{7,6},{9,8},{10,9},{11,10},{13,12},{... | collective-permute-start | bytes 319496 | tf_op jit(solution)/shard_map/ppermute | solution.py:247
  5.3 1.1 copy.12
  6.5 3.7 %collective-permute-start.1 = (f32[26,8,128]{2,1,0:T(8,128)}, f32[26,8,128]{2,1,0:T(8,128)}, u32[]{:S(2)}, u32[]{:S(2)}) collective-permute-start(f32[26,8,128]{2,1,0:T(8,128)} %copy.12), channel_id=1, source_target_pairs={{0,1},{1,2},{2,3},{4,5},{5,6},{6,7},{8,9},{9,10},{10,11},{12,13},{... | collective-permute-start | bytes 319496 | tf_op jit(solution)/shard_map/ppermute | solution.py:246
  11.5 1.3 pad_dynamic-slice_fusion.1
  14.3 1.4 %copy.13 = f32[26,8,128]{1,2,0:T(8,128)S(1)} copy(f32[26,8,128]{2,1,0:T(8,128)} %collective-permute-done.1) | data formatting | bytes 212992 | tf_op jit(solution)/shard_map/ppermute | solution.py:246
  15.8 2.9 %maximum_maximum_fusion.rest_0_.rest_1_.ys_r = f32[34,128,256]{2,1,0:T(8,128)S(1)} fusion(f32[8,128,8]{2,1,0:T(8,128)} %pad_dynamic-slice_fusion, f32[8,128,136]{2,1,0:T(8,128)} %pad_dynamic-slice_fusion.1, f32[26,128,8]{2,1,0:T(8,128)S(1)} %bitcast.30, f32[26,128,8]{2,1,0:T(8,128)S(1)} %bitcast.29, f32[2,128,128]{2,1,0:T(8,128)S(1)} %copy-done.11, ...), kind=kLoop, calls=%fused_computation.3 | loop fusion | flops 8912896 | bytes 7032832 | tf_op jit(solution)/shard_map/concatenate | solution.py:259
  18.7 2.0 %copy-done = f32[34,128,256]{2,1,0:T(8,128)} copy-done((f32[34,128,256]{2,1,0:T(8,128)}, f32[34,128,256]{2,1,0:T(8,128)S(1)}, u32[]{:S(2)}) %copy-start) | copy-done | bytes 4456472
  20.7 1.3 collective-permute-start.2
  22.1 5.8 %collective-permute-start.3 = (f32[34,8,256]{2,1,0:T(8,128)S(1)}, f32[34,8,256]{2,1,0:T(8,128)S(1)}, u32[]{:S(2)}, u32[]{:S(2)}) collective-permute-start(f32[34,8,256]{2,1,0:T(8,128)S(1)} %get-tuple-element.26), channel_id=1, source_target_pairs={{0,4},{4,8},{8,12},{1,5},{5,9},{9,13},{2,6},{6,10},{10,14},{3,7},{... | collective-permute-start | bytes 835592 | tf_op jit(solution)/shard_map/ppermute | solution.py:261
  27.9 2.8 %gather_fusion = f32[3,128,256]{2,1,0:T(8,128)S(1)} fusion(f32[34,128,256]{2,1,0:T(8,128)} %copy-done, s32[1024]{0:T(1024)S(1)} %pad_clamp_fusion), kind=kCustom, calls=%fused_computation | custom fusion | bytes 786444 | tf_op jit(solution)/shard_map/gather | solution.py:266
  30.7 2.4 %collective-permute-done.2.rest_1_.rest_2_.yb_r = f32[34,8,256]{2,1,0:T(8,128)S(1)} collective-permute-done((f32[34,8,256]{2,1,0:T(8,128)S(1)}, f32[34,8,256]{2,1,0:T(8,128)S(1)}, u32[]{:S(2)}, u32[]{:S(2)}) %collective-permute-start.2) | collective-permute-done | bytes 278560 | tf_op jit(solution)/shard_map/ppermute | solution.py:262
  35.0 1.6 %collective-permute-start.4 = (f32[2,144,256]{2,1,0:T(8,128)S(1)}, f32[2,144,256]{2,1,0:T(8,128)S(1)}, u32[]{:S(2)}, u32[]{:S(2)}) collective-permute-start(f32[2,144,256]{2,1,0:T(8,128)S(1)} %slice.45), channel_id=1, source_target_pairs={{0,16},{16,0},{1,17},{17,1},{2,18},{18,2},{3,19},{19,3},{4,20},{20... | collective-permute-start | bytes 884744 | tf_op jit(solution)/shard_map/ppermute | solution.py:292
  39.0 4.8 %collective-permute-done.4.rest_3_.rest_4_ = f32[2,144,256]{2,1,0:T(8,128)S(1)} collective-permute-done((f32[2,144,256]{2,1,0:T(8,128)S(1)}, f32[2,144,256]{2,1,0:T(8,128)S(1)}, u32[]{:S(2)}, u32[]{:S(2)}) %collective-permute-start.4) | collective-permute-done | bytes 294944 | tf_op jit(solution)/shard_map/ppermute | solution.py:292
  44.5 6.4 %shard_map.95 = (f32[16,144,256]{2,1,0:T(8,128)}, f32[2,144,256]{2,1,0:T(8,128)}) custom-call(s32[3]{0:T(128)} %pad_add_fusion.pos_r.r_0_, f32[8]{0:T(128)} %add_divide_fusion.prof_r, f32[2,128,128]{2,1,0:T(8,128)} %pad.8.fl_r.r_1_, f32[34,128,256]{2,1,0:T(8,128)} %copy-done, f32[34,8,256]{2,1,0:T(8,128)} %copy-done.3, f32[34,8,256]{2,1,0:T(8,128)} %copy-done.4, ...), custom_call_target="tpu_custom_call" | custom-call | tf_op jit(solution)/shard_map/pallas_call | solution.py:350
  52.0 7.0 %collective-permute-done.5.rest_4_.rest_5_ = f32[2,144,256]{2,1,0:T(8,128)S(1)} collective-permute-done((f32[2,144,256]{2,1,0:T(8,128)}, f32[2,144,256]{2,1,0:T(8,128)S(1)}, u32[]{:S(2)}, u32[]{:S(2)}) %collective-permute-start.5) | collective-permute-done | bytes 294944 | tf_op jit(solution)/shard_map/ppermute | solution.py:301
  59.7 7.1 %shard_map.96 = (f32[16,144,256]{2,1,0:T(8,128)}, f32[2,144,256]{2,1,0:T(8,128)}) custom-call(s32[3]{0:T(128)} %pad_add_fusion.pos_r.r_0_, f32[8]{0:T(128)} %add_divide_fusion.prof_r, f32[2,128,128]{2,1,0:T(8,128)} %pad.8.fl_r.r_1_, f32[16,144,256]{2,1,0:T(8,128)} %get-tuple-element.14.rest_0_, f32[34,128,256]{2,1,0:T(8,128)} %copy-done, ...), custom_call_target="tpu_custom_call" | custom-call | tf_op jit(solution)/shard_map/pallas_call | solution.py:350
  67.5 1.5 %collective-permute-start.7 = (f32[1,144,256]{2,1,0:T(8,128)S(1)}, f32[1,144,256]{2,1,0:T(8,128)S(1)}, u32[]{:S(2)}, u32[]{:S(2)}) collective-permute-start(f32[1,144,256]{2,1,0:T(8,128)S(1)} %slice.46), channel_id=1, source_target_pairs={{0,16},{16,0},{1,17},{17,1},{2,18},{18,2},{3,19},{19,3},{4,20},{20... | collective-permute-start | bytes 442376 | tf_op jit(solution)/shard_map/ppermute | solution.py:293
  68.9 8.2 %collective-permute-done.7.rest_0_ = f32[1,144,256]{2,1,0:T(8,128)S(1)} collective-permute-done((f32[1,144,256]{2,1,0:T(8,128)S(1)}, f32[1,144,256]{2,1,0:T(8,128)S(1)}, u32[]{:S(2)}, u32[]{:S(2)}) %collective-permute-start.7) | collective-permute-done | bytes 147488 | tf_op jit(solution)/shard_map/ppermute | solution.py:293
  77.9 9.5 %shard_map.97 = (f32[8,144,256]{2,1,0:T(8,128)}, f32[2,8,128,128]{3,2,1,0:T(8,128)}, f32[8,144,256]{2,1,0:T(8,128)}, f32[144,256]{1,0:T(8,128)}) custom-call(s32[3]{0:T(128)} %pad_add_fusion.pos_r.r_0_, f32[8]{0:T(128)} %add_divide_fusion.prof_r, f32[2,128,128]{2,1,0:T(8,128)} %pad.8.fl_r.r_1_, f32[16,144,256]{2,1,0:T(8,128)} %get-tuple-element.16.f_r, ...), custom_call_target="tpu_custom_call" | custom-call | tf_op jit(solution)/shard_map/pallas_call | solution.py:327
  87.7 5.1 %collective-permute-done.8.r_4_.r_5_ = f32[144,256]{1,0:T(8,128)S(1)} collective-permute-done((f32[144,256]{1,0:T(8,128)}, f32[144,256]{1,0:T(8,128)S(1)}, u32[]{:S(2)}, u32[]{:S(2)}) %collective-permute-start.8) | collective-permute-done | bytes 147488 | tf_op jit(solution)/shard_map/ppermute | solution.py:360
  93.4 5.5 %shard_map.98 = (f32[8,144,256]{2,1,0:T(8,128)}, f32[144,256]{1,0:T(8,128)}) custom-call(s32[3]{0:T(128)} %pad_add_fusion.pos_r.r_0_, f32[2,128,128]{2,1,0:T(8,128)} %pad.8.fl_r.r_1_, f32[8,144,256]{2,1,0:T(8,128)} %get-tuple-element.19.r_2_, f32[8,144,256]{2,1,0:T(8,128)} %get-tuple-element.20.r_3_, f32[144,256]{1,0:T(8,128)} %copy-done.10, ...), custom_call_target="tpu_custom_call" | custom-call | tf_op jit(solution)/shard_map/pallas_call | solution.py:365
  99.2 5.1 %collective-permute-done.9.r_4_.r_5_ = f32[144,256]{1,0:T(8,128)S(1)} collective-permute-done((f32[144,256]{1,0:T(8,128)}, f32[144,256]{1,0:T(8,128)S(1)}, u32[]{:S(2)}, u32[]{:S(2)}) %collective-permute-start.9) | collective-permute-done | bytes 147488 | tf_op jit(solution)/shard_map/ppermute | solution.py:360
  104.9 5.3 %shard_map.99 = (f32[8,144,256]{2,1,0:T(8,128)}, f32[144,256]{1,0:T(8,128)}) custom-call(s32[3]{0:T(128)} %pad_add_fusion.pos_r.r_0_, f32[2,128,128]{2,1,0:T(8,128)} %pad.8.fl_r.r_1_, f32[8,144,256]{2,1,0:T(8,128)} %get-tuple-element.22.r_2_, f32[8,144,256]{2,1,0:T(8,128)} %get-tuple-element.20.r_3_, f32[144,256]{1,0:T(8,128)} %copy-done.9, f32[144,256]{1,0:T(8,128)} %copy-done.9), custom_call_target="tpu_custom_call" | custom-call | tf_op jit(solution)/shard_map/pallas_call | solution.py:365
  110.5 5.1 %collective-permute-done.10.r_4_.r_5_ = f32[144,256]{1,0:T(8,128)S(1)} collective-permute-done((f32[144,256]{1,0:T(8,128)}, f32[144,256]{1,0:T(8,128)S(1)}, u32[]{:S(2)}, u32[]{:S(2)}) %collective-permute-start.10) | collective-permute-done | bytes 147488 | tf_op jit(solution)/shard_map/ppermute | solution.py:360
  116.2 3.9 %shard_map.100 = f32[8,128,128]{2,1,0:T(8,128)} custom-call(s32[3]{0:T(128)} %pad_add_fusion.pos_r.r_0_, f32[2,128,128]{2,1,0:T(8,128)} %pad.8.fl_r.r_1_, f32[8,144,256]{2,1,0:T(8,128)} %get-tuple-element.24.r_2_, f32[8,144,256]{2,1,0:T(8,128)} %get-tuple-element.20.r_3_, f32[144,256]{1,0:T(8,128)} %copy-done.8, f32[144,256]{1,0:T(8,128)} %copy-done.8), custom_call_target="tpu_custom_call" | custom-call | tf_op jit(solution)/shard_map/pallas_call | solution.py:365
  120.2 1.3 collective-permute-start.11
  121.5 10.0 %collective-permute-done.11 = f32[8,128,128]{2,1,0:T(8,128)S(1)} collective-permute-done((f32[8,128,128]{2,1,0:T(8,128)}, f32[8,128,128]{2,1,0:T(8,128)S(1)}, u32[]{:S(2)}, u32[]{:S(2)}) %collective-permute-start.11) | collective-permute-done | bytes 524320 | tf_op jit(solution)/shard_map/ppermute | solution.py:197
  131.4 1.1 select_bitcast_fusion.1
  132.7 2.6 %collective-permute-done.12 = f32[2,8,128,128]{3,2,1,0:T(8,128)S(1)} collective-permute-done((f32[2,8,128,128]{3,2,1,0:T(8,128)S(1)}, f32[2,8,128,128]{3,2,1,0:T(8,128)S(1)}, u32[]{:S(2)}, u32[]{:S(2)}) %collective-permute-start.12) | collective-permute-done | bytes 1048608 | tf_op jit(solution)/shard_map/ppermute | solution.py:200
  135.6 1.3 pad_maximum_fusion.1
  (64 shorter events, 14.3 us)
Async XLA Ops:
  3.9 7.6 %copy-start.1 = (f32[8,128,384]{2,1,0:T(8,128)S(1)}, f32[8,128,384]{2,1,0:T(8,128)}, u32[]{:S(2)}) copy-start(f32[8,128,384]{2,1,0:T(8,128)} %param.13) | copy-start | bytes 4718596
  3.9 9.9 %collective-permute-start = (f32[26,8,128]{2,1,0:T(8,128)}, f32[26,8,128]{2,1,0:T(8,128)S(1)}, u32[]{:S(2)}, u32[]{:S(2)}) collective-permute-start(f32[26,8,128]{2,1,0:T(8,128)} %copy.10), channel_id=1, source_target_pairs={{1,0},{2,1},{3,2},{5,4},{6,5},{7,6},{9,8},{10,9},{11,10},{13,12},{... | collective-permute-start | bytes 319496 | tf_op jit(solution)/shard_map/ppermute | solution.py:247
  6.5 7.9 %collective-permute-start.1 = (f32[26,8,128]{2,1,0:T(8,128)}, f32[26,8,128]{2,1,0:T(8,128)}, u32[]{:S(2)}, u32[]{:S(2)}) collective-permute-start(f32[26,8,128]{2,1,0:T(8,128)} %copy.12), channel_id=1, source_target_pairs={{0,1},{1,2},{2,3},{4,5},{5,6},{6,7},{8,9},{9,10},{10,11},{12,13},{... | collective-permute-start | bytes 319496 | tf_op jit(solution)/shard_map/ppermute | solution.py:246
  13.8 1.9 %copy-start.11 = (f32[2,128,128]{2,1,0:T(8,128)S(1)}, f32[2,128,128]{2,1,0:T(8,128)}, u32[]{:S(2)}) copy-start(f32[2,128,128]{2,1,0:T(8,128)} %param.10) | copy-start | bytes 393220
  15.7 6.3 %copy-start.14 = (s32[3]{0:T(128)S(1)}, s32[3]{0:T(128)}, u32[]{:S(2)}) copy-start(s32[3]{0:T(128)} %constant.76.clone) | copy-start | bytes 40
  15.7 6.3 %copy-start.15 = (s32[3]{0:T(128)S(1)}, s32[3]{0:T(128)}, u32[]{:S(2)}) copy-start(s32[3]{0:T(128)} %constant.77.clone) | copy-start | bytes 40
  18.6 2.1 %copy-start = (f32[34,128,256]{2,1,0:T(8,128)}, f32[34,128,256]{2,1,0:T(8,128)S(1)}, u32[]{:S(2)}) copy-start(f32[34,128,256]{2,1,0:T(8,128)S(1)} %maximum_maximum_fusion.rest_0_.rest_1_.ys_r) | copy-start | bytes 13369348
  20.7 16.5 %copy-start.13 = (s32[2,64,64]{2,1,0:T(8,128)S(1)}, s32[2,64,64]{2,1,0:T(8,128)}, u32[]{:S(2)}) copy-start(s32[2,64,64]{2,1,0:T(8,128)} %param.12) | copy-start | bytes 98308
  20.7 12.4 %collective-permute-start.2 = (f32[34,8,256]{2,1,0:T(8,128)S(1)}, f32[34,8,256]{2,1,0:T(8,128)S(1)}, u32[]{:S(2)}, u32[]{:S(2)}) collective-permute-start(f32[34,8,256]{2,1,0:T(8,128)S(1)} %get-tuple-element.27), channel_id=1, source_target_pairs={{4,0},{8,4},{12,8},{5,1},{9,5},{13,9},{6,2},{10,6},{14,10},{7,3},{... | collective-permute-start | bytes 835592 | tf_op jit(solution)/shard_map/ppermute | solution.py:262
  22.1 12.3 %collective-permute-start.3 = (f32[34,8,256]{2,1,0:T(8,128)S(1)}, f32[34,8,256]{2,1,0:T(8,128)S(1)}, u32[]{:S(2)}, u32[]{:S(2)}) collective-permute-start(f32[34,8,256]{2,1,0:T(8,128)S(1)} %get-tuple-element.26), channel_id=1, source_target_pairs={{0,4},{4,8},{8,12},{1,5},{5,9},{9,13},{2,6},{6,10},{10,14},{3,7},{... | collective-permute-start | bytes 835592 | tf_op jit(solution)/shard_map/ppermute | solution.py:261
  33.2 10.6 %copy-start.3 = (f32[34,8,256]{2,1,0:T(8,128)}, f32[34,8,256]{2,1,0:T(8,128)S(1)}, u32[]{:S(2)}) copy-start(f32[34,8,256]{2,1,0:T(8,128)S(1)} %collective-permute-done.2.rest_1_.rest_2_.yb_r) | copy-start | bytes 835588
  34.4 9.4 %copy-start.4 = (f32[34,8,256]{2,1,0:T(8,128)}, f32[34,8,256]{2,1,0:T(8,128)S(1)}, u32[]{:S(2)}) copy-start(f32[34,8,256]{2,1,0:T(8,128)S(1)} %collective-permute-done.3.rest_2_.rest_3_.ya_r) | copy-start | bytes 835588
  35.0 8.8 %collective-permute-start.4 = (f32[2,144,256]{2,1,0:T(8,128)S(1)}, f32[2,144,256]{2,1,0:T(8,128)S(1)}, u32[]{:S(2)}, u32[]{:S(2)}) collective-permute-start(f32[2,144,256]{2,1,0:T(8,128)S(1)} %slice.45), channel_id=1, source_target_pairs={{0,16},{16,0},{1,17},{17,1},{2,18},{18,2},{3,19},{19,3},{4,20},{20... | collective-permute-start | bytes 884744 | tf_op jit(solution)/shard_map/ppermute | solution.py:292
  43.8 0.7 copy-start.5
  50.9 8.1 %collective-permute-start.5 = (f32[2,144,256]{2,1,0:T(8,128)}, f32[2,144,256]{2,1,0:T(8,128)S(1)}, u32[]{:S(2)}, u32[]{:S(2)}) collective-permute-start(f32[2,144,256]{2,1,0:T(8,128)} %get-tuple-element.15), channel_id=1, source_target_pairs={{0,16},{16,0},{1,17},{17,1},{2,18},{18,2},{3,19},{19,3},{4,20},{20... | collective-permute-start | bytes 884744 | tf_op jit(solution)/shard_map/ppermute | solution.py:301
  59.0 0.7 copy-start.7
  66.8 10.3 %collective-permute-start.6 = (f32[2,144,256]{2,1,0:T(8,128)}, f32[2,144,256]{2,1,0:T(8,128)S(1)}, u32[]{:S(2)}, u32[]{:S(2)}) collective-permute-start(f32[2,144,256]{2,1,0:T(8,128)} %get-tuple-element.17), channel_id=1, source_target_pairs={{0,16},{16,0},{1,17},{17,1},{2,18},{18,2},{3,19},{19,3},{4,20},{20... | collective-permute-start | bytes 884744 | tf_op jit(solution)/shard_map/ppermute | solution.py:301
  67.5 9.7 %collective-permute-start.7 = (f32[1,144,256]{2,1,0:T(8,128)S(1)}, f32[1,144,256]{2,1,0:T(8,128)S(1)}, u32[]{:S(2)}, u32[]{:S(2)}) collective-permute-start(f32[1,144,256]{2,1,0:T(8,128)S(1)} %slice.46), channel_id=1, source_target_pairs={{0,16},{16,0},{1,17},{17,1},{2,18},{18,2},{3,19},{19,3},{4,20},{20... | collective-permute-start | bytes 442376 | tf_op jit(solution)/shard_map/ppermute | solution.py:293
  77.1 0.7 copy-start.12
  77.1 0.8 copy-start.6
  87.4 5.4 %collective-permute-start.8 = (f32[144,256]{1,0:T(8,128)}, f32[144,256]{1,0:T(8,128)S(1)}, u32[]{:S(2)}, u32[]{:S(2)}) collective-permute-start(f32[144,256]{1,0:T(8,128)} %get-tuple-element.21), channel_id=1, source_target_pairs={{0,16},{16,0},{1,17},{17,1},{2,18},{18,2},{3,19},{19,3},{4,20},{20... | collective-permute-start | bytes 442376 | tf_op jit(solution)/shard_map/ppermute | solution.py:360
  92.7 0.7 copy-start.10
  98.9 5.4 %collective-permute-start.9 = (f32[144,256]{1,0:T(8,128)}, f32[144,256]{1,0:T(8,128)S(1)}, u32[]{:S(2)}, u32[]{:S(2)}) collective-permute-start(f32[144,256]{1,0:T(8,128)} %get-tuple-element.23), channel_id=1, source_target_pairs={{0,16},{16,0},{1,17},{17,1},{2,18},{18,2},{3,19},{19,3},{4,20},{20... | collective-permute-start | bytes 442376 | tf_op jit(solution)/shard_map/ppermute | solution.py:360
  104.3 0.7 copy-start.9
  110.2 5.4 %collective-permute-start.10 = (f32[144,256]{1,0:T(8,128)}, f32[144,256]{1,0:T(8,128)S(1)}, u32[]{:S(2)}, u32[]{:S(2)}) collective-permute-start(f32[144,256]{1,0:T(8,128)} %get-tuple-element.25), channel_id=1, source_target_pairs={{0,16},{16,0},{1,17},{17,1},{2,18},{18,2},{3,19},{19,3},{4,20},{20... | collective-permute-start | bytes 442376 | tf_op jit(solution)/shard_map/ppermute | solution.py:360
  115.6 0.6 copy-start.8
  120.2 11.3 %collective-permute-start.11 = (f32[8,128,128]{2,1,0:T(8,128)}, f32[8,128,128]{2,1,0:T(8,128)S(1)}, u32[]{:S(2)}, u32[]{:S(2)}) collective-permute-start(f32[8,128,128]{2,1,0:T(8,128)} %shard_map.100), channel_id=1, source_target_pairs={{2,0},{3,1},{1,2},{6,4},{7,5},{5,6},{10,8},{11,9},{9,10},{14,12},{... | collective-permute-start | bytes 1572872 | tf_op jit(solution)/shard_map/ppermute | solution.py:197
  121.5 13.9 %copy-start.2 = (f32[8,128,128]{2,1,0:T(8,128)S(1)}, f32[8,128,128]{2,1,0:T(8,128)}, u32[]{:S(2)}) copy-start(f32[8,128,128]{2,1,0:T(8,128)} %shard_map.100) | copy-start | bytes 1572868
  132.7 2.7 %collective-permute-start.12 = (f32[2,8,128,128]{3,2,1,0:T(8,128)S(1)}, f32[2,8,128,128]{3,2,1,0:T(8,128)S(1)}, u32[]{:S(2)}, u32[]{:S(2)}) collective-permute-start(f32[2,8,128,128]{3,2,1,0:T(8,128)S(1)} %pad_maximum_fusion.2), channel_id=1, source_target_pairs={{0,1},{1,0},{2,3},{3,2},{4,5},{5,4},{6,7},{7,6},{8,9},{9,8},{10,11... | collective-permute-start | bytes 3145736 | tf_op jit(solution)/shard_map/ppermute | solution.py:200

commit v14 on v12

--- a/solution.py
+++ b/solution.py
@@ -249,10 +249,11 @@
          jnp.swapaxes(from_left, 1, 2)], axis=2)
 
     j_start = x_start - offset
-    kpad = jnp.pad(specimen_kelvin_values, ((0, 0), (0, 0), (H, H)))
-    t_body = lax.dynamic_slice_in_dim(kpad, j_start + H, breadth + H, 2)
-    t_tail = lax.dynamic_slice_in_dim(kpad, j_start, H, 2)
-    t_x = jnp.concatenate([t_body, jnp.zeros((depth, height, gap), jnp.float32), t_tail], axis=2)
+    t_own = lax.dynamic_slice_in_dim(specimen_kelvin_values, j_start, breadth, 2)
+    t_after = lax.dynamic_slice_in_dim(specimen_kelvin_values, j_start + breadth, H, 2)
+    t_tail = lax.dynamic_slice_in_dim(specimen_kelvin_values, j_start - H, H, 2)
+    t_x = jnp.concatenate(
+        [t_own, t_after, jnp.zeros((depth, height, gap), jnp.float32), t_tail], axis=2)
 
     ystack = jnp.concatenate([xext, t_x], axis=0)
     up_y, down_y = _line_pairs(n_gy)

time: 137 us -> 137 us (level)
  no operation moved by 1% of the time
where the time goes in v14:
time: 137 us
  waiting for transfers between devices  50.9 us (37%)
  Pallas kernels  37.7 us (28%)
  local copies, waits for them, and re-layouts  19.2 us (14%)
  starting transfers between devices  19.1 us (14%)
  other arithmetic  8.3 us (6%)
  between operations  1.58 us (1%)
    ppermute x3, waiting for transfers between devices, on_device(): tzlo = tzhi = lax.ppermute(send_t, 'gz', both)  15.2 us
    pallas_call x3, Pallas kernels, on_device(): _vmem_call(lambda *r, last=last: _heat_kernel(last, pair, depth, t_totals...  14.8 us
    pallas_call x2, Pallas kernels, on_device(): _vmem_call(sweep, outs, 8 + len(fargs), 2)  13.5 us
    ppermute x1, waiting for transfers between devices, _broadcast_blocks(): r1 = lax.ppermute(own, 'gx', [(2, 0), (3, 1), (1, 2)])  9.96 us
    pallas_call x1, Pallas kernels, on_device(): _vmem_call(fused, outs, 9 + len(extra), 2)  9.49 us
    ppermute x1, waiting for transfers between devices, on_device(): got_t = lax.ppermute(first[2:], 'gz', both)  8.22 us
    ppermute x2, waiting for transfers between devices, on_device(): zlo = zhi = got if i == 0 else lax.ppermute(send, 'gz', both)  6.99 us
    unnamed x34, local copies, waits for them, and re-layouts  6.31 us
  transfers between devices with their start and end apart: 13, of which 10 were waited for; matrix products, arithmetic and copies ran while one was open for 8% of the time, Pallas kernels for 0%

profile of v14, /device:TPU:0, one launch (start us, length us, event | category | flops | bytes accessed | tf_op | source)
XLA Modules:
  0.0 136.8 jit_solution(3387875294314597204)
XLA Ops:
  0.6 1.6 %pad_maximum_fusion = f32[26,128,128]{2,1,0:T(8,128)S(1)} fusion(f32[2,128,128]{2,1,0:T(8,128)} %param.10, f32[8,128,128]{2,1,0:T(8,128)} %param.9, f32[16,128,128]{2,1,0:T(8,128)} %bitcast.31), kind=kLoop, calls=%fused_computation.6 | loop fusion | flops 851968 | bytes 3407872 | tf_op jit(solution)/shard_map/concatenate | solution.py:240
  2.8 1.1 copy.10
  3.9 1.4 %collective-permute-start = (f32[26,8,128]{2,1,0:T(8,128)}, f32[26,8,128]{2,1,0:T(8,128)S(1)}, u32[]{:S(2)}, u32[]{:S(2)}) collective-permute-start(f32[26,8,128]{2,1,0:T(8,128)} %copy.10), channel_id=1, source_target_pairs={{1,0},{2,1},{3,2},{5,4},{6,5},{7,6},{9,8},{10,9},{11,10},{13,12},{... | collective-permute-start | bytes 319496 | tf_op jit(solution)/shard_map/ppermute | solution.py:245
  5.4 1.1 copy.12
  6.5 3.7 %collective-permute-start.1 = (f32[26,8,128]{2,1,0:T(8,128)}, f32[26,8,128]{2,1,0:T(8,128)}, u32[]{:S(2)}, u32[]{:S(2)}) collective-permute-start(f32[26,8,128]{2,1,0:T(8,128)} %copy.12), channel_id=1, source_target_pairs={{0,1},{1,2},{2,3},{4,5},{5,6},{6,7},{8,9},{9,10},{10,11},{12,13},{... | collective-permute-start | bytes 319496 | tf_op jit(solution)/shard_map/ppermute | solution.py:244
  11.5 1.3 constant_dynamic-slice_fusion.1
  14.2 1.4 %copy.13 = f32[26,8,128]{1,2,0:T(8,128)S(1)} copy(f32[26,8,128]{2,1,0:T(8,128)} %collective-permute-done.1) | data formatting | bytes 212992 | tf_op jit(solution)/shard_map/ppermute | solution.py:244
  15.6 2.9 %maximum_maximum_fusion.rest_0_.rest_1_.ys_r = f32[34,128,256]{2,1,0:T(8,128)S(1)} fusion(f32[8,128,8]{2,1,0:T(8,128)} %get-tuple-element.34, f32[8,128,8]{2,1,0:T(8,128)} %get-tuple-element.33, f32[8,128,128]{2,1,0:T(8,128)} %constant_dynamic-slice_fusion.2, f32[26,128,8]{2,1,0:T(8,128)S(1)} %bitcast.30, f32[26,128,8]{2,1,0:T(8,128)S(1)} %bitcast.29, ...), kind=kLoop, calls=%fused_computation.3 | loop fusion | flops 10027008 | bytes 7032832 | tf_op jit(solution)/shard_map/concatenate | solution.py:258
  18.5 2.1 %copy-done = f32[34,128,256]{2,1,0:T(8,128)} copy-done((f32[34,128,256]{2,1,0:T(8,128)}, f32[34,128,256]{2,1,0:T(8,128)S(1)}, u32[]{:S(2)}) %copy-start) | copy-done | bytes 4456472
  20.6 1.3 collective-permute-start.2
  21.9 5.8 %collective-permute-start.3 = (f32[34,8,256]{2,1,0:T(8,128)S(1)}, f32[34,8,256]{2,1,0:T(8,128)S(1)}, u32[]{:S(2)}, u32[]{:S(2)}) collective-permute-start(f32[34,8,256]{2,1,0:T(8,128)S(1)} %get-tuple-element.26), channel_id=1, source_target_pairs={{0,4},{4,8},{8,12},{1,5},{5,9},{9,13},{2,6},{6,10},{10,14},{3,7},{... | collective-permute-start | bytes 835592 | tf_op jit(solution)/shard_map/ppermute | solution.py:260
  27.7 2.8 %gather_fusion = f32[3,128,256]{2,1,0:T(8,128)S(1)} fusion(f32[34,128,256]{2,1,0:T(8,128)} %copy-done, s32[1024]{0:T(1024)S(1)} %pad_clamp_fusion), kind=kCustom, calls=%fused_computation | custom fusion | bytes 786444 | tf_op jit(solution)/shard_map/gather | solution.py:265
  30.6 2.4 %collective-permute-done.2.rest_1_.rest_2_.yb_r = f32[34,8,256]{2,1,0:T(8,128)S(1)} collective-permute-done((f32[34,8,256]{2,1,0:T(8,128)S(1)}, f32[34,8,256]{2,1,0:T(8,128)S(1)}, u32[]{:S(2)}, u32[]{:S(2)}) %collective-permute-start.2) | collective-permute-done | bytes 278560 | tf_op jit(solution)/shard_map/ppermute | solution.py:261
  34.9 1.6 %collective-permute-start.4 = (f32[2,144,256]{2,1,0:T(8,128)S(1)}, f32[2,144,256]{2,1,0:T(8,128)S(1)}, u32[]{:S(2)}, u32[]{:S(2)}) collective-permute-start(f32[2,144,256]{2,1,0:T(8,128)S(1)} %slice.45), channel_id=1, source_target_pairs={{0,16},{16,0},{1,17},{17,1},{2,18},{18,2},{3,19},{19,3},{4,20},{20... | collective-permute-start | bytes 884744 | tf_op jit(solution)/shard_map/ppermute | solution.py:291
  38.9 4.8 %collective-permute-done.4.rest_3_.rest_4_ = f32[2,144,256]{2,1,0:T(8,128)S(1)} collective-permute-done((f32[2,144,256]{2,1,0:T(8,128)S(1)}, f32[2,144,256]{2,1,0:T(8,128)S(1)}, u32[]{:S(2)}, u32[]{:S(2)}) %collective-permute-start.4) | collective-permute-done | bytes 294944 | tf_op jit(solution)/shard_map/ppermute | solution.py:291
  44.4 6.4 %shard_map.95 = (f32[16,144,256]{2,1,0:T(8,128)}, f32[2,144,256]{2,1,0:T(8,128)}) custom-call(s32[3]{0:T(128)} %pad_add_fusion.pos_r.r_0_, f32[8]{0:T(128)} %add_divide_fusion.prof_r, f32[2,128,128]{2,1,0:T(8,128)} %pad.4.fl_r.r_1_, f32[34,128,256]{2,1,0:T(8,128)} %copy-done, f32[34,8,256]{2,1,0:T(8,128)} %copy-done.2, f32[34,8,256]{2,1,0:T(8,128)} %copy-done.3, ...), custom_call_target="tpu_custom_call" | custom-call | tf_op jit(solution)/shard_map/pallas_call | solution.py:349
  51.9 7.0 %collective-permute-done.5.rest_4_.rest_5_ = f32[2,144,256]{2,1,0:T(8,128)S(1)} collective-permute-done((f32[2,144,256]{2,1,0:T(8,128)}, f32[2,144,256]{2,1,0:T(8,128)S(1)}, u32[]{:S(2)}, u32[]{:S(2)}) %collective-permute-start.5) | collective-permute-done | bytes 294944 | tf_op jit(solution)/shard_map/ppermute | solution.py:300
  59.6 7.0 %shard_map.96 = (f32[16,144,256]{2,1,0:T(8,128)}, f32[2,144,256]{2,1,0:T(8,128)}) custom-call(s32[3]{0:T(128)} %pad_add_fusion.pos_r.r_0_, f32[8]{0:T(128)} %add_divide_fusion.prof_r, f32[2,128,128]{2,1,0:T(8,128)} %pad.4.fl_r.r_1_, f32[16,144,256]{2,1,0:T(8,128)} %get-tuple-element.14.rest_0_, f32[34,128,256]{2,1,0:T(8,128)} %copy-done, ...), custom_call_target="tpu_custom_call" | custom-call | tf_op jit(solution)/shard_map/pallas_call | solution.py:349
  67.3 1.4 %collective-permute-start.7 = (f32[1,144,256]{2,1,0:T(8,128)S(1)}, f32[1,144,256]{2,1,0:T(8,128)S(1)}, u32[]{:S(2)}, u32[]{:S(2)}) collective-permute-start(f32[1,144,256]{2,1,0:T(8,128)S(1)} %slice.46), channel_id=1, source_target_pairs={{0,16},{16,0},{1,17},{17,1},{2,18},{18,2},{3,19},{19,3},{4,20},{20... | collective-permute-start | bytes 442376 | tf_op jit(solution)/shard_map/ppermute | solution.py:292
  68.8 8.2 %collective-permute-done.7.rest_0_ = f32[1,144,256]{2,1,0:T(8,128)S(1)} collective-permute-done((f32[1,144,256]{2,1,0:T(8,128)S(1)}, f32[1,144,256]{2,1,0:T(8,128)S(1)}, u32[]{:S(2)}, u32[]{:S(2)}) %collective-permute-start.7) | collective-permute-done | bytes 147488 | tf_op jit(solution)/shard_map/ppermute | solution.py:292
  77.8 9.5 %shard_map.97 = (f32[8,144,256]{2,1,0:T(8,128)}, f32[2,8,128,128]{3,2,1,0:T(8,128)}, f32[8,144,256]{2,1,0:T(8,128)}, f32[144,256]{1,0:T(8,128)}) custom-call(s32[3]{0:T(128)} %pad_add_fusion.pos_r.r_0_, f32[8]{0:T(128)} %add_divide_fusion.prof_r, f32[2,128,128]{2,1,0:T(8,128)} %pad.4.fl_r.r_1_, f32[16,144,256]{2,1,0:T(8,128)} %get-tuple-element.16.f_r, ...), custom_call_target="tpu_custom_call" | custom-call | tf_op jit(solution)/shard_map/pallas_call | solution.py:326
  87.6 5.1 %collective-permute-done.8.r_4_.r_5_ = f32[144,256]{1,0:T(8,128)S(1)} collective-permute-done((f32[144,256]{1,0:T(8,128)}, f32[144,256]{1,0:T(8,128)S(1)}, u32[]{:S(2)}, u32[]{:S(2)}) %collective-permute-start.8) | collective-permute-done | bytes 147488 | tf_op jit(solution)/shard_map/ppermute | solution.py:359
  93.3 5.5 %shard_map.98 = (f32[8,144,256]{2,1,0:T(8,128)}, f32[144,256]{1,0:T(8,128)}) custom-call(s32[3]{0:T(128)} %pad_add_fusion.pos_r.r_0_, f32[2,128,128]{2,1,0:T(8,128)} %pad.4.fl_r.r_1_, f32[8,144,256]{2,1,0:T(8,128)} %get-tuple-element.19.r_2_, f32[8,144,256]{2,1,0:T(8,128)} %get-tuple-element.20.r_3_, f32[144,256]{1,0:T(8,128)} %copy-done.10, ...), custom_call_target="tpu_custom_call" | custom-call | tf_op jit(solution)/shard_map/pallas_call | solution.py:364
  99.1 5.1 %collective-permute-done.9.r_4_.r_5_ = f32[144,256]{1,0:T(8,128)S(1)} collective-permute-done((f32[144,256]{1,0:T(8,128)}, f32[144,256]{1,0:T(8,128)S(1)}, u32[]{:S(2)}, u32[]{:S(2)}) %collective-permute-start.9) | collective-permute-done | bytes 147488 | tf_op jit(solution)/shard_map/ppermute | solution.py:359
  104.8 5.3 %shard_map.99 = (f32[8,144,256]{2,1,0:T(8,128)}, f32[144,256]{1,0:T(8,128)}) custom-call(s32[3]{0:T(128)} %pad_add_fusion.pos_r.r_0_, f32[2,128,128]{2,1,0:T(8,128)} %pad.4.fl_r.r_1_, f32[8,144,256]{2,1,0:T(8,128)} %get-tuple-element.22.r_2_, f32[8,144,256]{2,1,0:T(8,128)} %get-tuple-element.20.r_3_, f32[144,256]{1,0:T(8,128)} %copy-done.9, f32[144,256]{1,0:T(8,128)} %copy-done.9), custom_call_target="tpu_custom_call" | custom-call | tf_op jit(solution)/shard_map/pallas_call | solution.py:364
  110.4 5.1 %collective-permute-done.10.r_4_.r_5_ = f32[144,256]{1,0:T(8,128)S(1)} collective-permute-done((f32[144,256]{1,0:T(8,128)}, f32[144,256]{1,0:T(8,128)S(1)}, u32[]{:S(2)}, u32[]{:S(2)}) %collective-permute-start.10) | collective-permute-done | bytes 147488 | tf_op jit(solution)/shard_map/ppermute | solution.py:359
  116.1 3.9 %shard_map.100 = f32[8,128,128]{2,1,0:T(8,128)} custom-call(s32[3]{0:T(128)} %pad_add_fusion.pos_r.r_0_, f32[2,128,128]{2,1,0:T(8,128)} %pad.4.fl_r.r_1_, f32[8,144,256]{2,1,0:T(8,128)} %get-tuple-element.24.r_2_, f32[8,144,256]{2,1,0:T(8,128)} %get-tuple-element.20.r_3_, f32[144,256]{1,0:T(8,128)} %copy-done.8, f32[144,256]{1,0:T(8,128)} %copy-done.8), custom_call_target="tpu_custom_call" | custom-call | tf_op jit(solution)/shard_map/pallas_call | solution.py:364
  120.1 1.3 collective-permute-start.11
  121.4 10.0 %collective-permute-done.11 = f32[8,128,128]{2,1,0:T(8,128)S(1)} collective-permute-done((f32[8,128,128]{2,1,0:T(8,128)}, f32[8,128,128]{2,1,0:T(8,128)S(1)}, u32[]{:S(2)}, u32[]{:S(2)}) %collective-permute-start.11) | collective-permute-done | bytes 524320 | tf_op jit(solution)/shard_map/ppermute | solution.py:195
  131.4 1.1 select_bitcast_fusion.1
  132.7 2.6 %collective-permute-done.12 = f32[2,8,128,128]{3,2,1,0:T(8,128)S(1)} collective-permute-done((f32[2,8,128,128]{3,2,1,0:T(8,128)S(1)}, f32[2,8,128,128]{3,2,1,0:T(8,128)S(1)}, u32[]{:S(2)}, u32[]{:S(2)}) %collective-permute-start.12) | collective-permute-done | bytes 1048608 | tf_op jit(solution)/shard_map/ppermute | solution.py:198
  135.5 1.3 pad_maximum_fusion.1
  (64 shorter events, 14.2 us)
Async XLA Ops:
  3.9 7.6 %copy-start.4 = (f32[8,128,384]{2,1,0:T(8,128)S(1)}, f32[8,128,384]{2,1,0:T(8,128)}, u32[]{:S(2)}) copy-start(f32[8,128,384]{2,1,0:T(8,128)} %param.13) | copy-start | bytes 4718596
  3.9 9.7 %collective-permute-start = (f32[26,8,128]{2,1,0:T(8,128)}, f32[26,8,128]{2,1,0:T(8,128)S(1)}, u32[]{:S(2)}, u32[]{:S(2)}) collective-permute-start(f32[26,8,128]{2,1,0:T(8,128)} %copy.10), channel_id=1, source_target_pairs={{1,0},{2,1},{3,2},{5,4},{6,5},{7,6},{9,8},{10,9},{11,10},{13,12},{... | collective-permute-start | bytes 319496 | tf_op jit(solution)/shard_map/ppermute | solution.py:245
  6.5 7.7 %collective-permute-start.1 = (f32[26,8,128]{2,1,0:T(8,128)}, f32[26,8,128]{2,1,0:T(8,128)}, u32[]{:S(2)}, u32[]{:S(2)}) collective-permute-start(f32[26,8,128]{2,1,0:T(8,128)} %copy.12), channel_id=1, source_target_pairs={{0,1},{1,2},{2,3},{4,5},{5,6},{6,7},{8,9},{9,10},{10,11},{12,13},{... | collective-permute-start | bytes 319496 | tf_op jit(solution)/shard_map/ppermute | solution.py:244
  13.7 1.9 %copy-start.11 = (f32[2,128,128]{2,1,0:T(8,128)S(1)}, f32[2,128,128]{2,1,0:T(8,128)}, u32[]{:S(2)}) copy-start(f32[2,128,128]{2,1,0:T(8,128)} %param.10) | copy-start | bytes 393220
  15.6 6.3 %copy-start.14 = (s32[3]{0:T(128)S(1)}, s32[3]{0:T(128)}, u32[]{:S(2)}) copy-start(s32[3]{0:T(128)} %constant.80.clone) | copy-start | bytes 40
  15.6 6.3 %copy-start.15 = (s32[3]{0:T(128)S(1)}, s32[3]{0:T(128)}, u32[]{:S(2)}) copy-start(s32[3]{0:T(128)} %constant.81.clone) | copy-start | bytes 40
  18.5 2.1 %copy-start = (f32[34,128,256]{2,1,0:T(8,128)}, f32[34,128,256]{2,1,0:T(8,128)S(1)}, u32[]{:S(2)}) copy-start(f32[34,128,256]{2,1,0:T(8,128)S(1)} %maximum_maximum_fusion.rest_0_.rest_1_.ys_r) | copy-start | bytes 13369348
  20.6 16.5 %copy-start.13 = (s32[2,64,64]{2,1,0:T(8,128)S(1)}, s32[2,64,64]{2,1,0:T(8,128)}, u32[]{:S(2)}) copy-start(s32[2,64,64]{2,1,0:T(8,128)} %param.12) | copy-start | bytes 98308
  20.6 12.4 %collective-permute-start.2 = (f32[34,8,256]{2,1,0:T(8,128)S(1)}, f32[34,8,256]{2,1,0:T(8,128)S(1)}, u32[]{:S(2)}, u32[]{:S(2)}) collective-permute-start(f32[34,8,256]{2,1,0:T(8,128)S(1)} %get-tuple-element.27), channel_id=1, source_target_pairs={{4,0},{8,4},{12,8},{5,1},{9,5},{13,9},{6,2},{10,6},{14,10},{7,3},{... | collective-permute-start | bytes 835592 | tf_op jit(solution)/shard_map/ppermute | solution.py:261
  21.9 12.3 %collective-permute-start.3 = (f32[34,8,256]{2,1,0:T(8,128)S(1)}, f32[34,8,256]{2,1,0:T(8,128)S(1)}, u32[]{:S(2)}, u32[]{:S(2)}) collective-permute-start(f32[34,8,256]{2,1,0:T(8,128)S(1)} %get-tuple-element.26), channel_id=1, source_target_pairs={{0,4},{4,8},{8,12},{1,5},{5,9},{9,13},{2,6},{6,10},{10,14},{3,7},{... | collective-permute-start | bytes 835592 | tf_op jit(solution)/shard_map/ppermute | solution.py:260
  33.0 10.6 %copy-start.2 = (f32[34,8,256]{2,1,0:T(8,128)}, f32[34,8,256]{2,1,0:T(8,128)S(1)}, u32[]{:S(2)}) copy-start(f32[34,8,256]{2,1,0:T(8,128)S(1)} %collective-permute-done.2.rest_1_.rest_2_.yb_r) | copy-start | bytes 835588
  34.3 9.4 %copy-start.3 = (f32[34,8,256]{2,1,0:T(8,128)}, f32[34,8,256]{2,1,0:T(8,128)S(1)}, u32[]{:S(2)}) copy-start(f32[34,8,256]{2,1,0:T(8,128)S(1)} %collective-permute-done.3.rest_2_.rest_3_.ya_r) | copy-start | bytes 835588
  34.9 8.8 %collective-permute-start.4 = (f32[2,144,256]{2,1,0:T(8,128)S(1)}, f32[2,144,256]{2,1,0:T(8,128)S(1)}, u32[]{:S(2)}, u32[]{:S(2)}) collective-permute-start(f32[2,144,256]{2,1,0:T(8,128)S(1)} %slice.45), channel_id=1, source_target_pairs={{0,16},{16,0},{1,17},{17,1},{2,18},{18,2},{3,19},{19,3},{4,20},{20... | collective-permute-start | bytes 884744 | tf_op jit(solution)/shard_map/ppermute | solution.py:291
  43.7 0.7 copy-start.5
  50.8 8.1 %collective-permute-start.5 = (f32[2,144,256]{2,1,0:T(8,128)}, f32[2,144,256]{2,1,0:T(8,128)S(1)}, u32[]{:S(2)}, u32[]{:S(2)}) collective-permute-start(f32[2,144,256]{2,1,0:T(8,128)} %get-tuple-element.15), channel_id=1, source_target_pairs={{0,16},{16,0},{1,17},{17,1},{2,18},{18,2},{3,19},{19,3},{4,20},{20... | collective-permute-start | bytes 884744 | tf_op jit(solution)/shard_map/ppermute | solution.py:300
  58.9 0.7 copy-start.7
  66.7 10.3 %collective-permute-start.6 = (f32[2,144,256]{2,1,0:T(8,128)}, f32[2,144,256]{2,1,0:T(8,128)S(1)}, u32[]{:S(2)}, u32[]{:S(2)}) collective-permute-start(f32[2,144,256]{2,1,0:T(8,128)} %get-tuple-element.17), channel_id=1, source_target_pairs={{0,16},{16,0},{1,17},{17,1},{2,18},{18,2},{3,19},{19,3},{4,20},{20... | collective-permute-start | bytes 884744 | tf_op jit(solution)/shard_map/ppermute | solution.py:300
  67.3 9.7 %collective-permute-start.7 = (f32[1,144,256]{2,1,0:T(8,128)S(1)}, f32[1,144,256]{2,1,0:T(8,128)S(1)}, u32[]{:S(2)}, u32[]{:S(2)}) collective-permute-start(f32[1,144,256]{2,1,0:T(8,128)S(1)} %slice.46), channel_id=1, source_target_pairs={{0,16},{16,0},{1,17},{17,1},{2,18},{18,2},{3,19},{19,3},{4,20},{20... | collective-permute-start | bytes 442376 | tf_op jit(solution)/shard_map/ppermute | solution.py:292
  77.0 0.7 copy-start.12
  77.0 0.8 copy-start.6
  87.3 5.4 %collective-permute-start.8 = (f32[144,256]{1,0:T(8,128)}, f32[144,256]{1,0:T(8,128)S(1)}, u32[]{:S(2)}, u32[]{:S(2)}) collective-permute-start(f32[144,256]{1,0:T(8,128)} %get-tuple-element.21), channel_id=1, source_target_pairs={{0,16},{16,0},{1,17},{17,1},{2,18},{18,2},{3,19},{19,3},{4,20},{20... | collective-permute-start | bytes 442376 | tf_op jit(solution)/shard_map/ppermute | solution.py:359
  92.6 0.6 copy-start.10
  98.8 5.4 %collective-permute-start.9 = (f32[144,256]{1,0:T(8,128)}, f32[144,256]{1,0:T(8,128)S(1)}, u32[]{:S(2)}, u32[]{:S(2)}) collective-permute-start(f32[144,256]{1,0:T(8,128)} %get-tuple-element.23), channel_id=1, source_target_pairs={{0,16},{16,0},{1,17},{17,1},{2,18},{18,2},{3,19},{19,3},{4,20},{20... | collective-permute-start | bytes 442376 | tf_op jit(solution)/shard_map/ppermute | solution.py:359
  104.2 0.7 copy-start.9
  110.1 5.4 %collective-permute-start.10 = (f32[144,256]{1,0:T(8,128)}, f32[144,256]{1,0:T(8,128)S(1)}, u32[]{:S(2)}, u32[]{:S(2)}) collective-permute-start(f32[144,256]{1,0:T(8,128)} %get-tuple-element.25), channel_id=1, source_target_pairs={{0,16},{16,0},{1,17},{17,1},{2,18},{18,2},{3,19},{19,3},{4,20},{20... | collective-permute-start | bytes 442376 | tf_op jit(solution)/shard_map/ppermute | solution.py:359
  115.5 0.6 copy-start.8
  120.1 11.3 %collective-permute-start.11 = (f32[8,128,128]{2,1,0:T(8,128)}, f32[8,128,128]{2,1,0:T(8,128)S(1)}, u32[]{:S(2)}, u32[]{:S(2)}) collective-permute-start(f32[8,128,128]{2,1,0:T(8,128)} %shard_map.100), channel_id=1, source_target_pairs={{2,0},{3,1},{1,2},{6,4},{7,5},{5,6},{10,8},{11,9},{9,10},{14,12},{... | collective-permute-start | bytes 1572872 | tf_op jit(solution)/shard_map/ppermute | solution.py:195
  121.4 13.9 %copy-start.1 = (f32[8,128,128]{2,1,0:T(8,128)S(1)}, f32[8,128,128]{2,1,0:T(8,128)}, u32[]{:S(2)}) copy-start(f32[8,128,128]{2,1,0:T(8,128)} %shard_map.100) | copy-start | bytes 1572868
  132.6 2.7 %collective-permute-start.12 = (f32[2,8,128,128]{3,2,1,0:T(8,128)S(1)}, f32[2,8,128,128]{3,2,1,0:T(8,128)S(1)}, u32[]{:S(2)}, u32[]{:S(2)}) collective-permute-start(f32[2,8,128,128]{3,2,1,0:T(8,128)S(1)} %pad_maximum_fusion.2), channel_id=1, source_target_pairs={{0,1},{1,0},{2,3},{3,2},{4,5},{5,4},{6,7},{7,6},{8,9},{9,8},{10,11... | collective-permute-start | bytes 3145736 | tf_op jit(solution)/shard_map/ppermute | solution.py:198

commit v15 on v12

--- a/solution.py
+++ b/solution.py
@@ -193,11 +193,9 @@
 def _broadcast_blocks(own, me, n, first):
     if (n, first) == (4, 1):
         r1 = lax.ppermute(own, "gx", [(2, 0), (3, 1), (1, 2)])
-        a = jnp.where((me == 0) | (me == 2), r1, own)
-        b = jnp.where((me == 1) | (me == 0), r1, own)
-        r2 = lax.ppermute(jnp.stack([a, b]), "gx", [(0, 1), (1, 0), (2, 3), (3, 2)])
-        b1 = jnp.where(me == 1, own, jnp.where(me == 2, r1, r2[0]))
-        b2 = jnp.where(me == 0, r1, jnp.where(me == 1, r2[0], jnp.where(me == 2, own, r2[1])))
+        r2 = lax.ppermute(jnp.stack([own, r1]), "gx", [(0, 1), (1, 0), (2, 3), (3, 2)])
+        b1 = jnp.where(me == 1, own, jnp.where(me == 2, r1, jnp.where(me == 0, r2[0], r2[1])))
+        b2 = jnp.where(me == 0, r1, jnp.where(me == 1, r2[1], jnp.where(me == 2, own, r2[0])))
         b3 = jnp.where(me == 0, r2[1], jnp.where(me == 1, r1, jnp.where(me == 2, r2[0], own)))
         return jnp.concatenate([b1, b2, b3], axis=2)
     owners = list(range(first, n))

time: 137 us -> 137 us (level)
  no operation moved by 1% of the time
where the time goes in v15:
time: 137 us
  waiting for transfers between devices  50.8 us (37%)
  Pallas kernels  37.7 us (28%)
  local copies, waits for them, and re-layouts  19.4 us (14%)
  starting transfers between devices  19.2 us (14%)
  other arithmetic  8.29 us (6%)
  between operations  1.56 us (1%)
    ppermute x3, waiting for transfers between devices, on_device(): tzlo = tzhi = lax.ppermute(send_t, 'gz', both)  15.2 us
    pallas_call x3, Pallas kernels, on_device(): _vmem_call(lambda *r, last=last: _heat_kernel(last, pair, depth, t_totals...  14.8 us
    pallas_call x2, Pallas kernels, on_device(): _vmem_call(sweep, outs, 8 + len(fargs), 2)  13.5 us
    ppermute x1, waiting for transfers between devices, _broadcast_blocks(): r1 = lax.ppermute(own, 'gx', [(2, 0), (3, 1), (1, 2)])  9.98 us
    pallas_call x1, Pallas kernels, on_device(): _vmem_call(fused, outs, 9 + len(extra), 2)  9.48 us
    ppermute x1, waiting for transfers between devices, on_device(): got_t = lax.ppermute(first[2:], 'gz', both)  8.21 us
    ppermute x2, waiting for transfers between devices, on_device(): zlo = zhi = got if i == 0 else lax.ppermute(send, 'gz', both)  6.98 us
    unnamed x34, local copies, waits for them, and re-layouts  6.28 us
  transfers between devices with their start and end apart: 13, of which 10 were waited for; matrix products, arithmetic and copies ran while one was open for 8% of the time, Pallas kernels for 0%

profile of v15, /device:TPU:0, one launch (start us, length us, event | category | flops | bytes accessed | tf_op | source)
XLA Modules:
  0.0 137.0 jit_solution(16591902215740193528)
XLA Ops:
  0.6 1.6 %pad_maximum_fusion = f32[26,128,128]{2,1,0:T(8,128)S(1)} fusion(f32[2,128,128]{2,1,0:T(8,128)} %param.10, f32[8,128,128]{2,1,0:T(8,128)} %param.9, f32[16,128,128]{2,1,0:T(8,128)} %bitcast.32), kind=kLoop, calls=%fused_computation.8 | loop fusion | flops 851968 | bytes 3407872 | tf_op jit(solution)/shard_map/concatenate | solution.py:238
  2.8 1.1 copy.10
  3.9 1.4 %collective-permute-start = (f32[26,8,128]{2,1,0:T(8,128)}, f32[26,8,128]{2,1,0:T(8,128)S(1)}, u32[]{:S(2)}, u32[]{:S(2)}) collective-permute-start(f32[26,8,128]{2,1,0:T(8,128)} %copy.10), channel_id=1, source_target_pairs={{1,0},{2,1},{3,2},{5,4},{6,5},{7,6},{9,8},{10,9},{11,10},{13,12},{... | collective-permute-start | bytes 319496 | tf_op jit(solution)/shard_map/ppermute | solution.py:243
  5.4 1.1 copy.12
  6.5 3.7 %collective-permute-start.1 = (f32[26,8,128]{2,1,0:T(8,128)}, f32[26,8,128]{2,1,0:T(8,128)}, u32[]{:S(2)}, u32[]{:S(2)}) collective-permute-start(f32[26,8,128]{2,1,0:T(8,128)} %copy.12), channel_id=1, source_target_pairs={{0,1},{1,2},{2,3},{4,5},{5,6},{6,7},{8,9},{9,10},{10,11},{12,13},{... | collective-permute-start | bytes 319496 | tf_op jit(solution)/shard_map/ppermute | solution.py:242
  11.5 1.3 pad_dynamic-slice_fusion.1
  14.4 1.4 %copy.13 = f32[26,8,128]{1,2,0:T(8,128)S(1)} copy(f32[26,8,128]{2,1,0:T(8,128)} %collective-permute-done.1) | data formatting | bytes 212992 | tf_op jit(solution)/shard_map/ppermute | solution.py:242
  15.8 2.9 %maximum_maximum_fusion.rest_0_.rest_1_.ys_r = f32[34,128,256]{2,1,0:T(8,128)S(1)} fusion(f32[8,128,8]{2,1,0:T(8,128)} %pad_dynamic-slice_fusion, f32[8,128,136]{2,1,0:T(8,128)} %pad_dynamic-slice_fusion.1, f32[26,128,8]{2,1,0:T(8,128)S(1)} %bitcast.30, f32[26,128,8]{2,1,0:T(8,128)S(1)} %bitcast.29, f32[2,128,128]{2,1,0:T(8,128)S(1)} %copy-done.11, ...), kind=kLoop, calls=%fused_computation.3 | loop fusion | flops 8912896 | bytes 7032832 | tf_op jit(solution)/shard_map/concatenate | solution.py:255
  18.7 2.0 %copy-done = f32[34,128,256]{2,1,0:T(8,128)} copy-done((f32[34,128,256]{2,1,0:T(8,128)}, f32[34,128,256]{2,1,0:T(8,128)S(1)}, u32[]{:S(2)}) %copy-start) | copy-done | bytes 4456472
  20.8 1.3 collective-permute-start.2
  22.1 5.8 %collective-permute-start.3 = (f32[34,8,256]{2,1,0:T(8,128)S(1)}, f32[34,8,256]{2,1,0:T(8,128)S(1)}, u32[]{:S(2)}, u32[]{:S(2)}) collective-permute-start(f32[34,8,256]{2,1,0:T(8,128)S(1)} %get-tuple-element.26), channel_id=1, source_target_pairs={{0,4},{4,8},{8,12},{1,5},{5,9},{9,13},{2,6},{6,10},{10,14},{3,7},{... | collective-permute-start | bytes 835592 | tf_op jit(solution)/shard_map/ppermute | solution.py:257
  27.9 2.8 %gather_fusion = f32[3,128,256]{2,1,0:T(8,128)S(1)} fusion(f32[34,128,256]{2,1,0:T(8,128)} %copy-done, s32[1024]{0:T(1024)S(1)} %pad_clamp_fusion), kind=kCustom, calls=%fused_computation | custom fusion | bytes 786444 | tf_op jit(solution)/shard_map/gather | solution.py:262
  30.8 2.4 %collective-permute-done.2.rest_1_.rest_2_.yb_r = f32[34,8,256]{2,1,0:T(8,128)S(1)} collective-permute-done((f32[34,8,256]{2,1,0:T(8,128)S(1)}, f32[34,8,256]{2,1,0:T(8,128)S(1)}, u32[]{:S(2)}, u32[]{:S(2)}) %collective-permute-start.2) | collective-permute-done | bytes 278560 | tf_op jit(solution)/shard_map/ppermute | solution.py:258
  35.0 1.6 %collective-permute-start.4 = (f32[2,144,256]{2,1,0:T(8,128)S(1)}, f32[2,144,256]{2,1,0:T(8,128)S(1)}, u32[]{:S(2)}, u32[]{:S(2)}) collective-permute-start(f32[2,144,256]{2,1,0:T(8,128)S(1)} %slice.46), channel_id=1, source_target_pairs={{0,16},{16,0},{1,17},{17,1},{2,18},{18,2},{3,19},{19,3},{4,20},{20... | collective-permute-start | bytes 884744 | tf_op jit(solution)/shard_map/ppermute | solution.py:288
  39.2 4.7 %collective-permute-done.4.rest_3_.rest_4_ = f32[2,144,256]{2,1,0:T(8,128)S(1)} collective-permute-done((f32[2,144,256]{2,1,0:T(8,128)S(1)}, f32[2,144,256]{2,1,0:T(8,128)S(1)}, u32[]{:S(2)}, u32[]{:S(2)}) %collective-permute-start.4) | collective-permute-done | bytes 294944 | tf_op jit(solution)/shard_map/ppermute | solution.py:288
  44.5 6.4 %shard_map.95 = (f32[16,144,256]{2,1,0:T(8,128)}, f32[2,144,256]{2,1,0:T(8,128)}) custom-call(s32[3]{0:T(128)} %pad_add_fusion.pos_r.r_0_, f32[8]{0:T(128)} %add_divide_fusion.prof_r, f32[2,128,128]{2,1,0:T(8,128)} %pad.8.fl_r.r_1_, f32[34,128,256]{2,1,0:T(8,128)} %copy-done, f32[34,8,256]{2,1,0:T(8,128)} %copy-done.3, f32[34,8,256]{2,1,0:T(8,128)} %copy-done.4, ...), custom_call_target="tpu_custom_call" | custom-call | tf_op jit(solution)/shard_map/pallas_call | solution.py:346
  52.1 7.0 %collective-permute-done.5.rest_4_.rest_5_ = f32[2,144,256]{2,1,0:T(8,128)S(1)} collective-permute-done((f32[2,144,256]{2,1,0:T(8,128)}, f32[2,144,256]{2,1,0:T(8,128)S(1)}, u32[]{:S(2)}, u32[]{:S(2)}) %collective-permute-start.5) | collective-permute-done | bytes 294944 | tf_op jit(solution)/shard_map/ppermute | solution.py:297
  59.8 7.0 %shard_map.96 = (f32[16,144,256]{2,1,0:T(8,128)}, f32[2,144,256]{2,1,0:T(8,128)}) custom-call(s32[3]{0:T(128)} %pad_add_fusion.pos_r.r_0_, f32[8]{0:T(128)} %add_divide_fusion.prof_r, f32[2,128,128]{2,1,0:T(8,128)} %pad.8.fl_r.r_1_, f32[16,144,256]{2,1,0:T(8,128)} %get-tuple-element.14.rest_0_, f32[34,128,256]{2,1,0:T(8,128)} %copy-done, ...), custom_call_target="tpu_custom_call" | custom-call | tf_op jit(solution)/shard_map/pallas_call | solution.py:346
  67.5 1.4 %collective-permute-start.7 = (f32[1,144,256]{2,1,0:T(8,128)S(1)}, f32[1,144,256]{2,1,0:T(8,128)S(1)}, u32[]{:S(2)}, u32[]{:S(2)}) collective-permute-start(f32[1,144,256]{2,1,0:T(8,128)S(1)} %slice.47), channel_id=1, source_target_pairs={{0,16},{16,0},{1,17},{17,1},{2,18},{18,2},{3,19},{19,3},{4,20},{20... | collective-permute-start | bytes 442376 | tf_op jit(solution)/shard_map/ppermute | solution.py:289
  68.9 8.2 %collective-permute-done.7.rest_0_ = f32[1,144,256]{2,1,0:T(8,128)S(1)} collective-permute-done((f32[1,144,256]{2,1,0:T(8,128)S(1)}, f32[1,144,256]{2,1,0:T(8,128)S(1)}, u32[]{:S(2)}, u32[]{:S(2)}) %collective-permute-start.7) | collective-permute-done | bytes 147488 | tf_op jit(solution)/shard_map/ppermute | solution.py:289
  77.9 9.5 %shard_map.97 = (f32[8,144,256]{2,1,0:T(8,128)}, f32[2,8,128,128]{3,2,1,0:T(8,128)}, f32[8,144,256]{2,1,0:T(8,128)}, f32[144,256]{1,0:T(8,128)}) custom-call(s32[3]{0:T(128)} %pad_add_fusion.pos_r.r_0_, f32[8]{0:T(128)} %add_divide_fusion.prof_r, f32[2,128,128]{2,1,0:T(8,128)} %pad.8.fl_r.r_1_, f32[16,144,256]{2,1,0:T(8,128)} %get-tuple-element.16.f_r, ...), custom_call_target="tpu_custom_call" | custom-call | tf_op jit(solution)/shard_map/pallas_call | solution.py:323
  87.7 5.1 %collective-permute-done.8.r_4_.r_5_ = f32[144,256]{1,0:T(8,128)S(1)} collective-permute-done((f32[144,256]{1,0:T(8,128)}, f32[144,256]{1,0:T(8,128)S(1)}, u32[]{:S(2)}, u32[]{:S(2)}) %collective-permute-start.8) | collective-permute-done | bytes 147488 | tf_op jit(solution)/shard_map/ppermute | solution.py:356
  93.4 5.5 %shard_map.98 = (f32[8,144,256]{2,1,0:T(8,128)}, f32[144,256]{1,0:T(8,128)}) custom-call(s32[3]{0:T(128)} %pad_add_fusion.pos_r.r_0_, f32[2,128,128]{2,1,0:T(8,128)} %pad.8.fl_r.r_1_, f32[8,144,256]{2,1,0:T(8,128)} %get-tuple-element.19.r_2_, f32[8,144,256]{2,1,0:T(8,128)} %get-tuple-element.20.r_3_, f32[144,256]{1,0:T(8,128)} %copy-done.10, ...), custom_call_target="tpu_custom_call" | custom-call | tf_op jit(solution)/shard_map/pallas_call | solution.py:361
  99.2 5.1 %collective-permute-done.9.r_4_.r_5_ = f32[144,256]{1,0:T(8,128)S(1)} collective-permute-done((f32[144,256]{1,0:T(8,128)}, f32[144,256]{1,0:T(8,128)S(1)}, u32[]{:S(2)}, u32[]{:S(2)}) %collective-permute-start.9) | collective-permute-done | bytes 147488 | tf_op jit(solution)/shard_map/ppermute | solution.py:356
  105.0 5.3 %shard_map.99 = (f32[8,144,256]{2,1,0:T(8,128)}, f32[144,256]{1,0:T(8,128)}) custom-call(s32[3]{0:T(128)} %pad_add_fusion.pos_r.r_0_, f32[2,128,128]{2,1,0:T(8,128)} %pad.8.fl_r.r_1_, f32[8,144,256]{2,1,0:T(8,128)} %get-tuple-element.22.r_2_, f32[8,144,256]{2,1,0:T(8,128)} %get-tuple-element.20.r_3_, f32[144,256]{1,0:T(8,128)} %copy-done.9, f32[144,256]{1,0:T(8,128)} %copy-done.9), custom_call_target="tpu_custom_call" | custom-call | tf_op jit(solution)/shard_map/pallas_call | solution.py:361
  110.5 5.1 %collective-permute-done.10.r_4_.r_5_ = f32[144,256]{1,0:T(8,128)S(1)} collective-permute-done((f32[144,256]{1,0:T(8,128)}, f32[144,256]{1,0:T(8,128)S(1)}, u32[]{:S(2)}, u32[]{:S(2)}) %collective-permute-start.10) | collective-permute-done | bytes 147488 | tf_op jit(solution)/shard_map/ppermute | solution.py:356
  116.3 4.0 %shard_map.100 = f32[8,128,128]{2,1,0:T(8,128)} custom-call(s32[3]{0:T(128)} %pad_add_fusion.pos_r.r_0_, f32[2,128,128]{2,1,0:T(8,128)} %pad.8.fl_r.r_1_, f32[8,144,256]{2,1,0:T(8,128)} %get-tuple-element.24.r_2_, f32[8,144,256]{2,1,0:T(8,128)} %get-tuple-element.20.r_3_, f32[144,256]{1,0:T(8,128)} %copy-done.8, f32[144,256]{1,0:T(8,128)} %copy-done.8), custom_call_target="tpu_custom_call" | custom-call | tf_op jit(solution)/shard_map/pallas_call | solution.py:361
  120.2 1.4 %collective-permute-start.11 = (f32[8,128,128]{2,1,0:T(8,128)}, f32[8,128,128]{2,1,0:T(8,128)S(1)}, u32[]{:S(2)}, u32[]{:S(2)}) collective-permute-start(f32[8,128,128]{2,1,0:T(8,128)} %shard_map.100), channel_id=1, source_target_pairs={{2,0},{3,1},{1,2},{6,4},{7,5},{5,6},{10,8},{11,9},{9,10},{14,12},{... | collective-permute-start | bytes 1572872 | tf_op jit(solution)/shard_map/ppermute | solution.py:195
  121.6 10.0 %collective-permute-done.11 = f32[8,128,128]{2,1,0:T(8,128)S(1)} collective-permute-done((f32[8,128,128]{2,1,0:T(8,128)}, f32[8,128,128]{2,1,0:T(8,128)S(1)}, u32[]{:S(2)}, u32[]{:S(2)}) %collective-permute-start.11) | collective-permute-done | bytes 524320 | tf_op jit(solution)/shard_map/ppermute | solution.py:195
  131.6 1.1 pad_maximum_fusion.2
  132.8 2.6 %collective-permute-done.12 = f32[2,8,128,128]{3,2,1,0:T(8,128)S(1)} collective-permute-done((f32[2,8,128,128]{3,2,1,0:T(8,128)S(1)}, f32[2,8,128,128]{3,2,1,0:T(8,128)S(1)}, u32[]{:S(2)}, u32[]{:S(2)}) %collective-permute-start.12) | collective-permute-done | bytes 1048608 | tf_op jit(solution)/shard_map/ppermute | solution.py:196
  135.7 1.3 pad_maximum_fusion.1
  (63 shorter events, 14.4 us)
Async XLA Ops:
  3.9 7.6 %copy-start.1 = (f32[8,128,384]{2,1,0:T(8,128)S(1)}, f32[8,128,384]{2,1,0:T(8,128)}, u32[]{:S(2)}) copy-start(f32[8,128,384]{2,1,0:T(8,128)} %param.13) | copy-start | bytes 4718596
  3.9 9.9 %collective-permute-start = (f32[26,8,128]{2,1,0:T(8,128)}, f32[26,8,128]{2,1,0:T(8,128)S(1)}, u32[]{:S(2)}, u32[]{:S(2)}) collective-permute-start(f32[26,8,128]{2,1,0:T(8,128)} %copy.10), channel_id=1, source_target_pairs={{1,0},{2,1},{3,2},{5,4},{6,5},{7,6},{9,8},{10,9},{11,10},{13,12},{... | collective-permute-start | bytes 319496 | tf_op jit(solution)/shard_map/ppermute | solution.py:243
  6.5 7.9 %collective-permute-start.1 = (f32[26,8,128]{2,1,0:T(8,128)}, f32[26,8,128]{2,1,0:T(8,128)}, u32[]{:S(2)}, u32[]{:S(2)}) collective-permute-start(f32[26,8,128]{2,1,0:T(8,128)} %copy.12), channel_id=1, source_target_pairs={{0,1},{1,2},{2,3},{4,5},{5,6},{6,7},{8,9},{9,10},{10,11},{12,13},{... | collective-permute-start | bytes 319496 | tf_op jit(solution)/shard_map/ppermute | solution.py:242
  13.8 1.9 %copy-start.11 = (f32[2,128,128]{2,1,0:T(8,128)S(1)}, f32[2,128,128]{2,1,0:T(8,128)}, u32[]{:S(2)}) copy-start(f32[2,128,128]{2,1,0:T(8,128)} %param.10) | copy-start | bytes 393220
  15.8 6.3 %copy-start.14 = (s32[3]{0:T(128)S(1)}, s32[3]{0:T(128)}, u32[]{:S(2)}) copy-start(s32[3]{0:T(128)} %constant.76.clone) | copy-start | bytes 40
  15.8 6.3 %copy-start.15 = (s32[3]{0:T(128)S(1)}, s32[3]{0:T(128)}, u32[]{:S(2)}) copy-start(s32[3]{0:T(128)} %constant.77.clone) | copy-start | bytes 40
  18.7 2.0 %copy-start = (f32[34,128,256]{2,1,0:T(8,128)}, f32[34,128,256]{2,1,0:T(8,128)S(1)}, u32[]{:S(2)}) copy-start(f32[34,128,256]{2,1,0:T(8,128)S(1)} %maximum_maximum_fusion.rest_0_.rest_1_.ys_r) | copy-start | bytes 13369348
  20.7 16.5 %copy-start.13 = (s32[2,64,64]{2,1,0:T(8,128)S(1)}, s32[2,64,64]{2,1,0:T(8,128)}, u32[]{:S(2)}) copy-start(s32[2,64,64]{2,1,0:T(8,128)} %param.12) | copy-start | bytes 98308
  20.8 12.4 %collective-permute-start.2 = (f32[34,8,256]{2,1,0:T(8,128)S(1)}, f32[34,8,256]{2,1,0:T(8,128)S(1)}, u32[]{:S(2)}, u32[]{:S(2)}) collective-permute-start(f32[34,8,256]{2,1,0:T(8,128)S(1)} %get-tuple-element.27), channel_id=1, source_target_pairs={{4,0},{8,4},{12,8},{5,1},{9,5},{13,9},{6,2},{10,6},{14,10},{7,3},{... | collective-permute-start | bytes 835592 | tf_op jit(solution)/shard_map/ppermute | solution.py:258
  22.1 12.3 %collective-permute-start.3 = (f32[34,8,256]{2,1,0:T(8,128)S(1)}, f32[34,8,256]{2,1,0:T(8,128)S(1)}, u32[]{:S(2)}, u32[]{:S(2)}) collective-permute-start(f32[34,8,256]{2,1,0:T(8,128)S(1)} %get-tuple-element.26), channel_id=1, source_target_pairs={{0,4},{4,8},{8,12},{1,5},{5,9},{9,13},{2,6},{6,10},{10,14},{3,7},{... | collective-permute-start | bytes 835592 | tf_op jit(solution)/shard_map/ppermute | solution.py:257
  33.2 10.6 %copy-start.3 = (f32[34,8,256]{2,1,0:T(8,128)}, f32[34,8,256]{2,1,0:T(8,128)S(1)}, u32[]{:S(2)}) copy-start(f32[34,8,256]{2,1,0:T(8,128)S(1)} %collective-permute-done.2.rest_1_.rest_2_.yb_r) | copy-start | bytes 835588
  34.4 9.4 %copy-start.4 = (f32[34,8,256]{2,1,0:T(8,128)}, f32[34,8,256]{2,1,0:T(8,128)S(1)}, u32[]{:S(2)}) copy-start(f32[34,8,256]{2,1,0:T(8,128)S(1)} %collective-permute-done.3.rest_2_.rest_3_.ya_r) | copy-start | bytes 835588
  35.0 8.8 %collective-permute-start.4 = (f32[2,144,256]{2,1,0:T(8,128)S(1)}, f32[2,144,256]{2,1,0:T(8,128)S(1)}, u32[]{:S(2)}, u32[]{:S(2)}) collective-permute-start(f32[2,144,256]{2,1,0:T(8,128)S(1)} %slice.46), channel_id=1, source_target_pairs={{0,16},{16,0},{1,17},{17,1},{2,18},{18,2},{3,19},{19,3},{4,20},{20... | collective-permute-start | bytes 884744 | tf_op jit(solution)/shard_map/ppermute | solution.py:288
  43.8 0.7 copy-start.5
  51.0 8.1 %collective-permute-start.5 = (f32[2,144,256]{2,1,0:T(8,128)}, f32[2,144,256]{2,1,0:T(8,128)S(1)}, u32[]{:S(2)}, u32[]{:S(2)}) collective-permute-start(f32[2,144,256]{2,1,0:T(8,128)} %get-tuple-element.15), channel_id=1, source_target_pairs={{0,16},{16,0},{1,17},{17,1},{2,18},{18,2},{3,19},{19,3},{4,20},{20... | collective-permute-start | bytes 884744 | tf_op jit(solution)/shard_map/ppermute | solution.py:297
  59.1 0.7 copy-start.7
  66.8 10.3 %collective-permute-start.6 = (f32[2,144,256]{2,1,0:T(8,128)}, f32[2,144,256]{2,1,0:T(8,128)S(1)}, u32[]{:S(2)}, u32[]{:S(2)}) collective-permute-start(f32[2,144,256]{2,1,0:T(8,128)} %get-tuple-element.17), channel_id=1, source_target_pairs={{0,16},{16,0},{1,17},{17,1},{2,18},{18,2},{3,19},{19,3},{4,20},{20... | collective-permute-start | bytes 884744 | tf_op jit(solution)/shard_map/ppermute | solution.py:297
  67.5 9.6 %collective-permute-start.7 = (f32[1,144,256]{2,1,0:T(8,128)S(1)}, f32[1,144,256]{2,1,0:T(8,128)S(1)}, u32[]{:S(2)}, u32[]{:S(2)}) collective-permute-start(f32[1,144,256]{2,1,0:T(8,128)S(1)} %slice.47), channel_id=1, source_target_pairs={{0,16},{16,0},{1,17},{17,1},{2,18},{18,2},{3,19},{19,3},{4,20},{20... | collective-permute-start | bytes 442376 | tf_op jit(solution)/shard_map/ppermute | solution.py:289
  77.1 0.7 copy-start.12
  77.1 0.8 copy-start.6
  87.4 5.4 %collective-permute-start.8 = (f32[144,256]{1,0:T(8,128)}, f32[144,256]{1,0:T(8,128)S(1)}, u32[]{:S(2)}, u32[]{:S(2)}) collective-permute-start(f32[144,256]{1,0:T(8,128)} %get-tuple-element.21), channel_id=1, source_target_pairs={{0,16},{16,0},{1,17},{17,1},{2,18},{18,2},{3,19},{19,3},{4,20},{20... | collective-permute-start | bytes 442376 | tf_op jit(solution)/shard_map/ppermute | solution.py:356
  92.7 0.7 copy-start.10
  98.9 5.4 %collective-permute-start.9 = (f32[144,256]{1,0:T(8,128)}, f32[144,256]{1,0:T(8,128)S(1)}, u32[]{:S(2)}, u32[]{:S(2)}) collective-permute-start(f32[144,256]{1,0:T(8,128)} %get-tuple-element.23), channel_id=1, source_target_pairs={{0,16},{16,0},{1,17},{17,1},{2,18},{18,2},{3,19},{19,3},{4,20},{20... | collective-permute-start | bytes 442376 | tf_op jit(solution)/shard_map/ppermute | solution.py:356
  104.3 0.7 copy-start.9
  110.3 5.4 %collective-permute-start.10 = (f32[144,256]{1,0:T(8,128)}, f32[144,256]{1,0:T(8,128)S(1)}, u32[]{:S(2)}, u32[]{:S(2)}) collective-permute-start(f32[144,256]{1,0:T(8,128)} %get-tuple-element.25), channel_id=1, source_target_pairs={{0,16},{16,0},{1,17},{17,1},{2,18},{18,2},{3,19},{19,3},{4,20},{20... | collective-permute-start | bytes 442376 | tf_op jit(solution)/shard_map/ppermute | solution.py:356
  115.6 0.7 copy-start.8
  120.2 15.3 %copy-start.2 = (f32[8,128,128]{2,1,0:T(8,128)S(1)}, f32[8,128,128]{2,1,0:T(8,128)}, u32[]{:S(2)}) copy-start(f32[8,128,128]{2,1,0:T(8,128)} %shard_map.100) | copy-start | bytes 1572868
  120.2 11.4 %collective-permute-start.11 = (f32[8,128,128]{2,1,0:T(8,128)}, f32[8,128,128]{2,1,0:T(8,128)S(1)}, u32[]{:S(2)}, u32[]{:S(2)}) collective-permute-start(f32[8,128,128]{2,1,0:T(8,128)} %shard_map.100), channel_id=1, source_target_pairs={{2,0},{3,1},{1,2},{6,4},{7,5},{5,6},{10,8},{11,9},{9,10},{14,12},{... | collective-permute-start | bytes 1572872 | tf_op jit(solution)/shard_map/ppermute | solution.py:195
  132.8 2.7 %collective-permute-start.12 = (f32[2,8,128,128]{3,2,1,0:T(8,128)S(1)}, f32[2,8,128,128]{3,2,1,0:T(8,128)S(1)}, u32[]{:S(2)}, u32[]{:S(2)}) collective-permute-start(f32[2,8,128,128]{3,2,1,0:T(8,128)S(1)} %pad_maximum_fusion.2), channel_id=1, source_target_pairs={{0,1},{1,0},{2,3},{3,2},{4,5},{5,4},{6,7},{7,6},{8,9},{9,8},{10,11... | collective-permute-start | bytes 3145736 | tf_op jit(solution)/shard_map/ppermute | solution.py:196

commit v16 on v12

--- a/solution.py
+++ b/solution.py
@@ -120,7 +120,8 @@
                 oz1[1] = n1
 
 
-def _heat_kernel(last, pair, depth, totals, pos, fl, t, q, tzlo, tzhi, *outs):
+def _heat_kernel(last, pair, depth, totals, pos, fl, t, q, tzlo, tzhi, *outs, masks_in=None,
+                 masks_out=None):
     if last:
         (own,) = outs
     elif pair:
@@ -131,14 +132,22 @@
     bottom = pos[0] == 0
     height, breadth, x_first_block = totals
     rows, lanes = t.shape[1], t.shape[2]
-    sy, sx = _selectors(pos, rows, lanes, height, breadth, x_first_block)
-    zb_total = fl.shape[0]
-    below = pos[0] - 1
-    above = pos[0] + depth // MB
-    m_below = _cells(fl, jnp.maximum(below, 0), sy, sx) * jnp.where(below >= 0, 1.0, 0.0)
-    m_above = _cells(fl, jnp.minimum(above, zb_total - 1), sy, sx) * jnp.where(
-        above < zb_total, 1.0, 0.0)
-    m_own = [_cells(fl, pos[0] + zo, sy, sx) for zo in range(depth // MB)]
+    nb = depth // MB
+    if masks_in is not None:
+        m_below, m_above = masks_in[0], masks_in[nb + 1]
+        m_own = [masks_in[1 + zo] for zo in range(nb)]
+    else:
+        sy, sx = _selectors(pos, rows, lanes, height, breadth, x_first_block)
+        zb_total = fl.shape[0]
+        below = pos[0] - 1
+        above = pos[0] + nb
+        m_below = _cells(fl, jnp.maximum(below, 0), sy, sx) * jnp.where(below >= 0, 1.0, 0.0)
+        m_above = _cells(fl, jnp.minimum(above, zb_total - 1), sy, sx) * jnp.where(
+            above < zb_total, 1.0, 0.0)
+        m_own = [_cells(fl, pos[0] + zo, sy, sx) for zo in range(nb)]
+        if masks_out is not None:
+            for j, m in enumerate([m_below] + m_own + [m_above]):
+                masks_out[j] = m
     planes = [m_below] + [m_own[z // MB] for z in range(depth)] + [m_above]
     if pair:
         below_t = jnp.where(bottom, 0.0, tzlo[...])
@@ -301,8 +310,9 @@
             zlo = lax.ppermute(hi_plane, "gz", up_z)
             zhi = lax.ppermute(lo_plane, "gz", down_z)
         if last:
-            outs = (qshape, oshape, tshape, tplane) if pair else (
-                qshape, oshape, tshape, tplane, tplane)
+            mshape = jax.ShapeDtypeStruct((depth // MB + 2, rows, lanes), jnp.float32)
+            outs = (qshape, oshape, tshape, tplane, mshape) if pair else (
+                qshape, oshape, tshape, tplane, tplane, mshape)
 
             def fused(pos_r, prof_r, fl_r, f_r, ys_r, yb_r, ya_r, zlo_r, zhi_r, *rest,
                       factor=factor):
@@ -319,12 +329,12 @@
                 _em_kernel(factor, True, pair, depth, em_totals, pos_r, prof_r, fl_r, f_r, mat_r,
                            w_r, zlo_r, zhi_r, q_r, own_r)
                 _heat_kernel(False, pair, depth, t_totals, pos_r, fl_r, t_r, q_r, tzlo_r, tzhi_r,
-                             *outs_r[2:])
+                             *outs_r[2:-1], masks_out=outs_r[-1])
 
             extra = (got_t,) if pair else (tzlo0, tzhi0)
             res = _vmem_call(fused, outs, 9 + len(extra), 2)(
                 pos, profile, flags, field, *pieces, zlo, zhi, *extra)
-            heat, field_out, kelvin = res[0], res[1], res[2]
+            heat, field_out, kelvin, t_masks = res[0], res[1], res[2], res[-1]
             if pair:
                 send_t = res[3]
             else:
@@ -361,8 +371,9 @@
             tzhi = lax.ppermute(lo_t, "gz", down_z)
         outs = (town,) if last else (tshape, tplane) if pair else (tshape, tplane, tplane)
         res = _vmem_call(
-            lambda *r, last=last: _heat_kernel(last, pair, depth, t_totals, *r), outs, 6, 1
-        )(pos, flags, kelvin, heat, tzlo, tzhi)
+            lambda *r, last=last: _heat_kernel(
+                last, pair, depth, t_totals, *r[:6], *r[7:], masks_in=r[6]), outs, 7, 1
+        )(pos, flags, kelvin, heat, tzlo, tzhi, t_masks)
         if last:
             (own_t,) = res
         elif pair:

time: 137 us -> 138 us (level)
  no operation moved by 1% of the time
where the time goes in v16:
time: 138 us
  waiting for transfers between devices  50.9 us (37%)
  Pallas kernels  38.5 us (28%)
  local copies, waits for them, and re-layouts  19.4 us (14%)
  starting transfers between devices  19.1 us (14%)
  other arithmetic  8.3 us (6%)
  between operations  1.58 us (1%)
    ppermute x3, waiting for transfers between devices, on_device(): tzlo = tzhi = lax.ppermute(send_t, 'gz', both)  15.2 us
    pallas_call x3, Pallas kernels, on_device(): _vmem_call(lambda *r, last=last: _heat_kernel(last, pair, depth, t_totals...  15 us
    pallas_call x2, Pallas kernels, on_device(): _vmem_call(sweep, outs, 8 + len(fargs), 2)  13.5 us
    pallas_call x1, Pallas kernels, on_device(): _vmem_call(fused, outs, 9 + len(extra), 2)  10.1 us
    ppermute x1, waiting for transfers between devices, _broadcast_blocks(): r1 = lax.ppermute(own, 'gx', [(2, 0), (3, 1), (1, 2)])  9.96 us
    ppermute x1, waiting for transfers between devices, on_device(): got_t = lax.ppermute(first[2:], 'gz', both)  8.21 us
    ppermute x2, waiting for transfers between devices, on_device(): zlo = zhi = got if i == 0 else lax.ppermute(send, 'gz', both)  6.99 us
    unnamed x34, local copies, waits for them, and re-layouts  6.31 us
  transfers between devices with their start and end apart: 13, of which 10 were waited for; matrix products, arithmetic and copies ran while one was open for 8% of the time, Pallas kernels for 0%

profile of v16, /device:TPU:0, one launch (start us, length us, event | category | flops | bytes accessed | tf_op | source)
XLA Modules:
  0.0 137.7 jit_solution(13340261989026354639)
XLA Ops:
  0.6 1.6 %pad_maximum_fusion = f32[26,128,128]{2,1,0:T(8,128)S(1)} fusion(f32[2,128,128]{2,1,0:T(8,128)} %param.10, f32[8,128,128]{2,1,0:T(8,128)} %param.9, f32[16,128,128]{2,1,0:T(8,128)} %bitcast.31), kind=kLoop, calls=%fused_computation.8 | loop fusion | flops 851968 | bytes 3407872 | tf_op jit(solution)/shard_map/concatenate | solution.py:249
  2.8 1.1 copy.10
  3.9 1.4 %collective-permute-start = (f32[26,8,128]{2,1,0:T(8,128)}, f32[26,8,128]{2,1,0:T(8,128)S(1)}, u32[]{:S(2)}, u32[]{:S(2)}) collective-permute-start(f32[26,8,128]{2,1,0:T(8,128)} %copy.10), channel_id=1, source_target_pairs={{1,0},{2,1},{3,2},{5,4},{6,5},{7,6},{9,8},{10,9},{11,10},{13,12},{... | collective-permute-start | bytes 319496 | tf_op jit(solution)/shard_map/ppermute | solution.py:254
  5.3 1.1 copy.12
  6.5 3.7 %collective-permute-start.1 = (f32[26,8,128]{2,1,0:T(8,128)}, f32[26,8,128]{2,1,0:T(8,128)}, u32[]{:S(2)}, u32[]{:S(2)}) collective-permute-start(f32[26,8,128]{2,1,0:T(8,128)} %copy.12), channel_id=1, source_target_pairs={{0,1},{1,2},{2,3},{4,5},{5,6},{6,7},{8,9},{9,10},{10,11},{12,13},{... | collective-permute-start | bytes 319496 | tf_op jit(solution)/shard_map/ppermute | solution.py:253
  11.5 1.3 pad_dynamic-slice_fusion.1
  14.3 1.4 %copy.13 = f32[26,8,128]{1,2,0:T(8,128)S(1)} copy(f32[26,8,128]{2,1,0:T(8,128)} %collective-permute-done.1) | data formatting | bytes 212992 | tf_op jit(solution)/shard_map/ppermute | solution.py:253
  15.8 2.9 %maximum_maximum_fusion.rest_0_.rest_1_.ys_r = f32[34,128,256]{2,1,0:T(8,128)S(1)} fusion(f32[8,128,8]{2,1,0:T(8,128)} %pad_dynamic-slice_fusion, f32[8,128,136]{2,1,0:T(8,128)} %pad_dynamic-slice_fusion.1, f32[26,128,8]{2,1,0:T(8,128)S(1)} %bitcast.30, f32[26,128,8]{2,1,0:T(8,128)S(1)} %bitcast.29, f32[2,128,128]{2,1,0:T(8,128)S(1)} %copy-done.11, ...), kind=kLoop, calls=%fused_computation.3 | loop fusion | flops 8912896 | bytes 7032832 | tf_op jit(solution)/shard_map/concatenate | solution.py:266
  18.7 2.0 %copy-done = f32[34,128,256]{2,1,0:T(8,128)} copy-done((f32[34,128,256]{2,1,0:T(8,128)}, f32[34,128,256]{2,1,0:T(8,128)S(1)}, u32[]{:S(2)}) %copy-start) | copy-done | bytes 4456472
  20.7 1.3 collective-permute-start.2
  22.1 5.8 %collective-permute-start.3 = (f32[34,8,256]{2,1,0:T(8,128)S(1)}, f32[34,8,256]{2,1,0:T(8,128)S(1)}, u32[]{:S(2)}, u32[]{:S(2)}) collective-permute-start(f32[34,8,256]{2,1,0:T(8,128)S(1)} %get-tuple-element.28), channel_id=1, source_target_pairs={{0,4},{4,8},{8,12},{1,5},{5,9},{9,13},{2,6},{6,10},{10,14},{3,7},{... | collective-permute-start | bytes 835592 | tf_op jit(solution)/shard_map/ppermute | solution.py:268
  27.9 2.8 %gather_fusion = f32[3,128,256]{2,1,0:T(8,128)S(1)} fusion(f32[34,128,256]{2,1,0:T(8,128)} %copy-done, s32[1024]{0:T(1024)S(1)} %pad_clamp_fusion), kind=kCustom, calls=%fused_computation | custom fusion | bytes 786444 | tf_op jit(solution)/shard_map/gather | solution.py:273
  30.7 2.4 %collective-permute-done.2.rest_1_.rest_2_.yb_r = f32[34,8,256]{2,1,0:T(8,128)S(1)} collective-permute-done((f32[34,8,256]{2,1,0:T(8,128)S(1)}, f32[34,8,256]{2,1,0:T(8,128)S(1)}, u32[]{:S(2)}, u32[]{:S(2)}) %collective-permute-start.2) | collective-permute-done | bytes 278560 | tf_op jit(solution)/shard_map/ppermute | solution.py:269
  35.0 1.6 %collective-permute-start.4 = (f32[2,144,256]{2,1,0:T(8,128)S(1)}, f32[2,144,256]{2,1,0:T(8,128)S(1)}, u32[]{:S(2)}, u32[]{:S(2)}) collective-permute-start(f32[2,144,256]{2,1,0:T(8,128)S(1)} %slice.45), channel_id=1, source_target_pairs={{0,16},{16,0},{1,17},{17,1},{2,18},{18,2},{3,19},{19,3},{4,20},{20... | collective-permute-start | bytes 884744 | tf_op jit(solution)/shard_map/ppermute | solution.py:299
  39.0 4.8 %collective-permute-done.4.rest_3_.rest_4_ = f32[2,144,256]{2,1,0:T(8,128)S(1)} collective-permute-done((f32[2,144,256]{2,1,0:T(8,128)S(1)}, f32[2,144,256]{2,1,0:T(8,128)S(1)}, u32[]{:S(2)}, u32[]{:S(2)}) %collective-permute-start.4) | collective-permute-done | bytes 294944 | tf_op jit(solution)/shard_map/ppermute | solution.py:299
  44.5 6.4 %shard_map.95 = (f32[16,144,256]{2,1,0:T(8,128)}, f32[2,144,256]{2,1,0:T(8,128)}) custom-call(s32[3]{0:T(128)} %pad_add_fusion.pos_r.r_0_, f32[8]{0:T(128)} %add_divide_fusion.prof_r, f32[2,128,128]{2,1,0:T(8,128)} %pad.8.fl_r.r_1_, f32[34,128,256]{2,1,0:T(8,128)} %copy-done, f32[34,8,256]{2,1,0:T(8,128)} %copy-done.3, f32[34,8,256]{2,1,0:T(8,128)} %copy-done.4, ...), custom_call_target="tpu_custom_call" | custom-call | tf_op jit(solution)/shard_map/pallas_call | solution.py:358
  52.0 7.0 %collective-permute-done.5.rest_4_.rest_5_ = f32[2,144,256]{2,1,0:T(8,128)S(1)} collective-permute-done((f32[2,144,256]{2,1,0:T(8,128)}, f32[2,144,256]{2,1,0:T(8,128)S(1)}, u32[]{:S(2)}, u32[]{:S(2)}) %collective-permute-start.5) | collective-permute-done | bytes 294944 | tf_op jit(solution)/shard_map/ppermute | solution.py:308
  59.7 7.1 %shard_map.96 = (f32[16,144,256]{2,1,0:T(8,128)}, f32[2,144,256]{2,1,0:T(8,128)}) custom-call(s32[3]{0:T(128)} %pad_add_fusion.pos_r.r_0_, f32[8]{0:T(128)} %add_divide_fusion.prof_r, f32[2,128,128]{2,1,0:T(8,128)} %pad.8.fl_r.r_1_, f32[16,144,256]{2,1,0:T(8,128)} %get-tuple-element.15.rest_0_, f32[34,128,256]{2,1,0:T(8,128)} %copy-done, ...), custom_call_target="tpu_custom_call" | custom-call | tf_op jit(solution)/shard_map/pallas_call | solution.py:358
  67.5 1.5 %collective-permute-start.7 = (f32[1,144,256]{2,1,0:T(8,128)S(1)}, f32[1,144,256]{2,1,0:T(8,128)S(1)}, u32[]{:S(2)}, u32[]{:S(2)}) collective-permute-start(f32[1,144,256]{2,1,0:T(8,128)S(1)} %slice.46), channel_id=1, source_target_pairs={{0,16},{16,0},{1,17},{17,1},{2,18},{18,2},{3,19},{19,3},{4,20},{20... | collective-permute-start | bytes 442376 | tf_op jit(solution)/shard_map/ppermute | solution.py:300
  68.9 8.2 %collective-permute-done.7.rest_0_ = f32[1,144,256]{2,1,0:T(8,128)S(1)} collective-permute-done((f32[1,144,256]{2,1,0:T(8,128)S(1)}, f32[1,144,256]{2,1,0:T(8,128)S(1)}, u32[]{:S(2)}, u32[]{:S(2)}) %collective-permute-start.7) | collective-permute-done | bytes 147488 | tf_op jit(solution)/shard_map/ppermute | solution.py:300
  77.9 10.1 %shard_map.97 = (f32[8,144,256]{2,1,0:T(8,128)}, f32[2,8,128,128]{3,2,1,0:T(8,128)}, f32[8,144,256]{2,1,0:T(8,128)}, f32[144,256]{1,0:T(8,128)}, f32[3,144,256]{2,1,0:T(8,128)}) custom-call(s32[3]{0:T(128)} %pad_add_fusion.pos_r.r_0_, f32[8]{0:T(128)} %add_divide_fusion.prof_r, f32[2,128,128]{2,1,0:T(8,128)} %pad.8.fl_r.r_1_, ...), custom_call_target="tpu_custom_call" | custom-call | tf_op jit(solution)/shard_map/pallas_call | solution.py:335
  88.3 5.1 %collective-permute-done.8.r_4_.r_5_ = f32[144,256]{1,0:T(8,128)S(1)} collective-permute-done((f32[144,256]{1,0:T(8,128)}, f32[144,256]{1,0:T(8,128)S(1)}, u32[]{:S(2)}, u32[]{:S(2)}) %collective-permute-start.8) | collective-permute-done | bytes 147488 | tf_op jit(solution)/shard_map/ppermute | solution.py:368
  94.0 5.6 %shard_map.98 = (f32[8,144,256]{2,1,0:T(8,128)}, f32[144,256]{1,0:T(8,128)}) custom-call(s32[3]{0:T(128)} %pad_add_fusion.pos_r.r_0_, f32[2,128,128]{2,1,0:T(8,128)} %pad.8.fl_r.r_1_, f32[8,144,256]{2,1,0:T(8,128)} %get-tuple-element.20.r_2_, f32[8,144,256]{2,1,0:T(8,128)} %get-tuple-element.21.r_3_, f32[144,256]{1,0:T(8,128)} %copy-done.10, ...), custom_call_target="tpu_custom_call" | custom-call | tf_op jit(solution)/shard_map/pallas_call | solution.py:373
  99.9 5.1 %collective-permute-done.9.r_4_.r_5_ = f32[144,256]{1,0:T(8,128)S(1)} collective-permute-done((f32[144,256]{1,0:T(8,128)}, f32[144,256]{1,0:T(8,128)S(1)}, u32[]{:S(2)}, u32[]{:S(2)}) %collective-permute-start.9) | collective-permute-done | bytes 147488 | tf_op jit(solution)/shard_map/ppermute | solution.py:368
  105.6 5.4 %shard_map.99 = (f32[8,144,256]{2,1,0:T(8,128)}, f32[144,256]{1,0:T(8,128)}) custom-call(s32[3]{0:T(128)} %pad_add_fusion.pos_r.r_0_, f32[2,128,128]{2,1,0:T(8,128)} %pad.8.fl_r.r_1_, f32[8,144,256]{2,1,0:T(8,128)} %get-tuple-element.24.r_2_, f32[8,144,256]{2,1,0:T(8,128)} %get-tuple-element.21.r_3_, f32[144,256]{1,0:T(8,128)} %copy-done.9, ...), custom_call_target="tpu_custom_call" | custom-call | tf_op jit(solution)/shard_map/pallas_call | solution.py:373
  111.3 5.1 %collective-permute-done.10.r_4_.r_5_ = f32[144,256]{1,0:T(8,128)S(1)} collective-permute-done((f32[144,256]{1,0:T(8,128)}, f32[144,256]{1,0:T(8,128)S(1)}, u32[]{:S(2)}, u32[]{:S(2)}) %collective-permute-start.10) | collective-permute-done | bytes 147488 | tf_op jit(solution)/shard_map/ppermute | solution.py:368
  117.0 4.0 %shard_map.100 = f32[8,128,128]{2,1,0:T(8,128)} custom-call(s32[3]{0:T(128)} %pad_add_fusion.pos_r.r_0_, f32[2,128,128]{2,1,0:T(8,128)} %pad.8.fl_r.r_1_, f32[8,144,256]{2,1,0:T(8,128)} %get-tuple-element.26.r_2_, f32[8,144,256]{2,1,0:T(8,128)} %get-tuple-element.21.r_3_, f32[144,256]{1,0:T(8,128)} %copy-done.8, f32[144,256]{1,0:T(8,128)} %copy-done.8, ...), custom_call_target="tpu_custom_call" | custom-call | tf_op jit(solution)/shard_map/pallas_call | solution.py:373
  121.0 1.3 collective-permute-start.11
  122.3 10.0 %collective-permute-done.11 = f32[8,128,128]{2,1,0:T(8,128)S(1)} collective-permute-done((f32[8,128,128]{2,1,0:T(8,128)}, f32[8,128,128]{2,1,0:T(8,128)S(1)}, u32[]{:S(2)}, u32[]{:S(2)}) %collective-permute-start.11) | collective-permute-done | bytes 524320 | tf_op jit(solution)/shard_map/ppermute | solution.py:204
  132.3 1.1 select_bitcast_fusion.1
  133.6 2.6 %collective-permute-done.12 = f32[2,8,128,128]{3,2,1,0:T(8,128)S(1)} collective-permute-done((f32[2,8,128,128]{3,2,1,0:T(8,128)S(1)}, f32[2,8,128,128]{3,2,1,0:T(8,128)S(1)}, u32[]{:S(2)}, u32[]{:S(2)}) %collective-permute-start.12) | collective-permute-done | bytes 1048608 | tf_op jit(solution)/shard_map/ppermute | solution.py:207
  136.4 1.3 pad_maximum_fusion.1
  (64 shorter events, 14.3 us)
Async XLA Ops:
  3.9 7.6 %copy-start.1 = (f32[8,128,384]{2,1,0:T(8,128)S(1)}, f32[8,128,384]{2,1,0:T(8,128)}, u32[]{:S(2)}) copy-start(f32[8,128,384]{2,1,0:T(8,128)} %param.13) | copy-start | bytes 4718596
  3.9 9.9 %collective-permute-start = (f32[26,8,128]{2,1,0:T(8,128)}, f32[26,8,128]{2,1,0:T(8,128)S(1)}, u32[]{:S(2)}, u32[]{:S(2)}) collective-permute-start(f32[26,8,128]{2,1,0:T(8,128)} %copy.10), channel_id=1, source_target_pairs={{1,0},{2,1},{3,2},{5,4},{6,5},{7,6},{9,8},{10,9},{11,10},{13,12},{... | collective-permute-start | bytes 319496 | tf_op jit(solution)/shard_map/ppermute | solution.py:254
  6.5 7.9 %collective-permute-start.1 = (f32[26,8,128]{2,1,0:T(8,128)}, f32[26,8,128]{2,1,0:T(8,128)}, u32[]{:S(2)}, u32[]{:S(2)}) collective-permute-start(f32[26,8,128]{2,1,0:T(8,128)} %copy.12), channel_id=1, source_target_pairs={{0,1},{1,2},{2,3},{4,5},{5,6},{6,7},{8,9},{9,10},{10,11},{12,13},{... | collective-permute-start | bytes 319496 | tf_op jit(solution)/shard_map/ppermute | solution.py:253
  13.8 1.9 %copy-start.11 = (f32[2,128,128]{2,1,0:T(8,128)S(1)}, f32[2,128,128]{2,1,0:T(8,128)}, u32[]{:S(2)}) copy-start(f32[2,128,128]{2,1,0:T(8,128)} %param.10) | copy-start | bytes 393220
  15.7 6.3 %copy-start.14 = (s32[3]{0:T(128)S(1)}, s32[3]{0:T(128)}, u32[]{:S(2)}) copy-start(s32[3]{0:T(128)} %constant.76.clone) | copy-start | bytes 40
  15.7 6.3 %copy-start.15 = (s32[3]{0:T(128)S(1)}, s32[3]{0:T(128)}, u32[]{:S(2)}) copy-start(s32[3]{0:T(128)} %constant.77.clone) | copy-start | bytes 40
  18.6 2.1 %copy-start = (f32[34,128,256]{2,1,0:T(8,128)}, f32[34,128,256]{2,1,0:T(8,128)S(1)}, u32[]{:S(2)}) copy-start(f32[34,128,256]{2,1,0:T(8,128)S(1)} %maximum_maximum_fusion.rest_0_.rest_1_.ys_r) | copy-start | bytes 13369348
  20.7 16.5 %copy-start.13 = (s32[2,64,64]{2,1,0:T(8,128)S(1)}, s32[2,64,64]{2,1,0:T(8,128)}, u32[]{:S(2)}) copy-start(s32[2,64,64]{2,1,0:T(8,128)} %param.12) | copy-start | bytes 98308
  20.7 12.4 %collective-permute-start.2 = (f32[34,8,256]{2,1,0:T(8,128)S(1)}, f32[34,8,256]{2,1,0:T(8,128)S(1)}, u32[]{:S(2)}, u32[]{:S(2)}) collective-permute-start(f32[34,8,256]{2,1,0:T(8,128)S(1)} %get-tuple-element.29), channel_id=1, source_target_pairs={{4,0},{8,4},{12,8},{5,1},{9,5},{13,9},{6,2},{10,6},{14,10},{7,3},{... | collective-permute-start | bytes 835592 | tf_op jit(solution)/shard_map/ppermute | solution.py:269
  22.1 12.3 %collective-permute-start.3 = (f32[34,8,256]{2,1,0:T(8,128)S(1)}, f32[34,8,256]{2,1,0:T(8,128)S(1)}, u32[]{:S(2)}, u32[]{:S(2)}) collective-permute-start(f32[34,8,256]{2,1,0:T(8,128)S(1)} %get-tuple-element.28), channel_id=1, source_target_pairs={{0,4},{4,8},{8,12},{1,5},{5,9},{9,13},{2,6},{6,10},{10,14},{3,7},{... | collective-permute-start | bytes 835592 | tf_op jit(solution)/shard_map/ppermute | solution.py:268
  33.2 10.6 %copy-start.3 = (f32[34,8,256]{2,1,0:T(8,128)}, f32[34,8,256]{2,1,0:T(8,128)S(1)}, u32[]{:S(2)}) copy-start(f32[34,8,256]{2,1,0:T(8,128)S(1)} %collective-permute-done.2.rest_1_.rest_2_.yb_r) | copy-start | bytes 835588
  34.4 9.4 %copy-start.4 = (f32[34,8,256]{2,1,0:T(8,128)}, f32[34,8,256]{2,1,0:T(8,128)S(1)}, u32[]{:S(2)}) copy-start(f32[34,8,256]{2,1,0:T(8,128)S(1)} %collective-permute-done.3.rest_2_.rest_3_.ya_r) | copy-start | bytes 835588
  35.0 8.8 %collective-permute-start.4 = (f32[2,144,256]{2,1,0:T(8,128)S(1)}, f32[2,144,256]{2,1,0:T(8,128)S(1)}, u32[]{:S(2)}, u32[]{:S(2)}) collective-permute-start(f32[2,144,256]{2,1,0:T(8,128)S(1)} %slice.45), channel_id=1, source_target_pairs={{0,16},{16,0},{1,17},{17,1},{2,18},{18,2},{3,19},{19,3},{4,20},{20... | collective-permute-start | bytes 884744 | tf_op jit(solution)/shard_map/ppermute | solution.py:299
  43.8 0.7 copy-start.5
  50.9 8.1 %collective-permute-start.5 = (f32[2,144,256]{2,1,0:T(8,128)}, f32[2,144,256]{2,1,0:T(8,128)S(1)}, u32[]{:S(2)}, u32[]{:S(2)}) collective-permute-start(f32[2,144,256]{2,1,0:T(8,128)} %get-tuple-element.16), channel_id=1, source_target_pairs={{0,16},{16,0},{1,17},{17,1},{2,18},{18,2},{3,19},{19,3},{4,20},{20... | collective-permute-start | bytes 884744 | tf_op jit(solution)/shard_map/ppermute | solution.py:308
  59.0 0.7 copy-start.7
  66.8 10.3 %collective-permute-start.6 = (f32[2,144,256]{2,1,0:T(8,128)}, f32[2,144,256]{2,1,0:T(8,128)S(1)}, u32[]{:S(2)}, u32[]{:S(2)}) collective-permute-start(f32[2,144,256]{2,1,0:T(8,128)} %get-tuple-element.18), channel_id=1, source_target_pairs={{0,16},{16,0},{1,17},{17,1},{2,18},{18,2},{3,19},{19,3},{4,20},{20... | collective-permute-start | bytes 884744 | tf_op jit(solution)/shard_map/ppermute | solution.py:308
  67.5 9.7 %collective-permute-start.7 = (f32[1,144,256]{2,1,0:T(8,128)S(1)}, f32[1,144,256]{2,1,0:T(8,128)S(1)}, u32[]{:S(2)}, u32[]{:S(2)}) collective-permute-start(f32[1,144,256]{2,1,0:T(8,128)S(1)} %slice.46), channel_id=1, source_target_pairs={{0,16},{16,0},{1,17},{17,1},{2,18},{18,2},{3,19},{19,3},{4,20},{20... | collective-permute-start | bytes 442376 | tf_op jit(solution)/shard_map/ppermute | solution.py:300
  77.1 0.7 copy-start.12
  77.1 0.8 copy-start.6
  88.0 5.4 %collective-permute-start.8 = (f32[144,256]{1,0:T(8,128)}, f32[144,256]{1,0:T(8,128)S(1)}, u32[]{:S(2)}, u32[]{:S(2)}) collective-permute-start(f32[144,256]{1,0:T(8,128)} %get-tuple-element.22), channel_id=1, source_target_pairs={{0,16},{16,0},{1,17},{17,1},{2,18},{18,2},{3,19},{19,3},{4,20},{20... | collective-permute-start | bytes 442376 | tf_op jit(solution)/shard_map/ppermute | solution.py:368
  93.4 0.7 copy-start.10
  99.6 5.4 %collective-permute-start.9 = (f32[144,256]{1,0:T(8,128)}, f32[144,256]{1,0:T(8,128)S(1)}, u32[]{:S(2)}, u32[]{:S(2)}) collective-permute-start(f32[144,256]{1,0:T(8,128)} %get-tuple-element.25), channel_id=1, source_target_pairs={{0,16},{16,0},{1,17},{17,1},{2,18},{18,2},{3,19},{19,3},{4,20},{20... | collective-permute-start | bytes 442376 | tf_op jit(solution)/shard_map/ppermute | solution.py:368
  105.0 0.7 copy-start.9
  111.0 5.4 %collective-permute-start.10 = (f32[144,256]{1,0:T(8,128)}, f32[144,256]{1,0:T(8,128)S(1)}, u32[]{:S(2)}, u32[]{:S(2)}) collective-permute-start(f32[144,256]{1,0:T(8,128)} %get-tuple-element.27), channel_id=1, source_target_pairs={{0,16},{16,0},{1,17},{17,1},{2,18},{18,2},{3,19},{19,3},{4,20},{20... | collective-permute-start | bytes 442376 | tf_op jit(solution)/shard_map/ppermute | solution.py:368
  116.3 0.6 copy-start.8
  121.0 11.3 %collective-permute-start.11 = (f32[8,128,128]{2,1,0:T(8,128)}, f32[8,128,128]{2,1,0:T(8,128)S(1)}, u32[]{:S(2)}, u32[]{:S(2)}) collective-permute-start(f32[8,128,128]{2,1,0:T(8,128)} %shard_map.100), channel_id=1, source_target_pairs={{2,0},{3,1},{1,2},{6,4},{7,5},{5,6},{10,8},{11,9},{9,10},{14,12},{... | collective-permute-start | bytes 1572872 | tf_op jit(solution)/shard_map/ppermute | solution.py:204
  122.3 13.9 %copy-start.2 = (f32[8,128,128]{2,1,0:T(8,128)S(1)}, f32[8,128,128]{2,1,0:T(8,128)}, u32[]{:S(2)}) copy-start(f32[8,128,128]{2,1,0:T(8,128)} %shard_map.100) | copy-start | bytes 1572868
  133.5 2.7 %collective-permute-start.12 = (f32[2,8,128,128]{3,2,1,0:T(8,128)S(1)}, f32[2,8,128,128]{3,2,1,0:T(8,128)S(1)}, u32[]{:S(2)}, u32[]{:S(2)}) collective-permute-start(f32[2,8,128,128]{3,2,1,0:T(8,128)S(1)} %pad_maximum_fusion.2), channel_id=1, source_target_pairs={{0,1},{1,0},{2,3},{3,2},{4,5},{5,4},{6,7},{7,6},{8,9},{9,8},{10,11... | collective-permute-start | bytes 3145736 | tf_op jit(solution)/shard_map/ppermute | solution.py:207
